TPU v7x, 32 devices: a whole 2x2x4 slice. The times are simulated.
32 devices in a mesh: sec: 4 (over y, x), tile: 8 (over z, core).
Axes of the slice: x: 2, y: 2, z: 4, core: 2. Of those that a mesh axis runs over, the one named last changes fastest.
Arguments:
- tracers: bfloat16 [4, 72, 32, 1024], P(None, None, 'sec', 'tile'), may hold values from -6 to 6
- courant: bfloat16 [2, 72, 32, 1024], P(None, None, 'sec', 'tile'), may hold values from -0.44921875 to 0.44921875
- destination: int32 [32, 8], P(('sec', 'tile')), may hold values from 0 to 7, each once within a row
- diffusion: bfloat16 [32, 72, 72], P(('sec', 'tile')), may hold values from 0 to 1.25
- band: int32 [32], P(('sec', 'tile')), may hold values from 0 to 15
- band_table: bfloat16 [16, 72, 72], replicated, may hold values from -0.75 to 0.75
Outputs:
- column_state: bfloat16 [4, 72, 256, 128], P(None, None, ('sec', 'tile'))
Inputs may be any that keep to these rules, and one draw needn't show every extreme that they name: Each row of destination names every column block of its group once.
All inputs are finite; a program needn't handle non-finite values.
Results may differ from a plain program's by a relative error of at most 0.0066.
Values may be sent and summed in bfloat16 or wider, within the bound.
No kernel may reach another device: no remote copies, remote signals or barrier semaphores. Data moves between devices by JAX's collectives and lax.ppermute only.
A program may use at most 128 MiB of HBM per device.

v0:
```python
import jax
import jax.numpy as jnp
from jax import lax
from jax.sharding import PartitionSpec as P

STEPS = 3


def with_halo(cells, sides, width):
    for axis, dim in sides:
        count = lax.axis_size(axis)
        head = lax.slice_in_dim(cells, 0, width, axis=dim)
        tail = lax.slice_in_dim(cells, cells.shape[dim] - width, cells.shape[dim], axis=dim)
        cells = jnp.concatenate(
            [
                lax.ppermute(tail, axis, [(i, (i + 1) % count) for i in range(count)]),
                cells,
                lax.ppermute(head, axis, [((i + 1) % count, i) for i in range(count)]),
            ],
            axis=dim,
        )
    return cells


def advect_tile(padded, courant):
    centre = padded[:, :, 1:-1, 1:-1].astype(jnp.float32)
    north = padded[:, :, 2:, 1:-1].astype(jnp.float32)
    south = padded[:, :, :-2, 1:-1].astype(jnp.float32)
    east = padded[:, :, 1:-1, 2:].astype(jnp.float32)
    west = padded[:, :, 1:-1, :-2].astype(jnp.float32)
    cx = courant[0].astype(jnp.float32)
    cy = courant[1].astype(jnp.float32)
    out = centre - 0.5 * cx * (north - south) + 0.5 * cx * cx * (north - 2.0 * centre + south)
    out = out - 0.5 * cy * (east - west) + 0.5 * cy * cy * (east - 2.0 * centre + west)
    return out.astype(jnp.bfloat16)


def substep(field, courant):
    padded = with_halo(field, (("sec", 2), ("tile", 3)), 1)
    return advect_tile(padded, courant)


def per_device(tracers, courant, destination, diffusion, band, band_table):
    advected = tracers
    for step in range(STEPS):
        advected = substep(advected, courant)
    order = jnp.argsort(destination[0])
    band_count = band_table.shape[0]
    ordered = jnp.take(advected, order, axis=2)
    received = lax.all_to_all(ordered, "tile", split_axis=2, concat_axis=2, tiled=True)
    inverse = diffusion[0]
    diffused = jnp.einsum("kl,tlxy->tkxy", inverse, received, preferred_element_type=jnp.float32)
    diffused16 = diffused.astype(jnp.bfloat16)
    picked = (jnp.arange(band_count, dtype=jnp.int32) == band[0])[:, None, None]
    radiation = jnp.sum(jnp.where(picked, band_table, jnp.zeros_like(band_table)), axis=0)
    heating = jnp.einsum("kl,tlxy->tkxy", radiation, diffused16, preferred_element_type=jnp.float32)
    return (diffused + heating).astype(jnp.bfloat16)


def solution(mesh):
    placed = (
        P(None, None, "sec", "tile"),
        P(None, None, "sec", "tile"),
        P(("sec", "tile"), None),
        P(("sec", "tile"), None, None),
        P(("sec", "tile")),
        P(),
    )
    return jax.shard_map(
        per_device,
        mesh=mesh,
        in_specs=placed,
        out_specs=P(None, None, ("sec", "tile"), None),
        check_vma=False,
    )
```

profile of v0, /device:TPU:0, one launch (start us, length us, event | category | flops | bytes accessed | tf_op | source)
XLA Modules:
  0.0 81.5 jit_solution(5658749465886377989)
XLA Ops:
  0.0 1.2 %copy.20 = bf16[4,72,8,128]{3,1,2,0:T(8,128)(2,1)S(1)} copy(bf16[4,72,8,128]{3,2,1,0:T(8,128)(2,1)} %param.6) | data formatting | bytes 1179648 | tf_op args[0]
  1.2 3.0 %collective-permute-start.1 = (bf16[4,72,1,128]{3,1,2,0:T(8,128)(2,1)S(1)}, bf16[4,72,1,128]{3,1,2,0:T(8,128)(2,1)S(1)}, u32[]{:S(2)}, u32[]{:S(2)}) collective-permute-start(bf16[4,72,1,128]{3,1,2,0:T(8,128)(2,1)S(1)} %get-tuple-element.18), channel_id=1, source_target_pairs={{0,8},{8,16},{16,24},{24,0},{1,9},{9,17},{17,25},{25,1},{2,10},{10... | collective-permute-start | bytes 221192 | tf_op jit(solution)/shard_map/ppermute | solution.py:16
  4.2 1.0 %collective-permute-start = (bf16[4,72,1,128]{3,1,2,0:T(8,128)(2,1)S(1)}, bf16[4,72,1,128]{3,1,2,0:T(8,128)(2,1)S(1)}, u32[]{:S(2)}, u32[]{:S(2)}) collective-permute-start(bf16[4,72,1,128]{3,1,2,0:T(8,128)(2,1)S(1)} %get-tuple-element.17), channel_id=1, source_target_pairs={{8,0},{16,8},{24,16},{0,24},{9,1},{17,9},{25,17},{1,25},{10,2},{18... | collective-permute-start | bytes 221192 | tf_op jit(solution)/shard_map/ppermute | solution.py:18
  5.3 2.5 %collective-permute-done.1 = bf16[4,72,1,128]{3,1,2,0:T(8,128)(2,1)S(1)} collective-permute-done((bf16[4,72,1,128]{3,1,2,0:T(8,128)(2,1)S(1)}, bf16[4,72,1,128]{3,1,2,0:T(8,128)(2,1)S(1)}, u32[]{:S(2)}, u32[]{:S(2)}) %collective-permute-start.1) | collective-permute-done | bytes 73760 | tf_op jit(solution)/shard_map/ppermute | solution.py:16
  7.9 1.4 %collective-permute-done = bf16[4,72,1,128]{3,1,2,0:T(8,128)(2,1)S(1)} collective-permute-done((bf16[4,72,1,128]{3,1,2,0:T(8,128)(2,1)S(1)}, bf16[4,72,1,128]{3,1,2,0:T(8,128)(2,1)S(1)}, u32[]{:S(2)}, u32[]{:S(2)}) %collective-permute-start) | collective-permute-done | bytes 73760 | tf_op jit(solution)/shard_map/ppermute | solution.py:18
  9.3 1.1 %fusion.36 = (bf16[4,72,10,1]{3,1,2,0:T(8,128)(2,1)}, bf16[4,72,10,1]{3,1,2,0:T(8,128)(2,1)S(1)}) fusion(bf16[4,72,10,128]{3,1,2,0:T(8,128)(2,1)S(1)} %constant_dynamic-update-slice_fusion), kind=kLoop, calls=%fused_computation.97 | loop fusion | bytes 23040 | tf_op jit(solution)/shard_map/slice | solution.py:12
  10.4 1.5 %copy.29 = bf16[4,72,10,1]{1,0,3,2:T(4,128)(2,1)S(1)} copy(bf16[4,72,10,1]{3,1,2,0:T(8,128)(2,1)} %get-tuple-element.11) | data formatting | bytes 11520 | tf_op jit(solution)/shard_map/slice | solution.py:12
  11.9 2.2 %collective-permute-start.2 = (bf16[4,72,10,1]{1,0,3,2:T(4,128)(2,1)S(1)}, bf16[4,72,10,1]{1,0,3,2:T(4,128)(2,1)S(1)}, u32[]{:S(2)}, u32[]{:S(2)}) collective-permute-start(bf16[4,72,10,1]{1,0,3,2:T(4,128)(2,1)S(1)} %copy.29), channel_id=1, source_target_pairs={{1,0},{2,1},{3,2},{4,3},{5,4},{6,5},{7,6},{0,7},{9,8},{10,9},{11,1... | collective-permute-start | bytes 17288 | tf_op jit(solution)/shard_map/ppermute | solution.py:18
  14.1 0.4 copy.31
  14.9 0.6 collective-permute-done.2
  15.5 1.2 %copy.30 = bf16[4,72,10,1]{3,1,2,0:T(8,128)(2,1)} copy(bf16[4,72,10,1]{1,0,3,2:T(4,128)(2,1)S(1)} %collective-permute-done.2) | data formatting | bytes 11520 | tf_op jit(solution)/shard_map/ppermute | solution.py:18
  16.8 2.6 %collective-permute-done.3 = bf16[4,72,10,1]{1,0,3,2:T(4,128)(2,1)S(1)} collective-permute-done((bf16[4,72,10,1]{1,0,3,2:T(4,128)(2,1)S(1)}, bf16[4,72,10,1]{1,0,3,2:T(4,128)(2,1)S(1)}, u32[]{:S(2)}, u32[]{:S(2)}) %collective-permute-start.3) | collective-permute-done | bytes 5792 | tf_op jit(solution)/shard_map/ppermute | solution.py:16
  19.4 1.2 %copy.32 = bf16[4,72,10,1]{3,1,2,0:T(8,128)(2,1)} copy(bf16[4,72,10,1]{1,0,3,2:T(4,128)(2,1)S(1)} %collective-permute-done.3) | data formatting | bytes 11520 | tf_op jit(solution)/shard_map/ppermute | solution.py:16
  20.6 2.5 %fusion.5 = bf16[4,72,8,128]{3,1,2,0:T(8,128)(2,1)S(1)} fusion(bf16[4,72,8,128]{3,1,2,0:T(8,128)(2,1)S(1)} %copy.20, bf16[4,72,10,128]{3,1,2,0:T(8,128)(2,1)S(1)} %constant_dynamic-update-slice_fusion, bf16[4,72,10,1]{3,1,2,0:T(8,128)(2,1)} %copy.32, bf16[4,72,10,1]{3,1,2,0:T(8,128)(2,1)} %copy.30, bf16[4,72,1,128]{3,1,2,0:T(8,128)(2,1)S(1)} %collective-permute-done.1, ...), kind=kLoop, calls=%fused_computation.31 | loop fusion | flops 9732096 | bytes 3255552 | tf_op jit(solution)/shard_map/convert_element_type | solution.py:35
  23.1 2.2 %collective-permute-start.4 = (bf16[4,72,1,128]{3,1,2,0:T(8,128)(2,1)S(1)}, bf16[4,72,1,128]{3,1,2,0:T(8,128)(2,1)S(1)}, u32[]{:S(2)}, u32[]{:S(2)}) collective-permute-start(bf16[4,72,1,128]{3,1,2,0:T(8,128)(2,1)S(1)} %get-tuple-element.16), channel_id=1, source_target_pairs={{8,0},{16,8},{24,16},{0,24},{9,1},{17,9},{25,17},{1,25},{10,2},{18... | collective-permute-start | bytes 221192 | tf_op jit(solution)/shard_map/ppermute | solution.py:18
  25.5 1.0 %sort.17 = (s32[8]{0:T(128)}, s32[8]{0:T(128)S(1)}) sort(s32[8]{0:T(128)S(1)} %bitcast.30, s32[8]{0:T(128)S(1)} %iota.9), dimensions={0}, to_apply=%region_0.0 | sort | flops 24 | bytes 128 | tf_op jit(solution)/shard_map/jit(argsort)/sort | solution.py:47
  26.4 1.3 %collective-permute-done.4 = bf16[4,72,1,128]{3,1,2,0:T(8,128)(2,1)S(1)} collective-permute-done((bf16[4,72,1,128]{3,1,2,0:T(8,128)(2,1)S(1)}, bf16[4,72,1,128]{3,1,2,0:T(8,128)(2,1)S(1)}, u32[]{:S(2)}, u32[]{:S(2)}) %collective-permute-start.4) | collective-permute-done | bytes 73760 | tf_op jit(solution)/shard_map/ppermute | solution.py:18
  27.7 2.9 %collective-permute-done.5 = bf16[4,72,1,128]{3,1,2,0:T(8,128)(2,1)S(1)} collective-permute-done((bf16[4,72,1,128]{3,1,2,0:T(8,128)(2,1)S(1)}, bf16[4,72,1,128]{3,1,2,0:T(8,128)(2,1)S(1)}, u32[]{:S(2)}, u32[]{:S(2)}) %collective-permute-start.5) | collective-permute-done | bytes 73760 | tf_op jit(solution)/shard_map/ppermute | solution.py:16
  30.7 1.1 %fusion.35 = (bf16[4,72,10,1]{3,1,2,0:T(8,128)(2,1)}, bf16[4,72,10,1]{3,1,2,0:T(8,128)(2,1)S(1)}) fusion(bf16[4,72,10,128]{3,1,2,0:T(8,128)(2,1)S(1)} %pad_maximum_fusion), kind=kLoop, calls=%fused_computation.96 | loop fusion | bytes 23040 | tf_op jit(solution)/shard_map/slice | solution.py:12
  31.8 1.4 %copy.34 = bf16[4,72,10,1]{1,0,3,2:T(4,128)(2,1)S(1)} copy(bf16[4,72,10,1]{3,1,2,0:T(8,128)(2,1)} %get-tuple-element.9) | data formatting | bytes 11520 | tf_op jit(solution)/shard_map/slice | solution.py:12
  33.3 0.4 copy.36
  33.7 0.5 collective-permute-start.7
  34.2 0.5 collective-permute-done.6
  34.7 0.4 copy.35
  35.2 3.5 %collective-permute-done.7 = bf16[4,72,10,1]{1,0,3,2:T(4,128)(2,1)S(1)} collective-permute-done((bf16[4,72,10,1]{1,0,3,2:T(4,128)(2,1)S(1)}, bf16[4,72,10,1]{1,0,3,2:T(4,128)(2,1)S(1)}, u32[]{:S(2)}, u32[]{:S(2)}) %collective-permute-start.7) | collective-permute-done | bytes 5792 | tf_op jit(solution)/shard_map/ppermute | solution.py:16
  38.6 1.2 %copy.37 = bf16[4,72,10,1]{3,1,2,0:T(8,128)(2,1)} copy(bf16[4,72,10,1]{1,0,3,2:T(4,128)(2,1)S(1)} %collective-permute-done.7) | data formatting | bytes 11520 | tf_op jit(solution)/shard_map/ppermute | solution.py:16
  39.8 2.3 %fusion.13 = bf16[4,72,8,128]{3,1,2,0:T(8,128)(2,1)S(1)} fusion(bf16[4,72,8,128]{3,1,2,0:T(8,128)(2,1)S(1)} %fusion.5, bf16[4,72,10,1]{3,1,2,0:T(8,128)(2,1)} %copy.37, bf16[4,72,1,128]{3,1,2,0:T(8,128)(2,1)S(1)} %collective-permute-done.4, bf16[4,72,1,128]{3,1,2,0:T(8,128)(2,1)S(1)} %collective-permute-done.5, bf16[4,72,10,1]{3,1,2,0:T(8,128)(2,1)S(1)} %copy.35, ...), kind=kLoop, calls=%fused_computation.39 | loop fusion | flops 12091392 | bytes 2518272 | tf_op jit(solution)/shard_map/convert_element_type | solution.py:35
  42.2 1.2 %collective-permute-start.8 = (bf16[4,72,1,128]{3,1,2,0:T(8,128)(2,1)S(1)}, bf16[4,72,1,128]{3,1,2,0:T(8,128)(2,1)S(1)}, u32[]{:S(2)}, u32[]{:S(2)}) collective-permute-start(bf16[4,72,1,128]{3,1,2,0:T(8,128)(2,1)S(1)} %get-tuple-element.14), channel_id=1, source_target_pairs={{8,0},{16,8},{24,16},{0,24},{9,1},{17,9},{25,17},{1,25},{10,2},{18... | collective-permute-start | bytes 221192 | tf_op jit(solution)/shard_map/ppermute | solution.py:18
  43.3 0.9 %collective-permute-start.9 = (bf16[4,72,1,128]{3,1,2,0:T(8,128)(2,1)S(1)}, bf16[4,72,1,128]{3,1,2,0:T(8,128)(2,1)S(1)}, u32[]{:S(2)}, u32[]{:S(2)}) collective-permute-start(bf16[4,72,1,128]{3,1,2,0:T(8,128)(2,1)S(1)} %get-tuple-element.13), channel_id=1, source_target_pairs={{0,8},{8,16},{16,24},{24,0},{1,9},{9,17},{17,25},{25,1},{2,10},{10... | collective-permute-start | bytes 221192 | tf_op jit(solution)/shard_map/ppermute | solution.py:16
  44.2 2.3 %collective-permute-done.8 = bf16[4,72,1,128]{3,1,2,0:T(8,128)(2,1)S(1)} collective-permute-done((bf16[4,72,1,128]{3,1,2,0:T(8,128)(2,1)S(1)}, bf16[4,72,1,128]{3,1,2,0:T(8,128)(2,1)S(1)}, u32[]{:S(2)}, u32[]{:S(2)}) %collective-permute-start.8) | collective-permute-done | bytes 73760 | tf_op jit(solution)/shard_map/ppermute | solution.py:18
  46.6 2.0 %collective-permute-done.9 = bf16[4,72,1,128]{3,1,2,0:T(8,128)(2,1)S(1)} collective-permute-done((bf16[4,72,1,128]{3,1,2,0:T(8,128)(2,1)S(1)}, bf16[4,72,1,128]{3,1,2,0:T(8,128)(2,1)S(1)}, u32[]{:S(2)}, u32[]{:S(2)}) %collective-permute-start.9) | collective-permute-done | bytes 73760 | tf_op jit(solution)/shard_map/ppermute | solution.py:16
  48.7 0.3 fusion.34
  49.0 0.4 copy.38
  49.3 0.4 copy.40
  49.7 0.5 collective-permute-start.11
  50.2 0.5 collective-permute-done.10
  50.7 0.4 copy.39
  51.2 3.5 %collective-permute-done.11 = bf16[4,72,10,1]{1,0,3,2:T(4,128)(2,1)S(1)} collective-permute-done((bf16[4,72,10,1]{1,0,3,2:T(4,128)(2,1)S(1)}, bf16[4,72,10,1]{1,0,3,2:T(4,128)(2,1)S(1)}, u32[]{:S(2)}, u32[]{:S(2)}) %collective-permute-start.11) | collective-permute-done | bytes 5792 | tf_op jit(solution)/shard_map/ppermute | solution.py:16
  54.6 0.4 copy.41
  55.1 2.0 %fusion.21 = bf16[4,72,8,128]{3,1,2,0:T(8,128)(2,1)} fusion(bf16[4,72,8,128]{3,1,2,0:T(8,128)(2,1)S(1)} %fusion.13, bf16[4,72,10,1]{3,1,2,0:T(8,128)(2,1)S(1)} %copy.41, bf16[4,72,1,128]{3,1,2,0:T(8,128)(2,1)S(1)} %collective-permute-done.8, bf16[4,72,1,128]{3,1,2,0:T(8,128)(2,1)S(1)} %collective-permute-done.9, bf16[4,72,10,1]{3,1,2,0:T(8,128)(2,1)S(1)} %copy.39, ...), kind=kLoop, calls=%fused_computation.47 | loop fusion | flops 12091392 | bytes 2518272 | tf_op jit(solution)/shard_map/convert_element_type | solution.py:35
  57.1 1.7 %gather_fusion = bf16[8,4,72,128]{3,2,1,0:T(8,128)(2,1)S(1)} fusion(bf16[4,72,8,128]{3,1,2,0:T(8,128)(2,1)} %fusion.21, s32[1024]{0:T(1024)S(1)} %pad_clamp_fusion), kind=kCustom, calls=%fused_computation | custom fusion | bytes 1179680 | tf_op jit(solution)/shard_map/jit(_take)/gather | solution.py:49
  58.9 0.9 %select_bitcast_fusion = bf16[4,72,8,128]{3,1,0,2:T(8,128)(2,1)} fusion(bf16[8,4,72,128]{3,2,1,0:T(8,128)(2,1)S(1)} %gather_fusion, pred[8]{0:T(512)(128)(4,1)S(1)} %compare_and_fusion), kind=kLoop, calls=%fused_computation.77 | loop fusion | flops 294912 | bytes 1179656 | tf_op jit(solution)/shard_map/jit(_take)/select_n | solution.py:49
  59.8 3.5 %all-to-all-start = ((bf16[4,72,8,128]{3,1,0,2:T(8,128)(2,1)}), bf16[4,72,8,128]{3,1,0,2:T(8,128)(2,1)S(1)}, u32[]{:S(2)}, u32[]{:S(2)}) async-start(bf16[4,72,8,128]{3,1,0,2:T(8,128)(2,1)} %select_bitcast_fusion), calls=%async_computation | async-start | bytes 1179648 | tf_op jit(solution)/shard_map/all_to_all | solution.py:50
  64.0 0.1 select_reduce_fusion
  64.2 15.9 %all-to-all-done = bf16[4,72,8,128]{3,1,0,2:T(8,128)(2,1)S(1)} async-done(((bf16[4,72,8,128]{3,1,0,2:T(8,128)(2,1)}), bf16[4,72,8,128]{3,1,0,2:T(8,128)(2,1)S(1)}, u32[]{:S(2)}, u32[]{:S(2)}) %all-to-all-start) | async-done | bytes 589856 | tf_op jit(solution)/shard_map/all_to_all | solution.py:50
  80.0 0.3 fusion.27
  80.3 0.3 fusion.1
  80.6 0.9 %copy.43 = bf16[4,72,8,128]{3,2,1,0:T(8,128)(2,1)} copy(bf16[4,72,8,128]{3,1,2,0:T(8,128)(2,1)S(1)} %fusion.1) | data formatting | bytes 1179648 | tf_op jit(solution)/shard_map/convert_element_type | solution.py:57
  (32 shorter events, 1.0 us)
Async XLA Ops:
  0.0 80.0 %copy-start = (bf16[1,72,72]{2,1,0:T(8,128)(2,1)S(1)}, bf16[1,72,72]{2,1,0:T(8,128)(2,1)}, u32[]{:S(2)}) copy-start(bf16[1,72,72]{2,1,0:T(8,128)(2,1)} %param.9) | copy-start | bytes 31108
  0.0 7.8 %copy-start.1 = (bf16[4,72,8,128]{3,2,1,0:T(8,128)(2,1)S(1)}, bf16[4,72,8,128]{3,2,1,0:T(8,128)(2,1)}, u32[]{:S(2)}) copy-start(bf16[4,72,8,128]{3,2,1,0:T(8,128)(2,1)} %param.6) | copy-start | bytes 1769476
  1.2 6.5 %collective-permute-start.1 = (bf16[4,72,1,128]{3,1,2,0:T(8,128)(2,1)S(1)}, bf16[4,72,1,128]{3,1,2,0:T(8,128)(2,1)S(1)}, u32[]{:S(2)}, u32[]{:S(2)}) collective-permute-start(bf16[4,72,1,128]{3,1,2,0:T(8,128)(2,1)S(1)} %get-tuple-element.18), channel_id=1, source_target_pairs={{0,8},{8,16},{16,24},{24,0},{1,9},{9,17},{17,25},{25,1},{2,10},{10... | collective-permute-start | bytes 221192 | tf_op jit(solution)/shard_map/ppermute | solution.py:16
  4.2 5.1 %collective-permute-start = (bf16[4,72,1,128]{3,1,2,0:T(8,128)(2,1)S(1)}, bf16[4,72,1,128]{3,1,2,0:T(8,128)(2,1)S(1)}, u32[]{:S(2)}, u32[]{:S(2)}) collective-permute-start(bf16[4,72,1,128]{3,1,2,0:T(8,128)(2,1)S(1)} %get-tuple-element.17), channel_id=1, source_target_pairs={{8,0},{16,8},{24,16},{0,24},{9,1},{17,9},{25,17},{1,25},{10,2},{18... | collective-permute-start | bytes 221192 | tf_op jit(solution)/shard_map/ppermute | solution.py:18
  10.4 4.1 %copy-start.3 = (bf16[2,72,8,128]{3,2,1,0:T(8,128)(2,1)S(1)}, bf16[2,72,8,128]{3,2,1,0:T(8,128)(2,1)}, u32[]{:S(2)}) copy-start(bf16[2,72,8,128]{3,2,1,0:T(8,128)(2,1)} %param.7) | copy-start | bytes 884740
  11.9 3.6 %collective-permute-start.2 = (bf16[4,72,10,1]{1,0,3,2:T(4,128)(2,1)S(1)}, bf16[4,72,10,1]{1,0,3,2:T(4,128)(2,1)S(1)}, u32[]{:S(2)}, u32[]{:S(2)}) collective-permute-start(bf16[4,72,10,1]{1,0,3,2:T(4,128)(2,1)S(1)} %copy.29), channel_id=1, source_target_pairs={{1,0},{2,1},{3,2},{4,3},{5,4},{6,5},{7,6},{0,7},{9,8},{10,9},{11,1... | collective-permute-start | bytes 17288 | tf_op jit(solution)/shard_map/ppermute | solution.py:18
  14.5 4.9 %collective-permute-start.3 = (bf16[4,72,10,1]{1,0,3,2:T(4,128)(2,1)S(1)}, bf16[4,72,10,1]{1,0,3,2:T(4,128)(2,1)S(1)}, u32[]{:S(2)}, u32[]{:S(2)}) collective-permute-start(bf16[4,72,10,1]{1,0,3,2:T(4,128)(2,1)S(1)} %copy.31), channel_id=1, source_target_pairs={{0,1},{1,2},{2,3},{3,4},{4,5},{5,6},{6,7},{7,0},{8,9},{9,10},{10,1... | collective-permute-start | bytes 17288 | tf_op jit(solution)/shard_map/ppermute | solution.py:16
  20.6 4.8 %copy-start.4 = (s32[1,8]{1,0:T(1,128)S(1)}, s32[1,8]{1,0:T(1,128)}, u32[]{:S(2)}) copy-start(s32[1,8]{1,0:T(1,128)} %param.8) | copy-start | bytes 100
  23.1 4.6 %collective-permute-start.4 = (bf16[4,72,1,128]{3,1,2,0:T(8,128)(2,1)S(1)}, bf16[4,72,1,128]{3,1,2,0:T(8,128)(2,1)S(1)}, u32[]{:S(2)}, u32[]{:S(2)}) collective-permute-start(bf16[4,72,1,128]{3,1,2,0:T(8,128)(2,1)S(1)} %get-tuple-element.16), channel_id=1, source_target_pairs={{8,0},{16,8},{24,16},{0,24},{9,1},{17,9},{25,17},{1,25},{10,2},{18... | collective-permute-start | bytes 221192 | tf_op jit(solution)/shard_map/ppermute | solution.py:18
  25.4 5.3 %collective-permute-start.5 = (bf16[4,72,1,128]{3,1,2,0:T(8,128)(2,1)S(1)}, bf16[4,72,1,128]{3,1,2,0:T(8,128)(2,1)S(1)}, u32[]{:S(2)}, u32[]{:S(2)}) collective-permute-start(bf16[4,72,1,128]{3,1,2,0:T(8,128)(2,1)S(1)} %get-tuple-element.15), channel_id=1, source_target_pairs={{0,8},{8,16},{16,24},{24,0},{1,9},{9,17},{17,25},{25,1},{2,10},{10... | collective-permute-start | bytes 221192 | tf_op jit(solution)/shard_map/ppermute | solution.py:16
  33.3 1.4 %collective-permute-start.6 = (bf16[4,72,10,1]{1,0,3,2:T(4,128)(2,1)S(1)}, bf16[4,72,10,1]{1,0,3,2:T(4,128)(2,1)S(1)}, u32[]{:S(2)}, u32[]{:S(2)}) collective-permute-start(bf16[4,72,10,1]{1,0,3,2:T(4,128)(2,1)S(1)} %copy.34), channel_id=1, source_target_pairs={{1,0},{2,1},{3,2},{4,3},{5,4},{6,5},{7,6},{0,7},{9,8},{10,9},{11,1... | collective-permute-start | bytes 17288 | tf_op jit(solution)/shard_map/ppermute | solution.py:18
  33.7 4.9 %collective-permute-start.7 = (bf16[4,72,10,1]{1,0,3,2:T(4,128)(2,1)S(1)}, bf16[4,72,10,1]{1,0,3,2:T(4,128)(2,1)S(1)}, u32[]{:S(2)}, u32[]{:S(2)}) collective-permute-start(bf16[4,72,10,1]{1,0,3,2:T(4,128)(2,1)S(1)} %copy.36), channel_id=1, source_target_pairs={{0,1},{1,2},{2,3},{3,4},{4,5},{5,6},{6,7},{7,0},{8,9},{9,10},{10,1... | collective-permute-start | bytes 17288 | tf_op jit(solution)/shard_map/ppermute | solution.py:16
  42.2 4.4 %collective-permute-start.8 = (bf16[4,72,1,128]{3,1,2,0:T(8,128)(2,1)S(1)}, bf16[4,72,1,128]{3,1,2,0:T(8,128)(2,1)S(1)}, u32[]{:S(2)}, u32[]{:S(2)}) collective-permute-start(bf16[4,72,1,128]{3,1,2,0:T(8,128)(2,1)S(1)} %get-tuple-element.14), channel_id=1, source_target_pairs={{8,0},{16,8},{24,16},{0,24},{9,1},{17,9},{25,17},{1,25},{10,2},{18... | collective-permute-start | bytes 221192 | tf_op jit(solution)/shard_map/ppermute | solution.py:18
  43.3 5.3 %collective-permute-start.9 = (bf16[4,72,1,128]{3,1,2,0:T(8,128)(2,1)S(1)}, bf16[4,72,1,128]{3,1,2,0:T(8,128)(2,1)S(1)}, u32[]{:S(2)}, u32[]{:S(2)}) collective-permute-start(bf16[4,72,1,128]{3,1,2,0:T(8,128)(2,1)S(1)} %get-tuple-element.13), channel_id=1, source_target_pairs={{0,8},{8,16},{16,24},{24,0},{1,9},{9,17},{17,25},{25,1},{2,10},{10... | collective-permute-start | bytes 221192 | tf_op jit(solution)/shard_map/ppermute | solution.py:16
  49.3 1.4 %collective-permute-start.10 = (bf16[4,72,10,1]{1,0,3,2:T(4,128)(2,1)S(1)}, bf16[4,72,10,1]{1,0,3,2:T(4,128)(2,1)S(1)}, u32[]{:S(2)}, u32[]{:S(2)}) collective-permute-start(bf16[4,72,10,1]{1,0,3,2:T(4,128)(2,1)S(1)} %copy.38), channel_id=1, source_target_pairs={{1,0},{2,1},{3,2},{4,3},{5,4},{6,5},{7,6},{0,7},{9,8},{10,9},{11,1... | collective-permute-start | bytes 17288 | tf_op jit(solution)/shard_map/ppermute | solution.py:18
  49.7 4.9 %collective-permute-start.11 = (bf16[4,72,10,1]{1,0,3,2:T(4,128)(2,1)S(1)}, bf16[4,72,10,1]{1,0,3,2:T(4,128)(2,1)S(1)}, u32[]{:S(2)}, u32[]{:S(2)}) collective-permute-start(bf16[4,72,10,1]{1,0,3,2:T(4,128)(2,1)S(1)} %copy.40), channel_id=1, source_target_pairs={{0,1},{1,2},{2,3},{3,4},{4,5},{5,6},{6,7},{7,0},{8,9},{9,10},{10,1... | collective-permute-start | bytes 17288 | tf_op jit(solution)/shard_map/ppermute | solution.py:16
  58.8 5.2 %copy-start.2 = (bf16[16,72,72]{2,1,0:T(8,128)(2,1)S(1)}, bf16[16,72,72]{2,1,0:T(8,128)(2,1)}, u32[]{:S(2)}) copy-start(bf16[16,72,72]{2,1,0:T(8,128)(2,1)} %param.11) | copy-start | bytes 497668
  59.8 20.2 %all-to-all-start = ((bf16[4,72,8,128]{3,1,0,2:T(8,128)(2,1)}), bf16[4,72,8,128]{3,1,0,2:T(8,128)(2,1)S(1)}, u32[]{:S(2)}, u32[]{:S(2)}) async-start(bf16[4,72,8,128]{3,1,0,2:T(8,128)(2,1)} %select_bitcast_fusion), calls=%async_computation | async-start | bytes 1179648 | tf_op jit(solution)/shard_map/all_to_all | solution.py:50
where the time goes:
time: 81.9 us; the launch traced here: 81.5 us
  waiting for transfers between devices  39.4 us (48%)
  local copies, waits for them, and re-layouts  16.2 us (20%)
  starting transfers between devices  15.3 us (19%)
  other arithmetic  9.14 us (11%)
  between operations  0.86 us (1%)
    ppermute x6, waiting for transfers between devices, with_halo(): lax.ppermute(tail, axis, [(i, (i + 1) % count) for i in range(count)])  16.9 us
    all_to_all x1, waiting for transfers between devices, per_device(): lax.all_to_all(ordered, 'tile', split_axis=2, concat_axis=2, tiled=True)  15.9 us
    convert_element_type x3, other arithmetic, advect_tile(): return out.astype(jnp.bfloat16)  6.8 us
    ppermute x6, starting transfers between devices, with_halo(): lax.ppermute(head, axis, [((i + 1) % count, i) for i in range(count)])  6.67 us
    ppermute x6, waiting for transfers between devices, with_halo(): lax.ppermute(head, axis, [((i + 1) % count, i) for i in range(count)])  6.61 us
    slice x7, local copies, waits for them, and re-layouts, with_halo(): head = lax.slice_in_dim(cells, 0, width, axis=dim)  5.84 us
    ppermute x6, starting transfers between devices, with_halo(): lax.ppermute(tail, axis, [(i, (i + 1) % count) for i in range(count)])  5.11 us
    all_to_all x1, starting transfers between devices, per_device(): lax.all_to_all(ordered, 'tile', split_axis=2, concat_axis=2, tiled=True)  3.54 us
  transfers between devices with their start and end apart: 13, of which 13 were waited for; matrix products, arithmetic and copies ran while one was open for 6% of the time, Pallas kernels for 0%

commit v1 on v0

--- a/solution.py
+++ b/solution.py
@@ -35,15 +35,15 @@
     return out.astype(jnp.bfloat16)
 
 
-def substep(field, courant):
-    padded = with_halo(field, (("sec", 2), ("tile", 3)), 1)
-    return advect_tile(padded, courant)
-
-
 def per_device(tracers, courant, destination, diffusion, band, band_table):
-    advected = tracers
+    count = tracers.shape[0]
+    fields = jnp.concatenate([tracers, courant], axis=0)
+    padded = with_halo(fields, (("sec", 2), ("tile", 3)), STEPS)
+    advected = padded[:count]
+    wind = padded[count:]
     for step in range(STEPS):
-        advected = substep(advected, courant)
+        wind = wind[:, :, 1:-1, 1:-1]
+        advected = advect_tile(advected, wind)
     order = jnp.argsort(destination[0])
     band_count = band_table.shape[0]
     ordered = jnp.take(advected, order, axis=2)

time: 81.9 us -> 76.1 us (0.929)
  waiting for transfers between devices: 39.4 us -> 29 us
  other arithmetic: 9.14 us -> 15.7 us
  starting transfers between devices: 15.3 us -> 11.1 us
  local copies, waits for them, and re-layouts: 16.2 us -> 18.3 us
    ppermute x6 -> x2, waiting for transfers between devices: 16.9 us -> 6.64 us  [with_halo(): lax.ppermute(tail, axis, [(i, (i + 1) % count) for i in range(count)])]
    slice x7 -> x1, local copies, waits for them, and re-layouts: 5.84 us -> 1.51 us  [with_halo(): head = lax.slice_in_dim(cells, 0, width, axis=dim)]
    concatenate x2, other arithmetic: 0.19 us -> 4.04 us  [with_halo(): jnp.concatenate([lax.ppermute(tail, axis, [(i, (i + 1) % count) for i in...]
    slice x5 -> x3, local copies, waits for them, and re-layouts: 1.09 us -> 3.67 us  [with_halo(): lax.slice_in_dim(cells, cells.shape[dim] - width, cells.shape[dim], axis=...]
    ppermute x6 -> x2, starting transfers between devices: 6.67 us -> 4.54 us  [with_halo(): lax.ppermute(head, axis, [((i + 1) % count, i) for i in range(count)])]
    ppermute x6 -> x2, starting transfers between devices: 5.11 us -> 3.05 us  [with_halo(): lax.ppermute(tail, axis, [(i, (i + 1) % count) for i in range(count)])]
    mul x1, local copies, waits for them, and re-layouts: 0.06 us -> 1.75 us  [advect_tile(): 0.5 * cx * cx * (north - 2.0 * centre + south)]
    mul x1, local copies, waits for them, and re-layouts: 0.06 us -> 1.72 us  [advect_tile(): 0.5 * cy * (east - west)]
  transfers between devices with their start and end apart: 13 -> 5, of which waited for: 13 -> 3; matrix products, arithmetic and copies ran while one was open for 6% -> 14% of each run, Pallas kernels for 0% -> 0%
where the time goes in v1:
time: 76.1 us; the launch traced here: 75.6 us
  waiting for transfers between devices  29 us (38%)
  local copies, waits for them, and re-layouts  18.3 us (24%)
  other arithmetic  15.7 us (21%)
  starting transfers between devices  11.1 us (15%)
  between operations  0.87 us (1%)
    all_to_all x1, waiting for transfers between devices, per_device(): lax.all_to_all(ordered, 'tile', split_axis=2, concat_axis=2, tiled=True)  15.9 us
    convert_element_type x3, other arithmetic, advect_tile(): return out.astype(jnp.bfloat16)  7.91 us
    ppermute x2, waiting for transfers between devices, with_halo(): lax.ppermute(tail, axis, [(i, (i + 1) % count) for i in range(count)])  6.64 us
    ppermute x2, waiting for transfers between devices, with_halo(): lax.ppermute(head, axis, [((i + 1) % count, i) for i in range(count)])  6.53 us
    ppermute x2, starting transfers between devices, with_halo(): lax.ppermute(head, axis, [((i + 1) % count, i) for i in range(count)])  4.54 us
    concatenate x2, other arithmetic, with_halo(): jnp.concatenate([lax.ppermute(tail, axis, [(i, (i + 1) % count) for i in...  4.04 us
    slice x3, local copies, waits for them, and re-layouts, with_halo(): lax.slice_in_dim(cells, cells.shape[dim] - width, cells.shape[dim], axis=...  3.67 us
    all_to_all x1, starting transfers between devices, per_device(): lax.all_to_all(ordered, 'tile', split_axis=2, concat_axis=2, tiled=True)  3.54 us
  transfers between devices with their start and end apart: 5, of which 3 were waited for; matrix products, arithmetic and copies ran while one was open for 14% of the time, Pallas kernels for 0%

profile of v1, /device:TPU:0, one launch (start us, length us, event | category | flops | bytes accessed | tf_op | source)
XLA Modules:
  0.0 75.6 jit_solution(4373132909313817035)
XLA Ops:
  0.0 0.0 copy-start
  0.0 1.2 %copy_dynamic-update-slice_fusion = bf16[6,72,8,128]{3,1,2,0:T(8,128)(2,1)S(1)} fusion(bf16[4,72,8,128]{3,2,1,0:T(8,128)(2,1)} %param.6), kind=kLoop, calls=%fused_computation.69 | loop fusion | bytes 1179648
  1.2 1.0 %copy_dynamic-update-slice_fusion.1 = bf16[6,72,8,128]{3,1,2,0:T(8,128)(2,1)S(1)} fusion(bf16[6,72,8,128]{3,1,2,0:T(8,128)(2,1)S(1)} %copy_dynamic-update-slice_fusion, bf16[2,72,8,128]{3,2,1,0:T(8,128)(2,1)} %param.7), kind=kLoop, calls=%fused_computation.78 | loop fusion | bytes 589824 | tf_op jit(solution)/shard_map/concatenate | solution.py:40
  2.2 0.1 fusion.39
  2.3 3.0 %collective-permute-start = (bf16[6,72,3,128]{3,1,2,0:T(8,128)(2,1)S(1)}, bf16[6,72,3,128]{3,1,2,0:T(8,128)(2,1)S(1)}, u32[]{:S(2)}, u32[]{:S(2)}) collective-permute-start(bf16[6,72,3,128]{3,1,2,0:T(8,128)(2,1)S(1)} %get-tuple-element.17), channel_id=1, source_target_pairs={{0,8},{8,16},{16,24},{24,0},{1,9},{9,17},{17,25},{25,1},{2,10},{10... | collective-permute-start | bytes 995336 | tf_op jit(solution)/shard_map/ppermute | solution.py:16
  5.3 1.0 %collective-permute-start.1 = (bf16[6,72,3,128]{3,1,2,0:T(8,128)(2,1)S(1)}, bf16[6,72,3,128]{3,1,2,0:T(8,128)(2,1)S(1)}, u32[]{:S(2)}, u32[]{:S(2)}) collective-permute-start(bf16[6,72,3,128]{3,1,2,0:T(8,128)(2,1)S(1)} %get-tuple-element.18), channel_id=1, source_target_pairs={{8,0},{16,8},{24,16},{0,24},{9,1},{17,9},{25,17},{1,25},{10,2},{18... | collective-permute-start | bytes 995336 | tf_op jit(solution)/shard_map/ppermute | solution.py:18
  6.3 0.0 copy-done.6
  6.3 1.0 %sort.17 = (s32[8]{0:T(128)}, s32[8]{0:T(128)S(1)}) sort(s32[8]{0:T(128)S(1)} %bitcast.46, s32[8]{0:T(128)S(1)} %iota.9), dimensions={0}, to_apply=%region_0.0 | sort | flops 24 | bytes 128 | tf_op jit(solution)/shard_map/jit(argsort)/sort | solution.py:47
  7.3 0.0 copy-done.4
  7.3 0.9 %multiply_bitcast_fusion.5 = (f32[72,8,128]{2,1,0:T(8,128)}, f32[72,8,128]{2,1,0:T(8,128)}, f32[72,8,128]{2,1,0:T(8,128)S(1)}, f32[72,8,128]{2,1,0:T(8,128)}) fusion(bf16[2,72,8,128]{3,2,1,0:T(8,128)(2,1)S(1)} %copy-done.4), kind=kLoop, calls=%fused_computation.75 | loop fusion | flops 442368 | bytes 1474560 | tf_op jit(solution)/shard_map/mul | solution.py:33
  8.2 6.6 %collective-permute-done = bf16[6,72,3,128]{3,1,2,0:T(8,128)(2,1)S(1)} collective-permute-done((bf16[6,72,3,128]{3,1,2,0:T(8,128)(2,1)S(1)}, bf16[6,72,3,128]{3,1,2,0:T(8,128)(2,1)S(1)}, u32[]{:S(2)}, u32[]{:S(2)}) %collective-permute-start) | collective-permute-done | bytes 331808 | tf_op jit(solution)/shard_map/ppermute | solution.py:16
  14.9 6.5 %collective-permute-done.1 = bf16[6,72,3,128]{3,1,2,0:T(8,128)(2,1)S(1)} collective-permute-done((bf16[6,72,3,128]{3,1,2,0:T(8,128)(2,1)S(1)}, bf16[6,72,3,128]{3,1,2,0:T(8,128)(2,1)S(1)}, u32[]{:S(2)}, u32[]{:S(2)}) %collective-permute-start.1) | collective-permute-done | bytes 331808 | tf_op jit(solution)/shard_map/ppermute | solution.py:18
  21.4 0.2 pad_maximum_fusion.1
  21.6 1.7 %fusion.38 = (bf16[6,72,14,3]{3,1,2,0:T(8,128)(2,1)}, bf16[6,72,14,3]{3,1,2,0:T(8,128)(2,1)S(1)}) fusion(bf16[6,72,14,128]{3,1,2,0:T(8,128)(2,1)S(1)} %pad_maximum_fusion.1), kind=kLoop, calls=%fused_computation.86 | loop fusion | bytes 145152 | tf_op jit(solution)/shard_map/slice | solution.py:13
  23.3 1.9 %copy.18 = bf16[6,72,14,3]{1,2,3,0:T(8,128)(2,1)S(1)} copy(bf16[6,72,14,3]{3,1,2,0:T(8,128)(2,1)} %get-tuple-element.15) | data formatting | bytes 72576 | tf_op jit(solution)/shard_map/slice | solution.py:13
  25.2 0.1 collective-permute-start.2
  25.3 1.5 %copy.19 = bf16[6,72,14,3]{1,2,3,0:T(8,128)(2,1)} copy(bf16[6,72,14,3]{3,1,2,0:T(8,128)(2,1)S(1)} %get-tuple-element.16) | data formatting | bytes 72576 | tf_op jit(solution)/shard_map/slice | solution.py:12
  26.8 3.5 %collective-permute-start.3 = (bf16[6,72,14,3]{1,2,3,0:T(8,128)(2,1)}, bf16[6,72,14,3]{1,2,3,0:T(8,128)(2,1)}, u32[]{:S(2)}, u32[]{:S(2)}) collective-permute-start(bf16[6,72,14,3]{1,2,3,0:T(8,128)(2,1)} %copy.19), channel_id=1, source_target_pairs={{1,0},{2,1},{3,2},{4,3},{5,4},{6,5},{7,6},{0,7},{9,8},{10,9},{11,1... | collective-permute-start | bytes 108872 | tf_op jit(solution)/shard_map/ppermute | solution.py:18
  30.3 1.0 %copy.22 = f32[72,8,128]{2,0,1:T(8,128)S(1)} copy(f32[72,8,128]{2,1,0:T(8,128)} %get-tuple-element.19) | data formatting | bytes 589824 | tf_op jit(solution)/shard_map/mul | solution.py:33
  31.3 1.8 %copy.23 = f32[72,8,128]{2,0,1:T(8,128)} copy(f32[72,8,128]{2,1,0:T(8,128)} %get-tuple-element.20) | data formatting | bytes 589824 | tf_op jit(solution)/shard_map/mul | solution.py:33
  33.1 1.7 %copy.24 = f32[72,8,128]{2,0,1:T(8,128)} copy(f32[72,8,128]{2,1,0:T(8,128)} %get-tuple-element.22) | data formatting | bytes 589824 | tf_op jit(solution)/shard_map/mul | solution.py:34
  34.8 0.8 %copy.25 = f32[72,8,128]{2,0,1:T(8,128)} copy(f32[72,8,128]{2,1,0:T(8,128)S(1)} %get-tuple-element.21) | data formatting | bytes 589824 | tf_op jit(solution)/shard_map/mul | solution.py:34
  35.6 0.0 collective-permute-done.2
  35.6 1.6 %copy.20 = bf16[6,72,14,3]{3,1,2,0:T(8,128)(2,1)S(1)} copy(bf16[6,72,14,3]{1,2,3,0:T(8,128)(2,1)} %collective-permute-done.2) | data formatting | bytes 72576 | tf_op jit(solution)/shard_map/ppermute | solution.py:16
  37.2 0.0 collective-permute-done.3
  37.2 2.4 %copy.21 = bf16[6,72,14,3]{3,1,2,0:T(8,128)(2,1)} copy(bf16[6,72,14,3]{1,2,3,0:T(8,128)(2,1)} %collective-permute-done.3) | data formatting | bytes 72576 | tf_op jit(solution)/shard_map/ppermute | solution.py:18
  39.6 3.9 %pad_maximum_fusion = bf16[6,72,14,134]{3,1,2,0:T(8,128)(2,1)S(1)} fusion(bf16[6,72,14,3]{3,1,2,0:T(8,128)(2,1)} %copy.21, bf16[6,72,3,128]{3,1,2,0:T(8,128)(2,1)S(1)} %collective-permute-done.1, bf16[6,72,8,128]{3,1,2,0:T(8,128)(2,1)S(1)} %copy_dynamic-update-slice_fusion.1, bf16[6,72,3,128]{3,1,2,0:T(8,128)(2,1)S(1)} %collective-permute-done, ...), kind=kLoop, calls=%fused_computation.25 | loop fusion | flops 8104320 | bytes 3241728 | tf_op jit(solution)/shard_map/concatenate | solution.py:14
  43.5 0.4 multiply_bitcast_fusion.1
  43.9 0.3 multiply_bitcast_fusion.3
  44.2 3.7 %fusion.3 = bf16[4,72,12,132]{3,1,2,0:T(8,128)(2,1)S(1)} fusion(bf16[6,72,14,134]{3,1,2,0:T(8,128)(2,1)S(1)} %pad_maximum_fusion, f32[72,12,132]{2,0,1:T(8,128)S(1)} %get-tuple-element.13, f32[72,12,132]{2,0,1:T(8,128)S(1)} %get-tuple-element.14, f32[72,12,132]{2,0,1:T(8,128)S(1)} %get-tuple-element.12, f32[72,12,132]{2,0,1:T(8,128)S(1)} %get-tuple-element.11), kind=kLoop, calls=%fused_computation.20 | loop fusion | flops 9580032 | bytes 7299072 | tf_op jit(solution)/shard_map/convert_element_type | solution.py:35
  47.9 0.0 copy-start.1
  47.9 0.0 copy-start.2
  48.0 0.0 copy-start.3
  48.0 3.1 %fusion.11 = bf16[4,72,10,130]{3,1,2,0:T(8,128)(2,1)S(1)} fusion(bf16[4,72,12,132]{3,1,2,0:T(8,128)(2,1)S(1)} %fusion.3, f32[72,10,130]{2,0,1:T(8,128)S(1)} %get-tuple-element.9, f32[72,10,130]{2,0,1:T(8,128)S(1)} %get-tuple-element.10, f32[72,10,130]{2,0,1:T(8,128)S(1)} %get-tuple-element.8, f32[72,10,130]{2,0,1:T(8,128)S(1)} %get-tuple-element.7), kind=kLoop, calls=%fused_computation.29 | loop fusion | flops 7862400 | bytes 5990400 | tf_op jit(solution)/shard_map/convert_element_type | solution.py:35
  51.1 0.0 copy-done.1
  51.1 0.0 copy-done.2
  51.1 0.0 copy-done.3
  51.1 1.1 %fusion.21 = bf16[4,72,8,128]{3,1,2,0:T(8,128)(2,1)S(1)} fusion(bf16[4,72,10,130]{3,1,2,0:T(8,128)(2,1)S(1)} %fusion.11, f32[72,8,128]{2,0,1:T(8,128)S(1)} %copy-done.3, f32[72,8,128]{2,0,1:T(8,128)S(1)} %copy-done.2, f32[72,8,128]{2,0,1:T(8,128)S(1)} %copy-done.1, f32[72,8,128]{2,0,1:T(8,128)S(1)} %copy.22), kind=kLoop, calls=%fused_computation.53 | loop fusion | flops 6193152 | bytes 4718592 | tf_op jit(solution)/shard_map/convert_element_type | solution.py:35
  52.2 0.0 copy-start.5
  52.2 0.7 gather_fusion
  52.9 0.9 %select_bitcast_fusion = bf16[4,72,8,128]{3,1,0,2:T(8,128)(2,1)} fusion(bf16[8,4,72,128]{3,2,1,0:T(8,128)(2,1)S(1)} %gather_fusion, pred[8]{0:T(512)(128)(4,1)S(1)} %compare_and_fusion), kind=kLoop, calls=%fused_computation.70 | loop fusion | flops 294912 | bytes 1179656 | tf_op jit(solution)/shard_map/jit(_take)/select_n | solution.py:49
  53.8 3.5 %all-to-all-start = ((bf16[4,72,8,128]{3,1,0,2:T(8,128)(2,1)}), bf16[4,72,8,128]{3,1,0,2:T(8,128)(2,1)S(1)}, u32[]{:S(2)}, u32[]{:S(2)}) async-start(bf16[4,72,8,128]{3,1,0,2:T(8,128)(2,1)} %select_bitcast_fusion), calls=%async_computation | async-start | bytes 1179648 | tf_op jit(solution)/shard_map/all_to_all | solution.py:50
  58.1 0.0 copy-done.5
  58.1 0.1 select_reduce_fusion
  58.2 15.9 %all-to-all-done = bf16[4,72,8,128]{3,1,0,2:T(8,128)(2,1)S(1)} async-done(((bf16[4,72,8,128]{3,1,0,2:T(8,128)(2,1)}), bf16[4,72,8,128]{3,1,0,2:T(8,128)(2,1)S(1)}, u32[]{:S(2)}, u32[]{:S(2)}) %all-to-all-start) | async-done | bytes 589856 | tf_op jit(solution)/shard_map/all_to_all | solution.py:50
  74.1 0.3 fusion.31
  74.4 0.3 fusion.17
  74.7 0.9 %copy.27 = bf16[4,72,8,128]{3,2,1,0:T(8,128)(2,1)} copy(bf16[4,72,8,128]{3,1,2,0:T(8,128)(2,1)S(1)} %fusion.17) | data formatting | bytes 1179648 | tf_op jit(solution)/shard_map/convert_element_type | solution.py:57
  (8 shorter events, 0.0 us)
Async XLA Ops:
  0.0 74.1 %copy-start = (bf16[1,72,72]{2,1,0:T(8,128)(2,1)S(1)}, bf16[1,72,72]{2,1,0:T(8,128)(2,1)}, u32[]{:S(2)}) copy-start(bf16[1,72,72]{2,1,0:T(8,128)(2,1)} %param.9) | copy-start | bytes 31108
  0.0 7.3 %copy-start.4 = (bf16[2,72,8,128]{3,2,1,0:T(8,128)(2,1)S(1)}, bf16[2,72,8,128]{3,2,1,0:T(8,128)(2,1)}, u32[]{:S(2)}) copy-start(bf16[2,72,8,128]{3,2,1,0:T(8,128)(2,1)} %param.7) | copy-start | bytes 884740
  0.0 6.3 %copy-start.6 = (s32[1,8]{1,0:T(1,128)S(1)}, s32[1,8]{1,0:T(1,128)}, u32[]{:S(2)}) copy-start(s32[1,8]{1,0:T(1,128)} %param.8) | copy-start | bytes 100
  2.3 12.6 %collective-permute-start = (bf16[6,72,3,128]{3,1,2,0:T(8,128)(2,1)S(1)}, bf16[6,72,3,128]{3,1,2,0:T(8,128)(2,1)S(1)}, u32[]{:S(2)}, u32[]{:S(2)}) collective-permute-start(bf16[6,72,3,128]{3,1,2,0:T(8,128)(2,1)S(1)} %get-tuple-element.17), channel_id=1, source_target_pairs={{0,8},{8,16},{16,24},{24,0},{1,9},{9,17},{17,25},{25,1},{2,10},{10... | collective-permute-start | bytes 995336 | tf_op jit(solution)/shard_map/ppermute | solution.py:16
  5.3 16.1 %collective-permute-start.1 = (bf16[6,72,3,128]{3,1,2,0:T(8,128)(2,1)S(1)}, bf16[6,72,3,128]{3,1,2,0:T(8,128)(2,1)S(1)}, u32[]{:S(2)}, u32[]{:S(2)}) collective-permute-start(bf16[6,72,3,128]{3,1,2,0:T(8,128)(2,1)S(1)} %get-tuple-element.18), channel_id=1, source_target_pairs={{8,0},{16,8},{24,16},{0,24},{9,1},{17,9},{25,17},{1,25},{10,2},{18... | collective-permute-start | bytes 995336 | tf_op jit(solution)/shard_map/ppermute | solution.py:18
  25.2 10.4 %collective-permute-start.2 = (bf16[6,72,14,3]{1,2,3,0:T(8,128)(2,1)S(1)}, bf16[6,72,14,3]{1,2,3,0:T(8,128)(2,1)}, u32[]{:S(2)}, u32[]{:S(2)}) collective-permute-start(bf16[6,72,14,3]{1,2,3,0:T(8,128)(2,1)S(1)} %copy.18), channel_id=1, source_target_pairs={{0,1},{1,2},{2,3},{3,4},{4,5},{5,6},{6,7},{7,0},{8,9},{9,10},{10,1... | collective-permute-start | bytes 108872 | tf_op jit(solution)/shard_map/ppermute | solution.py:16
  26.8 10.4 %collective-permute-start.3 = (bf16[6,72,14,3]{1,2,3,0:T(8,128)(2,1)}, bf16[6,72,14,3]{1,2,3,0:T(8,128)(2,1)}, u32[]{:S(2)}, u32[]{:S(2)}) collective-permute-start(bf16[6,72,14,3]{1,2,3,0:T(8,128)(2,1)} %copy.19), channel_id=1, source_target_pairs={{1,0},{2,1},{3,2},{4,3},{5,4},{6,5},{7,6},{0,7},{9,8},{10,9},{11,1... | collective-permute-start | bytes 108872 | tf_op jit(solution)/shard_map/ppermute | solution.py:18
  47.9 3.1 %copy-start.1 = (f32[72,8,128]{2,0,1:T(8,128)S(1)}, f32[72,8,128]{2,0,1:T(8,128)}, u32[]{:S(2)}) copy-start(f32[72,8,128]{2,0,1:T(8,128)} %copy.23) | copy-start | bytes 884740
  47.9 3.1 %copy-start.2 = (f32[72,8,128]{2,0,1:T(8,128)S(1)}, f32[72,8,128]{2,0,1:T(8,128)}, u32[]{:S(2)}) copy-start(f32[72,8,128]{2,0,1:T(8,128)} %copy.24) | copy-start | bytes 884740
  48.0 3.1 %copy-start.3 = (f32[72,8,128]{2,0,1:T(8,128)S(1)}, f32[72,8,128]{2,0,1:T(8,128)}, u32[]{:S(2)}) copy-start(f32[72,8,128]{2,0,1:T(8,128)} %copy.25) | copy-start | bytes 884740
  52.2 5.8 %copy-start.5 = (bf16[16,72,72]{2,1,0:T(8,128)(2,1)S(1)}, bf16[16,72,72]{2,1,0:T(8,128)(2,1)}, u32[]{:S(2)}) copy-start(bf16[16,72,72]{2,1,0:T(8,128)(2,1)} %param.11) | copy-start | bytes 497668
  53.8 20.2 %all-to-all-start = ((bf16[4,72,8,128]{3,1,0,2:T(8,128)(2,1)}), bf16[4,72,8,128]{3,1,0,2:T(8,128)(2,1)S(1)}, u32[]{:S(2)}, u32[]{:S(2)}) async-start(bf16[4,72,8,128]{3,1,0,2:T(8,128)(2,1)} %select_bitcast_fusion), calls=%async_computation | async-start | bytes 1179648 | tf_op jit(solution)/shard_map/all_to_all | solution.py:50

commit v2 on v1

--- a/solution.py
+++ b/solution.py
@@ -35,7 +35,10 @@
     return out.astype(jnp.bfloat16)
 
 
-def per_device(tracers, courant, destination, diffusion, band, band_table):
+CHUNKS = 2
+
+
+def advect_levels(tracers, courant):
     count = tracers.shape[0]
     fields = jnp.concatenate([tracers, courant], axis=0)
     padded = with_halo(fields, (("sec", 2), ("tile", 3)), STEPS)
@@ -44,10 +47,38 @@
     for step in range(STEPS):
         wind = wind[:, :, 1:-1, 1:-1]
         advected = advect_tile(advected, wind)
-    order = jnp.argsort(destination[0])
+    return advected
+
+
+def regroup(advected, order):
+    count = lax.axis_size("tile")
+    if count > 8:
+        ordered = jnp.take(advected, order, axis=2)
+        return lax.all_to_all(ordered, "tile", split_axis=2, concat_axis=2, tiled=True)
+    me = lax.axis_index("tile")
+    pieces = []
+    for shift in range(count):
+        row = jnp.take(order, (me + shift) % count)
+        piece = lax.dynamic_slice_in_dim(advected, row, 1, axis=2)
+        if shift:
+            piece = lax.ppermute(piece, "tile", [(i, (i + shift) % count) for i in range(count)])
+        pieces.append(piece)
+    stacked = jnp.concatenate(pieces, axis=2)
+    source = (me - jnp.arange(count, dtype=jnp.int32)) % count
+    return jnp.take(stacked, source, axis=2)
+
+
+def per_device(tracers, courant, destination, diffusion, band, band_table):
+    order = jnp.argsort(destination[0]).astype(jnp.int32)
+    levels = tracers.shape[1]
+    size = -(-levels // CHUNKS)
+    pieces = []
+    for start in range(0, levels, size):
+        stop = min(start + size, levels)
+        advected = advect_levels(tracers[:, start:stop], courant[:, start:stop])
+        pieces.append(regroup(advected, order))
+    received = jnp.concatenate(pieces, axis=1)
     band_count = band_table.shape[0]
-    ordered = jnp.take(advected, order, axis=2)
-    received = lax.all_to_all(ordered, "tile", split_axis=2, concat_axis=2, tiled=True)
     inverse = diffusion[0]
     diffused = jnp.einsum("kl,tlxy->tkxy", inverse, received, preferred_element_type=jnp.float32)
     diffused16 = diffused.astype(jnp.bfloat16)

time: 76.1 us -> 104 us (1.37)
  waiting for transfers between devices: 29 us -> 0.6 us
  other arithmetic: 15.7 us -> 37.6 us
  starting transfers between devices: 11.1 us -> 31 us
  local copies, waits for them, and re-layouts: 18.3 us -> 27.6 us
  between operations: 0.87 us -> 6.64 us
    ppermute x0 -> x14, starting transfers between devices: none -> 16.9 us  [regroup(): lax.ppermute(piece, 'tile', [(i, (i + shift) % count) for i in range(coun...]
    all_to_all x1 -> x0, waiting for transfers between devices: 15.9 us -> none  [per_device(): lax.all_to_all(ordered, 'tile', split_axis=2, concat_axis=2, tiled=True)]
    convert_element_type x3 -> x6, other arithmetic: 7.91 us -> 16.9 us  [advect_tile(): return out.astype(jnp.bfloat16)]
    mul x3 -> x5, other arithmetic: 1.66 us -> 10 us  [advect_tile(): 0.5 * cx * (north - south)]
    ppermute x2 -> x4, waiting for transfers between devices: 6.64 us -> 0.01 us  [with_halo(): lax.ppermute(tail, axis, [(i, (i + 1) % count) for i in range(count)])]
    ppermute x2 -> x4, waiting for transfers between devices: 6.53 us -> 0.01 us  [with_halo(): lax.ppermute(head, axis, [((i + 1) % count, i) for i in range(count)])]
    ppermute x2 -> x4, starting transfers between devices: 4.54 us -> 10 us  [with_halo(): lax.ppermute(head, axis, [((i + 1) % count, i) for i in range(count)])]
    ppermute x1 -> x2, local copies, waits for them, and re-layouts: 1.61 us -> 5.89 us  [with_halo(): lax.ppermute(tail, axis, [(i, (i + 1) % count) for i in range(count)])]
  transfers between devices with their start and end apart: 5 -> 22, of which waited for: 3 -> 2; matrix products, arithmetic and copies ran while one was open for 14% -> 39% of each run, Pallas kernels for 0% -> 0%
where the time goes in v2:
time: 104 us
  other arithmetic  37.6 us (36%)
  starting transfers between devices  31 us (30%)
  local copies, waits for them, and re-layouts  27.6 us (27%)
  between operations  6.64 us (6%)
    ppermute x14, starting transfers between devices, regroup(): lax.ppermute(piece, 'tile', [(i, (i + shift) % count) for i in range(coun...  16.9 us
    convert_element_type x6, other arithmetic, advect_tile(): return out.astype(jnp.bfloat16)  16.9 us
    mul x5, other arithmetic, advect_tile(): 0.5 * cx * (north - south)  10 us
    ppermute x4, starting transfers between devices, with_halo(): lax.ppermute(head, axis, [((i + 1) % count, i) for i in range(count)])  10 us
    concatenate x4, other arithmetic, with_halo(): jnp.concatenate([lax.ppermute(tail, axis, [(i, (i + 1) % count) for i in...  8.14 us
    ppermute x2, local copies, waits for them, and re-layouts, with_halo(): lax.ppermute(tail, axis, [(i, (i + 1) % count) for i in range(count)])  5.89 us
    ppermute x2, local copies, waits for them, and re-layouts, with_halo(): lax.ppermute(head, axis, [((i + 1) % count, i) for i in range(count)])  5.82 us
    ppermute x4, starting transfers between devices, with_halo(): lax.ppermute(tail, axis, [(i, (i + 1) % count) for i in range(count)])  4.04 us
  transfers between devices with their start and end apart: 22, of which 2 were waited for; matrix products, arithmetic and copies ran while one was open for 39% of the time, Pallas kernels for 0%

profile of v2, /device:TPU:0, one launch (start us, length us, event | category | flops | bytes accessed | tf_op | source)
XLA Modules:
  0.0 104.0 jit_solution(3949033460510338144)
XLA Ops:
  0.0 1.1 %fusion.84 = (bf16[4,36,8,128]{3,2,1,0:T(8,128)(2,1)S(1)}, bf16[4,36,8,128]{3,2,1,0:T(8,128)(2,1)S(1)}) fusion(bf16[4,72,8,128]{3,2,1,0:T(8,128)(2,1)} %param.8), kind=kLoop, calls=%fused_computation.215 | loop fusion | bytes 1179648 | tf_op jit(solution)/shard_map/slice | solution.py:78
  1.7 3.0 %collective-permute-start.11 = (bf16[6,36,3,128]{3,0,2,1:T(8,128)(2,1)S(1)}, bf16[6,36,3,128]{3,0,2,1:T(8,128)(2,1)S(1)}, u32[]{:S(2)}, u32[]{:S(2)}) collective-permute-start(bf16[6,36,3,128]{3,0,2,1:T(8,128)(2,1)S(1)} %get-tuple-element.120), channel_id=1, source_target_pairs={{0,8},{8,16},{16,24},{24,0},{1,9},{9,17},{17,25},{25,1},{2,10},{10... | collective-permute-start | bytes 497672 | tf_op jit(solution)/shard_map/ppermute | solution.py:16
  4.7 1.0 collective-permute-start.12
  6.0 1.0 pad_maximum_fusion.7
  7.0 1.0 collective-permute-start
  8.0 1.9 %collective-permute-start.1 = (bf16[6,36,3,128]{3,0,2,1:T(8,128)(2,1)}, bf16[6,36,3,128]{3,0,2,1:T(8,128)(2,1)S(1)}, u32[]{:S(2)}, u32[]{:S(2)}) collective-permute-start(bf16[6,36,3,128]{3,0,2,1:T(8,128)(2,1)} %get-tuple-element.119), channel_id=1, source_target_pairs={{8,0},{16,8},{24,16},{0,24},{9,1},{17,9},{25,17},{1,25},{10,2},{18... | collective-permute-start | bytes 497672 | tf_op jit(solution)/shard_map/ppermute | solution.py:18
  9.9 1.1 %multiply_bitcast_fusion.3 = (f32[36,8,128]{2,1,0:T(8,128)}, f32[36,8,128]{2,1,0:T(8,128)}, f32[36,8,128]{2,1,0:T(8,128)}, f32[36,8,128]{2,1,0:T(8,128)}, f32[36...) fusion(bf16[2,72,8,128]{3,2,1,0:T(8,128)(2,1)S(1)} %copy-done.8), kind=kLoop, calls=%fused_computation.159 | loop fusion | flops 442368 | bytes 1474560 | tf_op jit(solution)/shard_map/mul | solution.py:33
  11.9 1.0 sort.17
  12.8 0.7 fusion.86
  18.8 0.7 copy-done.11
  19.5 0.7 copy-done.13
  20.6 0.5 fusion.83
  21.1 1.0 copy.79
  22.1 1.6 %copy.80 = bf16[6,36,14,3]{1,2,3,0:T(8,128)(2,1)} copy(bf16[6,36,14,3]{3,0,2,1:T(8,128)(2,1)S(1)} %get-tuple-element.115) | data formatting | bytes 36288 | tf_op jit(solution)/shard_map/slice | solution.py:12
  23.7 3.5 %collective-permute-start.14 = (bf16[6,36,14,3]{1,2,3,0:T(8,128)(2,1)}, bf16[6,36,14,3]{1,2,3,0:T(8,128)(2,1)}, u32[]{:S(2)}, u32[]{:S(2)}) collective-permute-start(bf16[6,36,14,3]{1,2,3,0:T(8,128)(2,1)} %copy.80), channel_id=1, source_target_pairs={{1,0},{2,1},{3,2},{4,3},{5,4},{6,5},{7,6},{0,7},{9,8},{10,9},{11,1... | collective-permute-start | bytes 54440 | tf_op jit(solution)/shard_map/ppermute | solution.py:18
  27.7 0.5 fusion.82
  28.2 1.6 %copy.56 = bf16[6,36,14,3]{1,2,3,0:T(8,128)(2,1)} copy(bf16[6,36,14,3]{3,0,2,1:T(8,128)(2,1)S(1)} %get-tuple-element.112) | data formatting | bytes 36288 | tf_op jit(solution)/shard_map/slice | solution.py:13
  29.8 1.6 %copy.57 = bf16[6,36,14,3]{1,2,3,0:T(8,128)(2,1)} copy(bf16[6,36,14,3]{3,0,2,1:T(8,128)(2,1)S(1)} %get-tuple-element.113) | data formatting | bytes 36288 | tf_op jit(solution)/shard_map/slice | solution.py:12
  31.4 3.5 %collective-permute-start.3 = (bf16[6,36,14,3]{1,2,3,0:T(8,128)(2,1)}, bf16[6,36,14,3]{1,2,3,0:T(8,128)(2,1)}, u32[]{:S(2)}, u32[]{:S(2)}) collective-permute-start(bf16[6,36,14,3]{1,2,3,0:T(8,128)(2,1)} %copy.57), channel_id=1, source_target_pairs={{1,0},{2,1},{3,2},{4,3},{5,4},{6,5},{7,6},{0,7},{9,8},{10,9},{11,1... | collective-permute-start | bytes 54440 | tf_op jit(solution)/shard_map/ppermute | solution.py:18
  34.9 2.9 %copy.81 = bf16[6,36,14,3]{3,0,2,1:T(8,128)(2,1)} copy(bf16[6,36,14,3]{1,2,3,0:T(8,128)(2,1)} %collective-permute-done.13) | data formatting | bytes 36288 | tf_op jit(solution)/shard_map/ppermute | solution.py:16
  37.9 2.9 %copy.82 = bf16[6,36,14,3]{3,0,2,1:T(8,128)(2,1)} copy(bf16[6,36,14,3]{1,2,3,0:T(8,128)(2,1)} %collective-permute-done.14) | data formatting | bytes 36288 | tf_op jit(solution)/shard_map/ppermute | solution.py:18
  40.8 3.7 %pad_maximum_fusion.1 = bf16[6,36,14,134]{3,0,2,1:T(8,128)(2,1)S(1)} fusion(bf16[6,36,14,3]{3,0,2,1:T(8,128)(2,1)} %copy.82, bf16[6,36,3,128]{3,0,2,1:T(8,128)(2,1)} %copy-done.13, bf16[2,36,8,128]{3,0,2,1:T(2,128)(2,1)S(1)} %copy.122, bf16[4,36,8,128]{3,0,2,1:T(4,128)(2,1)S(1)} %copy.121, bf16[6,36,3,128]{3,0,2,1:T(8,128)(2,1)S(1)} %copy-done.12, ...), kind=kLoop, calls=%fused_computation.19 | loop fusion | flops 4862592 | bytes 1620864 | tf_op jit(solution)/shard_map/concatenate | solution.py:14
  44.5 2.9 %fusion.63 = (f32[1,36,12,132]{3,0,2,1:T(1,128)}, f32[1,36,12,132]{3,0,2,1:T(1,128)S(1)}, f32[1,36,12,132]{3,0,2,1:T(1,128)}, f32[1,36,12,132]{3,0,2,1:T(1,128)}) fusion(bf16[6,36,14,134]{3,0,2,1:T(8,128)(2,1)S(1)} %pad_maximum_fusion.1), kind=kLoop, calls=%fused_computation.145 | loop fusion | flops 342144 | bytes 1140480 | tf_op jit(solution)/shard_map/mul | solution.py:33
  47.4 2.6 %fusion.71 = (f32[1,36,10,130]{3,0,2,1:T(1,128)}, f32[1,36,10,130]{3,0,2,1:T(1,128)}, f32[1,36,10,130]{3,0,2,1:T(1,128)}, f32[1,36,10,130]{3,0,2,1:T(1,128)}) fusion(bf16[6,36,14,134]{3,0,2,1:T(8,128)(2,1)S(1)} %pad_maximum_fusion.1), kind=kLoop, calls=%fused_computation.165 | loop fusion | flops 280800 | bytes 936000 | tf_op jit(solution)/shard_map/mul | solution.py:33
  50.0 2.9 %copy.58 = bf16[6,36,14,3]{3,0,2,1:T(8,128)(2,1)} copy(bf16[6,36,14,3]{1,2,3,0:T(8,128)(2,1)} %collective-permute-done.2) | data formatting | bytes 36288 | tf_op jit(solution)/shard_map/ppermute | solution.py:16
  53.0 2.9 %copy.59 = bf16[6,36,14,3]{3,0,2,1:T(8,128)(2,1)} copy(bf16[6,36,14,3]{1,2,3,0:T(8,128)(2,1)} %collective-permute-done.3) | data formatting | bytes 36288 | tf_op jit(solution)/shard_map/ppermute | solution.py:18
  55.9 3.6 %pad_maximum_fusion = bf16[6,36,14,134]{3,0,2,1:T(8,128)(2,1)S(1)} fusion(bf16[6,36,14,3]{3,0,2,1:T(8,128)(2,1)} %copy.59, bf16[6,36,3,128]{3,0,2,1:T(8,128)(2,1)S(1)} %copy-done.10, bf16[2,36,8,128]{3,0,2,1:T(2,128)(2,1)S(1)} %copy.120, bf16[4,36,8,128]{3,0,2,1:T(4,128)(2,1)S(1)} %copy.119, bf16[6,36,3,128]{3,0,2,1:T(8,128)(2,1)S(1)} %collective-permute-done, ...), kind=kLoop, calls=%fused_computation.18 | loop fusion | flops 4862592 | bytes 1620864 | tf_op jit(solution)/shard_map/concatenate | solution.py:14
  59.6 1.9 %fusion.59 = (f32[1,36,12,132]{3,0,2,1:T(1,128)S(1)}, f32[1,36,12,132]{3,0,2,1:T(1,128)S(1)}, f32[1,36,12,132]{3,0,2,1:T(1,128)S(1)}, f32[1,36,12,132]{3,0,2,1:T(1,128)S(1)}) fusion(bf16[6,36,14,134]{3,0,2,1:T(8,128)(2,1)S(1)} %pad_maximum_fusion), kind=kLoop, calls=%fused_computation.141 | loop fusion | flops 342144 | bytes 1140480 | tf_op jit(solution)/shard_map/mul | solution.py:33
  61.5 1.6 %fusion.67 = (f32[1,36,10,130]{3,0,2,1:T(1,128)S(1)}, f32[1,36,10,130]{3,0,2,1:T(1,128)S(1)}, f32[1,36,10,130]{3,0,2,1:T(1,128)S(1)}, f32[1,36,10,130]{3,0,2,1:T(1,128)S(1)}) fusion(bf16[6,36,14,134]{3,0,2,1:T(8,128)(2,1)S(1)} %pad_maximum_fusion), kind=kLoop, calls=%fused_computation.161 | loop fusion | flops 280800 | bytes 936000 | tf_op jit(solution)/shard_map/mul | solution.py:33
  63.4 0.6 copy-done.6
  64.5 4.1 %fusion.11 = bf16[4,36,12,132]{3,0,2,1:T(4,128)(2,1)S(1)} fusion(bf16[6,36,14,134]{3,0,2,1:T(8,128)(2,1)S(1)} %pad_maximum_fusion.1, f32[36,12,132]{2,1,0:T(8,128)S(1)} %get-tuple-element.166, f32[36,12,132]{2,1,0:T(8,128)S(1)} %get-tuple-element.167, f32[36,12,132]{2,1,0:T(8,128)S(1)} %get-tuple-element.168, f32[36,12,132]{2,1,0:T(8,128)S(1)} %get-tuple-element.169), kind=kLoop, calls=%fused_computation.47 | loop fusion | flops 4790016 | bytes 3649536 | tf_op jit(solution)/shard_map/convert_element_type | solution.py:35
  68.7 3.2 %fusion.27 = bf16[4,36,10,130]{3,0,2,1:T(4,128)(2,1)S(1)} fusion(bf16[4,36,12,132]{3,0,2,1:T(4,128)(2,1)S(1)} %fusion.11, f32[36,10,130]{2,1,0:T(8,128)S(1)} %get-tuple-element.170, f32[36,10,130]{2,1,0:T(8,128)S(1)} %get-tuple-element.171, f32[36,10,130]{2,1,0:T(8,128)S(1)} %get-tuple-element.172, f32[36,10,130]{2,1,0:T(8,128)S(1)} %get-tuple-element.173), kind=kLoop, calls=%fused_computation.63 | loop fusion | flops 3931200 | bytes 2995200 | tf_op jit(solution)/shard_map/convert_element_type | solution.py:35
  72.0 1.2 %fusion.45 = bf16[4,36,8,128]{3,0,2,1:T(4,128)(2,1)S(1)} fusion(bf16[4,36,10,130]{3,0,2,1:T(4,128)(2,1)S(1)} %fusion.27, f32[36,8,128]{2,1,0:T(8,128)S(1)} %copy-done.19, f32[36,8,128]{2,1,0:T(8,128)S(1)} %copy-done.20, f32[36,8,128]{2,1,0:T(8,128)S(1)} %copy-done.18, f32[36,8,128]{2,1,0:T(8,128)S(1)} %copy-done.21), kind=kLoop, calls=%fused_computation.100 | loop fusion | flops 3096576 | bytes 2359296 | tf_op jit(solution)/shard_map/convert_element_type | solution.py:35
  73.5 0.9 collective-permute-start.17
  74.4 3.2 %collective-permute-start.18 = (bf16[4,36,1,128]{3,0,2,1:T(4,128)(2,1)S(1)}, bf16[4,36,1,128]{3,0,2,1:T(4,128)(2,1)S(1)}, u32[]{:S(2)}, u32[]{:S(2)}) collective-permute-start(bf16[4,36,1,128]{3,0,2,1:T(4,128)(2,1)S(1)} %get-tuple-element.143), channel_id=1, source_target_pairs={{0,4},{1,5},{2,6},{3,7},{4,0},{5,1},{6,2},{7,3},{8,12},{9,13},{10,... | collective-permute-start | bytes 110600 | tf_op jit(solution)/shard_map/ppermute | solution.py:64
  78.1 3.9 %fusion.3 = bf16[4,36,12,132]{3,0,2,1:T(4,128)(2,1)S(1)} fusion(bf16[6,36,14,134]{3,0,2,1:T(8,128)(2,1)S(1)} %pad_maximum_fusion, f32[36,12,132]{2,1,0:T(8,128)S(1)} %get-tuple-element.158, f32[36,12,132]{2,1,0:T(8,128)S(1)} %get-tuple-element.159, f32[36,12,132]{2,1,0:T(8,128)S(1)} %get-tuple-element.160, f32[36,12,132]{2,1,0:T(8,128)S(1)} %get-tuple-element.161), kind=kLoop, calls=%fused_computation.39 | loop fusion | flops 4790016 | bytes 3649536 | tf_op jit(solution)/shard_map/convert_element_type | solution.py:35
  82.1 3.2 %fusion.19 = bf16[4,36,10,130]{3,0,2,1:T(4,128)(2,1)S(1)} fusion(bf16[4,36,12,132]{3,0,2,1:T(4,128)(2,1)S(1)} %fusion.3, f32[36,10,130]{2,1,0:T(8,128)S(1)} %get-tuple-element.162, f32[36,10,130]{2,1,0:T(8,128)S(1)} %get-tuple-element.163, f32[36,10,130]{2,1,0:T(8,128)S(1)} %get-tuple-element.164, f32[36,10,130]{2,1,0:T(8,128)S(1)} %get-tuple-element.165), kind=kLoop, calls=%fused_computation.55 | loop fusion | flops 3931200 | bytes 2995200 | tf_op jit(solution)/shard_map/convert_element_type | solution.py:35
  85.3 1.2 %fusion.37 = bf16[4,36,8,128]{3,0,2,1:T(4,128)(2,1)S(1)} fusion(bf16[4,36,10,130]{3,0,2,1:T(4,128)(2,1)S(1)} %fusion.19, f32[36,8,128]{2,1,0:T(8,128)S(1)} %copy-done.16, f32[36,8,128]{2,1,0:T(8,128)S(1)} %copy-done.17, f32[36,8,128]{2,1,0:T(8,128)S(1)} %copy-done.15, f32[36,8,128]{2,1,0:T(8,128)S(1)} %copy-done.14), kind=kLoop, calls=%fused_computation.92 | loop fusion | flops 3096576 | bytes 2359296 | tf_op jit(solution)/shard_map/convert_element_type | solution.py:35
  86.7 2.7 %collective-permute-start.20 = (bf16[4,36,1,128]{3,0,2,1:T(4,128)(2,1)S(1)}, bf16[4,36,1,128]{3,0,2,1:T(4,128)(2,1)S(1)}, u32[]{:S(2)}, u32[]{:S(2)}) collective-permute-start(bf16[4,36,1,128]{3,0,2,1:T(4,128)(2,1)S(1)} %get-tuple-element.141), channel_id=1, source_target_pairs={{0,6},{1,7},{2,0},{3,1},{4,2},{5,3},{6,4},{7,5},{8,14},{9,15},{10,... | collective-permute-start | bytes 110600 | tf_op jit(solution)/shard_map/ppermute | solution.py:64
  89.6 0.5 collective-permute-start.4
  90.1 1.4 %collective-permute-start.5 = (bf16[4,36,1,128]{3,0,2,1:T(4,128)(2,1)S(1)}, bf16[4,36,1,128]{3,0,2,1:T(4,128)(2,1)S(1)}, u32[]{:S(2)}, u32[]{:S(2)}) collective-permute-start(bf16[4,36,1,128]{3,0,2,1:T(4,128)(2,1)S(1)} %get-tuple-element.127), channel_id=1, source_target_pairs={{0,2},{1,3},{2,4},{3,5},{4,6},{5,7},{6,0},{7,1},{8,10},{9,11},{10,... | collective-permute-start | bytes 110600 | tf_op jit(solution)/shard_map/ppermute | solution.py:64
  91.6 1.4 %collective-permute-start.6 = (bf16[4,36,1,128]{3,0,2,1:T(4,128)(2,1)S(1)}, bf16[4,36,1,128]{3,0,2,1:T(4,128)(2,1)S(1)}, u32[]{:S(2)}, u32[]{:S(2)}) collective-permute-start(bf16[4,36,1,128]{3,0,2,1:T(4,128)(2,1)S(1)} %get-tuple-element.126), channel_id=1, source_target_pairs={{0,3},{1,4},{2,5},{3,6},{4,7},{5,0},{6,1},{7,2},{8,11},{9,12},{10,... | collective-permute-start | bytes 110600 | tf_op jit(solution)/shard_map/ppermute | solution.py:64
  93.0 2.4 %collective-permute-start.7 = (bf16[4,36,1,128]{3,0,2,1:T(4,128)(2,1)S(1)}, bf16[4,36,1,128]{3,0,2,1:T(4,128)(2,1)S(1)}, u32[]{:S(2)}, u32[]{:S(2)}) collective-permute-start(bf16[4,36,1,128]{3,0,2,1:T(4,128)(2,1)S(1)} %get-tuple-element.125), channel_id=1, source_target_pairs={{0,4},{1,5},{2,6},{3,7},{4,0},{5,1},{6,2},{7,3},{8,12},{9,13},{10,... | collective-permute-start | bytes 110600 | tf_op jit(solution)/shard_map/ppermute | solution.py:64
  95.6 2.7 %collective-permute-start.9 = (bf16[4,36,1,128]{3,0,2,1:T(4,128)(2,1)S(1)}, bf16[4,36,1,128]{3,0,2,1:T(4,128)(2,1)S(1)}, u32[]{:S(2)}, u32[]{:S(2)}) collective-permute-start(bf16[4,36,1,128]{3,0,2,1:T(4,128)(2,1)S(1)} %get-tuple-element.123), channel_id=1, source_target_pairs={{0,6},{1,7},{2,0},{3,1},{4,2},{5,3},{6,4},{7,5},{8,14},{9,15},{10,... | collective-permute-start | bytes 110600 | tf_op jit(solution)/shard_map/ppermute | solution.py:64
  98.3 1.5 %collective-permute-start.10 = (bf16[4,36,1,128]{3,0,2,1:T(4,128)(2,1)S(1)}, bf16[4,36,1,128]{3,0,2,1:T(4,128)(2,1)S(1)}, u32[]{:S(2)}, u32[]{:S(2)}) collective-permute-start(bf16[4,36,1,128]{3,0,2,1:T(4,128)(2,1)S(1)} %get-tuple-element.122), channel_id=1, source_target_pairs={{0,7},{1,0},{2,1},{3,2},{4,3},{5,4},{6,5},{7,6},{8,15},{9,8},{10,9... | collective-permute-start | bytes 110600 | tf_op jit(solution)/shard_map/ppermute | solution.py:64
  100.2 0.9 gather_fusion.1
  101.5 0.9 gather_fusion
  103.1 0.9 copy.100
  (115 shorter events, 5.6 us)
Async XLA Ops:
  0.0 102.5 %copy-start = (bf16[1,72,72]{2,1,0:T(8,128)(2,1)S(1)}, bf16[1,72,72]{2,1,0:T(8,128)(2,1)}, u32[]{:S(2)}) copy-start(bf16[1,72,72]{2,1,0:T(8,128)(2,1)} %param.11) | copy-start | bytes 31108
  0.0 1.3 %copy-start.8 = (bf16[2,72,8,128]{3,2,1,0:T(8,128)(2,1)S(1)}, bf16[2,72,8,128]{3,2,1,0:T(8,128)(2,1)}, u32[]{:S(2)}) copy-start(bf16[2,72,8,128]{3,2,1,0:T(8,128)(2,1)} %param.9) | copy-start | bytes 884740
  1.7 10.1 %copy-start.23 = (s32[1,8]{1,0:T(1,128)S(1)}, s32[1,8]{1,0:T(1,128)}, u32[]{:S(2)}) copy-start(s32[1,8]{1,0:T(1,128)} %param.10) | copy-start | bytes 100
  1.7 17.1 %collective-permute-start.11 = (bf16[6,36,3,128]{3,0,2,1:T(8,128)(2,1)S(1)}, bf16[6,36,3,128]{3,0,2,1:T(8,128)(2,1)S(1)}, u32[]{:S(2)}, u32[]{:S(2)}) collective-permute-start(bf16[6,36,3,128]{3,0,2,1:T(8,128)(2,1)S(1)} %get-tuple-element.120), channel_id=1, source_target_pairs={{0,8},{8,16},{16,24},{24,0},{1,9},{9,17},{17,25},{25,1},{2,10},{10... | collective-permute-start | bytes 497672 | tf_op jit(solution)/shard_map/ppermute | solution.py:16
  4.7 14.1 %collective-permute-start.12 = (bf16[6,36,3,128]{3,0,2,1:T(8,128)(2,1)S(1)}, bf16[6,36,3,128]{3,0,2,1:T(8,128)(2,1)S(1)}, u32[]{:S(2)}, u32[]{:S(2)}) collective-permute-start(bf16[6,36,3,128]{3,0,2,1:T(8,128)(2,1)S(1)} %get-tuple-element.121), channel_id=1, source_target_pairs={{8,0},{16,8},{24,16},{0,24},{9,1},{17,9},{25,17},{1,25},{10,2},{18... | collective-permute-start | bytes 497672 | tf_op jit(solution)/shard_map/ppermute | solution.py:18
  5.7 12.9 %copy-start.22 = (bf16[16,72,72]{2,1,0:T(8,128)(2,1)S(1)}, bf16[16,72,72]{2,1,0:T(8,128)(2,1)}, u32[]{:S(2)}) copy-start(bf16[16,72,72]{2,1,0:T(8,128)(2,1)} %param.13) | copy-start | bytes 497668
  7.0 20.2 %collective-permute-start = (bf16[6,36,3,128]{3,0,2,1:T(8,128)(2,1)}, bf16[6,36,3,128]{3,0,2,1:T(8,128)(2,1)S(1)}, u32[]{:S(2)}, u32[]{:S(2)}) collective-permute-start(bf16[6,36,3,128]{3,0,2,1:T(8,128)(2,1)} %get-tuple-element.118), channel_id=1, source_target_pairs={{0,8},{8,16},{16,24},{24,0},{1,9},{9,17},{17,25},{25,1},{2,10},{10... | collective-permute-start | bytes 497672 | tf_op jit(solution)/shard_map/ppermute | solution.py:16
  8.0 19.2 %collective-permute-start.1 = (bf16[6,36,3,128]{3,0,2,1:T(8,128)(2,1)}, bf16[6,36,3,128]{3,0,2,1:T(8,128)(2,1)S(1)}, u32[]{:S(2)}, u32[]{:S(2)}) collective-permute-start(bf16[6,36,3,128]{3,0,2,1:T(8,128)(2,1)} %get-tuple-element.119), channel_id=1, source_target_pairs={{8,0},{16,8},{24,16},{0,24},{9,1},{17,9},{25,17},{1,25},{10,2},{18... | collective-permute-start | bytes 497672 | tf_op jit(solution)/shard_map/ppermute | solution.py:18
  18.8 0.7 copy-start.11
  19.5 0.7 copy-start.13
  22.1 12.9 %collective-permute-start.13 = (bf16[6,36,14,3]{1,2,3,0:T(8,128)(2,1)S(1)}, bf16[6,36,14,3]{1,2,3,0:T(8,128)(2,1)}, u32[]{:S(2)}, u32[]{:S(2)}) collective-permute-start(bf16[6,36,14,3]{1,2,3,0:T(8,128)(2,1)S(1)} %copy.79), channel_id=1, source_target_pairs={{0,1},{1,2},{2,3},{3,4},{4,5},{5,6},{6,7},{7,0},{8,9},{9,10},{10,1... | collective-permute-start | bytes 54440 | tf_op jit(solution)/shard_map/ppermute | solution.py:16
  23.7 14.2 %collective-permute-start.14 = (bf16[6,36,14,3]{1,2,3,0:T(8,128)(2,1)}, bf16[6,36,14,3]{1,2,3,0:T(8,128)(2,1)}, u32[]{:S(2)}, u32[]{:S(2)}) collective-permute-start(bf16[6,36,14,3]{1,2,3,0:T(8,128)(2,1)} %copy.80), channel_id=1, source_target_pairs={{1,0},{2,1},{3,2},{4,3},{5,4},{6,5},{7,6},{0,7},{9,8},{10,9},{11,1... | collective-permute-start | bytes 54440 | tf_op jit(solution)/shard_map/ppermute | solution.py:18
  27.3 0.9 copy-start.9
  29.8 11.0 %copy-start.12 = (bf16[6,36,3,128]{3,0,2,1:T(8,128)(2,1)S(1)}, bf16[6,36,3,128]{3,0,2,1:T(8,128)(2,1)}, u32[]{:S(2)}) copy-start(bf16[6,36,3,128]{3,0,2,1:T(8,128)(2,1)} %copy-done.11) | copy-start | bytes 497668
  29.8 20.3 %collective-permute-start.2 = (bf16[6,36,14,3]{1,2,3,0:T(8,128)(2,1)}, bf16[6,36,14,3]{1,2,3,0:T(8,128)(2,1)}, u32[]{:S(2)}, u32[]{:S(2)}) collective-permute-start(bf16[6,36,14,3]{1,2,3,0:T(8,128)(2,1)} %copy.56), channel_id=1, source_target_pairs={{0,1},{1,2},{2,3},{3,4},{4,5},{5,6},{6,7},{7,0},{8,9},{9,10},{10,1... | collective-permute-start | bytes 54440 | tf_op jit(solution)/shard_map/ppermute | solution.py:16
  31.4 21.6 %collective-permute-start.3 = (bf16[6,36,14,3]{1,2,3,0:T(8,128)(2,1)}, bf16[6,36,14,3]{1,2,3,0:T(8,128)(2,1)}, u32[]{:S(2)}, u32[]{:S(2)}) collective-permute-start(bf16[6,36,14,3]{1,2,3,0:T(8,128)(2,1)} %copy.57), channel_id=1, source_target_pairs={{1,0},{2,1},{3,2},{4,3},{5,4},{6,5},{7,6},{0,7},{9,8},{10,9},{11,1... | collective-permute-start | bytes 54440 | tf_op jit(solution)/shard_map/ppermute | solution.py:18
  47.4 8.5 %copy-start.10 = (bf16[6,36,3,128]{3,0,2,1:T(8,128)(2,1)S(1)}, bf16[6,36,3,128]{3,0,2,1:T(8,128)(2,1)}, u32[]{:S(2)}) copy-start(bf16[6,36,3,128]{3,0,2,1:T(8,128)(2,1)} %copy-done.9) | copy-start | bytes 497668
  61.4 1.6 %copy-start.2 = (f32[1,36,12,132]{3,0,2,1:T(1,128)S(1)}, f32[1,36,12,132]{3,0,2,1:T(1,128)}, u32[]{:S(2)}) copy-start(f32[1,36,12,132]{3,0,2,1:T(1,128)} %get-tuple-element.108) | copy-start | bytes 684292
  61.4 1.6 %copy-start.3 = (f32[1,36,12,132]{3,0,2,1:T(1,128)S(1)}, f32[1,36,12,132]{3,0,2,1:T(1,128)}, u32[]{:S(2)}) copy-start(f32[1,36,12,132]{3,0,2,1:T(1,128)} %get-tuple-element.110) | copy-start | bytes 684292
  61.4 1.8 %copy-start.1 = (f32[1,36,12,132]{3,0,2,1:T(1,128)S(1)}, f32[1,36,12,132]{3,0,2,1:T(1,128)}, u32[]{:S(2)}) copy-start(f32[1,36,12,132]{3,0,2,1:T(1,128)} %get-tuple-element.111) | copy-start | bytes 684292
  63.0 1.0 copy-start.6
  63.0 1.1 %copy-start.7 = (f32[1,36,10,130]{3,0,2,1:T(1,128)S(1)}, f32[1,36,10,130]{3,0,2,1:T(1,128)}, u32[]{:S(2)}) copy-start(f32[1,36,10,130]{3,0,2,1:T(1,128)} %get-tuple-element.106) | copy-start | bytes 561604
  63.2 1.1 %copy-start.4 = (f32[1,36,10,130]{3,0,2,1:T(1,128)S(1)}, f32[1,36,10,130]{3,0,2,1:T(1,128)}, u32[]{:S(2)}) copy-start(f32[1,36,10,130]{3,0,2,1:T(1,128)} %get-tuple-element.105) | copy-start | bytes 561604
  63.2 1.2 %copy-start.5 = (f32[1,36,10,130]{3,0,2,1:T(1,128)S(1)}, f32[1,36,10,130]{3,0,2,1:T(1,128)}, u32[]{:S(2)}) copy-start(f32[1,36,10,130]{3,0,2,1:T(1,128)} %get-tuple-element.107) | copy-start | bytes 561604
  68.7 3.2 %copy-start.18 = (f32[36,8,128]{2,1,0:T(8,128)S(1)}, f32[36,8,128]{2,1,0:T(8,128)}, u32[]{:S(2)}) copy-start(f32[36,8,128]{2,1,0:T(8,128)} %get-tuple-element.133) | copy-start | bytes 442372
  68.7 3.2 %copy-start.19 = (f32[36,8,128]{2,1,0:T(8,128)S(1)}, f32[36,8,128]{2,1,0:T(8,128)}, u32[]{:S(2)}) copy-start(f32[36,8,128]{2,1,0:T(8,128)} %get-tuple-element.134) | copy-start | bytes 442372
  68.7 3.2 %copy-start.20 = (f32[36,8,128]{2,1,0:T(8,128)S(1)}, f32[36,8,128]{2,1,0:T(8,128)}, u32[]{:S(2)}) copy-start(f32[36,8,128]{2,1,0:T(8,128)} %get-tuple-element.136) | copy-start | bytes 442372
  68.7 3.2 %copy-start.21 = (f32[36,8,128]{2,1,0:T(8,128)S(1)}, f32[36,8,128]{2,1,0:T(8,128)}, u32[]{:S(2)}) copy-start(f32[36,8,128]{2,1,0:T(8,128)} %get-tuple-element.137) | copy-start | bytes 442372
  73.3 13.4 %collective-permute-start.15 = (bf16[4,36,1,128]{3,0,2,1:T(4,128)(2,1)S(1)}, bf16[4,36,1,128]{3,0,2,1:T(4,128)(2,1)S(1)}, u32[]{:S(2)}, u32[]{:S(2)}) collective-permute-start(bf16[4,36,1,128]{3,0,2,1:T(4,128)(2,1)S(1)} %get-tuple-element.146), channel_id=1, source_target_pairs={{0,1},{1,2},{2,3},{3,4},{4,5},{5,6},{6,7},{7,0},{8,9},{9,10},{10,1... | collective-permute-start | bytes 110600 | tf_op jit(solution)/shard_map/ppermute | solution.py:64
  73.4 16.0 %collective-permute-start.16 = (bf16[4,36,1,128]{3,0,2,1:T(4,128)(2,1)S(1)}, bf16[4,36,1,128]{3,0,2,1:T(4,128)(2,1)S(1)}, u32[]{:S(2)}, u32[]{:S(2)}) collective-permute-start(bf16[4,36,1,128]{3,0,2,1:T(4,128)(2,1)S(1)} %get-tuple-element.145), channel_id=1, source_target_pairs={{0,2},{1,3},{2,4},{3,5},{4,6},{5,7},{6,0},{7,1},{8,10},{9,11},{10,... | collective-permute-start | bytes 110600 | tf_op jit(solution)/shard_map/ppermute | solution.py:64
  73.5 16.1 %collective-permute-start.17 = (bf16[4,36,1,128]{3,0,2,1:T(4,128)(2,1)S(1)}, bf16[4,36,1,128]{3,0,2,1:T(4,128)(2,1)S(1)}, u32[]{:S(2)}, u32[]{:S(2)}) collective-permute-start(bf16[4,36,1,128]{3,0,2,1:T(4,128)(2,1)S(1)} %get-tuple-element.144), channel_id=1, source_target_pairs={{0,3},{1,4},{2,5},{3,6},{4,7},{5,0},{6,1},{7,2},{8,11},{9,12},{10,... | collective-permute-start | bytes 110600 | tf_op jit(solution)/shard_map/ppermute | solution.py:64
  74.4 15.7 %collective-permute-start.18 = (bf16[4,36,1,128]{3,0,2,1:T(4,128)(2,1)S(1)}, bf16[4,36,1,128]{3,0,2,1:T(4,128)(2,1)S(1)}, u32[]{:S(2)}, u32[]{:S(2)}) collective-permute-start(bf16[4,36,1,128]{3,0,2,1:T(4,128)(2,1)S(1)} %get-tuple-element.143), channel_id=1, source_target_pairs={{0,4},{1,5},{2,6},{3,7},{4,0},{5,1},{6,2},{7,3},{8,12},{9,13},{10,... | collective-permute-start | bytes 110600 | tf_op jit(solution)/shard_map/ppermute | solution.py:64
  77.5 14.0 %collective-permute-start.19 = (bf16[4,36,1,128]{3,0,2,1:T(4,128)(2,1)S(1)}, bf16[4,36,1,128]{3,0,2,1:T(4,128)(2,1)S(1)}, u32[]{:S(2)}, u32[]{:S(2)}) collective-permute-start(bf16[4,36,1,128]{3,0,2,1:T(4,128)(2,1)S(1)} %get-tuple-element.142), channel_id=1, source_target_pairs={{0,5},{1,6},{2,7},{3,0},{4,1},{5,2},{6,3},{7,4},{8,13},{9,14},{10,... | collective-permute-start | bytes 110600 | tf_op jit(solution)/shard_map/ppermute | solution.py:64
  82.1 3.2 %copy-start.14 = (f32[36,8,128]{2,1,0:T(8,128)S(1)}, f32[36,8,128]{2,1,0:T(8,128)}, u32[]{:S(2)}) copy-start(f32[36,8,128]{2,1,0:T(8,128)} %get-tuple-element.130) | copy-start | bytes 442372
  82.1 3.2 %copy-start.15 = (f32[36,8,128]{2,1,0:T(8,128)S(1)}, f32[36,8,128]{2,1,0:T(8,128)}, u32[]{:S(2)}) copy-start(f32[36,8,128]{2,1,0:T(8,128)} %get-tuple-element.131) | copy-start | bytes 442372
  82.1 3.2 %copy-start.16 = (f32[36,8,128]{2,1,0:T(8,128)S(1)}, f32[36,8,128]{2,1,0:T(8,128)}, u32[]{:S(2)}) copy-start(f32[36,8,128]{2,1,0:T(8,128)} %get-tuple-element.132) | copy-start | bytes 442372
  82.1 3.2 %copy-start.17 = (f32[36,8,128]{2,1,0:T(8,128)S(1)}, f32[36,8,128]{2,1,0:T(8,128)}, u32[]{:S(2)}) copy-start(f32[36,8,128]{2,1,0:T(8,128)} %get-tuple-element.135) | copy-start | bytes 442372
  86.7 6.3 %collective-permute-start.20 = (bf16[4,36,1,128]{3,0,2,1:T(4,128)(2,1)S(1)}, bf16[4,36,1,128]{3,0,2,1:T(4,128)(2,1)S(1)}, u32[]{:S(2)}, u32[]{:S(2)}) collective-permute-start(bf16[4,36,1,128]{3,0,2,1:T(4,128)(2,1)S(1)} %get-tuple-element.141), channel_id=1, source_target_pairs={{0,6},{1,7},{2,0},{3,1},{4,2},{5,3},{6,4},{7,5},{8,14},{9,15},{10,... | collective-permute-start | bytes 110600 | tf_op jit(solution)/shard_map/ppermute | solution.py:64
  89.4 6.1 %collective-permute-start.21 = (bf16[4,36,1,128]{3,0,2,1:T(4,128)(2,1)S(1)}, bf16[4,36,1,128]{3,0,2,1:T(4,128)(2,1)S(1)}, u32[]{:S(2)}, u32[]{:S(2)}) collective-permute-start(bf16[4,36,1,128]{3,0,2,1:T(4,128)(2,1)S(1)} %get-tuple-element.140), channel_id=1, source_target_pairs={{0,7},{1,0},{2,1},{3,2},{4,3},{5,4},{6,5},{7,6},{8,15},{9,8},{10,9... | collective-permute-start | bytes 110600 | tf_op jit(solution)/shard_map/ppermute | solution.py:64
  89.6 6.0 %collective-permute-start.4 = (bf16[4,36,1,128]{3,0,2,1:T(4,128)(2,1)S(1)}, bf16[4,36,1,128]{3,0,2,1:T(4,128)(2,1)S(1)}, u32[]{:S(2)}, u32[]{:S(2)}) collective-permute-start(bf16[4,36,1,128]{3,0,2,1:T(4,128)(2,1)S(1)} %get-tuple-element.128), channel_id=1, source_target_pairs={{0,1},{1,2},{2,3},{3,4},{4,5},{5,6},{6,7},{7,0},{8,9},{9,10},{10,1... | collective-permute-start | bytes 110600 | tf_op jit(solution)/shard_map/ppermute | solution.py:64
  90.1 8.2 %collective-permute-start.5 = (bf16[4,36,1,128]{3,0,2,1:T(4,128)(2,1)S(1)}, bf16[4,36,1,128]{3,0,2,1:T(4,128)(2,1)S(1)}, u32[]{:S(2)}, u32[]{:S(2)}) collective-permute-start(bf16[4,36,1,128]{3,0,2,1:T(4,128)(2,1)S(1)} %get-tuple-element.127), channel_id=1, source_target_pairs={{0,2},{1,3},{2,4},{3,5},{4,6},{5,7},{6,0},{7,1},{8,10},{9,11},{10,... | collective-permute-start | bytes 110600 | tf_op jit(solution)/shard_map/ppermute | solution.py:64
  91.6 8.3 %collective-permute-start.6 = (bf16[4,36,1,128]{3,0,2,1:T(4,128)(2,1)S(1)}, bf16[4,36,1,128]{3,0,2,1:T(4,128)(2,1)S(1)}, u32[]{:S(2)}, u32[]{:S(2)}) collective-permute-start(bf16[4,36,1,128]{3,0,2,1:T(4,128)(2,1)S(1)} %get-tuple-element.126), channel_id=1, source_target_pairs={{0,3},{1,4},{2,5},{3,6},{4,7},{5,0},{6,1},{7,2},{8,11},{9,12},{10,... | collective-permute-start | bytes 110600 | tf_op jit(solution)/shard_map/ppermute | solution.py:64
  93.0 6.9 %collective-permute-start.7 = (bf16[4,36,1,128]{3,0,2,1:T(4,128)(2,1)S(1)}, bf16[4,36,1,128]{3,0,2,1:T(4,128)(2,1)S(1)}, u32[]{:S(2)}, u32[]{:S(2)}) collective-permute-start(bf16[4,36,1,128]{3,0,2,1:T(4,128)(2,1)S(1)} %get-tuple-element.125), channel_id=1, source_target_pairs={{0,4},{1,5},{2,6},{3,7},{4,0},{5,1},{6,2},{7,3},{8,12},{9,13},{10,... | collective-permute-start | bytes 110600 | tf_op jit(solution)/shard_map/ppermute | solution.py:64
  95.5 4.5 %collective-permute-start.8 = (bf16[4,36,1,128]{3,0,2,1:T(4,128)(2,1)S(1)}, bf16[4,36,1,128]{3,0,2,1:T(4,128)(2,1)S(1)}, u32[]{:S(2)}, u32[]{:S(2)}) collective-permute-start(bf16[4,36,1,128]{3,0,2,1:T(4,128)(2,1)S(1)} %get-tuple-element.124), channel_id=1, source_target_pairs={{0,5},{1,6},{2,7},{3,0},{4,1},{5,2},{6,3},{7,4},{8,13},{9,14},{10,... | collective-permute-start | bytes 110600 | tf_op jit(solution)/shard_map/ppermute | solution.py:64
  95.6 4.6 %collective-permute-start.9 = (bf16[4,36,1,128]{3,0,2,1:T(4,128)(2,1)S(1)}, bf16[4,36,1,128]{3,0,2,1:T(4,128)(2,1)S(1)}, u32[]{:S(2)}, u32[]{:S(2)}) collective-permute-start(bf16[4,36,1,128]{3,0,2,1:T(4,128)(2,1)S(1)} %get-tuple-element.123), channel_id=1, source_target_pairs={{0,6},{1,7},{2,0},{3,1},{4,2},{5,3},{6,4},{7,5},{8,14},{9,15},{10,... | collective-permute-start | bytes 110600 | tf_op jit(solution)/shard_map/ppermute | solution.py:64
  98.3 3.1 %collective-permute-start.10 = (bf16[4,36,1,128]{3,0,2,1:T(4,128)(2,1)S(1)}, bf16[4,36,1,128]{3,0,2,1:T(4,128)(2,1)S(1)}, u32[]{:S(2)}, u32[]{:S(2)}) collective-permute-start(bf16[4,36,1,128]{3,0,2,1:T(4,128)(2,1)S(1)} %get-tuple-element.122), channel_id=1, source_target_pairs={{0,7},{1,0},{2,1},{3,2},{4,3},{5,4},{6,5},{7,6},{8,15},{9,8},{10,9... | collective-permute-start | bytes 110600 | tf_op jit(solution)/shard_map/ppermute | solution.py:64

commit v3 on v0

v3 whole, which is shorter than its diff:
```python
import functools

import jax
import jax.numpy as jnp
from jax import lax
from jax.experimental import pallas as pl
from jax.experimental.pallas import tpu as pltpu
from jax.sharding import PartitionSpec as P

STEPS = 3


def stencil_kernel(step, emit, *refs):
    if step:
        q_ref, wind_ref, north_ref, south_ref, east_ref, west_ref = refs[:6]
        refs = refs[6:]
    else:
        q_ref = refs[0]
        refs = refs[1:]
    if step:
        out_ref = refs[0]
        refs = refs[1:]
    if emit:
        top_ref, bottom_ref, first_ref, last_ref = refs[:4]
        refs = refs[4:]
    new_scr, row_scr = refs

    count, levels, rows, cols = q_ref.shape
    planes = levels * rows

    if step:
        cx = wind_ref[0].astype(jnp.float32)
        cy = wind_ref[1].astype(jnp.float32)
        half_x = 0.5 * cx
        full_x = half_x * cx
        half_y = 0.5 * cy
        full_y = half_y * cy
        strips = jnp.zeros((cols, count * planes), jnp.float32)
        strips = jnp.where(
            lax.broadcasted_iota(jnp.int32, strips.shape, 0) == 0,
            east_ref[...].astype(jnp.float32),
            jnp.where(
                lax.broadcasted_iota(jnp.int32, strips.shape, 0) == 1,
                west_ref[...].astype(jnp.float32),
                strips,
            ),
        )
        columns = strips.T
        sub = lax.broadcasted_iota(jnp.int32, (levels, rows, cols), 1)
        lane = lax.broadcasted_iota(jnp.int32, (levels, rows, cols), 2)

    for field in range(count):
        centre = q_ref[field].astype(jnp.float32)
        if step:
            row_scr[:, rows - 1, :] = north_ref[field].astype(jnp.float32)
            north_halo = row_scr[...]
            row_scr[:, 0, :] = south_ref[field].astype(jnp.float32)
            south_halo = row_scr[...]
            north = jnp.where(sub == rows - 1, north_halo, pltpu.roll(centre, rows - 1, 1))
            south = jnp.where(sub == 0, south_halo, pltpu.roll(centre, 1, 1))
            side = columns[field * planes:(field + 1) * planes].reshape(levels, rows, cols)
            side = pltpu.roll(side, cols - 1, 2)
            east = jnp.where(lane == cols - 1, side, pltpu.roll(centre, cols - 1, 2))
            west = jnp.where(lane == 0, side, pltpu.roll(centre, 1, 2))
            out = centre - half_x * (north - south) + full_x * (north - 2.0 * centre + south)
            out = out - half_y * (east - west) + full_y * (east - 2.0 * centre + west)
            new = out.astype(jnp.bfloat16)
            out_ref[field] = new
        else:
            new = q_ref[field]
        if emit:
            new_scr[...] = new.astype(jnp.float32)
            top_ref[field] = new_scr[:, 0, :].astype(top_ref.dtype)
            bottom_ref[field] = new_scr[:, rows - 1, :].astype(bottom_ref.dtype)
            flat = new.astype(jnp.float32).reshape(planes, cols).astype(jnp.bfloat16)
            pick = lax.broadcasted_iota(jnp.int32, (8, cols), 1)
            which = lax.broadcasted_iota(jnp.int32, (8, cols), 0)
            onehot = jnp.where(
                ((which == 0) & (pick == 0)) | ((which == 1) & (pick == cols - 1)), 1.0, 0.0
            ).astype(jnp.bfloat16)
            edges = lax.dot_general(
                onehot, flat, (((1,), (1,)), ((), ())), preferred_element_type=jnp.float32
            )
            first_ref[:, field * planes:(field + 1) * planes] = edges[0:1].astype(first_ref.dtype)
            last_ref[:, field * planes:(field + 1) * planes] = edges[1:2].astype(last_ref.dtype)


def stencil_call(step, emit, q, *extra):
    count, levels, rows, cols = q.shape
    planes = levels * rows
    outs = []
    if step:
        outs.append(jax.ShapeDtypeStruct(q.shape, q.dtype))
    if emit:
        outs += [
            jax.ShapeDtypeStruct((count, levels, cols), q.dtype),
            jax.ShapeDtypeStruct((count, levels, cols), q.dtype),
            jax.ShapeDtypeStruct((1, count * planes), q.dtype),
            jax.ShapeDtypeStruct((1, count * planes), q.dtype),
        ]
    vmem = pl.BlockSpec(memory_space=pltpu.VMEM)
    return pl.pallas_call(
        functools.partial(stencil_kernel, step, emit),
        out_shape=tuple(outs),
        in_specs=[vmem] * (1 + len(extra)),
        out_specs=tuple([vmem] * len(outs)),
        scratch_shapes=[
            pltpu.VMEM((levels, rows, cols), jnp.float32),
            pltpu.VMEM((levels, rows, cols), jnp.float32),
        ],
    )(q, *extra)


def exchange(top, bottom, first, last):
    sec = lax.axis_size("sec")
    tile = lax.axis_size("tile")
    north = lax.ppermute(top, "sec", [(i, (i - 1) % sec) for i in range(sec)])
    south = lax.ppermute(bottom, "sec", [(i, (i + 1) % sec) for i in range(sec)])
    east = lax.ppermute(first, "tile", [(i, (i - 1) % tile) for i in range(tile)])
    west = lax.ppermute(last, "tile", [(i, (i + 1) % tile) for i in range(tile)])
    return north, south, east, west


def per_device(tracers, courant, destination, diffusion, band, band_table):
    halos = stencil_call(0, True, tracers)
    advected = tracers
    for step in range(STEPS):
        emit = step < STEPS - 1
        result = stencil_call(1, emit, advected, courant, *exchange(*halos))
        advected = result[0]
        halos = result[1:]
    order = jnp.argsort(destination[0])
    band_count = band_table.shape[0]
    ordered = jnp.take(advected, order, axis=2)
    received = lax.all_to_all(ordered, "tile", split_axis=2, concat_axis=2, tiled=True)
    inverse = diffusion[0]
    diffused = jnp.einsum("kl,tlxy->tkxy", inverse, received, preferred_element_type=jnp.float32)
    diffused16 = diffused.astype(jnp.bfloat16)
    picked = (jnp.arange(band_count, dtype=jnp.int32) == band[0])[:, None, None]
    radiation = jnp.sum(jnp.where(picked, band_table, jnp.zeros_like(band_table)), axis=0)
    heating = jnp.einsum("kl,tlxy->tkxy", radiation, diffused16, preferred_element_type=jnp.float32)
    return (diffused + heating).astype(jnp.bfloat16)


def solution(mesh):
    placed = (
        P(None, None, "sec", "tile"),
        P(None, None, "sec", "tile"),
        P(("sec", "tile"), None),
        P(("sec", "tile"), None, None),
        P(("sec", "tile")),
        P(),
    )
    return jax.shard_map(
        per_device,
        mesh=mesh,
        in_specs=placed,
        out_specs=P(None, None, ("sec", "tile"), None),
        check_vma=False,
    )
```

time: 81.9 us -> 70.7 us (0.86)
  Pallas kernels: 0 us -> 15.2 us
  waiting for transfers between devices: 39.4 us -> 27.7 us
  local copies, waits for them, and re-layouts: 16.2 us -> 4.6 us
  other arithmetic: 9.14 us -> 2.78 us
  starting transfers between devices: 15.3 us -> 18.8 us
    pallas_call x0 -> x4, Pallas kernels: none -> 15.2 us  [stencil_call(): pl.pallas_call(functools.partial(stencil_kernel, step, emit), out_shape=t...]
    ppermute x12, waiting for transfers between devices: 23.5 us -> 11.8 us  [the longest x3 7.04 us: exchange(): lax.ppermute(last, 'tile', [(i, (i + 1) % tile) for i in range(tile)])]
    slice x12 -> x0, local copies, waits for them, and re-layouts: 6.94 us -> none  [the longest x7 5.84 us: with_halo(): head = lax.slice_in_dim(cells, 0, width, axis=dim)]
    convert_element_type x3 -> x0, other arithmetic: 6.8 us -> none  [advect_tile(): return out.astype(jnp.bfloat16)]
    ppermute x6 -> x0, local copies, waits for them, and re-layouts: 5.02 us -> none  [the longest x3 2.9 us: with_halo(): lax.ppermute(tail, axis, [(i, (i + 1) % count) for i in range(count)])]
    ppermute x12, starting transfers between devices: 11.8 us -> 15.2 us  [the longest x3 8.71 us: exchange(): lax.ppermute(first, 'tile', [(i, (i - 1) % tile) for i in range(tile)])]
    pallas_call x0 -> x1, local copies, waits for them, and re-layouts: none -> 1.14 us  [stencil_call(): pl.pallas_call(functools.partial(stencil_kernel, step, emit), out_shape=t...]
    gather x1, local copies, waits for them, and re-layouts: 1.73 us -> 0.67 us  [per_device(): ordered = jnp.take(advected, order, axis=2)]
  transfers between devices with their start and end apart: 13 -> 13, of which waited for: 13 -> 7; matrix products, arithmetic and copies ran while one was open for 6% -> 3% of each run, Pallas kernels for 0% -> 0%
where the time goes in v3:
time: 70.7 us; the launch traced here: 70.4 us
  waiting for transfers between devices  27.7 us (39%)
  starting transfers between devices  18.8 us (27%)
  Pallas kernels  15.2 us (21%)
  local copies, waits for them, and re-layouts  4.6 us (7%)
  other arithmetic  2.78 us (4%)
  between operations  0.78 us (1%)
    all_to_all x1, waiting for transfers between devices, per_device(): lax.all_to_all(ordered, 'tile', split_axis=2, concat_axis=2, tiled=True)  15.9 us
    pallas_call x4, Pallas kernels, stencil_call(): pl.pallas_call(functools.partial(stencil_kernel, step, emit), out_shape=t...  15.2 us
    ppermute x3, starting transfers between devices, exchange(): lax.ppermute(first, 'tile', [(i, (i - 1) % tile) for i in range(tile)])  8.71 us
    ppermute x3, waiting for transfers between devices, exchange(): lax.ppermute(last, 'tile', [(i, (i + 1) % tile) for i in range(tile)])  7.04 us
    ppermute x3, waiting for transfers between devices, exchange(): lax.ppermute(bottom, 'sec', [(i, (i + 1) % sec) for i in range(sec)])  4.73 us
    ppermute x3, starting transfers between devices, exchange(): north = lax.ppermute(top, 'sec', [(i, (i - 1) % sec) for i in range(sec)])  3.69 us
    all_to_all x1, starting transfers between devices, per_device(): lax.all_to_all(ordered, 'tile', split_axis=2, concat_axis=2, tiled=True)  3.54 us
    ppermute x3, starting transfers between devices, exchange(): lax.ppermute(bottom, 'sec', [(i, (i + 1) % sec) for i in range(sec)])  2.81 us
  transfers between devices with their start and end apart: 13, of which 7 were waited for; matrix products, arithmetic and copies ran while one was open for 3% of the time, Pallas kernels for 0%

profile of v3, /device:TPU:0, one launch (start us, length us, event | category | flops | bytes accessed | tf_op | source)
XLA Modules:
  0.0 70.4 jit_solution(11616180864477275623)
XLA Ops:
  0.0 0.0 copy-start
  0.0 2.2 %shard_map.64 = (bf16[4,72,128]{2,1,0:T(8,128)(2,1)}, bf16[4,72,128]{2,1,0:T(8,128)(2,1)}, bf16[1,2304]{1,0:T(2,128)(2,1)}, bf16[1,2304]{1,0:T(2,128)(2,1)}) custom-call(bf16[4,72,8,128]{3,2,1,0:T(8,128)(2,1)} %refs_0_.3), custom_call_target="tpu_custom_call" | custom-call | tf_op jit(solution)/shard_map/pallas_call | solution.py:102
  2.2 4.5 %collective-permute-start.2 = (bf16[1,2304]{1,0:T(2,128)(2,1)}, bf16[1,2304]{1,0:T(2,128)(2,1)S(1)}, u32[]{:S(2)}, u32[]{:S(2)}) collective-permute-start(bf16[1,2304]{1,0:T(2,128)(2,1)} %get-tuple-element.23), channel_id=1, source_target_pairs={{0,7},{1,0},{2,1},{3,2},{4,3},{5,4},{6,5},{7,6},{8,15},{9,8},{10,9... | collective-permute-start | bytes 13832 | tf_op jit(solution)/shard_map/ppermute | solution.py:119
  6.7 0.0 collective-permute-start.3
  6.7 2.4 %collective-permute-start = (bf16[4,72,128]{2,1,0:T(8,128)(2,1)}, bf16[4,72,128]{2,1,0:T(8,128)(2,1)S(1)}, u32[]{:S(2)}, u32[]{:S(2)}) collective-permute-start(bf16[4,72,128]{2,1,0:T(8,128)(2,1)} %get-tuple-element.21), channel_id=1, source_target_pairs={{0,24},{8,0},{16,8},{24,16},{1,25},{9,1},{17,9},{25,17},{2,26},{10... | collective-permute-start | bytes 221192 | tf_op jit(solution)/shard_map/ppermute | solution.py:117
  9.2 0.0 collective-permute-start.1
  9.2 1.7 %sort.17 = (s32[8]{0:T(128)}, s32[8]{0:T(128)S(1)}) sort(s32[8]{0:T(128)} %bitcast.22, s32[8]{0:T(128)S(1)} %iota.9), dimensions={0}, to_apply=%region_0.0 | sort | flops 24 | bytes 128 | tf_op jit(solution)/shard_map/jit(argsort)/sort | solution.py:132
  10.9 0.0 collective-permute-done.2.refs_4_
  10.9 0.0 copy-start.10
  10.9 0.9 %collective-permute-done.3.refs_5_ = bf16[1,2304]{1,0:T(2,128)(2,1)S(1)} collective-permute-done((bf16[1,2304]{1,0:T(2,128)(2,1)}, bf16[1,2304]{1,0:T(2,128)(2,1)S(1)}, u32[]{:S(2)}, u32[]{:S(2)}) %collective-permute-start.3) | collective-permute-done | bytes 4640 | tf_op jit(solution)/shard_map/ppermute | solution.py:120
  11.8 0.0 collective-permute-done.refs_2_
  11.9 2.8 %collective-permute-done.1.refs_3_ = bf16[4,72,128]{2,1,0:T(8,128)(2,1)S(1)} collective-permute-done((bf16[4,72,128]{2,1,0:T(8,128)(2,1)}, bf16[4,72,128]{2,1,0:T(8,128)(2,1)S(1)}, u32[]{:S(2)}, u32[]{:S(2)}) %collective-permute-start.1) | collective-permute-done | bytes 73760 | tf_op jit(solution)/shard_map/ppermute | solution.py:118
  14.7 0.0 copy-done.10
  14.7 0.0 copy-done.11
  14.7 0.6 copy-done.3
  15.3 4.5 %shard_map.65 = (bf16[4,72,8,128]{3,2,1,0:T(8,128)(2,1)}, bf16[4,72,128]{2,1,0:T(8,128)(2,1)}, bf16[4,72,128]{2,1,0:T(8,128)(2,1)}, bf16[1,2304]{1,0:T(2,128)(2,1)}, bf16[1,2304]{1,0:T(2,128)(2,1)}) custom-call(bf16[4,72,8,128]{3,2,1,0:T(8,128)(2,1)} %refs_0_.3, bf16[2,72,8,128]{3,2,1,0:T(8,128)(2,1)} %refs_1_.5, bf16[4,72,128]{2,1,0:T(8,128)(2,1)} %copy-done.2, ...), custom_call_target="tpu_custom_call" | custom-call | tf_op jit(solution)/shard_map/pallas_call | solution.py:102
  19.8 2.1 %collective-permute-start.6 = (bf16[1,2304]{1,0:T(2,128)(2,1)}, bf16[1,2304]{1,0:T(2,128)(2,1)S(1)}, u32[]{:S(2)}, u32[]{:S(2)}) collective-permute-start(bf16[1,2304]{1,0:T(2,128)(2,1)} %get-tuple-element.28), channel_id=1, source_target_pairs={{0,7},{1,0},{2,1},{3,2},{4,3},{5,4},{6,5},{7,6},{8,15},{9,8},{10,9... | collective-permute-start | bytes 13832 | tf_op jit(solution)/shard_map/ppermute | solution.py:119
  21.9 0.0 collective-permute-start.7
  21.9 0.9 %collective-permute-start.4 = (bf16[4,72,128]{2,1,0:T(8,128)(2,1)}, bf16[4,72,128]{2,1,0:T(8,128)(2,1)S(1)}, u32[]{:S(2)}, u32[]{:S(2)}) collective-permute-start(bf16[4,72,128]{2,1,0:T(8,128)(2,1)} %get-tuple-element.26), channel_id=1, source_target_pairs={{0,24},{8,0},{16,8},{24,16},{1,25},{9,1},{17,9},{25,17},{2,26},{10... | collective-permute-start | bytes 221192 | tf_op jit(solution)/shard_map/ppermute | solution.py:117
  22.8 1.1 %collective-permute-start.5 = (bf16[4,72,128]{2,1,0:T(8,128)(2,1)}, bf16[4,72,128]{2,1,0:T(8,128)(2,1)S(1)}, u32[]{:S(2)}, u32[]{:S(2)}) collective-permute-start(bf16[4,72,128]{2,1,0:T(8,128)(2,1)} %get-tuple-element.27), channel_id=1, source_target_pairs={{0,8},{8,16},{16,24},{24,0},{1,9},{9,17},{17,25},{25,1},{2,10},{10... | collective-permute-start | bytes 221192 | tf_op jit(solution)/shard_map/ppermute | solution.py:118
  23.9 0.0 collective-permute-done.6.refs_4_
  23.9 3.1 %collective-permute-done.7.refs_5_ = bf16[1,2304]{1,0:T(2,128)(2,1)S(1)} collective-permute-done((bf16[1,2304]{1,0:T(2,128)(2,1)}, bf16[1,2304]{1,0:T(2,128)(2,1)S(1)}, u32[]{:S(2)}, u32[]{:S(2)}) %collective-permute-start.7) | collective-permute-done | bytes 4640 | tf_op jit(solution)/shard_map/ppermute | solution.py:120
  27.0 0.0 collective-permute-done.4.refs_2_
  27.0 1.3 %collective-permute-done.5.refs_3_ = bf16[4,72,128]{2,1,0:T(8,128)(2,1)S(1)} collective-permute-done((bf16[4,72,128]{2,1,0:T(8,128)(2,1)}, bf16[4,72,128]{2,1,0:T(8,128)(2,1)S(1)}, u32[]{:S(2)}, u32[]{:S(2)}) %collective-permute-start.5) | collective-permute-done | bytes 73760 | tf_op jit(solution)/shard_map/ppermute | solution.py:118
  28.2 0.0 copy-done.4
  28.2 0.6 copy-done.5
  28.9 4.5 %shard_map.66 = (bf16[4,72,8,128]{3,2,1,0:T(8,128)(2,1)}, bf16[4,72,128]{2,1,0:T(8,128)(2,1)}, bf16[4,72,128]{2,1,0:T(8,128)(2,1)}, bf16[1,2304]{1,0:T(2,128)(2,1)}, bf16[1,2304]{1,0:T(2,128)(2,1)}) custom-call(bf16[4,72,8,128]{3,2,1,0:T(8,128)(2,1)} %get-tuple-element.25.refs_0_, bf16[2,72,8,128]{3,2,1,0:T(8,128)(2,1)} %refs_1_.5, ...), custom_call_target="tpu_custom_call" | custom-call | tf_op jit(solution)/shard_map/pallas_call | solution.py:102
  33.4 2.1 %collective-permute-start.10 = (bf16[1,2304]{1,0:T(2,128)(2,1)}, bf16[1,2304]{1,0:T(2,128)(2,1)S(1)}, u32[]{:S(2)}, u32[]{:S(2)}) collective-permute-start(bf16[1,2304]{1,0:T(2,128)(2,1)} %get-tuple-element.33), channel_id=1, source_target_pairs={{0,7},{1,0},{2,1},{3,2},{4,3},{5,4},{6,5},{7,6},{8,15},{9,8},{10,9... | collective-permute-start | bytes 13832 | tf_op jit(solution)/shard_map/ppermute | solution.py:119
  35.5 0.0 collective-permute-start.11
  35.5 0.3 collective-permute-start.8
  35.8 1.7 %collective-permute-start.9 = (bf16[4,72,128]{2,1,0:T(8,128)(2,1)}, bf16[4,72,128]{2,1,0:T(8,128)(2,1)S(1)}, u32[]{:S(2)}, u32[]{:S(2)}) collective-permute-start(bf16[4,72,128]{2,1,0:T(8,128)(2,1)} %get-tuple-element.32), channel_id=1, source_target_pairs={{0,8},{8,16},{16,24},{24,0},{1,9},{9,17},{17,25},{25,1},{2,10},{10... | collective-permute-start | bytes 221192 | tf_op jit(solution)/shard_map/ppermute | solution.py:118
  37.5 0.0 collective-permute-done.10.refs_4_
  37.5 3.0 %collective-permute-done.11.refs_5_ = bf16[1,2304]{1,0:T(2,128)(2,1)S(1)} collective-permute-done((bf16[1,2304]{1,0:T(2,128)(2,1)}, bf16[1,2304]{1,0:T(2,128)(2,1)S(1)}, u32[]{:S(2)}, u32[]{:S(2)}) %collective-permute-start.11) | collective-permute-done | bytes 4640 | tf_op jit(solution)/shard_map/ppermute | solution.py:120
  40.6 0.0 collective-permute-done.8.refs_2_
  40.6 0.7 %collective-permute-done.9.refs_3_ = bf16[4,72,128]{2,1,0:T(8,128)(2,1)S(1)} collective-permute-done((bf16[4,72,128]{2,1,0:T(8,128)(2,1)}, bf16[4,72,128]{2,1,0:T(8,128)(2,1)S(1)}, u32[]{:S(2)}, u32[]{:S(2)}) %collective-permute-start.9) | collective-permute-done | bytes 73760 | tf_op jit(solution)/shard_map/ppermute | solution.py:118
  41.3 0.6 copy-done.7
  41.9 3.9 %shard_map.67 = bf16[4,72,8,128]{3,2,1,0:T(8,128)(2,1)} custom-call(bf16[4,72,8,128]{3,2,1,0:T(8,128)(2,1)} %get-tuple-element.30.refs_0_, bf16[2,72,8,128]{3,2,1,0:T(8,128)(2,1)} %refs_1_.5, bf16[4,72,128]{2,1,0:T(8,128)(2,1)} %copy-done.6, bf16[4,72,128]{2,1,0:T(8,128)(2,1)} %copy-done.7, bf16[1,2304]{1,0:T(2,128)(2,1)} %copy-done.8, bf16[1,2304]{1,0:T(2,128)(2,1)} %copy-done.9), custom_call_target="tpu_custom_call" | custom-call | tf_op jit(solution)/shard_map/pallas_call | solution.py:102
  45.9 1.1 %copy.12 = bf16[4,72,8,128]{3,1,2,0:T(8,128)(2,1)S(1)} copy(bf16[4,72,8,128]{3,2,1,0:T(8,128)(2,1)} %shard_map.67) | data formatting | bytes 1179648 | tf_op jit(solution)/shard_map/pallas_call | solution.py:102
  47.0 0.7 gather_fusion
  47.7 0.0 copy-start.1
  47.7 0.9 %select_bitcast_fusion = bf16[4,72,8,128]{3,1,0,2:T(8,128)(2,1)} fusion(bf16[8,4,72,128]{3,2,1,0:T(8,128)(2,1)S(1)} %gather_fusion, pred[8]{0:T(512)(128)(4,1)S(1)} %compare_and_fusion), kind=kLoop, calls=%fused_computation.7 | loop fusion | flops 294912 | bytes 1179656 | tf_op jit(solution)/shard_map/jit(_take)/select_n | solution.py:134
  48.6 3.5 %all-to-all-start = ((bf16[4,72,8,128]{3,1,0,2:T(8,128)(2,1)}), bf16[4,72,8,128]{3,1,0,2:T(8,128)(2,1)S(1)}, u32[]{:S(2)}, u32[]{:S(2)}) async-start(bf16[4,72,8,128]{3,1,0,2:T(8,128)(2,1)} %select_bitcast_fusion), calls=%async_computation | async-start | bytes 1179648 | tf_op jit(solution)/shard_map/all_to_all | solution.py:135
  52.9 0.0 copy-done.1
  52.9 0.1 select_reduce_fusion
  53.0 15.9 %all-to-all-done = bf16[4,72,8,128]{3,1,0,2:T(8,128)(2,1)S(1)} async-done(((bf16[4,72,8,128]{3,1,0,2:T(8,128)(2,1)}), bf16[4,72,8,128]{3,1,0,2:T(8,128)(2,1)S(1)}, u32[]{:S(2)}, u32[]{:S(2)}) %all-to-all-start) | async-done | bytes 589856 | tf_op jit(solution)/shard_map/all_to_all | solution.py:135
  68.9 0.3 fusion.3
  69.2 0.3 fusion.1
  69.5 0.9 %copy.14 = bf16[4,72,8,128]{3,2,1,0:T(8,128)(2,1)} copy(bf16[4,72,8,128]{3,1,2,0:T(8,128)(2,1)S(1)} %fusion.1) | data formatting | bytes 1179648 | tf_op jit(solution)/shard_map/convert_element_type | solution.py:142
  (23 shorter events, 0.1 us)
Async XLA Ops:
  0.0 68.9 %copy-start = (bf16[1,72,72]{2,1,0:T(8,128)(2,1)S(1)}, bf16[1,72,72]{2,1,0:T(8,128)(2,1)}, u32[]{:S(2)}) copy-start(bf16[1,72,72]{2,1,0:T(8,128)(2,1)} %param.9) | copy-start | bytes 31108
  2.2 8.6 %collective-permute-start.2 = (bf16[1,2304]{1,0:T(2,128)(2,1)}, bf16[1,2304]{1,0:T(2,128)(2,1)S(1)}, u32[]{:S(2)}, u32[]{:S(2)}) collective-permute-start(bf16[1,2304]{1,0:T(2,128)(2,1)} %get-tuple-element.23), channel_id=1, source_target_pairs={{0,7},{1,0},{2,1},{3,2},{4,3},{5,4},{6,5},{7,6},{8,15},{9,8},{10,9... | collective-permute-start | bytes 13832 | tf_op jit(solution)/shard_map/ppermute | solution.py:119
  6.7 5.1 %collective-permute-start.3 = (bf16[1,2304]{1,0:T(2,128)(2,1)}, bf16[1,2304]{1,0:T(2,128)(2,1)S(1)}, u32[]{:S(2)}, u32[]{:S(2)}) collective-permute-start(bf16[1,2304]{1,0:T(2,128)(2,1)} %get-tuple-element.24), channel_id=1, source_target_pairs={{0,1},{1,2},{2,3},{3,4},{4,5},{5,6},{6,7},{7,0},{8,9},{9,10},{10,1... | collective-permute-start | bytes 13832 | tf_op jit(solution)/shard_map/ppermute | solution.py:120
  6.7 5.1 %collective-permute-start = (bf16[4,72,128]{2,1,0:T(8,128)(2,1)}, bf16[4,72,128]{2,1,0:T(8,128)(2,1)S(1)}, u32[]{:S(2)}, u32[]{:S(2)}) collective-permute-start(bf16[4,72,128]{2,1,0:T(8,128)(2,1)} %get-tuple-element.21), channel_id=1, source_target_pairs={{0,24},{8,0},{16,8},{24,16},{1,25},{9,1},{17,9},{25,17},{2,26},{10... | collective-permute-start | bytes 221192 | tf_op jit(solution)/shard_map/ppermute | solution.py:117
  9.2 5.5 %collective-permute-start.1 = (bf16[4,72,128]{2,1,0:T(8,128)(2,1)}, bf16[4,72,128]{2,1,0:T(8,128)(2,1)S(1)}, u32[]{:S(2)}, u32[]{:S(2)}) collective-permute-start(bf16[4,72,128]{2,1,0:T(8,128)(2,1)} %get-tuple-element.22), channel_id=1, source_target_pairs={{0,8},{8,16},{16,24},{24,0},{1,9},{9,17},{17,25},{25,1},{2,10},{10... | collective-permute-start | bytes 221192 | tf_op jit(solution)/shard_map/ppermute | solution.py:118
  10.9 3.8 %copy-start.10 = (bf16[1,2304]{1,0:T(2,128)(2,1)}, bf16[1,2304]{1,0:T(2,128)(2,1)S(1)}, u32[]{:S(2)}) copy-start(bf16[1,2304]{1,0:T(2,128)(2,1)S(1)} %collective-permute-done.2.refs_4_) | copy-start | bytes 13828
  11.8 2.8 %copy-start.11 = (bf16[1,2304]{1,0:T(2,128)(2,1)}, bf16[1,2304]{1,0:T(2,128)(2,1)S(1)}, u32[]{:S(2)}) copy-start(bf16[1,2304]{1,0:T(2,128)(2,1)S(1)} %collective-permute-done.3.refs_5_) | copy-start | bytes 13828
  11.9 2.8 %copy-start.2 = (bf16[4,72,128]{2,1,0:T(8,128)(2,1)}, bf16[4,72,128]{2,1,0:T(8,128)(2,1)S(1)}, u32[]{:S(2)}) copy-start(bf16[4,72,128]{2,1,0:T(8,128)(2,1)S(1)} %collective-permute-done.refs_2_) | copy-start | bytes 221188
  14.7 0.6 copy-start.3
  19.8 4.1 %collective-permute-start.6 = (bf16[1,2304]{1,0:T(2,128)(2,1)}, bf16[1,2304]{1,0:T(2,128)(2,1)S(1)}, u32[]{:S(2)}, u32[]{:S(2)}) collective-permute-start(bf16[1,2304]{1,0:T(2,128)(2,1)} %get-tuple-element.28), channel_id=1, source_target_pairs={{0,7},{1,0},{2,1},{3,2},{4,3},{5,4},{6,5},{7,6},{8,15},{9,8},{10,9... | collective-permute-start | bytes 13832 | tf_op jit(solution)/shard_map/ppermute | solution.py:119
  21.9 5.1 %collective-permute-start.7 = (bf16[1,2304]{1,0:T(2,128)(2,1)}, bf16[1,2304]{1,0:T(2,128)(2,1)S(1)}, u32[]{:S(2)}, u32[]{:S(2)}) collective-permute-start(bf16[1,2304]{1,0:T(2,128)(2,1)} %get-tuple-element.29), channel_id=1, source_target_pairs={{0,1},{1,2},{2,3},{3,4},{4,5},{5,6},{6,7},{7,0},{8,9},{9,10},{10,1... | collective-permute-start | bytes 13832 | tf_op jit(solution)/shard_map/ppermute | solution.py:120
  21.9 5.1 %collective-permute-start.4 = (bf16[4,72,128]{2,1,0:T(8,128)(2,1)}, bf16[4,72,128]{2,1,0:T(8,128)(2,1)S(1)}, u32[]{:S(2)}, u32[]{:S(2)}) collective-permute-start(bf16[4,72,128]{2,1,0:T(8,128)(2,1)} %get-tuple-element.26), channel_id=1, source_target_pairs={{0,24},{8,0},{16,8},{24,16},{1,25},{9,1},{17,9},{25,17},{2,26},{10... | collective-permute-start | bytes 221192 | tf_op jit(solution)/shard_map/ppermute | solution.py:117
  22.8 5.5 %collective-permute-start.5 = (bf16[4,72,128]{2,1,0:T(8,128)(2,1)}, bf16[4,72,128]{2,1,0:T(8,128)(2,1)S(1)}, u32[]{:S(2)}, u32[]{:S(2)}) collective-permute-start(bf16[4,72,128]{2,1,0:T(8,128)(2,1)} %get-tuple-element.27), channel_id=1, source_target_pairs={{0,8},{8,16},{16,24},{24,0},{1,9},{9,17},{17,25},{25,1},{2,10},{10... | collective-permute-start | bytes 221192 | tf_op jit(solution)/shard_map/ppermute | solution.py:118
  23.9 4.3 %copy-start.12 = (bf16[1,2304]{1,0:T(2,128)(2,1)}, bf16[1,2304]{1,0:T(2,128)(2,1)S(1)}, u32[]{:S(2)}) copy-start(bf16[1,2304]{1,0:T(2,128)(2,1)S(1)} %collective-permute-done.6.refs_4_) | copy-start | bytes 13828
  27.0 1.3 %copy-start.13 = (bf16[1,2304]{1,0:T(2,128)(2,1)}, bf16[1,2304]{1,0:T(2,128)(2,1)S(1)}, u32[]{:S(2)}) copy-start(bf16[1,2304]{1,0:T(2,128)(2,1)S(1)} %collective-permute-done.7.refs_5_) | copy-start | bytes 13828
  27.0 1.3 %copy-start.4 = (bf16[4,72,128]{2,1,0:T(8,128)(2,1)}, bf16[4,72,128]{2,1,0:T(8,128)(2,1)S(1)}, u32[]{:S(2)}) copy-start(bf16[4,72,128]{2,1,0:T(8,128)(2,1)S(1)} %collective-permute-done.4.refs_2_) | copy-start | bytes 221188
  28.2 0.6 copy-start.5
  33.4 4.2 %collective-permute-start.10 = (bf16[1,2304]{1,0:T(2,128)(2,1)}, bf16[1,2304]{1,0:T(2,128)(2,1)S(1)}, u32[]{:S(2)}, u32[]{:S(2)}) collective-permute-start(bf16[1,2304]{1,0:T(2,128)(2,1)} %get-tuple-element.33), channel_id=1, source_target_pairs={{0,7},{1,0},{2,1},{3,2},{4,3},{5,4},{6,5},{7,6},{8,15},{9,8},{10,9... | collective-permute-start | bytes 13832 | tf_op jit(solution)/shard_map/ppermute | solution.py:119
  35.5 5.1 %collective-permute-start.11 = (bf16[1,2304]{1,0:T(2,128)(2,1)}, bf16[1,2304]{1,0:T(2,128)(2,1)S(1)}, u32[]{:S(2)}, u32[]{:S(2)}) collective-permute-start(bf16[1,2304]{1,0:T(2,128)(2,1)} %get-tuple-element.34), channel_id=1, source_target_pairs={{0,1},{1,2},{2,3},{3,4},{4,5},{5,6},{6,7},{7,0},{8,9},{9,10},{10,1... | collective-permute-start | bytes 13832 | tf_op jit(solution)/shard_map/ppermute | solution.py:120
  35.5 5.1 %collective-permute-start.8 = (bf16[4,72,128]{2,1,0:T(8,128)(2,1)}, bf16[4,72,128]{2,1,0:T(8,128)(2,1)S(1)}, u32[]{:S(2)}, u32[]{:S(2)}) collective-permute-start(bf16[4,72,128]{2,1,0:T(8,128)(2,1)} %get-tuple-element.31), channel_id=1, source_target_pairs={{0,24},{8,0},{16,8},{24,16},{1,25},{9,1},{17,9},{25,17},{2,26},{10... | collective-permute-start | bytes 221192 | tf_op jit(solution)/shard_map/ppermute | solution.py:117
  35.8 5.5 %collective-permute-start.9 = (bf16[4,72,128]{2,1,0:T(8,128)(2,1)}, bf16[4,72,128]{2,1,0:T(8,128)(2,1)S(1)}, u32[]{:S(2)}, u32[]{:S(2)}) collective-permute-start(bf16[4,72,128]{2,1,0:T(8,128)(2,1)} %get-tuple-element.32), channel_id=1, source_target_pairs={{0,8},{8,16},{16,24},{24,0},{1,9},{9,17},{17,25},{25,1},{2,10},{10... | collective-permute-start | bytes 221192 | tf_op jit(solution)/shard_map/ppermute | solution.py:118
  37.5 3.8 %copy-start.8 = (bf16[1,2304]{1,0:T(2,128)(2,1)}, bf16[1,2304]{1,0:T(2,128)(2,1)S(1)}, u32[]{:S(2)}) copy-start(bf16[1,2304]{1,0:T(2,128)(2,1)S(1)} %collective-permute-done.10.refs_4_) | copy-start | bytes 13828
  40.6 0.7 %copy-start.9 = (bf16[1,2304]{1,0:T(2,128)(2,1)}, bf16[1,2304]{1,0:T(2,128)(2,1)S(1)}, u32[]{:S(2)}) copy-start(bf16[1,2304]{1,0:T(2,128)(2,1)S(1)} %collective-permute-done.11.refs_5_) | copy-start | bytes 13828
  40.6 0.7 %copy-start.6 = (bf16[4,72,128]{2,1,0:T(8,128)(2,1)}, bf16[4,72,128]{2,1,0:T(8,128)(2,1)S(1)}, u32[]{:S(2)}) copy-start(bf16[4,72,128]{2,1,0:T(8,128)(2,1)S(1)} %collective-permute-done.8.refs_2_) | copy-start | bytes 221188
  41.3 0.6 copy-start.7
  47.7 5.2 %copy-start.1 = (bf16[16,72,72]{2,1,0:T(8,128)(2,1)S(1)}, bf16[16,72,72]{2,1,0:T(8,128)(2,1)}, u32[]{:S(2)}) copy-start(bf16[16,72,72]{2,1,0:T(8,128)(2,1)} %param.11) | copy-start | bytes 497668
  48.6 20.2 %all-to-all-start = ((bf16[4,72,8,128]{3,1,0,2:T(8,128)(2,1)}), bf16[4,72,8,128]{3,1,0,2:T(8,128)(2,1)S(1)}, u32[]{:S(2)}, u32[]{:S(2)}) async-start(bf16[4,72,8,128]{3,1,0,2:T(8,128)(2,1)} %select_bitcast_fusion), calls=%async_computation | async-start | bytes 1179648 | tf_op jit(solution)/shard_map/all_to_all | solution.py:135

commit v4 on v3

--- a/solution.py
+++ b/solution.py
@@ -10,7 +10,10 @@
 STEPS = 3
 
 
-def stencil_kernel(step, emit, *refs):
+def stencil_kernel(step, emit, last, *refs):
+    if last:
+        order_ref = refs[0]
+        refs = refs[1:]
     if step:
         q_ref, wind_ref, north_ref, south_ref, east_ref, west_ref = refs[:6]
         refs = refs[6:]
@@ -65,7 +68,17 @@
             out = centre - half_x * (north - south) + full_x * (north - 2.0 * centre + south)
             out = out - half_y * (east - west) + full_y * (east - 2.0 * centre + west)
             new = out.astype(jnp.bfloat16)
-            out_ref[field] = new
+            if last:
+                new_scr[...] = new.astype(jnp.float32)
+                picked = [new_scr[:, row, :] for row in range(rows)]
+                for slot in range(rows):
+                    wanted = order_ref[slot]
+                    value = picked[0]
+                    for row in range(1, rows):
+                        value = jnp.where(wanted == row, picked[row], value)
+                    out_ref[slot, field] = value.astype(out_ref.dtype)
+            else:
+                out_ref[field] = new
         else:
             new = q_ref[field]
         if emit:
@@ -85,11 +98,14 @@
             last_ref[:, field * planes:(field + 1) * planes] = edges[1:2].astype(last_ref.dtype)
 
 
-def stencil_call(step, emit, q, *extra):
+def stencil_call(step, emit, q, *extra, order=None):
     count, levels, rows, cols = q.shape
     planes = levels * rows
+    last = order is not None
     outs = []
-    if step:
+    if last:
+        outs.append(jax.ShapeDtypeStruct((rows, count, levels, cols), q.dtype))
+    elif step:
         outs.append(jax.ShapeDtypeStruct(q.shape, q.dtype))
     if emit:
         outs += [
@@ -99,16 +115,21 @@
             jax.ShapeDtypeStruct((1, count * planes), q.dtype),
         ]
     vmem = pl.BlockSpec(memory_space=pltpu.VMEM)
+    ins = [vmem] * (1 + len(extra))
+    operands = (q,) + extra
+    if last:
+        ins = [pl.BlockSpec(memory_space=pltpu.SMEM)] + ins
+        operands = (order,) + operands
     return pl.pallas_call(
-        functools.partial(stencil_kernel, step, emit),
+        functools.partial(stencil_kernel, step, emit, last),
         out_shape=tuple(outs),
-        in_specs=[vmem] * (1 + len(extra)),
+        in_specs=ins,
         out_specs=tuple([vmem] * len(outs)),
         scratch_shapes=[
             pltpu.VMEM((levels, rows, cols), jnp.float32),
             pltpu.VMEM((levels, rows, cols), jnp.float32),
         ],
-    )(q, *extra)
+    )(*operands)
 
 
 def exchange(top, bottom, first, last):
@@ -122,19 +143,21 @@
 
 
 def per_device(tracers, courant, destination, diffusion, band, band_table):
+    order = jnp.argsort(destination[0]).astype(jnp.int32)
     halos = stencil_call(0, True, tracers)
     advected = tracers
     for step in range(STEPS):
         emit = step < STEPS - 1
-        result = stencil_call(1, emit, advected, courant, *exchange(*halos))
+        final = None if emit or tracers.shape[2] > 8 else order
+        result = stencil_call(1, emit, advected, courant, *exchange(*halos), order=final)
         advected = result[0]
         halos = result[1:]
-    order = jnp.argsort(destination[0])
+    if tracers.shape[2] > 8:
+        advected = jnp.take(advected, order, axis=2).transpose(2, 0, 1, 3)
+    received = lax.all_to_all(advected, "tile", split_axis=0, concat_axis=0, tiled=True)
     band_count = band_table.shape[0]
-    ordered = jnp.take(advected, order, axis=2)
-    received = lax.all_to_all(ordered, "tile", split_axis=2, concat_axis=2, tiled=True)
     inverse = diffusion[0]
-    diffused = jnp.einsum("kl,tlxy->tkxy", inverse, received, preferred_element_type=jnp.float32)
+    diffused = jnp.einsum("kl,itly->tkiy", inverse, received, preferred_element_type=jnp.float32)
     diffused16 = diffused.astype(jnp.bfloat16)
     picked = (jnp.arange(band_count, dtype=jnp.int32) == band[0])[:, None, None]
     radiation = jnp.sum(jnp.where(picked, band_table, jnp.zeros_like(band_table)), axis=0)

time: 70.7 us -> 72.7 us (1.028)
  Pallas kernels: 15.2 us -> 20.1 us
  starting transfers between devices: 18.8 us -> 16.5 us
  waiting for transfers between devices: 27.7 us -> 29.9 us
  other arithmetic: 2.78 us -> 1.12 us
  local copies, waits for them, and re-layouts: 4.6 us -> 3.58 us
    ppermute x3, starting transfers between devices: 8.71 us -> 2.77 us  [exchange(): lax.ppermute(first, 'tile', [(i, (i - 1) % tile) for i in range(tile)])]
    ppermute x3, starting transfers between devices: 3.69 us -> 9.13 us  [exchange(): north = lax.ppermute(top, 'sec', [(i, (i - 1) % sec) for i in range(sec)])]
    pallas_call x4, Pallas kernels: 15.2 us -> 20.1 us  [stencil_call(): pl.pallas_call(functools.partial(stencil_kernel, step, emit, last), out_s...]
    ppermute x3, waiting for transfers between devices: 4.73 us -> 0.71 us  [exchange(): lax.ppermute(bottom, 'sec', [(i, (i + 1) % sec) for i in range(sec)])]
    ppermute x3, waiting for transfers between devices: 7.04 us -> 10.5 us  [exchange(): lax.ppermute(last, 'tile', [(i, (i + 1) % tile) for i in range(tile)])]
    ppermute x3, starting transfers between devices: 2.81 us -> 0.01 us  [exchange(): lax.ppermute(bottom, 'sec', [(i, (i + 1) % sec) for i in range(sec)])]
    ppermute x3, waiting for transfers between devices: 0.01 us -> 2.77 us  [exchange(): lax.ppermute(first, 'tile', [(i, (i - 1) % tile) for i in range(tile)])]
    pallas_call x1 -> x0, local copies, waits for them, and re-layouts: 1.14 us -> none  [stencil_call(): pl.pallas_call(functools.partial(stencil_kernel, step, emit), out_shape=t...]
  transfers between devices with their start and end apart: 13 -> 13, of which waited for: 7 -> 9; matrix products, arithmetic and copies ran while one was open for 3% -> 2% of each run, Pallas kernels for 0% -> 0%
where the time goes in v4:
time: 72.7 us; the launch traced here: 72.5 us
  waiting for transfers between devices  29.9 us (41%)
  Pallas kernels  20.1 us (28%)
  starting transfers between devices  16.5 us (23%)
  local copies, waits for them, and re-layouts  3.58 us (5%)
  other arithmetic  1.12 us (2%)
  between operations  0.73 us (1%)
    pallas_call x4, Pallas kernels, stencil_call(): pl.pallas_call(functools.partial(stencil_kernel, step, emit, last), out_s...  20.1 us
    all_to_all x1, waiting for transfers between devices, per_device(): lax.all_to_all(advected, 'tile', split_axis=0, concat_axis=0, tiled=True)  15.9 us
    ppermute x3, waiting for transfers between devices, exchange(): lax.ppermute(last, 'tile', [(i, (i + 1) % tile) for i in range(tile)])  10.5 us
    ppermute x3, starting transfers between devices, exchange(): north = lax.ppermute(top, 'sec', [(i, (i - 1) % sec) for i in range(sec)])  9.13 us
    all_to_all x1, starting transfers between devices, per_device(): lax.all_to_all(advected, 'tile', split_axis=0, concat_axis=0, tiled=True)  3.54 us
    ppermute x3, waiting for transfers between devices, exchange(): lax.ppermute(first, 'tile', [(i, (i - 1) % tile) for i in range(tile)])  2.77 us
    ppermute x3, starting transfers between devices, exchange(): lax.ppermute(first, 'tile', [(i, (i - 1) % tile) for i in range(tile)])  2.77 us
    unnamed x30, local copies, waits for them, and re-layouts  2.53 us
  transfers between devices with their start and end apart: 13, of which 9 were waited for; matrix products, arithmetic and copies ran while one was open for 2% of the time, Pallas kernels for 0%

profile of v4, /device:TPU:0, one launch (start us, length us, event | category | flops | bytes accessed | tf_op | source)
XLA Modules:
  0.0 72.5 jit_solution(6681833833538839501)
XLA Ops:
  0.0 0.0 copy-start
  0.0 2.2 %shard_map.64 = (bf16[4,72,128]{2,1,0:T(8,128)(2,1)}, bf16[4,72,128]{2,1,0:T(8,128)(2,1)}, bf16[1,2304]{1,0:T(2,128)(2,1)}, bf16[1,2304]{1,0:T(2,128)(2,1)}) custom-call(bf16[4,72,8,128]{3,2,1,0:T(8,128)(2,1)} %refs_0_.3), custom_call_target="tpu_custom_call" | custom-call | tf_op jit(solution)/shard_map/pallas_call | solution.py:123
  2.2 3.9 %collective-permute-start = (bf16[4,72,128]{2,1,0:T(8,128)(2,1)}, bf16[4,72,128]{2,1,0:T(8,128)(2,1)S(1)}, u32[]{:S(2)}, u32[]{:S(2)}) collective-permute-start(bf16[4,72,128]{2,1,0:T(8,128)(2,1)} %get-tuple-element.21), channel_id=1, source_target_pairs={{0,24},{8,0},{16,8},{24,16},{1,25},{9,1},{17,9},{25,17},{2,26},{10... | collective-permute-start | bytes 221192 | tf_op jit(solution)/shard_map/ppermute | solution.py:138
  6.1 0.0 collective-permute-start.1
  6.1 2.8 %collective-permute-start.2 = (bf16[1,2304]{1,0:T(2,128)(2,1)}, bf16[1,2304]{1,0:T(2,128)(2,1)S(1)}, u32[]{:S(2)}, u32[]{:S(2)}) collective-permute-start(bf16[1,2304]{1,0:T(2,128)(2,1)} %get-tuple-element.23), channel_id=1, source_target_pairs={{0,7},{1,0},{2,1},{3,2},{4,3},{5,4},{6,5},{7,6},{8,15},{9,8},{10,9... | collective-permute-start | bytes 13832 | tf_op jit(solution)/shard_map/ppermute | solution.py:140
  8.9 0.0 collective-permute-start.3
  8.9 1.6 %collective-permute-done.2.refs_4_ = bf16[1,2304]{1,0:T(2,128)(2,1)S(1)} collective-permute-done((bf16[1,2304]{1,0:T(2,128)(2,1)}, bf16[1,2304]{1,0:T(2,128)(2,1)S(1)}, u32[]{:S(2)}, u32[]{:S(2)}) %collective-permute-start.2) | collective-permute-done | bytes 4640 | tf_op jit(solution)/shard_map/ppermute | solution.py:140
  10.5 3.5 %collective-permute-done.3.refs_5_ = bf16[1,2304]{1,0:T(2,128)(2,1)S(1)} collective-permute-done((bf16[1,2304]{1,0:T(2,128)(2,1)}, bf16[1,2304]{1,0:T(2,128)(2,1)S(1)}, u32[]{:S(2)}, u32[]{:S(2)}) %collective-permute-start.3) | collective-permute-done | bytes 4640 | tf_op jit(solution)/shard_map/ppermute | solution.py:141
  14.0 0.0 collective-permute-done.refs_2_
  14.0 0.0 collective-permute-done.1.refs_3_
  14.0 0.6 copy-done.13
  14.6 0.1 copy-done.4
  14.6 0.6 copy-done.7
  15.3 4.5 %shard_map.65 = (bf16[4,72,8,128]{3,2,1,0:T(8,128)(2,1)}, bf16[4,72,128]{2,1,0:T(8,128)(2,1)}, bf16[4,72,128]{2,1,0:T(8,128)(2,1)}, bf16[1,2304]{1,0:T(2,128)(2,1)}, bf16[1,2304]{1,0:T(2,128)(2,1)}) custom-call(bf16[4,72,8,128]{3,2,1,0:T(8,128)(2,1)} %refs_0_.3, bf16[2,72,8,128]{3,2,1,0:T(8,128)(2,1)} %refs_2_.1, bf16[4,72,128]{2,1,0:T(8,128)(2,1)} %copy-done.4, ...), custom_call_target="tpu_custom_call" | custom-call | tf_op jit(solution)/shard_map/pallas_call | solution.py:123
  19.8 2.6 %collective-permute-start.4 = (bf16[4,72,128]{2,1,0:T(8,128)(2,1)}, bf16[4,72,128]{2,1,0:T(8,128)(2,1)S(1)}, u32[]{:S(2)}, u32[]{:S(2)}) collective-permute-start(bf16[4,72,128]{2,1,0:T(8,128)(2,1)} %get-tuple-element.26), channel_id=1, source_target_pairs={{0,24},{8,0},{16,8},{24,16},{1,25},{9,1},{17,9},{25,17},{2,26},{10... | collective-permute-start | bytes 221192 | tf_op jit(solution)/shard_map/ppermute | solution.py:138
  22.4 0.0 collective-permute-start.5
  22.4 0.0 collective-permute-start.6
  22.4 0.5 collective-permute-start.7
  22.9 1.1 %collective-permute-done.6.refs_4_ = bf16[1,2304]{1,0:T(2,128)(2,1)S(1)} collective-permute-done((bf16[1,2304]{1,0:T(2,128)(2,1)}, bf16[1,2304]{1,0:T(2,128)(2,1)S(1)}, u32[]{:S(2)}, u32[]{:S(2)}) %collective-permute-start.6) | collective-permute-done | bytes 4640 | tf_op jit(solution)/shard_map/ppermute | solution.py:140
  24.0 3.5 %collective-permute-done.7.refs_5_ = bf16[1,2304]{1,0:T(2,128)(2,1)S(1)} collective-permute-done((bf16[1,2304]{1,0:T(2,128)(2,1)}, bf16[1,2304]{1,0:T(2,128)(2,1)S(1)}, u32[]{:S(2)}, u32[]{:S(2)}) %collective-permute-start.7) | collective-permute-done | bytes 4640 | tf_op jit(solution)/shard_map/ppermute | solution.py:141
  27.5 0.0 collective-permute-done.4.refs_2_
  27.5 0.4 collective-permute-done.5.refs_3_
  27.9 0.0 copy-done.10
  27.9 0.2 copy-done.12
  28.1 0.0 copy-done.3
  28.1 0.4 copy-done.6
  28.5 4.5 %shard_map.66 = (bf16[4,72,8,128]{3,2,1,0:T(8,128)(2,1)}, bf16[4,72,128]{2,1,0:T(8,128)(2,1)}, bf16[4,72,128]{2,1,0:T(8,128)(2,1)}, bf16[1,2304]{1,0:T(2,128)(2,1)}, bf16[1,2304]{1,0:T(2,128)(2,1)}) custom-call(bf16[4,72,8,128]{3,2,1,0:T(8,128)(2,1)} %get-tuple-element.25.refs_0_, bf16[2,72,8,128]{3,2,1,0:T(8,128)(2,1)} %refs_2_.1, ...), custom_call_target="tpu_custom_call" | custom-call | tf_op jit(solution)/shard_map/pallas_call | solution.py:123
  33.0 2.6 %collective-permute-start.8 = (bf16[4,72,128]{2,1,0:T(8,128)(2,1)}, bf16[4,72,128]{2,1,0:T(8,128)(2,1)S(1)}, u32[]{:S(2)}, u32[]{:S(2)}) collective-permute-start(bf16[4,72,128]{2,1,0:T(8,128)(2,1)} %get-tuple-element.31), channel_id=1, source_target_pairs={{0,24},{8,0},{16,8},{24,16},{1,25},{9,1},{17,9},{25,17},{2,26},{10... | collective-permute-start | bytes 221192 | tf_op jit(solution)/shard_map/ppermute | solution.py:138
  35.6 0.0 collective-permute-start.9
  35.6 0.0 collective-permute-start.10
  35.6 0.5 collective-permute-start.11
  36.1 1.0 %sort.17 = (s32[8]{0:T(128)}, s32[8]{0:T(128)}) sort(s32[8]{0:T(128)S(1)} %bitcast.22, s32[8]{0:T(128)S(1)} %iota.9), dimensions={0}, to_apply=%region_0.0 | sort | flops 24 | bytes 128 | tf_op jit(solution)/shard_map/jit(argsort)/sort | solution.py:146
  37.1 0.1 collective-permute-done.10.refs_5_
  37.2 3.5 %collective-permute-done.11.refs_6_ = bf16[1,2304]{1,0:T(2,128)(2,1)S(1)} collective-permute-done((bf16[1,2304]{1,0:T(2,128)(2,1)}, bf16[1,2304]{1,0:T(2,128)(2,1)S(1)}, u32[]{:S(2)}, u32[]{:S(2)}) %collective-permute-start.11) | collective-permute-done | bytes 4640 | tf_op jit(solution)/shard_map/ppermute | solution.py:141
  40.7 0.0 collective-permute-done.8.refs_3_
  40.7 0.4 collective-permute-done.9.refs_4_
  41.1 0.0 copy-done.8
  41.1 0.2 copy-done.9
  41.3 0.0 copy-done.2
  41.3 0.4 copy-done.5
  41.7 8.9 %shard_map.67 = bf16[8,4,72,128]{3,2,1,0:T(8,128)(2,1)} custom-call(s32[8]{0:T(128)} %get-tuple-element.20.refs_0_, bf16[4,72,8,128]{3,2,1,0:T(8,128)(2,1)} %get-tuple-element.30.refs_1_, bf16[2,72,8,128]{3,2,1,0:T(8,128)(2,1)} %refs_2_.1, bf16[4,72,128]{2,1,0:T(8,128)(2,1)} %copy-done.2, bf16[4,72,128]{2,1,0:T(8,128)(2,1)} %copy-done.5, ...), custom_call_target="tpu_custom_call" | custom-call | tf_op jit(solution)/shard_map/pallas_call | solution.py:123
  50.6 3.5 %all-to-all-start = ((bf16[8,4,72,128]{3,2,1,0:T(8,128)(2,1)}), bf16[8,4,72,128]{3,2,1,0:T(8,128)(2,1)S(1)}, u32[]{:S(2)}, u32[]{:S(2)}) async-start(bf16[8,4,72,128]{3,2,1,0:T(8,128)(2,1)} %shard_map.67), calls=%async_computation | async-start | bytes 1179648 | tf_op jit(solution)/shard_map/all_to_all | solution.py:157
  54.8 0.1 select_reduce_fusion
  54.9 15.9 %all-to-all-done = bf16[8,4,72,128]{3,2,1,0:T(8,128)(2,1)S(1)} async-done(((bf16[8,4,72,128]{3,2,1,0:T(8,128)(2,1)}), bf16[8,4,72,128]{3,2,1,0:T(8,128)(2,1)S(1)}, u32[]{:S(2)}, u32[]{:S(2)}) %all-to-all-start) | async-done | bytes 589856 | tf_op jit(solution)/shard_map/all_to_all | solution.py:157
  70.8 0.0 copy-done
  70.8 0.3 convolution_bitcast_fusion.1
  71.1 0.3 fusion.1
  71.4 1.0 %copy.9 = bf16[4,72,8,128]{3,2,1,0:T(8,128)(2,1)} copy(bf16[4,72,8,128]{3,1,0,2:T(8,128)(2,1)S(1)} %fusion.1) | data formatting | bytes 1179648 | tf_op jit(solution)/shard_map/convert_element_type | solution.py:165
  (19 shorter events, 0.0 us)
Async XLA Ops:
  0.0 70.8 %copy-start = (bf16[1,72,72]{2,1,0:T(8,128)(2,1)S(1)}, bf16[1,72,72]{2,1,0:T(8,128)(2,1)}, u32[]{:S(2)}) copy-start(bf16[1,72,72]{2,1,0:T(8,128)(2,1)} %param.9) | copy-start | bytes 31108
  2.2 33.9 %copy-start.14 = (s32[1,8]{1,0:T(1,128)S(1)}, s32[1,8]{1,0:T(1,128)}, u32[]{:S(2)}) copy-start(s32[1,8]{1,0:T(1,128)} %param.8) | copy-start | bytes 100
  2.2 11.8 %collective-permute-start = (bf16[4,72,128]{2,1,0:T(8,128)(2,1)}, bf16[4,72,128]{2,1,0:T(8,128)(2,1)S(1)}, u32[]{:S(2)}, u32[]{:S(2)}) collective-permute-start(bf16[4,72,128]{2,1,0:T(8,128)(2,1)} %get-tuple-element.21), channel_id=1, source_target_pairs={{0,24},{8,0},{16,8},{24,16},{1,25},{9,1},{17,9},{25,17},{2,26},{10... | collective-permute-start | bytes 221192 | tf_op jit(solution)/shard_map/ppermute | solution.py:138
  6.1 7.9 %collective-permute-start.1 = (bf16[4,72,128]{2,1,0:T(8,128)(2,1)}, bf16[4,72,128]{2,1,0:T(8,128)(2,1)S(1)}, u32[]{:S(2)}, u32[]{:S(2)}) collective-permute-start(bf16[4,72,128]{2,1,0:T(8,128)(2,1)} %get-tuple-element.22), channel_id=1, source_target_pairs={{0,8},{8,16},{16,24},{24,0},{1,9},{9,17},{17,25},{25,1},{2,10},{10... | collective-permute-start | bytes 221192 | tf_op jit(solution)/shard_map/ppermute | solution.py:139
  6.1 4.3 %collective-permute-start.2 = (bf16[1,2304]{1,0:T(2,128)(2,1)}, bf16[1,2304]{1,0:T(2,128)(2,1)S(1)}, u32[]{:S(2)}, u32[]{:S(2)}) collective-permute-start(bf16[1,2304]{1,0:T(2,128)(2,1)} %get-tuple-element.23), channel_id=1, source_target_pairs={{0,7},{1,0},{2,1},{3,2},{4,3},{5,4},{6,5},{7,6},{8,15},{9,8},{10,9... | collective-permute-start | bytes 13832 | tf_op jit(solution)/shard_map/ppermute | solution.py:140
  8.9 5.1 %collective-permute-start.3 = (bf16[1,2304]{1,0:T(2,128)(2,1)}, bf16[1,2304]{1,0:T(2,128)(2,1)S(1)}, u32[]{:S(2)}, u32[]{:S(2)}) collective-permute-start(bf16[1,2304]{1,0:T(2,128)(2,1)} %get-tuple-element.24), channel_id=1, source_target_pairs={{0,1},{1,2},{2,3},{3,4},{4,5},{5,6},{6,7},{7,0},{8,9},{9,10},{10,1... | collective-permute-start | bytes 13832 | tf_op jit(solution)/shard_map/ppermute | solution.py:141
  10.5 3.5 %copy-start.11 = (bf16[1,2304]{1,0:T(2,128)(2,1)}, bf16[1,2304]{1,0:T(2,128)(2,1)S(1)}, u32[]{:S(2)}) copy-start(bf16[1,2304]{1,0:T(2,128)(2,1)S(1)} %collective-permute-done.2.refs_4_) | copy-start | bytes 13828
  14.0 0.6 copy-start.13
  14.0 0.6 copy-start.4
  14.6 0.6 copy-start.7
  19.8 7.8 %collective-permute-start.4 = (bf16[4,72,128]{2,1,0:T(8,128)(2,1)}, bf16[4,72,128]{2,1,0:T(8,128)(2,1)S(1)}, u32[]{:S(2)}, u32[]{:S(2)}) collective-permute-start(bf16[4,72,128]{2,1,0:T(8,128)(2,1)} %get-tuple-element.26), channel_id=1, source_target_pairs={{0,24},{8,0},{16,8},{24,16},{1,25},{9,1},{17,9},{25,17},{2,26},{10... | collective-permute-start | bytes 221192 | tf_op jit(solution)/shard_map/ppermute | solution.py:138
  22.4 5.5 %collective-permute-start.5 = (bf16[4,72,128]{2,1,0:T(8,128)(2,1)}, bf16[4,72,128]{2,1,0:T(8,128)(2,1)S(1)}, u32[]{:S(2)}, u32[]{:S(2)}) collective-permute-start(bf16[4,72,128]{2,1,0:T(8,128)(2,1)} %get-tuple-element.27), channel_id=1, source_target_pairs={{0,8},{8,16},{16,24},{24,0},{1,9},{9,17},{17,25},{25,1},{2,10},{10... | collective-permute-start | bytes 221192 | tf_op jit(solution)/shard_map/ppermute | solution.py:139
  22.4 1.6 %collective-permute-start.6 = (bf16[1,2304]{1,0:T(2,128)(2,1)}, bf16[1,2304]{1,0:T(2,128)(2,1)S(1)}, u32[]{:S(2)}, u32[]{:S(2)}) collective-permute-start(bf16[1,2304]{1,0:T(2,128)(2,1)} %get-tuple-element.28), channel_id=1, source_target_pairs={{0,7},{1,0},{2,1},{3,2},{4,3},{5,4},{6,5},{7,6},{8,15},{9,8},{10,9... | collective-permute-start | bytes 13832 | tf_op jit(solution)/shard_map/ppermute | solution.py:140
  22.4 5.1 %collective-permute-start.7 = (bf16[1,2304]{1,0:T(2,128)(2,1)}, bf16[1,2304]{1,0:T(2,128)(2,1)S(1)}, u32[]{:S(2)}, u32[]{:S(2)}) collective-permute-start(bf16[1,2304]{1,0:T(2,128)(2,1)} %get-tuple-element.29), channel_id=1, source_target_pairs={{0,1},{1,2},{2,3},{3,4},{4,5},{5,6},{6,7},{7,0},{8,9},{9,10},{10,1... | collective-permute-start | bytes 13832 | tf_op jit(solution)/shard_map/ppermute | solution.py:141
  24.0 3.9 %copy-start.10 = (bf16[1,2304]{1,0:T(2,128)(2,1)}, bf16[1,2304]{1,0:T(2,128)(2,1)S(1)}, u32[]{:S(2)}) copy-start(bf16[1,2304]{1,0:T(2,128)(2,1)S(1)} %collective-permute-done.6.refs_4_) | copy-start | bytes 13828
  27.5 0.6 copy-start.12
  27.5 0.6 copy-start.3
  27.9 0.6 copy-start.6
  33.0 7.7 %collective-permute-start.8 = (bf16[4,72,128]{2,1,0:T(8,128)(2,1)}, bf16[4,72,128]{2,1,0:T(8,128)(2,1)S(1)}, u32[]{:S(2)}, u32[]{:S(2)}) collective-permute-start(bf16[4,72,128]{2,1,0:T(8,128)(2,1)} %get-tuple-element.31), channel_id=1, source_target_pairs={{0,24},{8,0},{16,8},{24,16},{1,25},{9,1},{17,9},{25,17},{2,26},{10... | collective-permute-start | bytes 221192 | tf_op jit(solution)/shard_map/ppermute | solution.py:138
  35.6 5.5 %collective-permute-start.9 = (bf16[4,72,128]{2,1,0:T(8,128)(2,1)}, bf16[4,72,128]{2,1,0:T(8,128)(2,1)S(1)}, u32[]{:S(2)}, u32[]{:S(2)}) collective-permute-start(bf16[4,72,128]{2,1,0:T(8,128)(2,1)} %get-tuple-element.32), channel_id=1, source_target_pairs={{0,8},{8,16},{16,24},{24,0},{1,9},{9,17},{17,25},{25,1},{2,10},{10... | collective-permute-start | bytes 221192 | tf_op jit(solution)/shard_map/ppermute | solution.py:139
  35.6 1.6 %collective-permute-start.10 = (bf16[1,2304]{1,0:T(2,128)(2,1)}, bf16[1,2304]{1,0:T(2,128)(2,1)S(1)}, u32[]{:S(2)}, u32[]{:S(2)}) collective-permute-start(bf16[1,2304]{1,0:T(2,128)(2,1)} %get-tuple-element.33), channel_id=1, source_target_pairs={{0,7},{1,0},{2,1},{3,2},{4,3},{5,4},{6,5},{7,6},{8,15},{9,8},{10,9... | collective-permute-start | bytes 13832 | tf_op jit(solution)/shard_map/ppermute | solution.py:140
  35.6 5.1 %collective-permute-start.11 = (bf16[1,2304]{1,0:T(2,128)(2,1)}, bf16[1,2304]{1,0:T(2,128)(2,1)S(1)}, u32[]{:S(2)}, u32[]{:S(2)}) collective-permute-start(bf16[1,2304]{1,0:T(2,128)(2,1)} %get-tuple-element.34), channel_id=1, source_target_pairs={{0,1},{1,2},{2,3},{3,4},{4,5},{5,6},{6,7},{7,0},{8,9},{9,10},{10,1... | collective-permute-start | bytes 13832 | tf_op jit(solution)/shard_map/ppermute | solution.py:141
  37.2 3.9 %copy-start.8 = (bf16[1,2304]{1,0:T(2,128)(2,1)}, bf16[1,2304]{1,0:T(2,128)(2,1)S(1)}, u32[]{:S(2)}) copy-start(bf16[1,2304]{1,0:T(2,128)(2,1)S(1)} %collective-permute-done.10.refs_5_) | copy-start | bytes 13828
  40.7 0.6 copy-start.9
  40.7 0.6 copy-start.2
  41.1 0.6 copy-start.5
  41.7 13.1 %copy-start.1 = (bf16[16,72,72]{2,1,0:T(8,128)(2,1)S(1)}, bf16[16,72,72]{2,1,0:T(8,128)(2,1)}, u32[]{:S(2)}) copy-start(bf16[16,72,72]{2,1,0:T(8,128)(2,1)} %param.11) | copy-start | bytes 497668
  50.6 20.2 %all-to-all-start = ((bf16[8,4,72,128]{3,2,1,0:T(8,128)(2,1)}), bf16[8,4,72,128]{3,2,1,0:T(8,128)(2,1)S(1)}, u32[]{:S(2)}, u32[]{:S(2)}) async-start(bf16[8,4,72,128]{3,2,1,0:T(8,128)(2,1)} %shard_map.67), calls=%async_computation | async-start | bytes 1179648 | tf_op jit(solution)/shard_map/all_to_all | solution.py:157

commit v5 on v4

--- a/solution.py
+++ b/solution.py
@@ -11,9 +11,6 @@
 
 
 def stencil_kernel(step, emit, last, *refs):
-    if last:
-        order_ref = refs[0]
-        refs = refs[1:]
     if step:
         q_ref, wind_ref, north_ref, south_ref, east_ref, west_ref = refs[:6]
         refs = refs[6:]
@@ -70,13 +67,8 @@
             new = out.astype(jnp.bfloat16)
             if last:
                 new_scr[...] = new.astype(jnp.float32)
-                picked = [new_scr[:, row, :] for row in range(rows)]
-                for slot in range(rows):
-                    wanted = order_ref[slot]
-                    value = picked[0]
-                    for row in range(1, rows):
-                        value = jnp.where(wanted == row, picked[row], value)
-                    out_ref[slot, field] = value.astype(out_ref.dtype)
+                for row in range(rows):
+                    out_ref[row, field] = new_scr[:, row, :].astype(out_ref.dtype)
             else:
                 out_ref[field] = new
         else:
@@ -117,9 +109,6 @@
     vmem = pl.BlockSpec(memory_space=pltpu.VMEM)
     ins = [vmem] * (1 + len(extra))
     operands = (q,) + extra
-    if last:
-        ins = [pl.BlockSpec(memory_space=pltpu.SMEM)] + ins
-        operands = (order,) + operands
     return pl.pallas_call(
         functools.partial(stencil_kernel, step, emit, last),
         out_shape=tuple(outs),
@@ -153,7 +142,8 @@
         advected = result[0]
         halos = result[1:]
     if tracers.shape[2] > 8:
-        advected = jnp.take(advected, order, axis=2).transpose(2, 0, 1, 3)
+        advected = advected.transpose(2, 0, 1, 3)
+    advected = jnp.take(advected, order, axis=0)
     received = lax.all_to_all(advected, "tile", split_axis=0, concat_axis=0, tiled=True)
     band_count = band_table.shape[0]
     inverse = diffusion[0]

time: 72.7 us -> 72.2 us (level)
  Pallas kernels: 20.1 us -> 16.6 us
  starting transfers between devices: 16.5 us -> 18.8 us
  waiting for transfers between devices: 29.9 us -> 27.7 us
  other arithmetic: 1.12 us -> 2.78 us
  local copies, waits for them, and re-layouts: 3.58 us -> 4.66 us
    ppermute x3, starting transfers between devices: 2.77 us -> 8.71 us  [exchange(): lax.ppermute(first, 'tile', [(i, (i - 1) % tile) for i in range(tile)])]
    ppermute x3, starting transfers between devices: 9.13 us -> 3.69 us  [exchange(): north = lax.ppermute(top, 'sec', [(i, (i - 1) % sec) for i in range(sec)])]
    ppermute x3, waiting for transfers between devices: 0.71 us -> 4.73 us  [exchange(): lax.ppermute(bottom, 'sec', [(i, (i + 1) % sec) for i in range(sec)])]
    pallas_call x4, Pallas kernels: 20.1 us -> 16.6 us  [stencil_call(): pl.pallas_call(functools.partial(stencil_kernel, step, emit, last), out_s...]
    ppermute x3, waiting for transfers between devices: 10.5 us -> 7.04 us  [exchange(): lax.ppermute(last, 'tile', [(i, (i + 1) % tile) for i in range(tile)])]
    ppermute x3, starting transfers between devices: 0.01 us -> 2.81 us  [exchange(): lax.ppermute(bottom, 'sec', [(i, (i + 1) % sec) for i in range(sec)])]
    ppermute x3, waiting for transfers between devices: 2.77 us -> 0.01 us  [exchange(): lax.ppermute(first, 'tile', [(i, (i - 1) % tile) for i in range(tile)])]
    gather x0 -> x1, local copies, waits for them, and re-layouts: none -> 1.72 us  [per_device(): advected = jnp.take(advected, order, axis=0)]
  transfers between devices with their start and end apart: 13 -> 13, of which waited for: 9 -> 7; matrix products, arithmetic and copies ran while one was open for 2% -> 3% of each run, Pallas kernels for 0% -> 0%
where the time goes in v5:
time: 72.2 us; the launch traced here: 71.8 us
  waiting for transfers between devices  27.7 us (38%)
  starting transfers between devices  18.8 us (26%)
  Pallas kernels  16.6 us (23%)
  local copies, waits for them, and re-layouts  4.66 us (6%)
  other arithmetic  2.78 us (4%)
  between operations  0.77 us (1%)
    pallas_call x4, Pallas kernels, stencil_call(): pl.pallas_call(functools.partial(stencil_kernel, step, emit, last), out_s...  16.6 us
    all_to_all x1, waiting for transfers between devices, per_device(): lax.all_to_all(advected, 'tile', split_axis=0, concat_axis=0, tiled=True)  15.9 us
    ppermute x3, starting transfers between devices, exchange(): lax.ppermute(first, 'tile', [(i, (i - 1) % tile) for i in range(tile)])  8.71 us
    ppermute x3, waiting for transfers between devices, exchange(): lax.ppermute(last, 'tile', [(i, (i + 1) % tile) for i in range(tile)])  7.04 us
    ppermute x3, waiting for transfers between devices, exchange(): lax.ppermute(bottom, 'sec', [(i, (i + 1) % sec) for i in range(sec)])  4.73 us
    ppermute x3, starting transfers between devices, exchange(): north = lax.ppermute(top, 'sec', [(i, (i - 1) % sec) for i in range(sec)])  3.69 us
    all_to_all x1, starting transfers between devices, per_device(): lax.all_to_all(advected, 'tile', split_axis=0, concat_axis=0, tiled=True)  3.54 us
    ppermute x3, starting transfers between devices, exchange(): lax.ppermute(bottom, 'sec', [(i, (i + 1) % sec) for i in range(sec)])  2.81 us
  transfers between devices with their start and end apart: 13, of which 7 were waited for; matrix products, arithmetic and copies ran while one was open for 3% of the time, Pallas kernels for 0%

profile of v5, /device:TPU:0, one launch (start us, length us, event | category | flops | bytes accessed | tf_op | source)
XLA Modules:
  0.0 71.8 jit_solution(5451524025265731370)
XLA Ops:
  0.0 0.0 copy-start
  0.0 2.2 %shard_map.64 = (bf16[4,72,128]{2,1,0:T(8,128)(2,1)}, bf16[4,72,128]{2,1,0:T(8,128)(2,1)}, bf16[1,2304]{1,0:T(2,128)(2,1)}, bf16[1,2304]{1,0:T(2,128)(2,1)}) custom-call(bf16[4,72,8,128]{3,2,1,0:T(8,128)(2,1)} %refs_0_.3), custom_call_target="tpu_custom_call" | custom-call | tf_op jit(solution)/shard_map/pallas_call | solution.py:112
  2.2 4.5 %collective-permute-start.2 = (bf16[1,2304]{1,0:T(2,128)(2,1)}, bf16[1,2304]{1,0:T(2,128)(2,1)S(1)}, u32[]{:S(2)}, u32[]{:S(2)}) collective-permute-start(bf16[1,2304]{1,0:T(2,128)(2,1)} %get-tuple-element.23), channel_id=1, source_target_pairs={{0,7},{1,0},{2,1},{3,2},{4,3},{5,4},{6,5},{7,6},{8,15},{9,8},{10,9... | collective-permute-start | bytes 13832 | tf_op jit(solution)/shard_map/ppermute | solution.py:129
  6.7 0.0 collective-permute-start.3
  6.7 2.4 %collective-permute-start = (bf16[4,72,128]{2,1,0:T(8,128)(2,1)}, bf16[4,72,128]{2,1,0:T(8,128)(2,1)S(1)}, u32[]{:S(2)}, u32[]{:S(2)}) collective-permute-start(bf16[4,72,128]{2,1,0:T(8,128)(2,1)} %get-tuple-element.21), channel_id=1, source_target_pairs={{0,24},{8,0},{16,8},{24,16},{1,25},{9,1},{17,9},{25,17},{2,26},{10... | collective-permute-start | bytes 221192 | tf_op jit(solution)/shard_map/ppermute | solution.py:127
  9.2 0.0 collective-permute-start.1
  9.2 1.7 %sort.17 = (s32[8]{0:T(128)}, s32[8]{0:T(128)S(1)}) sort(s32[8]{0:T(128)} %bitcast.22, s32[8]{0:T(128)S(1)} %iota.9), dimensions={0}, to_apply=%region_0.0 | sort | flops 24 | bytes 128 | tf_op jit(solution)/shard_map/jit(argsort)/sort | solution.py:135
  10.9 0.0 collective-permute-done.2.refs_4_
  10.9 0.0 copy-start.10
  10.9 0.9 %collective-permute-done.3.refs_5_ = bf16[1,2304]{1,0:T(2,128)(2,1)S(1)} collective-permute-done((bf16[1,2304]{1,0:T(2,128)(2,1)}, bf16[1,2304]{1,0:T(2,128)(2,1)S(1)}, u32[]{:S(2)}, u32[]{:S(2)}) %collective-permute-start.3) | collective-permute-done | bytes 4640 | tf_op jit(solution)/shard_map/ppermute | solution.py:130
  11.8 0.0 collective-permute-done.refs_2_
  11.9 2.8 %collective-permute-done.1.refs_3_ = bf16[4,72,128]{2,1,0:T(8,128)(2,1)S(1)} collective-permute-done((bf16[4,72,128]{2,1,0:T(8,128)(2,1)}, bf16[4,72,128]{2,1,0:T(8,128)(2,1)S(1)}, u32[]{:S(2)}, u32[]{:S(2)}) %collective-permute-start.1) | collective-permute-done | bytes 73760 | tf_op jit(solution)/shard_map/ppermute | solution.py:128
  14.7 0.0 copy-done.10
  14.7 0.0 copy-done.11
  14.7 0.0 copy-done.2
  14.7 0.0 copy-start.3
  14.7 0.6 copy-done.3
  15.3 4.5 %shard_map.65 = (bf16[4,72,8,128]{3,2,1,0:T(8,128)(2,1)}, bf16[4,72,128]{2,1,0:T(8,128)(2,1)}, bf16[4,72,128]{2,1,0:T(8,128)(2,1)}, bf16[1,2304]{1,0:T(2,128)(2,1)}, bf16[1,2304]{1,0:T(2,128)(2,1)}) custom-call(bf16[4,72,8,128]{3,2,1,0:T(8,128)(2,1)} %refs_0_.3, bf16[2,72,8,128]{3,2,1,0:T(8,128)(2,1)} %refs_1_.5, bf16[4,72,128]{2,1,0:T(8,128)(2,1)} %copy-done.2, ...), custom_call_target="tpu_custom_call" | custom-call | tf_op jit(solution)/shard_map/pallas_call | solution.py:112
  19.8 2.1 %collective-permute-start.6 = (bf16[1,2304]{1,0:T(2,128)(2,1)}, bf16[1,2304]{1,0:T(2,128)(2,1)S(1)}, u32[]{:S(2)}, u32[]{:S(2)}) collective-permute-start(bf16[1,2304]{1,0:T(2,128)(2,1)} %get-tuple-element.28), channel_id=1, source_target_pairs={{0,7},{1,0},{2,1},{3,2},{4,3},{5,4},{6,5},{7,6},{8,15},{9,8},{10,9... | collective-permute-start | bytes 13832 | tf_op jit(solution)/shard_map/ppermute | solution.py:129
  21.9 0.0 collective-permute-start.7
  21.9 0.9 %collective-permute-start.4 = (bf16[4,72,128]{2,1,0:T(8,128)(2,1)}, bf16[4,72,128]{2,1,0:T(8,128)(2,1)S(1)}, u32[]{:S(2)}, u32[]{:S(2)}) collective-permute-start(bf16[4,72,128]{2,1,0:T(8,128)(2,1)} %get-tuple-element.26), channel_id=1, source_target_pairs={{0,24},{8,0},{16,8},{24,16},{1,25},{9,1},{17,9},{25,17},{2,26},{10... | collective-permute-start | bytes 221192 | tf_op jit(solution)/shard_map/ppermute | solution.py:127
  22.8 1.1 %collective-permute-start.5 = (bf16[4,72,128]{2,1,0:T(8,128)(2,1)}, bf16[4,72,128]{2,1,0:T(8,128)(2,1)S(1)}, u32[]{:S(2)}, u32[]{:S(2)}) collective-permute-start(bf16[4,72,128]{2,1,0:T(8,128)(2,1)} %get-tuple-element.27), channel_id=1, source_target_pairs={{0,8},{8,16},{16,24},{24,0},{1,9},{9,17},{17,25},{25,1},{2,10},{10... | collective-permute-start | bytes 221192 | tf_op jit(solution)/shard_map/ppermute | solution.py:128
  23.9 0.0 collective-permute-done.6.refs_4_
  23.9 3.1 %collective-permute-done.7.refs_5_ = bf16[1,2304]{1,0:T(2,128)(2,1)S(1)} collective-permute-done((bf16[1,2304]{1,0:T(2,128)(2,1)}, bf16[1,2304]{1,0:T(2,128)(2,1)S(1)}, u32[]{:S(2)}, u32[]{:S(2)}) %collective-permute-start.7) | collective-permute-done | bytes 4640 | tf_op jit(solution)/shard_map/ppermute | solution.py:130
  27.0 0.0 collective-permute-done.4.refs_2_
  27.0 1.3 %collective-permute-done.5.refs_3_ = bf16[4,72,128]{2,1,0:T(8,128)(2,1)S(1)} collective-permute-done((bf16[4,72,128]{2,1,0:T(8,128)(2,1)}, bf16[4,72,128]{2,1,0:T(8,128)(2,1)S(1)}, u32[]{:S(2)}, u32[]{:S(2)}) %collective-permute-start.5) | collective-permute-done | bytes 73760 | tf_op jit(solution)/shard_map/ppermute | solution.py:128
  28.2 0.0 copy-done.13
  28.2 0.6 copy-done.5
  28.9 4.5 %shard_map.66 = (bf16[4,72,8,128]{3,2,1,0:T(8,128)(2,1)}, bf16[4,72,128]{2,1,0:T(8,128)(2,1)}, bf16[4,72,128]{2,1,0:T(8,128)(2,1)}, bf16[1,2304]{1,0:T(2,128)(2,1)}, bf16[1,2304]{1,0:T(2,128)(2,1)}) custom-call(bf16[4,72,8,128]{3,2,1,0:T(8,128)(2,1)} %get-tuple-element.25.refs_0_, bf16[2,72,8,128]{3,2,1,0:T(8,128)(2,1)} %refs_1_.5, ...), custom_call_target="tpu_custom_call" | custom-call | tf_op jit(solution)/shard_map/pallas_call | solution.py:112
  33.4 2.1 %collective-permute-start.10 = (bf16[1,2304]{1,0:T(2,128)(2,1)}, bf16[1,2304]{1,0:T(2,128)(2,1)S(1)}, u32[]{:S(2)}, u32[]{:S(2)}) collective-permute-start(bf16[1,2304]{1,0:T(2,128)(2,1)} %get-tuple-element.33), channel_id=1, source_target_pairs={{0,7},{1,0},{2,1},{3,2},{4,3},{5,4},{6,5},{7,6},{8,15},{9,8},{10,9... | collective-permute-start | bytes 13832 | tf_op jit(solution)/shard_map/ppermute | solution.py:129
  35.5 0.0 collective-permute-start.11
  35.5 0.3 collective-permute-start.8
  35.8 1.7 %collective-permute-start.9 = (bf16[4,72,128]{2,1,0:T(8,128)(2,1)}, bf16[4,72,128]{2,1,0:T(8,128)(2,1)S(1)}, u32[]{:S(2)}, u32[]{:S(2)}) collective-permute-start(bf16[4,72,128]{2,1,0:T(8,128)(2,1)} %get-tuple-element.32), channel_id=1, source_target_pairs={{0,8},{8,16},{16,24},{24,0},{1,9},{9,17},{17,25},{25,1},{2,10},{10... | collective-permute-start | bytes 221192 | tf_op jit(solution)/shard_map/ppermute | solution.py:128
  37.5 0.0 collective-permute-done.10.refs_4_
  37.5 3.0 %collective-permute-done.11.refs_5_ = bf16[1,2304]{1,0:T(2,128)(2,1)S(1)} collective-permute-done((bf16[1,2304]{1,0:T(2,128)(2,1)}, bf16[1,2304]{1,0:T(2,128)(2,1)S(1)}, u32[]{:S(2)}, u32[]{:S(2)}) %collective-permute-start.11) | collective-permute-done | bytes 4640 | tf_op jit(solution)/shard_map/ppermute | solution.py:130
  40.6 0.0 collective-permute-done.8.refs_2_
  40.6 0.7 collective-permute-done.9.refs_3_
  41.3 0.6 copy-done.7
  41.9 5.4 %shard_map.67 = bf16[8,4,72,128]{3,2,1,0:T(8,128)(2,1)} custom-call(bf16[4,72,8,128]{3,2,1,0:T(8,128)(2,1)} %get-tuple-element.30.refs_0_, bf16[2,72,8,128]{3,2,1,0:T(8,128)(2,1)} %refs_1_.5, bf16[4,72,128]{2,1,0:T(8,128)(2,1)} %copy-done.6, bf16[4,72,128]{2,1,0:T(8,128)(2,1)} %copy-done.7, bf16[1,2304]{1,0:T(2,128)(2,1)} %copy-done.8, bf16[1,2304]{1,0:T(2,128)(2,1)} %copy-done.9), custom_call_target="tpu_custom_call" | custom-call | tf_op jit(solution)/shard_map/pallas_call | solution.py:112
  47.3 1.7 %gather_fusion = bf16[8,4,72,128]{3,2,1,0:T(8,128)(2,1)S(1)} fusion(bf16[8,4,72,128]{3,2,1,0:T(8,128)(2,1)} %shard_map.67, s32[1024]{0:T(1024)S(1)} %pad_clamp_fusion), kind=kCustom, calls=%fused_computation | custom fusion | bytes 1179680 | tf_op jit(solution)/shard_map/jit(_take)/gather | solution.py:146
  49.0 0.0 copy-start.1
  49.0 0.9 %broadcast_select_fusion = bf16[8,4,72,128]{3,2,1,0:T(8,128)(2,1)} fusion(bf16[8,4,72,128]{3,2,1,0:T(8,128)(2,1)S(1)} %gather_fusion, pred[8]{0:T(512)(128)(4,1)S(1)} %compare_and_fusion), kind=kLoop, calls=%fused_computation.6 | loop fusion | flops 294912 | bytes 1179656 | tf_op jit(solution)/shard_map/jit(_take)/select_n | solution.py:146
  50.0 3.5 %all-to-all-start = ((bf16[8,4,72,128]{3,2,1,0:T(8,128)(2,1)}), bf16[8,4,72,128]{3,2,1,0:T(8,128)(2,1)S(1)}, u32[]{:S(2)}, u32[]{:S(2)}) async-start(bf16[8,4,72,128]{3,2,1,0:T(8,128)(2,1)} %broadcast_select_fusion), calls=%async_computation | async-start | bytes 1179648 | tf_op jit(solution)/shard_map/all_to_all | solution.py:147
  54.2 0.1 select_reduce_fusion
  54.3 15.9 %all-to-all-done = bf16[8,4,72,128]{3,2,1,0:T(8,128)(2,1)S(1)} async-done(((bf16[8,4,72,128]{3,2,1,0:T(8,128)(2,1)}), bf16[8,4,72,128]{3,2,1,0:T(8,128)(2,1)S(1)}, u32[]{:S(2)}, u32[]{:S(2)}) %all-to-all-start) | async-done | bytes 589856 | tf_op jit(solution)/shard_map/all_to_all | solution.py:147
  70.2 0.3 convolution_bitcast_fusion.1
  70.5 0.3 fusion.1
  70.8 1.0 %copy.9 = bf16[4,72,8,128]{3,2,1,0:T(8,128)(2,1)} copy(bf16[4,72,8,128]{3,1,0,2:T(8,128)(2,1)S(1)} %fusion.1) | data formatting | bytes 1179648 | tf_op jit(solution)/shard_map/convert_element_type | solution.py:155
  (22 shorter events, 0.1 us)
Async XLA Ops:
  0.0 70.2 %copy-start = (bf16[1,72,72]{2,1,0:T(8,128)(2,1)S(1)}, bf16[1,72,72]{2,1,0:T(8,128)(2,1)}, u32[]{:S(2)}) copy-start(bf16[1,72,72]{2,1,0:T(8,128)(2,1)} %param.9) | copy-start | bytes 31108
  2.2 8.6 %collective-permute-start.2 = (bf16[1,2304]{1,0:T(2,128)(2,1)}, bf16[1,2304]{1,0:T(2,128)(2,1)S(1)}, u32[]{:S(2)}, u32[]{:S(2)}) collective-permute-start(bf16[1,2304]{1,0:T(2,128)(2,1)} %get-tuple-element.23), channel_id=1, source_target_pairs={{0,7},{1,0},{2,1},{3,2},{4,3},{5,4},{6,5},{7,6},{8,15},{9,8},{10,9... | collective-permute-start | bytes 13832 | tf_op jit(solution)/shard_map/ppermute | solution.py:129
  6.7 5.1 %collective-permute-start.3 = (bf16[1,2304]{1,0:T(2,128)(2,1)}, bf16[1,2304]{1,0:T(2,128)(2,1)S(1)}, u32[]{:S(2)}, u32[]{:S(2)}) collective-permute-start(bf16[1,2304]{1,0:T(2,128)(2,1)} %get-tuple-element.24), channel_id=1, source_target_pairs={{0,1},{1,2},{2,3},{3,4},{4,5},{5,6},{6,7},{7,0},{8,9},{9,10},{10,1... | collective-permute-start | bytes 13832 | tf_op jit(solution)/shard_map/ppermute | solution.py:130
  6.7 5.1 %collective-permute-start = (bf16[4,72,128]{2,1,0:T(8,128)(2,1)}, bf16[4,72,128]{2,1,0:T(8,128)(2,1)S(1)}, u32[]{:S(2)}, u32[]{:S(2)}) collective-permute-start(bf16[4,72,128]{2,1,0:T(8,128)(2,1)} %get-tuple-element.21), channel_id=1, source_target_pairs={{0,24},{8,0},{16,8},{24,16},{1,25},{9,1},{17,9},{25,17},{2,26},{10... | collective-permute-start | bytes 221192 | tf_op jit(solution)/shard_map/ppermute | solution.py:127
  9.2 5.5 %collective-permute-start.1 = (bf16[4,72,128]{2,1,0:T(8,128)(2,1)}, bf16[4,72,128]{2,1,0:T(8,128)(2,1)S(1)}, u32[]{:S(2)}, u32[]{:S(2)}) collective-permute-start(bf16[4,72,128]{2,1,0:T(8,128)(2,1)} %get-tuple-element.22), channel_id=1, source_target_pairs={{0,8},{8,16},{16,24},{24,0},{1,9},{9,17},{17,25},{25,1},{2,10},{10... | collective-permute-start | bytes 221192 | tf_op jit(solution)/shard_map/ppermute | solution.py:128
  10.9 3.8 %copy-start.10 = (bf16[1,2304]{1,0:T(2,128)(2,1)}, bf16[1,2304]{1,0:T(2,128)(2,1)S(1)}, u32[]{:S(2)}) copy-start(bf16[1,2304]{1,0:T(2,128)(2,1)S(1)} %collective-permute-done.2.refs_4_) | copy-start | bytes 13828
  11.8 2.8 %copy-start.11 = (bf16[1,2304]{1,0:T(2,128)(2,1)}, bf16[1,2304]{1,0:T(2,128)(2,1)S(1)}, u32[]{:S(2)}) copy-start(bf16[1,2304]{1,0:T(2,128)(2,1)S(1)} %collective-permute-done.3.refs_5_) | copy-start | bytes 13828
  11.9 2.8 %copy-start.2 = (bf16[4,72,128]{2,1,0:T(8,128)(2,1)}, bf16[4,72,128]{2,1,0:T(8,128)(2,1)S(1)}, u32[]{:S(2)}) copy-start(bf16[4,72,128]{2,1,0:T(8,128)(2,1)S(1)} %collective-permute-done.refs_2_) | copy-start | bytes 221188
  14.7 0.6 copy-start.3
  19.8 4.1 %collective-permute-start.6 = (bf16[1,2304]{1,0:T(2,128)(2,1)}, bf16[1,2304]{1,0:T(2,128)(2,1)S(1)}, u32[]{:S(2)}, u32[]{:S(2)}) collective-permute-start(bf16[1,2304]{1,0:T(2,128)(2,1)} %get-tuple-element.28), channel_id=1, source_target_pairs={{0,7},{1,0},{2,1},{3,2},{4,3},{5,4},{6,5},{7,6},{8,15},{9,8},{10,9... | collective-permute-start | bytes 13832 | tf_op jit(solution)/shard_map/ppermute | solution.py:129
  21.9 5.1 %collective-permute-start.7 = (bf16[1,2304]{1,0:T(2,128)(2,1)}, bf16[1,2304]{1,0:T(2,128)(2,1)S(1)}, u32[]{:S(2)}, u32[]{:S(2)}) collective-permute-start(bf16[1,2304]{1,0:T(2,128)(2,1)} %get-tuple-element.29), channel_id=1, source_target_pairs={{0,1},{1,2},{2,3},{3,4},{4,5},{5,6},{6,7},{7,0},{8,9},{9,10},{10,1... | collective-permute-start | bytes 13832 | tf_op jit(solution)/shard_map/ppermute | solution.py:130
  21.9 5.1 %collective-permute-start.4 = (bf16[4,72,128]{2,1,0:T(8,128)(2,1)}, bf16[4,72,128]{2,1,0:T(8,128)(2,1)S(1)}, u32[]{:S(2)}, u32[]{:S(2)}) collective-permute-start(bf16[4,72,128]{2,1,0:T(8,128)(2,1)} %get-tuple-element.26), channel_id=1, source_target_pairs={{0,24},{8,0},{16,8},{24,16},{1,25},{9,1},{17,9},{25,17},{2,26},{10... | collective-permute-start | bytes 221192 | tf_op jit(solution)/shard_map/ppermute | solution.py:127
  22.8 5.5 %collective-permute-start.5 = (bf16[4,72,128]{2,1,0:T(8,128)(2,1)}, bf16[4,72,128]{2,1,0:T(8,128)(2,1)S(1)}, u32[]{:S(2)}, u32[]{:S(2)}) collective-permute-start(bf16[4,72,128]{2,1,0:T(8,128)(2,1)} %get-tuple-element.27), channel_id=1, source_target_pairs={{0,8},{8,16},{16,24},{24,0},{1,9},{9,17},{17,25},{25,1},{2,10},{10... | collective-permute-start | bytes 221192 | tf_op jit(solution)/shard_map/ppermute | solution.py:128
  23.9 4.3 %copy-start.12 = (bf16[1,2304]{1,0:T(2,128)(2,1)}, bf16[1,2304]{1,0:T(2,128)(2,1)S(1)}, u32[]{:S(2)}) copy-start(bf16[1,2304]{1,0:T(2,128)(2,1)S(1)} %collective-permute-done.6.refs_4_) | copy-start | bytes 13828
  27.0 1.3 %copy-start.13 = (bf16[1,2304]{1,0:T(2,128)(2,1)}, bf16[1,2304]{1,0:T(2,128)(2,1)S(1)}, u32[]{:S(2)}) copy-start(bf16[1,2304]{1,0:T(2,128)(2,1)S(1)} %collective-permute-done.7.refs_5_) | copy-start | bytes 13828
  27.0 1.3 %copy-start.4 = (bf16[4,72,128]{2,1,0:T(8,128)(2,1)}, bf16[4,72,128]{2,1,0:T(8,128)(2,1)S(1)}, u32[]{:S(2)}) copy-start(bf16[4,72,128]{2,1,0:T(8,128)(2,1)S(1)} %collective-permute-done.4.refs_2_) | copy-start | bytes 221188
  28.2 0.6 copy-start.5
  33.4 4.2 %collective-permute-start.10 = (bf16[1,2304]{1,0:T(2,128)(2,1)}, bf16[1,2304]{1,0:T(2,128)(2,1)S(1)}, u32[]{:S(2)}, u32[]{:S(2)}) collective-permute-start(bf16[1,2304]{1,0:T(2,128)(2,1)} %get-tuple-element.33), channel_id=1, source_target_pairs={{0,7},{1,0},{2,1},{3,2},{4,3},{5,4},{6,5},{7,6},{8,15},{9,8},{10,9... | collective-permute-start | bytes 13832 | tf_op jit(solution)/shard_map/ppermute | solution.py:129
  35.5 5.1 %collective-permute-start.11 = (bf16[1,2304]{1,0:T(2,128)(2,1)}, bf16[1,2304]{1,0:T(2,128)(2,1)S(1)}, u32[]{:S(2)}, u32[]{:S(2)}) collective-permute-start(bf16[1,2304]{1,0:T(2,128)(2,1)} %get-tuple-element.34), channel_id=1, source_target_pairs={{0,1},{1,2},{2,3},{3,4},{4,5},{5,6},{6,7},{7,0},{8,9},{9,10},{10,1... | collective-permute-start | bytes 13832 | tf_op jit(solution)/shard_map/ppermute | solution.py:130
  35.5 5.1 %collective-permute-start.8 = (bf16[4,72,128]{2,1,0:T(8,128)(2,1)}, bf16[4,72,128]{2,1,0:T(8,128)(2,1)S(1)}, u32[]{:S(2)}, u32[]{:S(2)}) collective-permute-start(bf16[4,72,128]{2,1,0:T(8,128)(2,1)} %get-tuple-element.31), channel_id=1, source_target_pairs={{0,24},{8,0},{16,8},{24,16},{1,25},{9,1},{17,9},{25,17},{2,26},{10... | collective-permute-start | bytes 221192 | tf_op jit(solution)/shard_map/ppermute | solution.py:127
  35.8 5.5 %collective-permute-start.9 = (bf16[4,72,128]{2,1,0:T(8,128)(2,1)}, bf16[4,72,128]{2,1,0:T(8,128)(2,1)S(1)}, u32[]{:S(2)}, u32[]{:S(2)}) collective-permute-start(bf16[4,72,128]{2,1,0:T(8,128)(2,1)} %get-tuple-element.32), channel_id=1, source_target_pairs={{0,8},{8,16},{16,24},{24,0},{1,9},{9,17},{17,25},{25,1},{2,10},{10... | collective-permute-start | bytes 221192 | tf_op jit(solution)/shard_map/ppermute | solution.py:128
  37.5 3.8 %copy-start.8 = (bf16[1,2304]{1,0:T(2,128)(2,1)}, bf16[1,2304]{1,0:T(2,128)(2,1)S(1)}, u32[]{:S(2)}) copy-start(bf16[1,2304]{1,0:T(2,128)(2,1)S(1)} %collective-permute-done.10.refs_4_) | copy-start | bytes 13828
  40.6 0.7 %copy-start.9 = (bf16[1,2304]{1,0:T(2,128)(2,1)}, bf16[1,2304]{1,0:T(2,128)(2,1)S(1)}, u32[]{:S(2)}) copy-start(bf16[1,2304]{1,0:T(2,128)(2,1)S(1)} %collective-permute-done.11.refs_5_) | copy-start | bytes 13828
  40.6 0.7 %copy-start.6 = (bf16[4,72,128]{2,1,0:T(8,128)(2,1)}, bf16[4,72,128]{2,1,0:T(8,128)(2,1)S(1)}, u32[]{:S(2)}) copy-start(bf16[4,72,128]{2,1,0:T(8,128)(2,1)S(1)} %collective-permute-done.8.refs_2_) | copy-start | bytes 221188
  41.3 0.6 copy-start.7
  49.0 5.2 %copy-start.1 = (bf16[16,72,72]{2,1,0:T(8,128)(2,1)S(1)}, bf16[16,72,72]{2,1,0:T(8,128)(2,1)}, u32[]{:S(2)}) copy-start(bf16[16,72,72]{2,1,0:T(8,128)(2,1)} %param.11) | copy-start | bytes 497668
  50.0 20.2 %all-to-all-start = ((bf16[8,4,72,128]{3,2,1,0:T(8,128)(2,1)}), bf16[8,4,72,128]{3,2,1,0:T(8,128)(2,1)S(1)}, u32[]{:S(2)}, u32[]{:S(2)}) async-start(bf16[8,4,72,128]{3,2,1,0:T(8,128)(2,1)} %broadcast_select_fusion), calls=%async_computation | async-start | bytes 1179648 | tf_op jit(solution)/shard_map/all_to_all | solution.py:147

commit v6 on v3

--- a/solution.py
+++ b/solution.py
@@ -8,6 +8,9 @@
 from jax.sharding import PartitionSpec as P
 
 STEPS = 3
+
+
+LEVEL_BLOCK = 8
 
 
 def stencil_kernel(step, emit, *refs):
@@ -23,18 +26,13 @@
     if emit:
         top_ref, bottom_ref, first_ref, last_ref = refs[:4]
         refs = refs[4:]
-    new_scr, row_scr = refs
+    new_scr, row_scr, halo_scr, side_scr = refs
 
     count, levels, rows, cols = q_ref.shape
     planes = levels * rows
+    block = LEVEL_BLOCK if levels % LEVEL_BLOCK == 0 else 1
 
     if step:
-        cx = wind_ref[0].astype(jnp.float32)
-        cy = wind_ref[1].astype(jnp.float32)
-        half_x = 0.5 * cx
-        full_x = half_x * cx
-        half_y = 0.5 * cy
-        full_y = half_y * cy
         strips = jnp.zeros((cols, count * planes), jnp.float32)
         strips = jnp.where(
             lax.broadcasted_iota(jnp.int32, strips.shape, 0) == 0,
@@ -45,34 +43,48 @@
                 strips,
             ),
         )
-        columns = strips.T
-        sub = lax.broadcasted_iota(jnp.int32, (levels, rows, cols), 1)
-        lane = lax.broadcasted_iota(jnp.int32, (levels, rows, cols), 2)
+        side_scr[...] = strips.T
+        halo_scr[0] = north_ref[...].astype(jnp.float32)
+        halo_scr[1] = south_ref[...].astype(jnp.float32)
+        sub = lax.broadcasted_iota(jnp.int32, (block, rows, cols), 1)
+        lane = lax.broadcasted_iota(jnp.int32, (block, rows, cols), 2)
 
     for field in range(count):
-        centre = q_ref[field].astype(jnp.float32)
         if step:
-            row_scr[:, rows - 1, :] = north_ref[field].astype(jnp.float32)
-            north_halo = row_scr[...]
-            row_scr[:, 0, :] = south_ref[field].astype(jnp.float32)
-            south_halo = row_scr[...]
-            north = jnp.where(sub == rows - 1, north_halo, pltpu.roll(centre, rows - 1, 1))
-            south = jnp.where(sub == 0, south_halo, pltpu.roll(centre, 1, 1))
-            side = columns[field * planes:(field + 1) * planes].reshape(levels, rows, cols)
-            side = pltpu.roll(side, cols - 1, 2)
-            east = jnp.where(lane == cols - 1, side, pltpu.roll(centre, cols - 1, 2))
-            west = jnp.where(lane == 0, side, pltpu.roll(centre, 1, 2))
-            out = centre - half_x * (north - south) + full_x * (north - 2.0 * centre + south)
-            out = out - half_y * (east - west) + full_y * (east - 2.0 * centre + west)
-            new = out.astype(jnp.bfloat16)
-            out_ref[field] = new
-        else:
-            new = q_ref[field]
+            def body(index, carry):
+                first = pl.multiple_of(index * block, block)
+                levels_here = pl.ds(first, block)
+                centre = q_ref[field, levels_here].astype(jnp.float32)
+                cx = wind_ref[0, levels_here].astype(jnp.float32)
+                cy = wind_ref[1, levels_here].astype(jnp.float32)
+                half_x = 0.5 * cx
+                full_x = half_x * cx
+                half_y = 0.5 * cy
+                full_y = half_y * cy
+                row_scr[:, rows - 1, :] = halo_scr[0, field, levels_here]
+                north = jnp.where(sub == rows - 1, row_scr[...], pltpu.roll(centre, rows - 1, 1))
+                row_scr[:, 0, :] = halo_scr[1, field, levels_here]
+                south = jnp.where(sub == 0, row_scr[...], pltpu.roll(centre, 1, 1))
+                offset = pl.multiple_of(field * planes + first * rows, 8)
+                side = side_scr[pl.ds(offset, block * rows)].reshape(block, rows, cols)
+                side = pltpu.roll(side, cols - 1, 2)
+                east = jnp.where(lane == cols - 1, side, pltpu.roll(centre, cols - 1, 2))
+                west = jnp.where(lane == 0, side, pltpu.roll(centre, 1, 2))
+                out = centre - half_x * (north - south) + full_x * (north - 2.0 * centre + south)
+                out = out - half_y * (east - west) + full_y * (east - 2.0 * centre + west)
+                new = out.astype(jnp.bfloat16)
+                out_ref[field, levels_here] = new
+                if emit:
+                    new_scr[levels_here] = new.astype(jnp.float32)
+                return carry
+
+            lax.fori_loop(0, levels // block, body, 0)
+        elif emit:
+            new_scr[...] = q_ref[field].astype(jnp.float32)
         if emit:
-            new_scr[...] = new.astype(jnp.float32)
             top_ref[field] = new_scr[:, 0, :].astype(top_ref.dtype)
             bottom_ref[field] = new_scr[:, rows - 1, :].astype(bottom_ref.dtype)
-            flat = new.astype(jnp.float32).reshape(planes, cols).astype(jnp.bfloat16)
+            flat = new_scr[...].reshape(planes, cols).astype(jnp.bfloat16)
             pick = lax.broadcasted_iota(jnp.int32, (8, cols), 1)
             which = lax.broadcasted_iota(jnp.int32, (8, cols), 0)
             onehot = jnp.where(
@@ -106,7 +118,9 @@
         out_specs=tuple([vmem] * len(outs)),
         scratch_shapes=[
             pltpu.VMEM((levels, rows, cols), jnp.float32),
-            pltpu.VMEM((levels, rows, cols), jnp.float32),
+            pltpu.VMEM((LEVEL_BLOCK, rows, cols), jnp.float32),
+            pltpu.VMEM((2, count, levels, cols), jnp.float32),
+            pltpu.VMEM((count * planes, cols), jnp.float32),
         ],
     )(q, *extra)
 

time: 70.7 us -> 77.7 us (1.099)
  Pallas kernels: 15.2 us -> 22.1 us
    pallas_call x4, Pallas kernels: 15.2 us -> 22.1 us  [stencil_call(): pl.pallas_call(functools.partial(stencil_kernel, step, emit), out_shape=t...]
  transfers between devices with their start and end apart: 13 -> 13, of which waited for: 7 -> 7; matrix products, arithmetic and copies ran while one was open for 3% -> 2% of each run, Pallas kernels for 0% -> 0%
where the time goes in v6:
time: 77.7 us; the launch traced here: 77.3 us
  waiting for transfers between devices  27.7 us (36%)
  Pallas kernels  22.1 us (28%)
  starting transfers between devices  18.8 us (24%)
  local copies, waits for them, and re-layouts  4.6 us (6%)
  other arithmetic  2.78 us (4%)
  between operations  0.78 us (1%)
    pallas_call x4, Pallas kernels, stencil_call(): pl.pallas_call(functools.partial(stencil_kernel, step, emit), out_shape=t...  22.1 us
    all_to_all x1, waiting for transfers between devices, per_device(): lax.all_to_all(ordered, 'tile', split_axis=2, concat_axis=2, tiled=True)  15.9 us
    ppermute x3, starting transfers between devices, exchange(): lax.ppermute(first, 'tile', [(i, (i - 1) % tile) for i in range(tile)])  8.71 us
    ppermute x3, waiting for transfers between devices, exchange(): lax.ppermute(last, 'tile', [(i, (i + 1) % tile) for i in range(tile)])  7.04 us
    ppermute x3, waiting for transfers between devices, exchange(): lax.ppermute(bottom, 'sec', [(i, (i + 1) % sec) for i in range(sec)])  4.73 us
    ppermute x3, starting transfers between devices, exchange(): north = lax.ppermute(top, 'sec', [(i, (i - 1) % sec) for i in range(sec)])  3.69 us
    all_to_all x1, starting transfers between devices, per_device(): lax.all_to_all(ordered, 'tile', split_axis=2, concat_axis=2, tiled=True)  3.54 us
    ppermute x3, starting transfers between devices, exchange(): lax.ppermute(bottom, 'sec', [(i, (i + 1) % sec) for i in range(sec)])  2.81 us
  transfers between devices with their start and end apart: 13, of which 7 were waited for; matrix products, arithmetic and copies ran while one was open for 2% of the time, Pallas kernels for 0%

profile of v6, /device:TPU:0, one launch (start us, length us, event | category | flops | bytes accessed | tf_op | source)
XLA Modules:
  0.0 77.3 jit_solution(8726952970187965719)
XLA Ops:
  0.0 0.0 copy-start
  0.0 2.3 %shard_map.64 = (bf16[4,72,128]{2,1,0:T(8,128)(2,1)}, bf16[4,72,128]{2,1,0:T(8,128)(2,1)}, bf16[1,2304]{1,0:T(2,128)(2,1)}, bf16[1,2304]{1,0:T(2,128)(2,1)}) custom-call(bf16[4,72,8,128]{3,2,1,0:T(8,128)(2,1)} %refs_0_.3), custom_call_target="tpu_custom_call" | custom-call | tf_op jit(solution)/shard_map/pallas_call | solution.py:114
  2.3 4.5 %collective-permute-start.2 = (bf16[1,2304]{1,0:T(2,128)(2,1)}, bf16[1,2304]{1,0:T(2,128)(2,1)S(1)}, u32[]{:S(2)}, u32[]{:S(2)}) collective-permute-start(bf16[1,2304]{1,0:T(2,128)(2,1)} %get-tuple-element.23), channel_id=1, source_target_pairs={{0,7},{1,0},{2,1},{3,2},{4,3},{5,4},{6,5},{7,6},{8,15},{9,8},{10,9... | collective-permute-start | bytes 13832 | tf_op jit(solution)/shard_map/ppermute | solution.py:133
  6.8 0.0 collective-permute-start.3
  6.8 2.4 %collective-permute-start = (bf16[4,72,128]{2,1,0:T(8,128)(2,1)}, bf16[4,72,128]{2,1,0:T(8,128)(2,1)S(1)}, u32[]{:S(2)}, u32[]{:S(2)}) collective-permute-start(bf16[4,72,128]{2,1,0:T(8,128)(2,1)} %get-tuple-element.21), channel_id=1, source_target_pairs={{0,24},{8,0},{16,8},{24,16},{1,25},{9,1},{17,9},{25,17},{2,26},{10... | collective-permute-start | bytes 221192 | tf_op jit(solution)/shard_map/ppermute | solution.py:131
  9.3 0.0 collective-permute-start.1
  9.3 1.7 %sort.17 = (s32[8]{0:T(128)}, s32[8]{0:T(128)S(1)}) sort(s32[8]{0:T(128)} %bitcast.22, s32[8]{0:T(128)S(1)} %iota.9), dimensions={0}, to_apply=%region_0.0 | sort | flops 24 | bytes 128 | tf_op jit(solution)/shard_map/jit(argsort)/sort | solution.py:146
  10.9 0.0 collective-permute-done.2.refs_4_
  10.9 0.0 copy-start.10
  11.0 0.9 %collective-permute-done.3.refs_5_ = bf16[1,2304]{1,0:T(2,128)(2,1)S(1)} collective-permute-done((bf16[1,2304]{1,0:T(2,128)(2,1)}, bf16[1,2304]{1,0:T(2,128)(2,1)S(1)}, u32[]{:S(2)}, u32[]{:S(2)}) %collective-permute-start.3) | collective-permute-done | bytes 4640 | tf_op jit(solution)/shard_map/ppermute | solution.py:134
  11.9 0.0 collective-permute-done.refs_2_
  12.0 2.8 %collective-permute-done.1.refs_3_ = bf16[4,72,128]{2,1,0:T(8,128)(2,1)S(1)} collective-permute-done((bf16[4,72,128]{2,1,0:T(8,128)(2,1)}, bf16[4,72,128]{2,1,0:T(8,128)(2,1)S(1)}, u32[]{:S(2)}, u32[]{:S(2)}) %collective-permute-start.1) | collective-permute-done | bytes 73760 | tf_op jit(solution)/shard_map/ppermute | solution.py:132
  14.7 0.0 copy-done.10
  14.7 0.0 copy-done.11
  14.7 0.0 copy-done.2
  14.7 0.0 copy-start.3
  14.7 0.6 copy-done.3
  15.3 6.9 %shard_map.65 = (bf16[4,72,8,128]{3,2,1,0:T(8,128)(2,1)}, bf16[4,72,128]{2,1,0:T(8,128)(2,1)}, bf16[4,72,128]{2,1,0:T(8,128)(2,1)}, bf16[1,2304]{1,0:T(2,128)(2,1)}, bf16[1,2304]{1,0:T(2,128)(2,1)}) custom-call(bf16[4,72,8,128]{3,2,1,0:T(8,128)(2,1)} %refs_0_.3, bf16[2,72,8,128]{3,2,1,0:T(8,128)(2,1)} %refs_1_.5, bf16[4,72,128]{2,1,0:T(8,128)(2,1)} %copy-done.2, ...), custom_call_target="tpu_custom_call" | custom-call | tf_op jit(solution)/shard_map/pallas_call | solution.py:114
  22.3 2.1 %collective-permute-start.6 = (bf16[1,2304]{1,0:T(2,128)(2,1)}, bf16[1,2304]{1,0:T(2,128)(2,1)S(1)}, u32[]{:S(2)}, u32[]{:S(2)}) collective-permute-start(bf16[1,2304]{1,0:T(2,128)(2,1)} %get-tuple-element.28), channel_id=1, source_target_pairs={{0,7},{1,0},{2,1},{3,2},{4,3},{5,4},{6,5},{7,6},{8,15},{9,8},{10,9... | collective-permute-start | bytes 13832 | tf_op jit(solution)/shard_map/ppermute | solution.py:133
  24.4 0.0 collective-permute-start.7
  24.4 0.9 %collective-permute-start.4 = (bf16[4,72,128]{2,1,0:T(8,128)(2,1)}, bf16[4,72,128]{2,1,0:T(8,128)(2,1)S(1)}, u32[]{:S(2)}, u32[]{:S(2)}) collective-permute-start(bf16[4,72,128]{2,1,0:T(8,128)(2,1)} %get-tuple-element.26), channel_id=1, source_target_pairs={{0,24},{8,0},{16,8},{24,16},{1,25},{9,1},{17,9},{25,17},{2,26},{10... | collective-permute-start | bytes 221192 | tf_op jit(solution)/shard_map/ppermute | solution.py:131
  25.3 1.1 %collective-permute-start.5 = (bf16[4,72,128]{2,1,0:T(8,128)(2,1)}, bf16[4,72,128]{2,1,0:T(8,128)(2,1)S(1)}, u32[]{:S(2)}, u32[]{:S(2)}) collective-permute-start(bf16[4,72,128]{2,1,0:T(8,128)(2,1)} %get-tuple-element.27), channel_id=1, source_target_pairs={{0,8},{8,16},{16,24},{24,0},{1,9},{9,17},{17,25},{25,1},{2,10},{10... | collective-permute-start | bytes 221192 | tf_op jit(solution)/shard_map/ppermute | solution.py:132
  26.4 0.0 collective-permute-done.6.refs_4_
  26.4 3.1 %collective-permute-done.7.refs_5_ = bf16[1,2304]{1,0:T(2,128)(2,1)S(1)} collective-permute-done((bf16[1,2304]{1,0:T(2,128)(2,1)}, bf16[1,2304]{1,0:T(2,128)(2,1)S(1)}, u32[]{:S(2)}, u32[]{:S(2)}) %collective-permute-start.7) | collective-permute-done | bytes 4640 | tf_op jit(solution)/shard_map/ppermute | solution.py:134
  29.5 0.0 collective-permute-done.4.refs_2_
  29.5 1.3 %collective-permute-done.5.refs_3_ = bf16[4,72,128]{2,1,0:T(8,128)(2,1)S(1)} collective-permute-done((bf16[4,72,128]{2,1,0:T(8,128)(2,1)}, bf16[4,72,128]{2,1,0:T(8,128)(2,1)S(1)}, u32[]{:S(2)}, u32[]{:S(2)}) %collective-permute-start.5) | collective-permute-done | bytes 73760 | tf_op jit(solution)/shard_map/ppermute | solution.py:132
  30.7 0.6 copy-done.5
  31.4 6.9 %shard_map.66 = (bf16[4,72,8,128]{3,2,1,0:T(8,128)(2,1)}, bf16[4,72,128]{2,1,0:T(8,128)(2,1)}, bf16[4,72,128]{2,1,0:T(8,128)(2,1)}, bf16[1,2304]{1,0:T(2,128)(2,1)}, bf16[1,2304]{1,0:T(2,128)(2,1)}) custom-call(bf16[4,72,8,128]{3,2,1,0:T(8,128)(2,1)} %get-tuple-element.25.refs_0_, bf16[2,72,8,128]{3,2,1,0:T(8,128)(2,1)} %refs_1_.5, ...), custom_call_target="tpu_custom_call" | custom-call | tf_op jit(solution)/shard_map/pallas_call | solution.py:114
  38.3 2.1 %collective-permute-start.10 = (bf16[1,2304]{1,0:T(2,128)(2,1)}, bf16[1,2304]{1,0:T(2,128)(2,1)S(1)}, u32[]{:S(2)}, u32[]{:S(2)}) collective-permute-start(bf16[1,2304]{1,0:T(2,128)(2,1)} %get-tuple-element.33), channel_id=1, source_target_pairs={{0,7},{1,0},{2,1},{3,2},{4,3},{5,4},{6,5},{7,6},{8,15},{9,8},{10,9... | collective-permute-start | bytes 13832 | tf_op jit(solution)/shard_map/ppermute | solution.py:133
  40.4 0.0 collective-permute-start.11
  40.4 0.3 collective-permute-start.8
  40.7 1.7 %collective-permute-start.9 = (bf16[4,72,128]{2,1,0:T(8,128)(2,1)}, bf16[4,72,128]{2,1,0:T(8,128)(2,1)S(1)}, u32[]{:S(2)}, u32[]{:S(2)}) collective-permute-start(bf16[4,72,128]{2,1,0:T(8,128)(2,1)} %get-tuple-element.32), channel_id=1, source_target_pairs={{0,8},{8,16},{16,24},{24,0},{1,9},{9,17},{17,25},{25,1},{2,10},{10... | collective-permute-start | bytes 221192 | tf_op jit(solution)/shard_map/ppermute | solution.py:132
  42.4 0.0 collective-permute-done.10.refs_4_
  42.4 3.0 %collective-permute-done.11.refs_5_ = bf16[1,2304]{1,0:T(2,128)(2,1)S(1)} collective-permute-done((bf16[1,2304]{1,0:T(2,128)(2,1)}, bf16[1,2304]{1,0:T(2,128)(2,1)S(1)}, u32[]{:S(2)}, u32[]{:S(2)}) %collective-permute-start.11) | collective-permute-done | bytes 4640 | tf_op jit(solution)/shard_map/ppermute | solution.py:134
  45.5 0.0 collective-permute-done.8.refs_2_
  45.5 0.7 collective-permute-done.9.refs_3_
  46.2 0.6 copy-done.7
  46.8 6.0 %shard_map.67 = bf16[4,72,8,128]{3,2,1,0:T(8,128)(2,1)} custom-call(bf16[4,72,8,128]{3,2,1,0:T(8,128)(2,1)} %get-tuple-element.30.refs_0_, bf16[2,72,8,128]{3,2,1,0:T(8,128)(2,1)} %refs_1_.5, bf16[4,72,128]{2,1,0:T(8,128)(2,1)} %copy-done.6, bf16[4,72,128]{2,1,0:T(8,128)(2,1)} %copy-done.7, bf16[1,2304]{1,0:T(2,128)(2,1)} %copy-done.8, bf16[1,2304]{1,0:T(2,128)(2,1)} %copy-done.9), custom_call_target="tpu_custom_call" | custom-call | tf_op jit(solution)/shard_map/pallas_call | solution.py:114
  52.8 1.1 %copy.12 = bf16[4,72,8,128]{3,1,2,0:T(8,128)(2,1)S(1)} copy(bf16[4,72,8,128]{3,2,1,0:T(8,128)(2,1)} %shard_map.67) | data formatting | bytes 1179648 | tf_op jit(solution)/shard_map/pallas_call | solution.py:114
  54.0 0.7 gather_fusion
  54.6 0.0 copy-start.1
  54.7 0.9 %select_bitcast_fusion = bf16[4,72,8,128]{3,1,0,2:T(8,128)(2,1)} fusion(bf16[8,4,72,128]{3,2,1,0:T(8,128)(2,1)S(1)} %gather_fusion, pred[8]{0:T(512)(128)(4,1)S(1)} %compare_and_fusion), kind=kLoop, calls=%fused_computation.7 | loop fusion | flops 294912 | bytes 1179656 | tf_op jit(solution)/shard_map/jit(_take)/select_n | solution.py:148
  55.6 3.5 %all-to-all-start = ((bf16[4,72,8,128]{3,1,0,2:T(8,128)(2,1)}), bf16[4,72,8,128]{3,1,0,2:T(8,128)(2,1)S(1)}, u32[]{:S(2)}, u32[]{:S(2)}) async-start(bf16[4,72,8,128]{3,1,0,2:T(8,128)(2,1)} %select_bitcast_fusion), calls=%async_computation | async-start | bytes 1179648 | tf_op jit(solution)/shard_map/all_to_all | solution.py:149
  59.8 0.1 select_reduce_fusion
  60.0 15.9 %all-to-all-done = bf16[4,72,8,128]{3,1,0,2:T(8,128)(2,1)S(1)} async-done(((bf16[4,72,8,128]{3,1,0,2:T(8,128)(2,1)}), bf16[4,72,8,128]{3,1,0,2:T(8,128)(2,1)S(1)}, u32[]{:S(2)}, u32[]{:S(2)}) %all-to-all-start) | async-done | bytes 589856 | tf_op jit(solution)/shard_map/all_to_all | solution.py:149
  75.8 0.3 fusion.3
  76.1 0.3 fusion.1
  76.4 0.9 %copy.14 = bf16[4,72,8,128]{3,2,1,0:T(8,128)(2,1)} copy(bf16[4,72,8,128]{3,1,2,0:T(8,128)(2,1)S(1)} %fusion.1) | data formatting | bytes 1179648 | tf_op jit(solution)/shard_map/convert_element_type | solution.py:156
  (23 shorter events, 0.1 us)
Async XLA Ops:
  0.0 75.8 %copy-start = (bf16[1,72,72]{2,1,0:T(8,128)(2,1)S(1)}, bf16[1,72,72]{2,1,0:T(8,128)(2,1)}, u32[]{:S(2)}) copy-start(bf16[1,72,72]{2,1,0:T(8,128)(2,1)} %param.9) | copy-start | bytes 31108
  2.3 8.6 %collective-permute-start.2 = (bf16[1,2304]{1,0:T(2,128)(2,1)}, bf16[1,2304]{1,0:T(2,128)(2,1)S(1)}, u32[]{:S(2)}, u32[]{:S(2)}) collective-permute-start(bf16[1,2304]{1,0:T(2,128)(2,1)} %get-tuple-element.23), channel_id=1, source_target_pairs={{0,7},{1,0},{2,1},{3,2},{4,3},{5,4},{6,5},{7,6},{8,15},{9,8},{10,9... | collective-permute-start | bytes 13832 | tf_op jit(solution)/shard_map/ppermute | solution.py:133
  6.8 5.1 %collective-permute-start.3 = (bf16[1,2304]{1,0:T(2,128)(2,1)}, bf16[1,2304]{1,0:T(2,128)(2,1)S(1)}, u32[]{:S(2)}, u32[]{:S(2)}) collective-permute-start(bf16[1,2304]{1,0:T(2,128)(2,1)} %get-tuple-element.24), channel_id=1, source_target_pairs={{0,1},{1,2},{2,3},{3,4},{4,5},{5,6},{6,7},{7,0},{8,9},{9,10},{10,1... | collective-permute-start | bytes 13832 | tf_op jit(solution)/shard_map/ppermute | solution.py:134
  6.8 5.1 %collective-permute-start = (bf16[4,72,128]{2,1,0:T(8,128)(2,1)}, bf16[4,72,128]{2,1,0:T(8,128)(2,1)S(1)}, u32[]{:S(2)}, u32[]{:S(2)}) collective-permute-start(bf16[4,72,128]{2,1,0:T(8,128)(2,1)} %get-tuple-element.21), channel_id=1, source_target_pairs={{0,24},{8,0},{16,8},{24,16},{1,25},{9,1},{17,9},{25,17},{2,26},{10... | collective-permute-start | bytes 221192 | tf_op jit(solution)/shard_map/ppermute | solution.py:131
  9.3 5.5 %collective-permute-start.1 = (bf16[4,72,128]{2,1,0:T(8,128)(2,1)}, bf16[4,72,128]{2,1,0:T(8,128)(2,1)S(1)}, u32[]{:S(2)}, u32[]{:S(2)}) collective-permute-start(bf16[4,72,128]{2,1,0:T(8,128)(2,1)} %get-tuple-element.22), channel_id=1, source_target_pairs={{0,8},{8,16},{16,24},{24,0},{1,9},{9,17},{17,25},{25,1},{2,10},{10... | collective-permute-start | bytes 221192 | tf_op jit(solution)/shard_map/ppermute | solution.py:132
  10.9 3.8 %copy-start.10 = (bf16[1,2304]{1,0:T(2,128)(2,1)}, bf16[1,2304]{1,0:T(2,128)(2,1)S(1)}, u32[]{:S(2)}) copy-start(bf16[1,2304]{1,0:T(2,128)(2,1)S(1)} %collective-permute-done.2.refs_4_) | copy-start | bytes 13828
  11.9 2.8 %copy-start.11 = (bf16[1,2304]{1,0:T(2,128)(2,1)}, bf16[1,2304]{1,0:T(2,128)(2,1)S(1)}, u32[]{:S(2)}) copy-start(bf16[1,2304]{1,0:T(2,128)(2,1)S(1)} %collective-permute-done.3.refs_5_) | copy-start | bytes 13828
  12.0 2.8 %copy-start.2 = (bf16[4,72,128]{2,1,0:T(8,128)(2,1)}, bf16[4,72,128]{2,1,0:T(8,128)(2,1)S(1)}, u32[]{:S(2)}) copy-start(bf16[4,72,128]{2,1,0:T(8,128)(2,1)S(1)} %collective-permute-done.refs_2_) | copy-start | bytes 221188
  14.7 0.6 copy-start.3
  22.3 4.1 %collective-permute-start.6 = (bf16[1,2304]{1,0:T(2,128)(2,1)}, bf16[1,2304]{1,0:T(2,128)(2,1)S(1)}, u32[]{:S(2)}, u32[]{:S(2)}) collective-permute-start(bf16[1,2304]{1,0:T(2,128)(2,1)} %get-tuple-element.28), channel_id=1, source_target_pairs={{0,7},{1,0},{2,1},{3,2},{4,3},{5,4},{6,5},{7,6},{8,15},{9,8},{10,9... | collective-permute-start | bytes 13832 | tf_op jit(solution)/shard_map/ppermute | solution.py:133
  24.4 5.1 %collective-permute-start.7 = (bf16[1,2304]{1,0:T(2,128)(2,1)}, bf16[1,2304]{1,0:T(2,128)(2,1)S(1)}, u32[]{:S(2)}, u32[]{:S(2)}) collective-permute-start(bf16[1,2304]{1,0:T(2,128)(2,1)} %get-tuple-element.29), channel_id=1, source_target_pairs={{0,1},{1,2},{2,3},{3,4},{4,5},{5,6},{6,7},{7,0},{8,9},{9,10},{10,1... | collective-permute-start | bytes 13832 | tf_op jit(solution)/shard_map/ppermute | solution.py:134
  24.4 5.1 %collective-permute-start.4 = (bf16[4,72,128]{2,1,0:T(8,128)(2,1)}, bf16[4,72,128]{2,1,0:T(8,128)(2,1)S(1)}, u32[]{:S(2)}, u32[]{:S(2)}) collective-permute-start(bf16[4,72,128]{2,1,0:T(8,128)(2,1)} %get-tuple-element.26), channel_id=1, source_target_pairs={{0,24},{8,0},{16,8},{24,16},{1,25},{9,1},{17,9},{25,17},{2,26},{10... | collective-permute-start | bytes 221192 | tf_op jit(solution)/shard_map/ppermute | solution.py:131
  25.3 5.5 %collective-permute-start.5 = (bf16[4,72,128]{2,1,0:T(8,128)(2,1)}, bf16[4,72,128]{2,1,0:T(8,128)(2,1)S(1)}, u32[]{:S(2)}, u32[]{:S(2)}) collective-permute-start(bf16[4,72,128]{2,1,0:T(8,128)(2,1)} %get-tuple-element.27), channel_id=1, source_target_pairs={{0,8},{8,16},{16,24},{24,0},{1,9},{9,17},{17,25},{25,1},{2,10},{10... | collective-permute-start | bytes 221192 | tf_op jit(solution)/shard_map/ppermute | solution.py:132
  26.4 4.3 %copy-start.12 = (bf16[1,2304]{1,0:T(2,128)(2,1)}, bf16[1,2304]{1,0:T(2,128)(2,1)S(1)}, u32[]{:S(2)}) copy-start(bf16[1,2304]{1,0:T(2,128)(2,1)S(1)} %collective-permute-done.6.refs_4_) | copy-start | bytes 13828
  29.5 1.3 %copy-start.13 = (bf16[1,2304]{1,0:T(2,128)(2,1)}, bf16[1,2304]{1,0:T(2,128)(2,1)S(1)}, u32[]{:S(2)}) copy-start(bf16[1,2304]{1,0:T(2,128)(2,1)S(1)} %collective-permute-done.7.refs_5_) | copy-start | bytes 13828
  29.5 1.3 %copy-start.4 = (bf16[4,72,128]{2,1,0:T(8,128)(2,1)}, bf16[4,72,128]{2,1,0:T(8,128)(2,1)S(1)}, u32[]{:S(2)}) copy-start(bf16[4,72,128]{2,1,0:T(8,128)(2,1)S(1)} %collective-permute-done.4.refs_2_) | copy-start | bytes 221188
  30.7 0.6 copy-start.5
  38.3 4.2 %collective-permute-start.10 = (bf16[1,2304]{1,0:T(2,128)(2,1)}, bf16[1,2304]{1,0:T(2,128)(2,1)S(1)}, u32[]{:S(2)}, u32[]{:S(2)}) collective-permute-start(bf16[1,2304]{1,0:T(2,128)(2,1)} %get-tuple-element.33), channel_id=1, source_target_pairs={{0,7},{1,0},{2,1},{3,2},{4,3},{5,4},{6,5},{7,6},{8,15},{9,8},{10,9... | collective-permute-start | bytes 13832 | tf_op jit(solution)/shard_map/ppermute | solution.py:133
  40.4 5.1 %collective-permute-start.11 = (bf16[1,2304]{1,0:T(2,128)(2,1)}, bf16[1,2304]{1,0:T(2,128)(2,1)S(1)}, u32[]{:S(2)}, u32[]{:S(2)}) collective-permute-start(bf16[1,2304]{1,0:T(2,128)(2,1)} %get-tuple-element.34), channel_id=1, source_target_pairs={{0,1},{1,2},{2,3},{3,4},{4,5},{5,6},{6,7},{7,0},{8,9},{9,10},{10,1... | collective-permute-start | bytes 13832 | tf_op jit(solution)/shard_map/ppermute | solution.py:134
  40.4 5.1 %collective-permute-start.8 = (bf16[4,72,128]{2,1,0:T(8,128)(2,1)}, bf16[4,72,128]{2,1,0:T(8,128)(2,1)S(1)}, u32[]{:S(2)}, u32[]{:S(2)}) collective-permute-start(bf16[4,72,128]{2,1,0:T(8,128)(2,1)} %get-tuple-element.31), channel_id=1, source_target_pairs={{0,24},{8,0},{16,8},{24,16},{1,25},{9,1},{17,9},{25,17},{2,26},{10... | collective-permute-start | bytes 221192 | tf_op jit(solution)/shard_map/ppermute | solution.py:131
  40.7 5.5 %collective-permute-start.9 = (bf16[4,72,128]{2,1,0:T(8,128)(2,1)}, bf16[4,72,128]{2,1,0:T(8,128)(2,1)S(1)}, u32[]{:S(2)}, u32[]{:S(2)}) collective-permute-start(bf16[4,72,128]{2,1,0:T(8,128)(2,1)} %get-tuple-element.32), channel_id=1, source_target_pairs={{0,8},{8,16},{16,24},{24,0},{1,9},{9,17},{17,25},{25,1},{2,10},{10... | collective-permute-start | bytes 221192 | tf_op jit(solution)/shard_map/ppermute | solution.py:132
  42.4 3.8 %copy-start.8 = (bf16[1,2304]{1,0:T(2,128)(2,1)}, bf16[1,2304]{1,0:T(2,128)(2,1)S(1)}, u32[]{:S(2)}) copy-start(bf16[1,2304]{1,0:T(2,128)(2,1)S(1)} %collective-permute-done.10.refs_4_) | copy-start | bytes 13828
  45.5 0.7 copy-start.9
  45.5 0.7 copy-start.6
  46.2 0.6 copy-start.7
  54.6 5.2 %copy-start.1 = (bf16[16,72,72]{2,1,0:T(8,128)(2,1)S(1)}, bf16[16,72,72]{2,1,0:T(8,128)(2,1)}, u32[]{:S(2)}) copy-start(bf16[16,72,72]{2,1,0:T(8,128)(2,1)} %param.11) | copy-start | bytes 497668
  55.6 20.2 %all-to-all-start = ((bf16[4,72,8,128]{3,1,0,2:T(8,128)(2,1)}), bf16[4,72,8,128]{3,1,0,2:T(8,128)(2,1)S(1)}, u32[]{:S(2)}, u32[]{:S(2)}) async-start(bf16[4,72,8,128]{3,1,0,2:T(8,128)(2,1)} %select_bitcast_fusion), calls=%async_computation | async-start | bytes 1179648 | tf_op jit(solution)/shard_map/all_to_all | solution.py:149

commit v7 on v6

--- a/solution.py
+++ b/solution.py
@@ -26,7 +26,7 @@
     if emit:
         top_ref, bottom_ref, first_ref, last_ref = refs[:4]
         refs = refs[4:]
-    new_scr, row_scr, halo_scr, side_scr = refs
+    new_scr, row_scr, halo_scr, side_scr, factor_scr = refs
 
     count, levels, rows, cols = q_ref.shape
     planes = levels * rows
@@ -48,24 +48,32 @@
         halo_scr[1] = south_ref[...].astype(jnp.float32)
         sub = lax.broadcasted_iota(jnp.int32, (block, rows, cols), 1)
         lane = lax.broadcasted_iota(jnp.int32, (block, rows, cols), 2)
+        for index in range(levels // block):
+            levels_here = pl.ds(index * block, block)
+            cx = wind_ref[0, levels_here].astype(jnp.float32)
+            cy = wind_ref[1, levels_here].astype(jnp.float32)
+            half_x = 0.5 * cx
+            half_y = 0.5 * cy
+            factor_scr[0, levels_here] = half_x
+            factor_scr[1, levels_here] = half_x * cx
+            factor_scr[2, levels_here] = half_y
+            factor_scr[3, levels_here] = half_y * cy
 
     for field in range(count):
         if step:
-            def body(index, carry):
-                first = pl.multiple_of(index * block, block)
+            for index in range(levels // block):
+                first = index * block
                 levels_here = pl.ds(first, block)
                 centre = q_ref[field, levels_here].astype(jnp.float32)
-                cx = wind_ref[0, levels_here].astype(jnp.float32)
-                cy = wind_ref[1, levels_here].astype(jnp.float32)
-                half_x = 0.5 * cx
-                full_x = half_x * cx
-                half_y = 0.5 * cy
-                full_y = half_y * cy
+                half_x = factor_scr[0, levels_here]
+                full_x = factor_scr[1, levels_here]
+                half_y = factor_scr[2, levels_here]
+                full_y = factor_scr[3, levels_here]
                 row_scr[:, rows - 1, :] = halo_scr[0, field, levels_here]
                 north = jnp.where(sub == rows - 1, row_scr[...], pltpu.roll(centre, rows - 1, 1))
                 row_scr[:, 0, :] = halo_scr[1, field, levels_here]
                 south = jnp.where(sub == 0, row_scr[...], pltpu.roll(centre, 1, 1))
-                offset = pl.multiple_of(field * planes + first * rows, 8)
+                offset = field * planes + first * rows
                 side = side_scr[pl.ds(offset, block * rows)].reshape(block, rows, cols)
                 side = pltpu.roll(side, cols - 1, 2)
                 east = jnp.where(lane == cols - 1, side, pltpu.roll(centre, cols - 1, 2))
@@ -76,9 +84,6 @@
                 out_ref[field, levels_here] = new
                 if emit:
                     new_scr[levels_here] = new.astype(jnp.float32)
-                return carry
-
-            lax.fori_loop(0, levels // block, body, 0)
         elif emit:
             new_scr[...] = q_ref[field].astype(jnp.float32)
         if emit:
@@ -121,6 +126,7 @@
             pltpu.VMEM((LEVEL_BLOCK, rows, cols), jnp.float32),
             pltpu.VMEM((2, count, levels, cols), jnp.float32),
             pltpu.VMEM((count * planes, cols), jnp.float32),
+            pltpu.VMEM((4, levels, rows, cols), jnp.float32),
         ],
     )(q, *extra)
 

time: 77.7 us -> 70.3 us (0.905)
  Pallas kernels: 22.1 us -> 14.8 us
    pallas_call x4, Pallas kernels: 22.1 us -> 14.8 us  [stencil_call(): pl.pallas_call(functools.partial(stencil_kernel, step, emit), out_shape=t...]
  transfers between devices with their start and end apart: 13 -> 13, of which waited for: 7 -> 7; matrix products, arithmetic and copies ran while one was open for 2% -> 3% of each run, Pallas kernels for 0% -> 0%
where the time goes in v7:
time: 70.3 us; the launch traced here: 70 us
  waiting for transfers between devices  27.7 us (39%)
  starting transfers between devices  18.8 us (27%)
  Pallas kernels  14.8 us (21%)
  local copies, waits for them, and re-layouts  4.59 us (7%)
  other arithmetic  2.78 us (4%)
  between operations  0.78 us (1%)
    all_to_all x1, waiting for transfers between devices, per_device(): lax.all_to_all(ordered, 'tile', split_axis=2, concat_axis=2, tiled=True)  15.9 us
    pallas_call x4, Pallas kernels, stencil_call(): pl.pallas_call(functools.partial(stencil_kernel, step, emit), out_shape=t...  14.8 us
    ppermute x3, starting transfers between devices, exchange(): lax.ppermute(first, 'tile', [(i, (i - 1) % tile) for i in range(tile)])  8.71 us
    ppermute x3, waiting for transfers between devices, exchange(): lax.ppermute(last, 'tile', [(i, (i + 1) % tile) for i in range(tile)])  7.04 us
    ppermute x3, waiting for transfers between devices, exchange(): lax.ppermute(bottom, 'sec', [(i, (i + 1) % sec) for i in range(sec)])  4.73 us
    ppermute x3, starting transfers between devices, exchange(): north = lax.ppermute(top, 'sec', [(i, (i - 1) % sec) for i in range(sec)])  3.69 us
    all_to_all x1, starting transfers between devices, per_device(): lax.all_to_all(ordered, 'tile', split_axis=2, concat_axis=2, tiled=True)  3.54 us
    ppermute x3, starting transfers between devices, exchange(): lax.ppermute(bottom, 'sec', [(i, (i + 1) % sec) for i in range(sec)])  2.81 us
  transfers between devices with their start and end apart: 13, of which 7 were waited for; matrix products, arithmetic and copies ran while one was open for 3% of the time, Pallas kernels for 0%

profile of v7, /device:TPU:0, one launch (start us, length us, event | category | flops | bytes accessed | tf_op | source)
XLA Modules:
  0.0 70.0 jit_solution(10973369970369919753)
XLA Ops:
  0.0 0.0 copy-start
  0.0 2.3 %shard_map.64 = (bf16[4,72,128]{2,1,0:T(8,128)(2,1)}, bf16[4,72,128]{2,1,0:T(8,128)(2,1)}, bf16[1,2304]{1,0:T(2,128)(2,1)}, bf16[1,2304]{1,0:T(2,128)(2,1)}) custom-call(bf16[4,72,8,128]{3,2,1,0:T(8,128)(2,1)} %refs_0_.3), custom_call_target="tpu_custom_call" | custom-call | tf_op jit(solution)/shard_map/pallas_call | solution.py:119
  2.3 4.5 %collective-permute-start.2 = (bf16[1,2304]{1,0:T(2,128)(2,1)}, bf16[1,2304]{1,0:T(2,128)(2,1)S(1)}, u32[]{:S(2)}, u32[]{:S(2)}) collective-permute-start(bf16[1,2304]{1,0:T(2,128)(2,1)} %get-tuple-element.23), channel_id=1, source_target_pairs={{0,7},{1,0},{2,1},{3,2},{4,3},{5,4},{6,5},{7,6},{8,15},{9,8},{10,9... | collective-permute-start | bytes 13832 | tf_op jit(solution)/shard_map/ppermute | solution.py:139
  6.8 0.0 collective-permute-start.3
  6.8 2.4 %collective-permute-start = (bf16[4,72,128]{2,1,0:T(8,128)(2,1)}, bf16[4,72,128]{2,1,0:T(8,128)(2,1)S(1)}, u32[]{:S(2)}, u32[]{:S(2)}) collective-permute-start(bf16[4,72,128]{2,1,0:T(8,128)(2,1)} %get-tuple-element.21), channel_id=1, source_target_pairs={{0,24},{8,0},{16,8},{24,16},{1,25},{9,1},{17,9},{25,17},{2,26},{10... | collective-permute-start | bytes 221192 | tf_op jit(solution)/shard_map/ppermute | solution.py:137
  9.3 0.0 collective-permute-start.1
  9.3 1.7 %sort.17 = (s32[8]{0:T(128)}, s32[8]{0:T(128)S(1)}) sort(s32[8]{0:T(128)} %bitcast.22, s32[8]{0:T(128)S(1)} %iota.9), dimensions={0}, to_apply=%region_0.0 | sort | flops 24 | bytes 128 | tf_op jit(solution)/shard_map/jit(argsort)/sort | solution.py:152
  10.9 0.0 collective-permute-done.2.refs_4_
  10.9 0.0 copy-start.10
  11.0 0.9 %collective-permute-done.3.refs_5_ = bf16[1,2304]{1,0:T(2,128)(2,1)S(1)} collective-permute-done((bf16[1,2304]{1,0:T(2,128)(2,1)}, bf16[1,2304]{1,0:T(2,128)(2,1)S(1)}, u32[]{:S(2)}, u32[]{:S(2)}) %collective-permute-start.3) | collective-permute-done | bytes 4640 | tf_op jit(solution)/shard_map/ppermute | solution.py:140
  11.9 0.0 collective-permute-done.refs_2_
  12.0 2.8 %collective-permute-done.1.refs_3_ = bf16[4,72,128]{2,1,0:T(8,128)(2,1)S(1)} collective-permute-done((bf16[4,72,128]{2,1,0:T(8,128)(2,1)}, bf16[4,72,128]{2,1,0:T(8,128)(2,1)S(1)}, u32[]{:S(2)}, u32[]{:S(2)}) %collective-permute-start.1) | collective-permute-done | bytes 73760 | tf_op jit(solution)/shard_map/ppermute | solution.py:138
  14.7 0.0 copy-done.10
  14.7 0.0 copy-done.11
  14.7 0.0 copy-done.2
  14.7 0.6 copy-done.3
  15.3 4.3 %shard_map.65 = (bf16[4,72,8,128]{3,2,1,0:T(8,128)(2,1)}, bf16[4,72,128]{2,1,0:T(8,128)(2,1)}, bf16[4,72,128]{2,1,0:T(8,128)(2,1)}, bf16[1,2304]{1,0:T(2,128)(2,1)}, bf16[1,2304]{1,0:T(2,128)(2,1)}) custom-call(bf16[4,72,8,128]{3,2,1,0:T(8,128)(2,1)} %refs_0_.3, bf16[2,72,8,128]{3,2,1,0:T(8,128)(2,1)} %refs_1_.5, bf16[4,72,128]{2,1,0:T(8,128)(2,1)} %copy-done.2, ...), custom_call_target="tpu_custom_call" | custom-call | tf_op jit(solution)/shard_map/pallas_call | solution.py:119
  19.6 2.1 %collective-permute-start.6 = (bf16[1,2304]{1,0:T(2,128)(2,1)}, bf16[1,2304]{1,0:T(2,128)(2,1)S(1)}, u32[]{:S(2)}, u32[]{:S(2)}) collective-permute-start(bf16[1,2304]{1,0:T(2,128)(2,1)} %get-tuple-element.28), channel_id=1, source_target_pairs={{0,7},{1,0},{2,1},{3,2},{4,3},{5,4},{6,5},{7,6},{8,15},{9,8},{10,9... | collective-permute-start | bytes 13832 | tf_op jit(solution)/shard_map/ppermute | solution.py:139
  21.8 0.0 collective-permute-start.7
  21.8 0.9 %collective-permute-start.4 = (bf16[4,72,128]{2,1,0:T(8,128)(2,1)}, bf16[4,72,128]{2,1,0:T(8,128)(2,1)S(1)}, u32[]{:S(2)}, u32[]{:S(2)}) collective-permute-start(bf16[4,72,128]{2,1,0:T(8,128)(2,1)} %get-tuple-element.26), channel_id=1, source_target_pairs={{0,24},{8,0},{16,8},{24,16},{1,25},{9,1},{17,9},{25,17},{2,26},{10... | collective-permute-start | bytes 221192 | tf_op jit(solution)/shard_map/ppermute | solution.py:137
  22.7 1.1 %collective-permute-start.5 = (bf16[4,72,128]{2,1,0:T(8,128)(2,1)}, bf16[4,72,128]{2,1,0:T(8,128)(2,1)S(1)}, u32[]{:S(2)}, u32[]{:S(2)}) collective-permute-start(bf16[4,72,128]{2,1,0:T(8,128)(2,1)} %get-tuple-element.27), channel_id=1, source_target_pairs={{0,8},{8,16},{16,24},{24,0},{1,9},{9,17},{17,25},{25,1},{2,10},{10... | collective-permute-start | bytes 221192 | tf_op jit(solution)/shard_map/ppermute | solution.py:138
  23.8 0.0 collective-permute-done.6.refs_4_
  23.8 3.1 %collective-permute-done.7.refs_5_ = bf16[1,2304]{1,0:T(2,128)(2,1)S(1)} collective-permute-done((bf16[1,2304]{1,0:T(2,128)(2,1)}, bf16[1,2304]{1,0:T(2,128)(2,1)S(1)}, u32[]{:S(2)}, u32[]{:S(2)}) %collective-permute-start.7) | collective-permute-done | bytes 4640 | tf_op jit(solution)/shard_map/ppermute | solution.py:140
  26.9 0.0 collective-permute-done.4.refs_2_
  26.9 1.3 %collective-permute-done.5.refs_3_ = bf16[4,72,128]{2,1,0:T(8,128)(2,1)S(1)} collective-permute-done((bf16[4,72,128]{2,1,0:T(8,128)(2,1)}, bf16[4,72,128]{2,1,0:T(8,128)(2,1)S(1)}, u32[]{:S(2)}, u32[]{:S(2)}) %collective-permute-start.5) | collective-permute-done | bytes 73760 | tf_op jit(solution)/shard_map/ppermute | solution.py:138
  28.1 0.6 copy-done.5
  28.7 4.3 %shard_map.66 = (bf16[4,72,8,128]{3,2,1,0:T(8,128)(2,1)}, bf16[4,72,128]{2,1,0:T(8,128)(2,1)}, bf16[4,72,128]{2,1,0:T(8,128)(2,1)}, bf16[1,2304]{1,0:T(2,128)(2,1)}, bf16[1,2304]{1,0:T(2,128)(2,1)}) custom-call(bf16[4,72,8,128]{3,2,1,0:T(8,128)(2,1)} %get-tuple-element.25.refs_0_, bf16[2,72,8,128]{3,2,1,0:T(8,128)(2,1)} %refs_1_.5, ...), custom_call_target="tpu_custom_call" | custom-call | tf_op jit(solution)/shard_map/pallas_call | solution.py:119
  33.1 2.1 %collective-permute-start.10 = (bf16[1,2304]{1,0:T(2,128)(2,1)}, bf16[1,2304]{1,0:T(2,128)(2,1)S(1)}, u32[]{:S(2)}, u32[]{:S(2)}) collective-permute-start(bf16[1,2304]{1,0:T(2,128)(2,1)} %get-tuple-element.33), channel_id=1, source_target_pairs={{0,7},{1,0},{2,1},{3,2},{4,3},{5,4},{6,5},{7,6},{8,15},{9,8},{10,9... | collective-permute-start | bytes 13832 | tf_op jit(solution)/shard_map/ppermute | solution.py:139
  35.2 0.0 collective-permute-start.11
  35.2 0.3 collective-permute-start.8
  35.5 1.7 %collective-permute-start.9 = (bf16[4,72,128]{2,1,0:T(8,128)(2,1)}, bf16[4,72,128]{2,1,0:T(8,128)(2,1)S(1)}, u32[]{:S(2)}, u32[]{:S(2)}) collective-permute-start(bf16[4,72,128]{2,1,0:T(8,128)(2,1)} %get-tuple-element.32), channel_id=1, source_target_pairs={{0,8},{8,16},{16,24},{24,0},{1,9},{9,17},{17,25},{25,1},{2,10},{10... | collective-permute-start | bytes 221192 | tf_op jit(solution)/shard_map/ppermute | solution.py:138
  37.2 0.0 collective-permute-done.10.refs_4_
  37.2 0.0 copy-start.8
  37.2 3.0 %collective-permute-done.11.refs_5_ = bf16[1,2304]{1,0:T(2,128)(2,1)S(1)} collective-permute-done((bf16[1,2304]{1,0:T(2,128)(2,1)}, bf16[1,2304]{1,0:T(2,128)(2,1)S(1)}, u32[]{:S(2)}, u32[]{:S(2)}) %collective-permute-start.11) | collective-permute-done | bytes 4640 | tf_op jit(solution)/shard_map/ppermute | solution.py:140
  40.3 0.0 collective-permute-done.8.refs_2_
  40.3 0.7 %collective-permute-done.9.refs_3_ = bf16[4,72,128]{2,1,0:T(8,128)(2,1)S(1)} collective-permute-done((bf16[4,72,128]{2,1,0:T(8,128)(2,1)}, bf16[4,72,128]{2,1,0:T(8,128)(2,1)S(1)}, u32[]{:S(2)}, u32[]{:S(2)}) %collective-permute-start.9) | collective-permute-done | bytes 73760 | tf_op jit(solution)/shard_map/ppermute | solution.py:138
  41.0 0.6 copy-done.7
  41.6 3.8 %shard_map.67 = bf16[4,72,8,128]{3,2,1,0:T(8,128)(2,1)} custom-call(bf16[4,72,8,128]{3,2,1,0:T(8,128)(2,1)} %get-tuple-element.30.refs_0_, bf16[2,72,8,128]{3,2,1,0:T(8,128)(2,1)} %refs_1_.5, bf16[4,72,128]{2,1,0:T(8,128)(2,1)} %copy-done.6, bf16[4,72,128]{2,1,0:T(8,128)(2,1)} %copy-done.7, bf16[1,2304]{1,0:T(2,128)(2,1)} %copy-done.8, bf16[1,2304]{1,0:T(2,128)(2,1)} %copy-done.9), custom_call_target="tpu_custom_call" | custom-call | tf_op jit(solution)/shard_map/pallas_call | solution.py:119
  45.5 1.1 %copy.12 = bf16[4,72,8,128]{3,1,2,0:T(8,128)(2,1)S(1)} copy(bf16[4,72,8,128]{3,2,1,0:T(8,128)(2,1)} %shard_map.67) | data formatting | bytes 1179648 | tf_op jit(solution)/shard_map/pallas_call | solution.py:119
  46.6 0.7 gather_fusion
  47.3 0.0 copy-start.1
  47.3 0.9 %select_bitcast_fusion = bf16[4,72,8,128]{3,1,0,2:T(8,128)(2,1)} fusion(bf16[8,4,72,128]{3,2,1,0:T(8,128)(2,1)S(1)} %gather_fusion, pred[8]{0:T(512)(128)(4,1)S(1)} %compare_and_fusion), kind=kLoop, calls=%fused_computation.7 | loop fusion | flops 294912 | bytes 1179656 | tf_op jit(solution)/shard_map/jit(_take)/select_n | solution.py:154
  48.2 3.5 %all-to-all-start = ((bf16[4,72,8,128]{3,1,0,2:T(8,128)(2,1)}), bf16[4,72,8,128]{3,1,0,2:T(8,128)(2,1)S(1)}, u32[]{:S(2)}, u32[]{:S(2)}) async-start(bf16[4,72,8,128]{3,1,0,2:T(8,128)(2,1)} %select_bitcast_fusion), calls=%async_computation | async-start | bytes 1179648 | tf_op jit(solution)/shard_map/all_to_all | solution.py:155
  52.5 0.1 select_reduce_fusion
  52.6 15.9 %all-to-all-done = bf16[4,72,8,128]{3,1,0,2:T(8,128)(2,1)S(1)} async-done(((bf16[4,72,8,128]{3,1,0,2:T(8,128)(2,1)}), bf16[4,72,8,128]{3,1,0,2:T(8,128)(2,1)S(1)}, u32[]{:S(2)}, u32[]{:S(2)}) %all-to-all-start) | async-done | bytes 589856 | tf_op jit(solution)/shard_map/all_to_all | solution.py:155
  68.5 0.3 fusion.3
  68.8 0.3 fusion.1
  69.1 0.9 %copy.14 = bf16[4,72,8,128]{3,2,1,0:T(8,128)(2,1)} copy(bf16[4,72,8,128]{3,1,2,0:T(8,128)(2,1)S(1)} %fusion.1) | data formatting | bytes 1179648 | tf_op jit(solution)/shard_map/convert_element_type | solution.py:162
  (23 shorter events, 0.1 us)
Async XLA Ops:
  0.0 68.5 %copy-start = (bf16[1,72,72]{2,1,0:T(8,128)(2,1)S(1)}, bf16[1,72,72]{2,1,0:T(8,128)(2,1)}, u32[]{:S(2)}) copy-start(bf16[1,72,72]{2,1,0:T(8,128)(2,1)} %param.9) | copy-start | bytes 31108
  2.3 8.6 %collective-permute-start.2 = (bf16[1,2304]{1,0:T(2,128)(2,1)}, bf16[1,2304]{1,0:T(2,128)(2,1)S(1)}, u32[]{:S(2)}, u32[]{:S(2)}) collective-permute-start(bf16[1,2304]{1,0:T(2,128)(2,1)} %get-tuple-element.23), channel_id=1, source_target_pairs={{0,7},{1,0},{2,1},{3,2},{4,3},{5,4},{6,5},{7,6},{8,15},{9,8},{10,9... | collective-permute-start | bytes 13832 | tf_op jit(solution)/shard_map/ppermute | solution.py:139
  6.8 5.1 %collective-permute-start.3 = (bf16[1,2304]{1,0:T(2,128)(2,1)}, bf16[1,2304]{1,0:T(2,128)(2,1)S(1)}, u32[]{:S(2)}, u32[]{:S(2)}) collective-permute-start(bf16[1,2304]{1,0:T(2,128)(2,1)} %get-tuple-element.24), channel_id=1, source_target_pairs={{0,1},{1,2},{2,3},{3,4},{4,5},{5,6},{6,7},{7,0},{8,9},{9,10},{10,1... | collective-permute-start | bytes 13832 | tf_op jit(solution)/shard_map/ppermute | solution.py:140
  6.8 5.1 %collective-permute-start = (bf16[4,72,128]{2,1,0:T(8,128)(2,1)}, bf16[4,72,128]{2,1,0:T(8,128)(2,1)S(1)}, u32[]{:S(2)}, u32[]{:S(2)}) collective-permute-start(bf16[4,72,128]{2,1,0:T(8,128)(2,1)} %get-tuple-element.21), channel_id=1, source_target_pairs={{0,24},{8,0},{16,8},{24,16},{1,25},{9,1},{17,9},{25,17},{2,26},{10... | collective-permute-start | bytes 221192 | tf_op jit(solution)/shard_map/ppermute | solution.py:137
  9.3 5.5 %collective-permute-start.1 = (bf16[4,72,128]{2,1,0:T(8,128)(2,1)}, bf16[4,72,128]{2,1,0:T(8,128)(2,1)S(1)}, u32[]{:S(2)}, u32[]{:S(2)}) collective-permute-start(bf16[4,72,128]{2,1,0:T(8,128)(2,1)} %get-tuple-element.22), channel_id=1, source_target_pairs={{0,8},{8,16},{16,24},{24,0},{1,9},{9,17},{17,25},{25,1},{2,10},{10... | collective-permute-start | bytes 221192 | tf_op jit(solution)/shard_map/ppermute | solution.py:138
  10.9 3.8 %copy-start.10 = (bf16[1,2304]{1,0:T(2,128)(2,1)}, bf16[1,2304]{1,0:T(2,128)(2,1)S(1)}, u32[]{:S(2)}) copy-start(bf16[1,2304]{1,0:T(2,128)(2,1)S(1)} %collective-permute-done.2.refs_4_) | copy-start | bytes 13828
  11.9 2.8 %copy-start.11 = (bf16[1,2304]{1,0:T(2,128)(2,1)}, bf16[1,2304]{1,0:T(2,128)(2,1)S(1)}, u32[]{:S(2)}) copy-start(bf16[1,2304]{1,0:T(2,128)(2,1)S(1)} %collective-permute-done.3.refs_5_) | copy-start | bytes 13828
  12.0 2.8 %copy-start.2 = (bf16[4,72,128]{2,1,0:T(8,128)(2,1)}, bf16[4,72,128]{2,1,0:T(8,128)(2,1)S(1)}, u32[]{:S(2)}) copy-start(bf16[4,72,128]{2,1,0:T(8,128)(2,1)S(1)} %collective-permute-done.refs_2_) | copy-start | bytes 221188
  14.7 0.6 copy-start.3
  19.6 4.1 %collective-permute-start.6 = (bf16[1,2304]{1,0:T(2,128)(2,1)}, bf16[1,2304]{1,0:T(2,128)(2,1)S(1)}, u32[]{:S(2)}, u32[]{:S(2)}) collective-permute-start(bf16[1,2304]{1,0:T(2,128)(2,1)} %get-tuple-element.28), channel_id=1, source_target_pairs={{0,7},{1,0},{2,1},{3,2},{4,3},{5,4},{6,5},{7,6},{8,15},{9,8},{10,9... | collective-permute-start | bytes 13832 | tf_op jit(solution)/shard_map/ppermute | solution.py:139
  21.8 5.1 %collective-permute-start.7 = (bf16[1,2304]{1,0:T(2,128)(2,1)}, bf16[1,2304]{1,0:T(2,128)(2,1)S(1)}, u32[]{:S(2)}, u32[]{:S(2)}) collective-permute-start(bf16[1,2304]{1,0:T(2,128)(2,1)} %get-tuple-element.29), channel_id=1, source_target_pairs={{0,1},{1,2},{2,3},{3,4},{4,5},{5,6},{6,7},{7,0},{8,9},{9,10},{10,1... | collective-permute-start | bytes 13832 | tf_op jit(solution)/shard_map/ppermute | solution.py:140
  21.8 5.1 %collective-permute-start.4 = (bf16[4,72,128]{2,1,0:T(8,128)(2,1)}, bf16[4,72,128]{2,1,0:T(8,128)(2,1)S(1)}, u32[]{:S(2)}, u32[]{:S(2)}) collective-permute-start(bf16[4,72,128]{2,1,0:T(8,128)(2,1)} %get-tuple-element.26), channel_id=1, source_target_pairs={{0,24},{8,0},{16,8},{24,16},{1,25},{9,1},{17,9},{25,17},{2,26},{10... | collective-permute-start | bytes 221192 | tf_op jit(solution)/shard_map/ppermute | solution.py:137
  22.7 5.5 %collective-permute-start.5 = (bf16[4,72,128]{2,1,0:T(8,128)(2,1)}, bf16[4,72,128]{2,1,0:T(8,128)(2,1)S(1)}, u32[]{:S(2)}, u32[]{:S(2)}) collective-permute-start(bf16[4,72,128]{2,1,0:T(8,128)(2,1)} %get-tuple-element.27), channel_id=1, source_target_pairs={{0,8},{8,16},{16,24},{24,0},{1,9},{9,17},{17,25},{25,1},{2,10},{10... | collective-permute-start | bytes 221192 | tf_op jit(solution)/shard_map/ppermute | solution.py:138
  23.8 4.3 %copy-start.12 = (bf16[1,2304]{1,0:T(2,128)(2,1)}, bf16[1,2304]{1,0:T(2,128)(2,1)S(1)}, u32[]{:S(2)}) copy-start(bf16[1,2304]{1,0:T(2,128)(2,1)S(1)} %collective-permute-done.6.refs_4_) | copy-start | bytes 13828
  26.9 1.3 %copy-start.13 = (bf16[1,2304]{1,0:T(2,128)(2,1)}, bf16[1,2304]{1,0:T(2,128)(2,1)S(1)}, u32[]{:S(2)}) copy-start(bf16[1,2304]{1,0:T(2,128)(2,1)S(1)} %collective-permute-done.7.refs_5_) | copy-start | bytes 13828
  26.9 1.3 %copy-start.4 = (bf16[4,72,128]{2,1,0:T(8,128)(2,1)}, bf16[4,72,128]{2,1,0:T(8,128)(2,1)S(1)}, u32[]{:S(2)}) copy-start(bf16[4,72,128]{2,1,0:T(8,128)(2,1)S(1)} %collective-permute-done.4.refs_2_) | copy-start | bytes 221188
  28.1 0.6 copy-start.5
  33.1 4.2 %collective-permute-start.10 = (bf16[1,2304]{1,0:T(2,128)(2,1)}, bf16[1,2304]{1,0:T(2,128)(2,1)S(1)}, u32[]{:S(2)}, u32[]{:S(2)}) collective-permute-start(bf16[1,2304]{1,0:T(2,128)(2,1)} %get-tuple-element.33), channel_id=1, source_target_pairs={{0,7},{1,0},{2,1},{3,2},{4,3},{5,4},{6,5},{7,6},{8,15},{9,8},{10,9... | collective-permute-start | bytes 13832 | tf_op jit(solution)/shard_map/ppermute | solution.py:139
  35.2 5.1 %collective-permute-start.11 = (bf16[1,2304]{1,0:T(2,128)(2,1)}, bf16[1,2304]{1,0:T(2,128)(2,1)S(1)}, u32[]{:S(2)}, u32[]{:S(2)}) collective-permute-start(bf16[1,2304]{1,0:T(2,128)(2,1)} %get-tuple-element.34), channel_id=1, source_target_pairs={{0,1},{1,2},{2,3},{3,4},{4,5},{5,6},{6,7},{7,0},{8,9},{9,10},{10,1... | collective-permute-start | bytes 13832 | tf_op jit(solution)/shard_map/ppermute | solution.py:140
  35.2 5.1 %collective-permute-start.8 = (bf16[4,72,128]{2,1,0:T(8,128)(2,1)}, bf16[4,72,128]{2,1,0:T(8,128)(2,1)S(1)}, u32[]{:S(2)}, u32[]{:S(2)}) collective-permute-start(bf16[4,72,128]{2,1,0:T(8,128)(2,1)} %get-tuple-element.31), channel_id=1, source_target_pairs={{0,24},{8,0},{16,8},{24,16},{1,25},{9,1},{17,9},{25,17},{2,26},{10... | collective-permute-start | bytes 221192 | tf_op jit(solution)/shard_map/ppermute | solution.py:137
  35.5 5.5 %collective-permute-start.9 = (bf16[4,72,128]{2,1,0:T(8,128)(2,1)}, bf16[4,72,128]{2,1,0:T(8,128)(2,1)S(1)}, u32[]{:S(2)}, u32[]{:S(2)}) collective-permute-start(bf16[4,72,128]{2,1,0:T(8,128)(2,1)} %get-tuple-element.32), channel_id=1, source_target_pairs={{0,8},{8,16},{16,24},{24,0},{1,9},{9,17},{17,25},{25,1},{2,10},{10... | collective-permute-start | bytes 221192 | tf_op jit(solution)/shard_map/ppermute | solution.py:138
  37.2 3.8 %copy-start.8 = (bf16[1,2304]{1,0:T(2,128)(2,1)}, bf16[1,2304]{1,0:T(2,128)(2,1)S(1)}, u32[]{:S(2)}) copy-start(bf16[1,2304]{1,0:T(2,128)(2,1)S(1)} %collective-permute-done.10.refs_4_) | copy-start | bytes 13828
  40.3 0.7 %copy-start.9 = (bf16[1,2304]{1,0:T(2,128)(2,1)}, bf16[1,2304]{1,0:T(2,128)(2,1)S(1)}, u32[]{:S(2)}) copy-start(bf16[1,2304]{1,0:T(2,128)(2,1)S(1)} %collective-permute-done.11.refs_5_) | copy-start | bytes 13828
  40.3 0.7 %copy-start.6 = (bf16[4,72,128]{2,1,0:T(8,128)(2,1)}, bf16[4,72,128]{2,1,0:T(8,128)(2,1)S(1)}, u32[]{:S(2)}) copy-start(bf16[4,72,128]{2,1,0:T(8,128)(2,1)S(1)} %collective-permute-done.8.refs_2_) | copy-start | bytes 221188
  41.0 0.6 copy-start.7
  47.3 5.2 %copy-start.1 = (bf16[16,72,72]{2,1,0:T(8,128)(2,1)S(1)}, bf16[16,72,72]{2,1,0:T(8,128)(2,1)}, u32[]{:S(2)}) copy-start(bf16[16,72,72]{2,1,0:T(8,128)(2,1)} %param.11) | copy-start | bytes 497668
  48.2 20.2 %all-to-all-start = ((bf16[4,72,8,128]{3,1,0,2:T(8,128)(2,1)}), bf16[4,72,8,128]{3,1,0,2:T(8,128)(2,1)S(1)}, u32[]{:S(2)}, u32[]{:S(2)}) async-start(bf16[4,72,8,128]{3,1,0,2:T(8,128)(2,1)} %select_bitcast_fusion), calls=%async_computation | async-start | bytes 1179648 | tf_op jit(solution)/shard_map/all_to_all | solution.py:155

commit v8 on v7

--- a/solution.py
+++ b/solution.py
@@ -151,7 +151,7 @@
         halos = result[1:]
     order = jnp.argsort(destination[0])
     band_count = band_table.shape[0]
-    ordered = jnp.take(advected, order, axis=2)
+    ordered = jnp.take(advected, order, axis=2, mode="clip")
     received = lax.all_to_all(ordered, "tile", split_axis=2, concat_axis=2, tiled=True)
     inverse = diffusion[0]
     diffused = jnp.einsum("kl,tlxy->tkxy", inverse, received, preferred_element_type=jnp.float32)

time: 70.3 us -> 70.4 us (level)
  waiting for transfers between devices: 27.7 us -> 30.4 us
  starting transfers between devices: 18.8 us -> 16.5 us
  other arithmetic: 2.78 us -> 1.13 us
  local copies, waits for them, and re-layouts: 4.59 us -> 6.02 us
    ppermute x3, starting transfers between devices: 8.71 us -> 2.77 us  [exchange(): lax.ppermute(first, 'tile', [(i, (i - 1) % tile) for i in range(tile)])]
    ppermute x3, starting transfers between devices: 3.69 us -> 9.14 us  [exchange(): north = lax.ppermute(top, 'sec', [(i, (i - 1) % sec) for i in range(sec)])]
    ppermute x3, starting transfers between devices: 2.81 us -> 0.01 us  [exchange(): lax.ppermute(bottom, 'sec', [(i, (i + 1) % sec) for i in range(sec)])]
    ppermute x3, waiting for transfers between devices: 7.04 us -> 8.99 us  [exchange(): lax.ppermute(last, 'tile', [(i, (i + 1) % tile) for i in range(tile)])]
    ppermute x3, waiting for transfers between devices: 4.73 us -> 3.01 us  [exchange(): lax.ppermute(bottom, 'sec', [(i, (i + 1) % sec) for i in range(sec)])]
    ppermute x3, waiting for transfers between devices: 0.01 us -> 1.69 us  [exchange(): lax.ppermute(first, 'tile', [(i, (i - 1) % tile) for i in range(tile)])]
    ppermute x3, starting transfers between devices: 0.01 us -> 1.02 us  [exchange(): lax.ppermute(last, 'tile', [(i, (i + 1) % tile) for i in range(tile)])]
    select_n x2 -> x0, other arithmetic: 0.94 us -> none  [per_device(): ordered = jnp.take(advected, order, axis=2)]
  transfers between devices with their start and end apart: 13 -> 13, of which waited for: 7 -> 9; matrix products, arithmetic and copies ran while one was open for 3% -> 2% of each run, Pallas kernels for 0% -> 0%
where the time goes in v8:
time: 70.4 us; the launch traced here: 70.1 us
  waiting for transfers between devices  30.4 us (43%)
  starting transfers between devices  16.5 us (23%)
  Pallas kernels  14.8 us (21%)
  local copies, waits for them, and re-layouts  6.02 us (9%)
  other arithmetic  1.13 us (2%)
  between operations  0.76 us (1%)
    all_to_all x1, waiting for transfers between devices, per_device(): lax.all_to_all(ordered, 'tile', split_axis=2, concat_axis=2, tiled=True)  15.9 us
    pallas_call x4, Pallas kernels, stencil_call(): pl.pallas_call(functools.partial(stencil_kernel, step, emit), out_shape=t...  14.8 us
    ppermute x3, starting transfers between devices, exchange(): north = lax.ppermute(top, 'sec', [(i, (i - 1) % sec) for i in range(sec)])  9.14 us
    ppermute x3, waiting for transfers between devices, exchange(): lax.ppermute(last, 'tile', [(i, (i + 1) % tile) for i in range(tile)])  8.99 us
    all_to_all x1, starting transfers between devices, per_device(): lax.all_to_all(ordered, 'tile', split_axis=2, concat_axis=2, tiled=True)  3.54 us
    ppermute x3, waiting for transfers between devices, exchange(): lax.ppermute(bottom, 'sec', [(i, (i + 1) % sec) for i in range(sec)])  3.01 us
    ppermute x3, starting transfers between devices, exchange(): lax.ppermute(first, 'tile', [(i, (i - 1) % tile) for i in range(tile)])  2.77 us
    unnamed x30, local copies, waits for them, and re-layouts  2.54 us
  transfers between devices with their start and end apart: 13, of which 9 were waited for; matrix products, arithmetic and copies ran while one was open for 2% of the time, Pallas kernels for 0%

profile of v8, /device:TPU:0, one launch (start us, length us, event | category | flops | bytes accessed | tf_op | source)
XLA Modules:
  0.0 70.1 jit_solution(5783257022743955245)
XLA Ops:
  0.0 2.3 %shard_map.64 = (bf16[4,72,128]{2,1,0:T(8,128)(2,1)}, bf16[4,72,128]{2,1,0:T(8,128)(2,1)}, bf16[1,2304]{1,0:T(2,128)(2,1)}, bf16[1,2304]{1,0:T(2,128)(2,1)}) custom-call(bf16[4,72,8,128]{3,2,1,0:T(8,128)(2,1)} %refs_0_.3), custom_call_target="tpu_custom_call" | custom-call | tf_op jit(solution)/shard_map/pallas_call | solution.py:119
  2.3 3.9 %collective-permute-start = (bf16[4,72,128]{2,1,0:T(8,128)(2,1)}, bf16[4,72,128]{2,1,0:T(8,128)(2,1)S(1)}, u32[]{:S(2)}, u32[]{:S(2)}) collective-permute-start(bf16[4,72,128]{2,1,0:T(8,128)(2,1)} %get-tuple-element.20), channel_id=1, source_target_pairs={{0,24},{8,0},{16,8},{24,16},{1,25},{9,1},{17,9},{25,17},{2,26},{10... | collective-permute-start | bytes 221192 | tf_op jit(solution)/shard_map/ppermute | solution.py:137
  6.2 0.0 collective-permute-start.1
  6.2 2.8 %collective-permute-start.2 = (bf16[1,2304]{1,0:T(2,128)(2,1)}, bf16[1,2304]{1,0:T(2,128)(2,1)S(1)}, u32[]{:S(2)}, u32[]{:S(2)}) collective-permute-start(bf16[1,2304]{1,0:T(2,128)(2,1)} %get-tuple-element.22), channel_id=1, source_target_pairs={{0,7},{1,0},{2,1},{3,2},{4,3},{5,4},{6,5},{7,6},{8,15},{9,8},{10,9... | collective-permute-start | bytes 13832 | tf_op jit(solution)/shard_map/ppermute | solution.py:139
  9.0 0.0 collective-permute-start.3
  9.0 1.6 %collective-permute-done.2.refs_4_ = bf16[1,2304]{1,0:T(2,128)(2,1)S(1)} collective-permute-done((bf16[1,2304]{1,0:T(2,128)(2,1)}, bf16[1,2304]{1,0:T(2,128)(2,1)S(1)}, u32[]{:S(2)}, u32[]{:S(2)}) %collective-permute-start.2) | collective-permute-done | bytes 4640 | tf_op jit(solution)/shard_map/ppermute | solution.py:139
  10.6 3.5 %collective-permute-done.3.refs_5_ = bf16[1,2304]{1,0:T(2,128)(2,1)S(1)} collective-permute-done((bf16[1,2304]{1,0:T(2,128)(2,1)}, bf16[1,2304]{1,0:T(2,128)(2,1)S(1)}, u32[]{:S(2)}, u32[]{:S(2)}) %collective-permute-start.3) | collective-permute-done | bytes 4640 | tf_op jit(solution)/shard_map/ppermute | solution.py:140
  14.1 0.0 collective-permute-done.refs_2_
  14.1 0.0 collective-permute-done.1.refs_3_
  14.1 0.6 copy-done.13
  14.7 0.0 copy-done.4
  14.7 0.6 copy-done.5
  15.4 4.3 %shard_map.65 = (bf16[4,72,8,128]{3,2,1,0:T(8,128)(2,1)}, bf16[4,72,128]{2,1,0:T(8,128)(2,1)}, bf16[4,72,128]{2,1,0:T(8,128)(2,1)}, bf16[1,2304]{1,0:T(2,128)(2,1)}, bf16[1,2304]{1,0:T(2,128)(2,1)}) custom-call(bf16[4,72,8,128]{3,2,1,0:T(8,128)(2,1)} %refs_0_.3, bf16[2,72,8,128]{3,2,1,0:T(8,128)(2,1)} %refs_1_.5, bf16[4,72,128]{2,1,0:T(8,128)(2,1)} %copy-done.4, ...), custom_call_target="tpu_custom_call" | custom-call | tf_op jit(solution)/shard_map/pallas_call | solution.py:119
  19.7 2.6 %collective-permute-start.4 = (bf16[4,72,128]{2,1,0:T(8,128)(2,1)}, bf16[4,72,128]{2,1,0:T(8,128)(2,1)S(1)}, u32[]{:S(2)}, u32[]{:S(2)}) collective-permute-start(bf16[4,72,128]{2,1,0:T(8,128)(2,1)} %get-tuple-element.25), channel_id=1, source_target_pairs={{0,24},{8,0},{16,8},{24,16},{1,25},{9,1},{17,9},{25,17},{2,26},{10... | collective-permute-start | bytes 221192 | tf_op jit(solution)/shard_map/ppermute | solution.py:137
  22.3 0.0 collective-permute-start.5
  22.3 0.0 collective-permute-start.6
  22.3 0.5 collective-permute-start.7
  22.8 0.0 copy-done.14
  22.8 1.0 %sort.17 = (s32[8]{0:T(128)}, s32[8]{0:T(128)S(1)}) sort(s32[8]{0:T(128)S(1)} %bitcast.21, s32[8]{0:T(128)S(1)} %iota.9), dimensions={0}, to_apply=%region_0.0 | sort | flops 24 | bytes 128 | tf_op jit(solution)/shard_map/jit(argsort)/sort | solution.py:152
  23.8 0.1 collective-permute-done.6.refs_4_
  23.9 3.5 %collective-permute-done.7.refs_5_ = bf16[1,2304]{1,0:T(2,128)(2,1)S(1)} collective-permute-done((bf16[1,2304]{1,0:T(2,128)(2,1)}, bf16[1,2304]{1,0:T(2,128)(2,1)S(1)}, u32[]{:S(2)}, u32[]{:S(2)}) %collective-permute-start.7) | collective-permute-done | bytes 4640 | tf_op jit(solution)/shard_map/ppermute | solution.py:140
  27.4 0.0 collective-permute-done.4.refs_2_
  27.4 0.4 collective-permute-done.5.refs_3_
  27.8 0.0 copy-done.10
  27.8 0.2 copy-done.11
  28.0 0.0 copy-done.2
  28.0 0.3 copy-done.3
  28.4 4.3 %shard_map.66 = (bf16[4,72,8,128]{3,2,1,0:T(8,128)(2,1)}, bf16[4,72,128]{2,1,0:T(8,128)(2,1)}, bf16[4,72,128]{2,1,0:T(8,128)(2,1)}, bf16[1,2304]{1,0:T(2,128)(2,1)}, bf16[1,2304]{1,0:T(2,128)(2,1)}) custom-call(bf16[4,72,8,128]{3,2,1,0:T(8,128)(2,1)} %get-tuple-element.24.refs_0_, bf16[2,72,8,128]{3,2,1,0:T(8,128)(2,1)} %refs_1_.5, ...), custom_call_target="tpu_custom_call" | custom-call | tf_op jit(solution)/shard_map/pallas_call | solution.py:119
  32.7 0.0 collective-permute-start.10
  32.7 0.5 collective-permute-start.11
  33.2 2.6 %collective-permute-start.8 = (bf16[4,72,128]{2,1,0:T(8,128)(2,1)}, bf16[4,72,128]{2,1,0:T(8,128)(2,1)S(1)}, u32[]{:S(2)}, u32[]{:S(2)}) collective-permute-start(bf16[4,72,128]{2,1,0:T(8,128)(2,1)} %get-tuple-element.30), channel_id=1, source_target_pairs={{0,24},{8,0},{16,8},{24,16},{1,25},{9,1},{17,9},{25,17},{2,26},{10... | collective-permute-start | bytes 221192 | tf_op jit(solution)/shard_map/ppermute | solution.py:137
  35.8 0.0 collective-permute-start.9
  35.9 0.0 collective-permute-done.10.refs_4_
  35.9 2.0 %collective-permute-done.11.refs_5_ = bf16[1,2304]{1,0:T(2,128)(2,1)S(1)} collective-permute-done((bf16[1,2304]{1,0:T(2,128)(2,1)}, bf16[1,2304]{1,0:T(2,128)(2,1)S(1)}, u32[]{:S(2)}, u32[]{:S(2)}) %collective-permute-start.11) | collective-permute-done | bytes 4640 | tf_op jit(solution)/shard_map/ppermute | solution.py:140
  37.9 0.8 %collective-permute-done.8.refs_2_ = bf16[4,72,128]{2,1,0:T(8,128)(2,1)S(1)} collective-permute-done((bf16[4,72,128]{2,1,0:T(8,128)(2,1)}, bf16[4,72,128]{2,1,0:T(8,128)(2,1)S(1)}, u32[]{:S(2)}, u32[]{:S(2)}) %collective-permute-start.8) | collective-permute-done | bytes 73760 | tf_op jit(solution)/shard_map/ppermute | solution.py:137
  38.6 2.7 %collective-permute-done.9.refs_3_ = bf16[4,72,128]{2,1,0:T(8,128)(2,1)S(1)} collective-permute-done((bf16[4,72,128]{2,1,0:T(8,128)(2,1)}, bf16[4,72,128]{2,1,0:T(8,128)(2,1)S(1)}, u32[]{:S(2)}, u32[]{:S(2)}) %collective-permute-start.9) | collective-permute-done | bytes 73760 | tf_op jit(solution)/shard_map/ppermute | solution.py:138
  41.3 0.0 copy-done.9
  41.3 0.6 copy-done.7
  41.9 3.8 %shard_map.67 = bf16[4,72,8,128]{3,2,1,0:T(8,128)(2,1)} custom-call(bf16[4,72,8,128]{3,2,1,0:T(8,128)(2,1)} %get-tuple-element.29.refs_0_, bf16[2,72,8,128]{3,2,1,0:T(8,128)(2,1)} %refs_1_.5, bf16[4,72,128]{2,1,0:T(8,128)(2,1)} %copy-done.6, bf16[4,72,128]{2,1,0:T(8,128)(2,1)} %copy-done.7, bf16[1,2304]{1,0:T(2,128)(2,1)} %copy-done.8, bf16[1,2304]{1,0:T(2,128)(2,1)} %copy-done.9), custom_call_target="tpu_custom_call" | custom-call | tf_op jit(solution)/shard_map/pallas_call | solution.py:119
  45.8 1.1 %copy.12 = bf16[4,72,8,128]{3,1,2,0:T(8,128)(2,1)S(1)} copy(bf16[4,72,8,128]{3,2,1,0:T(8,128)(2,1)} %shard_map.67) | data formatting | bytes 1179648 | tf_op jit(solution)/shard_map/pallas_call | solution.py:119
  46.9 0.0 copy-start.1
  46.9 1.4 %gather_fusion = bf16[8,4,72,128]{3,2,1,0:T(8,128)(2,1)} fusion(bf16[4,72,8,128]{3,1,2,0:T(8,128)(2,1)S(1)} %copy.12, s32[1024]{0:T(1024)S(1)} %pad_clamp_fusion), kind=kCustom, calls=%fused_computation | custom fusion | bytes 1179680 | tf_op jit(solution)/shard_map/jit(_take)/gather | solution.py:154
  48.4 3.5 %all-to-all-start = ((bf16[4,72,8,128]{3,1,0,2:T(8,128)(2,1)}), bf16[4,72,8,128]{3,1,0,2:T(8,128)(2,1)S(1)}, u32[]{:S(2)}, u32[]{:S(2)}) async-start(bf16[4,72,8,128]{3,1,0,2:T(8,128)(2,1)} %bitcast.1), calls=%async_computation | async-start | bytes 1179648 | tf_op jit(solution)/shard_map/all_to_all | solution.py:155
  52.6 0.1 select_reduce_fusion
  52.7 15.9 %all-to-all-done = bf16[4,72,8,128]{3,1,0,2:T(8,128)(2,1)S(1)} async-done(((bf16[4,72,8,128]{3,1,0,2:T(8,128)(2,1)}), bf16[4,72,8,128]{3,1,0,2:T(8,128)(2,1)S(1)}, u32[]{:S(2)}, u32[]{:S(2)}) %all-to-all-start) | async-done | bytes 589856 | tf_op jit(solution)/shard_map/all_to_all | solution.py:155
  68.6 0.3 fusion.3
  68.9 0.3 fusion.1
  69.2 0.9 %copy.14 = bf16[4,72,8,128]{3,2,1,0:T(8,128)(2,1)} copy(bf16[4,72,8,128]{3,1,2,0:T(8,128)(2,1)S(1)} %fusion.1) | data formatting | bytes 1179648 | tf_op jit(solution)/shard_map/convert_element_type | solution.py:162
  (22 shorter events, 0.0 us)
Async XLA Ops:
  0.0 68.6 %copy-start = (bf16[1,72,72]{2,1,0:T(8,128)(2,1)S(1)}, bf16[1,72,72]{2,1,0:T(8,128)(2,1)}, u32[]{:S(2)}) copy-start(bf16[1,72,72]{2,1,0:T(8,128)(2,1)} %param.9) | copy-start | bytes 31108
  0.0 22.8 %copy-start.14 = (s32[1,8]{1,0:T(1,128)S(1)}, s32[1,8]{1,0:T(1,128)}, u32[]{:S(2)}) copy-start(s32[1,8]{1,0:T(1,128)} %param.8) | copy-start | bytes 100
  2.3 11.8 %collective-permute-start = (bf16[4,72,128]{2,1,0:T(8,128)(2,1)}, bf16[4,72,128]{2,1,0:T(8,128)(2,1)S(1)}, u32[]{:S(2)}, u32[]{:S(2)}) collective-permute-start(bf16[4,72,128]{2,1,0:T(8,128)(2,1)} %get-tuple-element.20), channel_id=1, source_target_pairs={{0,24},{8,0},{16,8},{24,16},{1,25},{9,1},{17,9},{25,17},{2,26},{10... | collective-permute-start | bytes 221192 | tf_op jit(solution)/shard_map/ppermute | solution.py:137
  6.2 7.9 %collective-permute-start.1 = (bf16[4,72,128]{2,1,0:T(8,128)(2,1)}, bf16[4,72,128]{2,1,0:T(8,128)(2,1)S(1)}, u32[]{:S(2)}, u32[]{:S(2)}) collective-permute-start(bf16[4,72,128]{2,1,0:T(8,128)(2,1)} %get-tuple-element.21), channel_id=1, source_target_pairs={{0,8},{8,16},{16,24},{24,0},{1,9},{9,17},{17,25},{25,1},{2,10},{10... | collective-permute-start | bytes 221192 | tf_op jit(solution)/shard_map/ppermute | solution.py:138
  6.2 4.3 %collective-permute-start.2 = (bf16[1,2304]{1,0:T(2,128)(2,1)}, bf16[1,2304]{1,0:T(2,128)(2,1)S(1)}, u32[]{:S(2)}, u32[]{:S(2)}) collective-permute-start(bf16[1,2304]{1,0:T(2,128)(2,1)} %get-tuple-element.22), channel_id=1, source_target_pairs={{0,7},{1,0},{2,1},{3,2},{4,3},{5,4},{6,5},{7,6},{8,15},{9,8},{10,9... | collective-permute-start | bytes 13832 | tf_op jit(solution)/shard_map/ppermute | solution.py:139
  9.0 5.1 %collective-permute-start.3 = (bf16[1,2304]{1,0:T(2,128)(2,1)}, bf16[1,2304]{1,0:T(2,128)(2,1)S(1)}, u32[]{:S(2)}, u32[]{:S(2)}) collective-permute-start(bf16[1,2304]{1,0:T(2,128)(2,1)} %get-tuple-element.23), channel_id=1, source_target_pairs={{0,1},{1,2},{2,3},{3,4},{4,5},{5,6},{6,7},{7,0},{8,9},{9,10},{10,1... | collective-permute-start | bytes 13832 | tf_op jit(solution)/shard_map/ppermute | solution.py:140
  10.6 3.5 %copy-start.12 = (bf16[1,2304]{1,0:T(2,128)(2,1)}, bf16[1,2304]{1,0:T(2,128)(2,1)S(1)}, u32[]{:S(2)}) copy-start(bf16[1,2304]{1,0:T(2,128)(2,1)S(1)} %collective-permute-done.2.refs_4_) | copy-start | bytes 13828
  14.1 0.6 copy-start.13
  14.1 0.6 copy-start.4
  14.7 0.6 copy-start.5
  19.7 7.8 %collective-permute-start.4 = (bf16[4,72,128]{2,1,0:T(8,128)(2,1)}, bf16[4,72,128]{2,1,0:T(8,128)(2,1)S(1)}, u32[]{:S(2)}, u32[]{:S(2)}) collective-permute-start(bf16[4,72,128]{2,1,0:T(8,128)(2,1)} %get-tuple-element.25), channel_id=1, source_target_pairs={{0,24},{8,0},{16,8},{24,16},{1,25},{9,1},{17,9},{25,17},{2,26},{10... | collective-permute-start | bytes 221192 | tf_op jit(solution)/shard_map/ppermute | solution.py:137
  22.3 5.5 %collective-permute-start.5 = (bf16[4,72,128]{2,1,0:T(8,128)(2,1)}, bf16[4,72,128]{2,1,0:T(8,128)(2,1)S(1)}, u32[]{:S(2)}, u32[]{:S(2)}) collective-permute-start(bf16[4,72,128]{2,1,0:T(8,128)(2,1)} %get-tuple-element.26), channel_id=1, source_target_pairs={{0,8},{8,16},{16,24},{24,0},{1,9},{9,17},{17,25},{25,1},{2,10},{10... | collective-permute-start | bytes 221192 | tf_op jit(solution)/shard_map/ppermute | solution.py:138
  22.3 1.6 %collective-permute-start.6 = (bf16[1,2304]{1,0:T(2,128)(2,1)}, bf16[1,2304]{1,0:T(2,128)(2,1)S(1)}, u32[]{:S(2)}, u32[]{:S(2)}) collective-permute-start(bf16[1,2304]{1,0:T(2,128)(2,1)} %get-tuple-element.27), channel_id=1, source_target_pairs={{0,7},{1,0},{2,1},{3,2},{4,3},{5,4},{6,5},{7,6},{8,15},{9,8},{10,9... | collective-permute-start | bytes 13832 | tf_op jit(solution)/shard_map/ppermute | solution.py:139
  22.3 5.1 %collective-permute-start.7 = (bf16[1,2304]{1,0:T(2,128)(2,1)}, bf16[1,2304]{1,0:T(2,128)(2,1)S(1)}, u32[]{:S(2)}, u32[]{:S(2)}) collective-permute-start(bf16[1,2304]{1,0:T(2,128)(2,1)} %get-tuple-element.28), channel_id=1, source_target_pairs={{0,1},{1,2},{2,3},{3,4},{4,5},{5,6},{6,7},{7,0},{8,9},{9,10},{10,1... | collective-permute-start | bytes 13832 | tf_op jit(solution)/shard_map/ppermute | solution.py:140
  23.9 3.9 %copy-start.10 = (bf16[1,2304]{1,0:T(2,128)(2,1)}, bf16[1,2304]{1,0:T(2,128)(2,1)S(1)}, u32[]{:S(2)}) copy-start(bf16[1,2304]{1,0:T(2,128)(2,1)S(1)} %collective-permute-done.6.refs_4_) | copy-start | bytes 13828
  27.4 0.6 copy-start.11
  27.4 0.6 copy-start.2
  27.8 0.6 copy-start.3
  32.7 3.1 %collective-permute-start.10 = (bf16[1,2304]{1,0:T(2,128)(2,1)}, bf16[1,2304]{1,0:T(2,128)(2,1)S(1)}, u32[]{:S(2)}, u32[]{:S(2)}) collective-permute-start(bf16[1,2304]{1,0:T(2,128)(2,1)} %get-tuple-element.32), channel_id=1, source_target_pairs={{0,7},{1,0},{2,1},{3,2},{4,3},{5,4},{6,5},{7,6},{8,15},{9,8},{10,9... | collective-permute-start | bytes 13832 | tf_op jit(solution)/shard_map/ppermute | solution.py:139
  32.7 5.1 %collective-permute-start.11 = (bf16[1,2304]{1,0:T(2,128)(2,1)}, bf16[1,2304]{1,0:T(2,128)(2,1)S(1)}, u32[]{:S(2)}, u32[]{:S(2)}) collective-permute-start(bf16[1,2304]{1,0:T(2,128)(2,1)} %get-tuple-element.33), channel_id=1, source_target_pairs={{0,1},{1,2},{2,3},{3,4},{4,5},{5,6},{6,7},{7,0},{8,9},{9,10},{10,1... | collective-permute-start | bytes 13832 | tf_op jit(solution)/shard_map/ppermute | solution.py:140
  33.2 5.4 %collective-permute-start.8 = (bf16[4,72,128]{2,1,0:T(8,128)(2,1)}, bf16[4,72,128]{2,1,0:T(8,128)(2,1)S(1)}, u32[]{:S(2)}, u32[]{:S(2)}) collective-permute-start(bf16[4,72,128]{2,1,0:T(8,128)(2,1)} %get-tuple-element.30), channel_id=1, source_target_pairs={{0,24},{8,0},{16,8},{24,16},{1,25},{9,1},{17,9},{25,17},{2,26},{10... | collective-permute-start | bytes 221192 | tf_op jit(solution)/shard_map/ppermute | solution.py:137
  35.8 5.5 %collective-permute-start.9 = (bf16[4,72,128]{2,1,0:T(8,128)(2,1)}, bf16[4,72,128]{2,1,0:T(8,128)(2,1)S(1)}, u32[]{:S(2)}, u32[]{:S(2)}) collective-permute-start(bf16[4,72,128]{2,1,0:T(8,128)(2,1)} %get-tuple-element.31), channel_id=1, source_target_pairs={{0,8},{8,16},{16,24},{24,0},{1,9},{9,17},{17,25},{25,1},{2,10},{10... | collective-permute-start | bytes 221192 | tf_op jit(solution)/shard_map/ppermute | solution.py:138
  35.9 5.4 %copy-start.8 = (bf16[1,2304]{1,0:T(2,128)(2,1)}, bf16[1,2304]{1,0:T(2,128)(2,1)S(1)}, u32[]{:S(2)}) copy-start(bf16[1,2304]{1,0:T(2,128)(2,1)S(1)} %collective-permute-done.10.refs_4_) | copy-start | bytes 13828
  37.8 3.5 %copy-start.9 = (bf16[1,2304]{1,0:T(2,128)(2,1)}, bf16[1,2304]{1,0:T(2,128)(2,1)S(1)}, u32[]{:S(2)}) copy-start(bf16[1,2304]{1,0:T(2,128)(2,1)S(1)} %collective-permute-done.11.refs_5_) | copy-start | bytes 13828
  38.6 2.7 %copy-start.6 = (bf16[4,72,128]{2,1,0:T(8,128)(2,1)}, bf16[4,72,128]{2,1,0:T(8,128)(2,1)S(1)}, u32[]{:S(2)}) copy-start(bf16[4,72,128]{2,1,0:T(8,128)(2,1)S(1)} %collective-permute-done.8.refs_2_) | copy-start | bytes 221188
  41.3 0.6 copy-start.7
  46.9 5.7 %copy-start.1 = (bf16[16,72,72]{2,1,0:T(8,128)(2,1)S(1)}, bf16[16,72,72]{2,1,0:T(8,128)(2,1)}, u32[]{:S(2)}) copy-start(bf16[16,72,72]{2,1,0:T(8,128)(2,1)} %param.11) | copy-start | bytes 497668
  48.4 20.2 %all-to-all-start = ((bf16[4,72,8,128]{3,1,0,2:T(8,128)(2,1)}), bf16[4,72,8,128]{3,1,0,2:T(8,128)(2,1)S(1)}, u32[]{:S(2)}, u32[]{:S(2)}) async-start(bf16[4,72,8,128]{3,1,0,2:T(8,128)(2,1)} %bitcast.1), calls=%async_computation | async-start | bytes 1179648 | tf_op jit(solution)/shard_map/all_to_all | solution.py:155

commit v9 on v8

--- a/solution.py
+++ b/solution.py
@@ -143,6 +143,7 @@
 
 def per_device(tracers, courant, destination, diffusion, band, band_table):
     halos = stencil_call(0, True, tracers)
+    halos = (tracers[:, :, 0, :], tracers[:, :, -1, :]) + tuple(halos[2:])
     advected = tracers
     for step in range(STEPS):
         emit = step < STEPS - 1

time: 70.4 us -> 72.3 us (1.027)
  local copies, waits for them, and re-layouts: 6.02 us -> 7.68 us
    slice x0 -> x1, local copies, waits for them, and re-layouts: none -> 1.62 us  [per_device(): halos = (tracers[:, :, 0, :], tracers[:, :, -1, :]) + tuple(halos[2:])]
    unnamed x30 -> x32, local copies, waits for them, and re-layouts: 2.54 us -> 2.58 us
  transfers between devices with their start and end apart: 13 -> 13, of which waited for: 9 -> 9; matrix products, arithmetic and copies ran while one was open for 2% -> 2% of each run, Pallas kernels for 0% -> 3%
where the time goes in v9:
time: 72.3 us; the launch traced here: 71.9 us
  waiting for transfers between devices  30.4 us (42%)
  starting transfers between devices  16.6 us (23%)
  Pallas kernels  14.8 us (20%)
  local copies, waits for them, and re-layouts  7.68 us (11%)
  other arithmetic  1.11 us (2%)
  between operations  0.79 us (1%)
    all_to_all x1, waiting for transfers between devices, per_device(): lax.all_to_all(ordered, 'tile', split_axis=2, concat_axis=2, tiled=True)  15.9 us
    pallas_call x4, Pallas kernels, stencil_call(): pl.pallas_call(functools.partial(stencil_kernel, step, emit), out_shape=t...  14.8 us
    ppermute x3, starting transfers between devices, exchange(): north = lax.ppermute(top, 'sec', [(i, (i - 1) % sec) for i in range(sec)])  9.17 us
    ppermute x3, waiting for transfers between devices, exchange(): lax.ppermute(last, 'tile', [(i, (i + 1) % tile) for i in range(tile)])  9 us
    all_to_all x1, starting transfers between devices, per_device(): lax.all_to_all(ordered, 'tile', split_axis=2, concat_axis=2, tiled=True)  3.54 us
    ppermute x3, waiting for transfers between devices, exchange(): lax.ppermute(bottom, 'sec', [(i, (i + 1) % sec) for i in range(sec)])  3.01 us
    ppermute x3, starting transfers between devices, exchange(): lax.ppermute(first, 'tile', [(i, (i - 1) % tile) for i in range(tile)])  2.77 us
    unnamed x32, local copies, waits for them, and re-layouts  2.58 us
  transfers between devices with their start and end apart: 13, of which 9 were waited for; matrix products, arithmetic and copies ran while one was open for 2% of the time, Pallas kernels for 3%

profile of v9, /device:TPU:0, one launch (start us, length us, event | category | flops | bytes accessed | tf_op | source)
XLA Modules:
  0.0 71.9 jit_solution(9970566392596305880)
XLA Ops:
  0.0 1.6 %fusion.8 = (bf16[4,72,1,128]{3,2,1,0:T(2,128)(2,1)S(1)}, bf16[4,72,1,128]{3,2,1,0:T(2,128)(2,1)S(1)}) fusion(bf16[4,72,8,128]{3,2,1,0:T(8,128)(2,1)} %refs_0_.3), kind=kLoop, calls=%fused_computation.15 | loop fusion | bytes 294912 | tf_op jit(solution)/shard_map/slice | solution.py:146
  1.6 0.0 copy-start.14
  1.7 3.9 %collective-permute-start = (bf16[4,72,128]{2,1,0:T(8,128)(2,1)S(1)}, bf16[4,72,128]{2,1,0:T(8,128)(2,1)S(1)}, u32[]{:S(2)}, u32[]{:S(2)}) collective-permute-start(bf16[4,72,128]{2,1,0:T(8,128)(2,1)S(1)} %bitcast.27), channel_id=1, source_target_pairs={{0,24},{8,0},{16,8},{24,16},{1,25},{9,1},{17,9},{25,17},{2,26},{10... | collective-permute-start | bytes 221192 | tf_op jit(solution)/shard_map/ppermute | solution.py:137
  5.6 0.1 collective-permute-start.1
  5.7 2.3 %shard_map.64 = (bf16[4,72,128]{2,1,0:T(8,128)(2,1)}, bf16[4,72,128]{2,1,0:T(8,128)(2,1)}, bf16[1,2304]{1,0:T(2,128)(2,1)}, bf16[1,2304]{1,0:T(2,128)(2,1)}) custom-call(bf16[4,72,8,128]{3,2,1,0:T(8,128)(2,1)} %refs_0_.3), custom_call_target="tpu_custom_call" | custom-call | tf_op jit(solution)/shard_map/pallas_call | solution.py:119
  8.0 2.8 %collective-permute-start.2 = (bf16[1,2304]{1,0:T(2,128)(2,1)}, bf16[1,2304]{1,0:T(2,128)(2,1)S(1)}, u32[]{:S(2)}, u32[]{:S(2)}) collective-permute-start(bf16[1,2304]{1,0:T(2,128)(2,1)} %get-tuple-element.18), channel_id=1, source_target_pairs={{0,7},{1,0},{2,1},{3,2},{4,3},{5,4},{6,5},{7,6},{8,15},{9,8},{10,9... | collective-permute-start | bytes 13832 | tf_op jit(solution)/shard_map/ppermute | solution.py:139
  10.7 0.0 collective-permute-start.3
  10.7 1.6 %collective-permute-done.2.refs_4_ = bf16[1,2304]{1,0:T(2,128)(2,1)S(1)} collective-permute-done((bf16[1,2304]{1,0:T(2,128)(2,1)}, bf16[1,2304]{1,0:T(2,128)(2,1)S(1)}, u32[]{:S(2)}, u32[]{:S(2)}) %collective-permute-start.2) | collective-permute-done | bytes 4640 | tf_op jit(solution)/shard_map/ppermute | solution.py:139
  12.3 3.5 %collective-permute-done.3.refs_5_ = bf16[1,2304]{1,0:T(2,128)(2,1)S(1)} collective-permute-done((bf16[1,2304]{1,0:T(2,128)(2,1)}, bf16[1,2304]{1,0:T(2,128)(2,1)S(1)}, u32[]{:S(2)}, u32[]{:S(2)}) %collective-permute-start.3) | collective-permute-done | bytes 4640 | tf_op jit(solution)/shard_map/ppermute | solution.py:140
  15.8 0.0 collective-permute-done.refs_2_
  15.8 0.0 collective-permute-done.1.refs_3_
  15.9 0.6 copy-done.13
  16.4 0.1 copy-done.2
  16.5 0.6 copy-done.4
  17.1 4.3 %shard_map.65 = (bf16[4,72,8,128]{3,2,1,0:T(8,128)(2,1)}, bf16[4,72,128]{2,1,0:T(8,128)(2,1)}, bf16[4,72,128]{2,1,0:T(8,128)(2,1)}, bf16[1,2304]{1,0:T(2,128)(2,1)}, bf16[1,2304]{1,0:T(2,128)(2,1)}) custom-call(bf16[4,72,8,128]{3,2,1,0:T(8,128)(2,1)} %refs_0_.3, bf16[2,72,8,128]{3,2,1,0:T(8,128)(2,1)} %refs_1_.5, bf16[4,72,128]{2,1,0:T(8,128)(2,1)} %copy-done.2, ...), custom_call_target="tpu_custom_call" | custom-call | tf_op jit(solution)/shard_map/pallas_call | solution.py:119
  21.4 2.6 %collective-permute-start.4 = (bf16[4,72,128]{2,1,0:T(8,128)(2,1)}, bf16[4,72,128]{2,1,0:T(8,128)(2,1)S(1)}, u32[]{:S(2)}, u32[]{:S(2)}) collective-permute-start(bf16[4,72,128]{2,1,0:T(8,128)(2,1)} %get-tuple-element.21), channel_id=1, source_target_pairs={{0,24},{8,0},{16,8},{24,16},{1,25},{9,1},{17,9},{25,17},{2,26},{10... | collective-permute-start | bytes 221192 | tf_op jit(solution)/shard_map/ppermute | solution.py:137
  24.0 0.0 collective-permute-start.5
  24.1 0.0 collective-permute-start.6
  24.1 0.5 collective-permute-start.7
  24.6 0.0 copy-done.14
  24.6 1.0 %sort.17 = (s32[8]{0:T(128)}, s32[8]{0:T(128)S(1)}) sort(s32[8]{0:T(128)S(1)} %bitcast.29, s32[8]{0:T(128)S(1)} %iota.9), dimensions={0}, to_apply=%region_0.0 | sort | flops 24 | bytes 128 | tf_op jit(solution)/shard_map/jit(argsort)/sort | solution.py:153
  25.5 0.1 collective-permute-done.6.refs_4_
  25.6 3.5 %collective-permute-done.7.refs_5_ = bf16[1,2304]{1,0:T(2,128)(2,1)S(1)} collective-permute-done((bf16[1,2304]{1,0:T(2,128)(2,1)}, bf16[1,2304]{1,0:T(2,128)(2,1)S(1)}, u32[]{:S(2)}, u32[]{:S(2)}) %collective-permute-start.7) | collective-permute-done | bytes 4640 | tf_op jit(solution)/shard_map/ppermute | solution.py:140
  29.2 0.0 collective-permute-done.4.refs_2_
  29.2 0.4 collective-permute-done.5.refs_3_
  29.5 0.2 copy-done.11
  29.7 0.0 copy-done.3
  29.8 0.4 copy-done.5
  30.1 4.3 %shard_map.66 = (bf16[4,72,8,128]{3,2,1,0:T(8,128)(2,1)}, bf16[4,72,128]{2,1,0:T(8,128)(2,1)}, bf16[4,72,128]{2,1,0:T(8,128)(2,1)}, bf16[1,2304]{1,0:T(2,128)(2,1)}, bf16[1,2304]{1,0:T(2,128)(2,1)}) custom-call(bf16[4,72,8,128]{3,2,1,0:T(8,128)(2,1)} %get-tuple-element.20.refs_0_, bf16[2,72,8,128]{3,2,1,0:T(8,128)(2,1)} %refs_1_.5, ...), custom_call_target="tpu_custom_call" | custom-call | tf_op jit(solution)/shard_map/pallas_call | solution.py:119
  34.5 0.0 collective-permute-start.10
  34.5 0.5 collective-permute-start.11
  35.0 2.6 %collective-permute-start.8 = (bf16[4,72,128]{2,1,0:T(8,128)(2,1)}, bf16[4,72,128]{2,1,0:T(8,128)(2,1)S(1)}, u32[]{:S(2)}, u32[]{:S(2)}) collective-permute-start(bf16[4,72,128]{2,1,0:T(8,128)(2,1)} %get-tuple-element.26), channel_id=1, source_target_pairs={{0,24},{8,0},{16,8},{24,16},{1,25},{9,1},{17,9},{25,17},{2,26},{10... | collective-permute-start | bytes 221192 | tf_op jit(solution)/shard_map/ppermute | solution.py:137
  37.6 0.0 collective-permute-start.9
  37.6 0.0 collective-permute-done.10.refs_4_
  37.6 2.0 %collective-permute-done.11.refs_5_ = bf16[1,2304]{1,0:T(2,128)(2,1)S(1)} collective-permute-done((bf16[1,2304]{1,0:T(2,128)(2,1)}, bf16[1,2304]{1,0:T(2,128)(2,1)S(1)}, u32[]{:S(2)}, u32[]{:S(2)}) %collective-permute-start.11) | collective-permute-done | bytes 4640 | tf_op jit(solution)/shard_map/ppermute | solution.py:140
  39.6 0.8 %collective-permute-done.8.refs_2_ = bf16[4,72,128]{2,1,0:T(8,128)(2,1)S(1)} collective-permute-done((bf16[4,72,128]{2,1,0:T(8,128)(2,1)}, bf16[4,72,128]{2,1,0:T(8,128)(2,1)S(1)}, u32[]{:S(2)}, u32[]{:S(2)}) %collective-permute-start.8) | collective-permute-done | bytes 73760 | tf_op jit(solution)/shard_map/ppermute | solution.py:137
  40.4 2.7 %collective-permute-done.9.refs_3_ = bf16[4,72,128]{2,1,0:T(8,128)(2,1)S(1)} collective-permute-done((bf16[4,72,128]{2,1,0:T(8,128)(2,1)}, bf16[4,72,128]{2,1,0:T(8,128)(2,1)S(1)}, u32[]{:S(2)}, u32[]{:S(2)}) %collective-permute-start.9) | collective-permute-done | bytes 73760 | tf_op jit(solution)/shard_map/ppermute | solution.py:138
  43.1 0.6 copy-done.7
  43.7 3.8 %shard_map.67 = bf16[4,72,8,128]{3,2,1,0:T(8,128)(2,1)} custom-call(bf16[4,72,8,128]{3,2,1,0:T(8,128)(2,1)} %get-tuple-element.25.refs_0_, bf16[2,72,8,128]{3,2,1,0:T(8,128)(2,1)} %refs_1_.5, bf16[4,72,128]{2,1,0:T(8,128)(2,1)} %copy-done.6, bf16[4,72,128]{2,1,0:T(8,128)(2,1)} %copy-done.7, bf16[1,2304]{1,0:T(2,128)(2,1)} %copy-done.8, bf16[1,2304]{1,0:T(2,128)(2,1)} %copy-done.9), custom_call_target="tpu_custom_call" | custom-call | tf_op jit(solution)/shard_map/pallas_call | solution.py:119
  47.5 1.1 %copy.18 = bf16[4,72,8,128]{3,1,2,0:T(8,128)(2,1)S(1)} copy(bf16[4,72,8,128]{3,2,1,0:T(8,128)(2,1)} %shard_map.67) | data formatting | bytes 1179648 | tf_op jit(solution)/shard_map/pallas_call | solution.py:119
  48.7 0.0 copy-start.1
  48.7 1.4 %gather_fusion = bf16[8,4,72,128]{3,2,1,0:T(8,128)(2,1)} fusion(bf16[4,72,8,128]{3,1,2,0:T(8,128)(2,1)S(1)} %copy.18, s32[1024]{0:T(1024)S(1)} %pad_clamp_fusion), kind=kCustom, calls=%fused_computation | custom fusion | bytes 1179680 | tf_op jit(solution)/shard_map/jit(_take)/gather | solution.py:155
  50.1 3.5 %all-to-all-start = ((bf16[4,72,8,128]{3,1,0,2:T(8,128)(2,1)}), bf16[4,72,8,128]{3,1,0,2:T(8,128)(2,1)S(1)}, u32[]{:S(2)}, u32[]{:S(2)}) async-start(bf16[4,72,8,128]{3,1,0,2:T(8,128)(2,1)} %bitcast.3), calls=%async_computation | async-start | bytes 1179648 | tf_op jit(solution)/shard_map/all_to_all | solution.py:156
  54.3 0.1 select_reduce_fusion
  54.5 15.9 %all-to-all-done = bf16[4,72,8,128]{3,1,0,2:T(8,128)(2,1)S(1)} async-done(((bf16[4,72,8,128]{3,1,0,2:T(8,128)(2,1)}), bf16[4,72,8,128]{3,1,0,2:T(8,128)(2,1)S(1)}, u32[]{:S(2)}, u32[]{:S(2)}) %all-to-all-start) | async-done | bytes 589856 | tf_op jit(solution)/shard_map/all_to_all | solution.py:156
  70.4 0.3 fusion.3
  70.7 0.3 fusion.1
  71.0 0.9 %copy.20 = bf16[4,72,8,128]{3,2,1,0:T(8,128)(2,1)} copy(bf16[4,72,8,128]{3,1,2,0:T(8,128)(2,1)S(1)} %fusion.1) | data formatting | bytes 1179648 | tf_op jit(solution)/shard_map/convert_element_type | solution.py:163
  (25 shorter events, 0.1 us)
Async XLA Ops:
  0.0 70.4 %copy-start = (bf16[1,72,72]{2,1,0:T(8,128)(2,1)S(1)}, bf16[1,72,72]{2,1,0:T(8,128)(2,1)}, u32[]{:S(2)}) copy-start(bf16[1,72,72]{2,1,0:T(8,128)(2,1)} %param.9) | copy-start | bytes 31108
  1.6 22.9 %copy-start.14 = (s32[1,8]{1,0:T(1,128)S(1)}, s32[1,8]{1,0:T(1,128)}, u32[]{:S(2)}) copy-start(s32[1,8]{1,0:T(1,128)} %param.8) | copy-start | bytes 100
  1.7 14.2 %collective-permute-start = (bf16[4,72,128]{2,1,0:T(8,128)(2,1)S(1)}, bf16[4,72,128]{2,1,0:T(8,128)(2,1)S(1)}, u32[]{:S(2)}, u32[]{:S(2)}) collective-permute-start(bf16[4,72,128]{2,1,0:T(8,128)(2,1)S(1)} %bitcast.27), channel_id=1, source_target_pairs={{0,24},{8,0},{16,8},{24,16},{1,25},{9,1},{17,9},{25,17},{2,26},{10... | collective-permute-start | bytes 221192 | tf_op jit(solution)/shard_map/ppermute | solution.py:137
  5.6 10.2 %collective-permute-start.1 = (bf16[4,72,128]{2,1,0:T(8,128)(2,1)S(1)}, bf16[4,72,128]{2,1,0:T(8,128)(2,1)S(1)}, u32[]{:S(2)}, u32[]{:S(2)}) collective-permute-start(bf16[4,72,128]{2,1,0:T(8,128)(2,1)S(1)} %bitcast.28), channel_id=1, source_target_pairs={{0,8},{8,16},{16,24},{24,0},{1,9},{9,17},{17,25},{25,1},{2,10},{10... | collective-permute-start | bytes 221192 | tf_op jit(solution)/shard_map/ppermute | solution.py:138
  8.0 4.3 %collective-permute-start.2 = (bf16[1,2304]{1,0:T(2,128)(2,1)}, bf16[1,2304]{1,0:T(2,128)(2,1)S(1)}, u32[]{:S(2)}, u32[]{:S(2)}) collective-permute-start(bf16[1,2304]{1,0:T(2,128)(2,1)} %get-tuple-element.18), channel_id=1, source_target_pairs={{0,7},{1,0},{2,1},{3,2},{4,3},{5,4},{6,5},{7,6},{8,15},{9,8},{10,9... | collective-permute-start | bytes 13832 | tf_op jit(solution)/shard_map/ppermute | solution.py:139
  10.7 5.1 %collective-permute-start.3 = (bf16[1,2304]{1,0:T(2,128)(2,1)}, bf16[1,2304]{1,0:T(2,128)(2,1)S(1)}, u32[]{:S(2)}, u32[]{:S(2)}) collective-permute-start(bf16[1,2304]{1,0:T(2,128)(2,1)} %get-tuple-element.19), channel_id=1, source_target_pairs={{0,1},{1,2},{2,3},{3,4},{4,5},{5,6},{6,7},{7,0},{8,9},{9,10},{10,1... | collective-permute-start | bytes 13832 | tf_op jit(solution)/shard_map/ppermute | solution.py:140
  12.3 3.5 %copy-start.12 = (bf16[1,2304]{1,0:T(2,128)(2,1)}, bf16[1,2304]{1,0:T(2,128)(2,1)S(1)}, u32[]{:S(2)}) copy-start(bf16[1,2304]{1,0:T(2,128)(2,1)S(1)} %collective-permute-done.2.refs_4_) | copy-start | bytes 13828
  15.8 0.6 copy-start.13
  15.8 0.6 copy-start.2
  16.5 0.6 copy-start.4
  21.4 7.7 %collective-permute-start.4 = (bf16[4,72,128]{2,1,0:T(8,128)(2,1)}, bf16[4,72,128]{2,1,0:T(8,128)(2,1)S(1)}, u32[]{:S(2)}, u32[]{:S(2)}) collective-permute-start(bf16[4,72,128]{2,1,0:T(8,128)(2,1)} %get-tuple-element.21), channel_id=1, source_target_pairs={{0,24},{8,0},{16,8},{24,16},{1,25},{9,1},{17,9},{25,17},{2,26},{10... | collective-permute-start | bytes 221192 | tf_op jit(solution)/shard_map/ppermute | solution.py:137
  24.0 5.5 %collective-permute-start.5 = (bf16[4,72,128]{2,1,0:T(8,128)(2,1)}, bf16[4,72,128]{2,1,0:T(8,128)(2,1)S(1)}, u32[]{:S(2)}, u32[]{:S(2)}) collective-permute-start(bf16[4,72,128]{2,1,0:T(8,128)(2,1)} %get-tuple-element.22), channel_id=1, source_target_pairs={{0,8},{8,16},{16,24},{24,0},{1,9},{9,17},{17,25},{25,1},{2,10},{10... | collective-permute-start | bytes 221192 | tf_op jit(solution)/shard_map/ppermute | solution.py:138
  24.1 1.6 %collective-permute-start.6 = (bf16[1,2304]{1,0:T(2,128)(2,1)}, bf16[1,2304]{1,0:T(2,128)(2,1)S(1)}, u32[]{:S(2)}, u32[]{:S(2)}) collective-permute-start(bf16[1,2304]{1,0:T(2,128)(2,1)} %get-tuple-element.23), channel_id=1, source_target_pairs={{0,7},{1,0},{2,1},{3,2},{4,3},{5,4},{6,5},{7,6},{8,15},{9,8},{10,9... | collective-permute-start | bytes 13832 | tf_op jit(solution)/shard_map/ppermute | solution.py:139
  24.1 5.1 %collective-permute-start.7 = (bf16[1,2304]{1,0:T(2,128)(2,1)}, bf16[1,2304]{1,0:T(2,128)(2,1)S(1)}, u32[]{:S(2)}, u32[]{:S(2)}) collective-permute-start(bf16[1,2304]{1,0:T(2,128)(2,1)} %get-tuple-element.24), channel_id=1, source_target_pairs={{0,1},{1,2},{2,3},{3,4},{4,5},{5,6},{6,7},{7,0},{8,9},{9,10},{10,1... | collective-permute-start | bytes 13832 | tf_op jit(solution)/shard_map/ppermute | solution.py:140
  25.6 3.9 %copy-start.10 = (bf16[1,2304]{1,0:T(2,128)(2,1)}, bf16[1,2304]{1,0:T(2,128)(2,1)S(1)}, u32[]{:S(2)}) copy-start(bf16[1,2304]{1,0:T(2,128)(2,1)S(1)} %collective-permute-done.6.refs_4_) | copy-start | bytes 13828
  29.1 0.6 copy-start.11
  29.2 0.6 copy-start.3
  29.5 0.6 copy-start.5
  34.5 3.1 %collective-permute-start.10 = (bf16[1,2304]{1,0:T(2,128)(2,1)}, bf16[1,2304]{1,0:T(2,128)(2,1)S(1)}, u32[]{:S(2)}, u32[]{:S(2)}) collective-permute-start(bf16[1,2304]{1,0:T(2,128)(2,1)} %get-tuple-element.28), channel_id=1, source_target_pairs={{0,7},{1,0},{2,1},{3,2},{4,3},{5,4},{6,5},{7,6},{8,15},{9,8},{10,9... | collective-permute-start | bytes 13832 | tf_op jit(solution)/shard_map/ppermute | solution.py:139
  34.5 5.1 %collective-permute-start.11 = (bf16[1,2304]{1,0:T(2,128)(2,1)}, bf16[1,2304]{1,0:T(2,128)(2,1)S(1)}, u32[]{:S(2)}, u32[]{:S(2)}) collective-permute-start(bf16[1,2304]{1,0:T(2,128)(2,1)} %get-tuple-element.29), channel_id=1, source_target_pairs={{0,1},{1,2},{2,3},{3,4},{4,5},{5,6},{6,7},{7,0},{8,9},{9,10},{10,1... | collective-permute-start | bytes 13832 | tf_op jit(solution)/shard_map/ppermute | solution.py:140
  35.0 5.4 %collective-permute-start.8 = (bf16[4,72,128]{2,1,0:T(8,128)(2,1)}, bf16[4,72,128]{2,1,0:T(8,128)(2,1)S(1)}, u32[]{:S(2)}, u32[]{:S(2)}) collective-permute-start(bf16[4,72,128]{2,1,0:T(8,128)(2,1)} %get-tuple-element.26), channel_id=1, source_target_pairs={{0,24},{8,0},{16,8},{24,16},{1,25},{9,1},{17,9},{25,17},{2,26},{10... | collective-permute-start | bytes 221192 | tf_op jit(solution)/shard_map/ppermute | solution.py:137
  37.6 5.5 %collective-permute-start.9 = (bf16[4,72,128]{2,1,0:T(8,128)(2,1)}, bf16[4,72,128]{2,1,0:T(8,128)(2,1)S(1)}, u32[]{:S(2)}, u32[]{:S(2)}) collective-permute-start(bf16[4,72,128]{2,1,0:T(8,128)(2,1)} %get-tuple-element.27), channel_id=1, source_target_pairs={{0,8},{8,16},{16,24},{24,0},{1,9},{9,17},{17,25},{25,1},{2,10},{10... | collective-permute-start | bytes 221192 | tf_op jit(solution)/shard_map/ppermute | solution.py:138
  37.6 5.4 %copy-start.8 = (bf16[1,2304]{1,0:T(2,128)(2,1)}, bf16[1,2304]{1,0:T(2,128)(2,1)S(1)}, u32[]{:S(2)}) copy-start(bf16[1,2304]{1,0:T(2,128)(2,1)S(1)} %collective-permute-done.10.refs_4_) | copy-start | bytes 13828
  39.6 3.5 %copy-start.9 = (bf16[1,2304]{1,0:T(2,128)(2,1)}, bf16[1,2304]{1,0:T(2,128)(2,1)S(1)}, u32[]{:S(2)}) copy-start(bf16[1,2304]{1,0:T(2,128)(2,1)S(1)} %collective-permute-done.11.refs_5_) | copy-start | bytes 13828
  40.4 2.7 %copy-start.6 = (bf16[4,72,128]{2,1,0:T(8,128)(2,1)}, bf16[4,72,128]{2,1,0:T(8,128)(2,1)S(1)}, u32[]{:S(2)}) copy-start(bf16[4,72,128]{2,1,0:T(8,128)(2,1)S(1)} %collective-permute-done.8.refs_2_) | copy-start | bytes 221188
  43.1 0.7 copy-start.7
  48.7 5.7 %copy-start.1 = (bf16[16,72,72]{2,1,0:T(8,128)(2,1)S(1)}, bf16[16,72,72]{2,1,0:T(8,128)(2,1)}, u32[]{:S(2)}) copy-start(bf16[16,72,72]{2,1,0:T(8,128)(2,1)} %param.11) | copy-start | bytes 497668
  50.1 20.2 %all-to-all-start = ((bf16[4,72,8,128]{3,1,0,2:T(8,128)(2,1)}), bf16[4,72,8,128]{3,1,0,2:T(8,128)(2,1)S(1)}, u32[]{:S(2)}, u32[]{:S(2)}) async-start(bf16[4,72,8,128]{3,1,0,2:T(8,128)(2,1)} %bitcast.3), calls=%async_computation | async-start | bytes 1179648 | tf_op jit(solution)/shard_map/all_to_all | solution.py:156

commit v10 on v8

--- a/solution.py
+++ b/solution.py
@@ -142,13 +142,19 @@
 
 
 def per_device(tracers, courant, destination, diffusion, band, band_table):
-    halos = stencil_call(0, True, tracers)
-    advected = tracers
+    count = tracers.shape[0]
+    split = count // 2 if count % 2 == 0 and tracers.shape[2] <= 8 else count
+    groups = [tracers[start:start + split] for start in range(0, count, split)]
+    halos = [stencil_call(0, True, group) for group in groups]
     for step in range(STEPS):
         emit = step < STEPS - 1
-        result = stencil_call(1, emit, advected, courant, *exchange(*halos))
-        advected = result[0]
-        halos = result[1:]
+        results = [
+            stencil_call(1, emit, group, courant, *exchange(*halo))
+            for group, halo in zip(groups, halos)
+        ]
+        groups = [result[0] for result in results]
+        halos = [result[1:] for result in results]
+    advected = jnp.concatenate(groups, axis=0) if len(groups) > 1 else groups[0]
     order = jnp.argsort(destination[0])
     band_count = band_table.shape[0]
     ordered = jnp.take(advected, order, axis=2, mode="clip")

time: 70.4 us -> 96.7 us (1.37)
  starting transfers between devices: 16.5 us -> 36 us
  Pallas kernels: 14.8 us -> 21.6 us
  waiting for transfers between devices: 30.4 us -> 26.1 us
  local copies, waits for them, and re-layouts: 6.02 us -> 8.69 us
  other arithmetic: 1.13 us -> 2.29 us
    ppermute x3 -> x6, starting transfers between devices: 2.77 us -> 14.5 us  [exchange(): lax.ppermute(first, 'tile', [(i, (i - 1) % tile) for i in range(tile)])]
    ppermute x3 -> x6, starting transfers between devices: 9.14 us -> 17.4 us  [exchange(): north = lax.ppermute(top, 'sec', [(i, (i - 1) % sec) for i in range(sec)])]
    pallas_call x4 -> x8, Pallas kernels: 14.8 us -> 21.6 us  [stencil_call(): pl.pallas_call(functools.partial(stencil_kernel, step, emit), out_shape=t...]
    ppermute x3 -> x6, waiting for transfers between devices: 8.99 us -> 5.47 us  [exchange(): lax.ppermute(last, 'tile', [(i, (i + 1) % tile) for i in range(tile)])]
    slice x0 -> x1, local copies, waits for them, and re-layouts: none -> 1.9 us  [per_device(): groups = [tracers[start:start + split] for start in range(0, count, split)]]
    unnamed x30 -> x54, local copies, waits for them, and re-layouts: 2.54 us -> 4.37 us
    ppermute x3 -> x6, waiting for transfers between devices: 1.69 us -> 3.09 us  [exchange(): lax.ppermute(first, 'tile', [(i, (i - 1) % tile) for i in range(tile)])]
    ppermute x3 -> x6, waiting for transfers between devices: 3.01 us -> 1.68 us  [exchange(): lax.ppermute(bottom, 'sec', [(i, (i + 1) % sec) for i in range(sec)])]
  transfers between devices with their start and end apart: 13 -> 25, of which waited for: 9 -> 6; matrix products, arithmetic and copies ran while one was open for 2% -> 1% of each run, Pallas kernels for 0% -> 18%
where the time goes in v10:
time: 96.7 us; the launch traced here: 96.3 us
  starting transfers between devices  36 us (37%)
  waiting for transfers between devices  26.1 us (27%)
  Pallas kernels  21.6 us (22%)
  local copies, waits for them, and re-layouts  8.69 us (9%)
  other arithmetic  2.29 us (2%)
  between operations  0.97 us (1%)
    pallas_call x8, Pallas kernels, stencil_call(): pl.pallas_call(functools.partial(stencil_kernel, step, emit), out_shape=t...  21.6 us
    ppermute x6, starting transfers between devices, exchange(): north = lax.ppermute(top, 'sec', [(i, (i - 1) % sec) for i in range(sec)])  17.4 us
    all_to_all x1, waiting for transfers between devices, per_device(): lax.all_to_all(ordered, 'tile', split_axis=2, concat_axis=2, tiled=True)  15.9 us
    ppermute x6, starting transfers between devices, exchange(): lax.ppermute(first, 'tile', [(i, (i - 1) % tile) for i in range(tile)])  14.5 us
    ppermute x6, waiting for transfers between devices, exchange(): lax.ppermute(last, 'tile', [(i, (i + 1) % tile) for i in range(tile)])  5.47 us
    unnamed x54, local copies, waits for them, and re-layouts  4.37 us
    all_to_all x1, starting transfers between devices, per_device(): lax.all_to_all(ordered, 'tile', split_axis=2, concat_axis=2, tiled=True)  3.54 us
    ppermute x6, waiting for transfers between devices, exchange(): lax.ppermute(first, 'tile', [(i, (i - 1) % tile) for i in range(tile)])  3.09 us
  transfers between devices with their start and end apart: 25, of which 6 were waited for; matrix products, arithmetic and copies ran while one was open for 1% of the time, Pallas kernels for 18%

profile of v10, /device:TPU:0, one launch (start us, length us, event | category | flops | bytes accessed | tf_op | source)
XLA Modules:
  0.0 96.3 jit_solution(11358994374544884987)
XLA Ops:
  0.0 1.9 %fusion.8 = (bf16[2,72,8,128]{3,2,1,0:T(8,128)(2,1)}, bf16[2,72,8,128]{3,2,1,0:T(8,128)(2,1)}) fusion(bf16[4,72,8,128]{3,2,1,0:T(8,128)(2,1)} %param.6), kind=kLoop, calls=%fused_computation.14 | loop fusion | bytes 1179648 | tf_op jit(solution)/shard_map/slice | solution.py:147
  1.9 2.0 %shard_map.64 = (bf16[2,72,128]{2,1,0:T(8,128)(2,1)}, bf16[2,72,128]{2,1,0:T(8,128)(2,1)}, bf16[1,1152]{1,0:T(2,128)(2,1)}, bf16[1,1152]{1,0:T(2,128)(2,1)}) custom-call(bf16[2,72,8,128]{3,2,1,0:T(8,128)(2,1)} %get-tuple-element.63.refs_0_), custom_call_target="tpu_custom_call" | custom-call | tf_op jit(solution)/shard_map/pallas_call | solution.py:119
  3.9 3.9 %collective-permute-start = (bf16[2,72,128]{2,1,0:T(8,128)(2,1)}, bf16[2,72,128]{2,1,0:T(8,128)(2,1)S(1)}, u32[]{:S(2)}, u32[]{:S(2)}) collective-permute-start(bf16[2,72,128]{2,1,0:T(8,128)(2,1)} %get-tuple-element.34), channel_id=1, source_target_pairs={{0,24},{8,0},{16,8},{24,16},{1,25},{9,1},{17,9},{25,17},{2,26},{10... | collective-permute-start | bytes 110600 | tf_op jit(solution)/shard_map/ppermute | solution.py:137
  7.8 2.8 %collective-permute-start.2 = (bf16[1,1152]{1,0:T(2,128)(2,1)}, bf16[1,1152]{1,0:T(2,128)(2,1)S(1)}, u32[]{:S(2)}, u32[]{:S(2)}) collective-permute-start(bf16[1,1152]{1,0:T(2,128)(2,1)} %get-tuple-element.36), channel_id=1, source_target_pairs={{0,7},{1,0},{2,1},{3,2},{4,3},{5,4},{6,5},{7,6},{8,15},{9,8},{10,9... | collective-permute-start | bytes 6920 | tf_op jit(solution)/shard_map/ppermute | solution.py:139
  10.5 2.0 %shard_map.68 = (bf16[2,72,128]{2,1,0:T(8,128)(2,1)}, bf16[2,72,128]{2,1,0:T(8,128)(2,1)}, bf16[1,1152]{1,0:T(2,128)(2,1)}, bf16[1,1152]{1,0:T(2,128)(2,1)}) custom-call(bf16[2,72,8,128]{3,2,1,0:T(8,128)(2,1)} %get-tuple-element.64.refs_0_), custom_call_target="tpu_custom_call" | custom-call | tf_op jit(solution)/shard_map/pallas_call | solution.py:119
  12.5 2.6 %collective-permute-start.12 = (bf16[2,72,128]{2,1,0:T(8,128)(2,1)}, bf16[2,72,128]{2,1,0:T(8,128)(2,1)S(1)}, u32[]{:S(2)}, u32[]{:S(2)}) collective-permute-start(bf16[2,72,128]{2,1,0:T(8,128)(2,1)} %get-tuple-element.48), channel_id=1, source_target_pairs={{0,24},{8,0},{16,8},{24,16},{1,25},{9,1},{17,9},{25,17},{2,26},{10... | collective-permute-start | bytes 110600 | tf_op jit(solution)/shard_map/ppermute | solution.py:137
  15.2 0.4 collective-permute-done.3.refs_5_
  15.6 0.2 copy-done.22
  15.8 0.4 copy-done.23
  16.2 0.0 copy-done.12
  16.2 0.6 copy-done.13
  16.8 3.1 %shard_map.65 = (bf16[2,72,8,128]{3,2,1,0:T(8,128)(2,1)}, bf16[2,72,128]{2,1,0:T(8,128)(2,1)}, bf16[2,72,128]{2,1,0:T(8,128)(2,1)}, bf16[1,1152]{1,0:T(2,128)(2,1)}, bf16[1,1152]{1,0:T(2,128)(2,1)}) custom-call(bf16[2,72,8,128]{3,2,1,0:T(8,128)(2,1)} %get-tuple-element.63.refs_0_, bf16[2,72,8,128]{3,2,1,0:T(8,128)(2,1)} %refs_1_.11, ...), custom_call_target="tpu_custom_call" | custom-call | tf_op jit(solution)/shard_map/pallas_call | solution.py:119
  19.9 2.6 %collective-permute-start.4 = (bf16[2,72,128]{2,1,0:T(8,128)(2,1)}, bf16[2,72,128]{2,1,0:T(8,128)(2,1)S(1)}, u32[]{:S(2)}, u32[]{:S(2)}) collective-permute-start(bf16[2,72,128]{2,1,0:T(8,128)(2,1)} %get-tuple-element.39), channel_id=1, source_target_pairs={{0,24},{8,0},{16,8},{24,16},{1,25},{9,1},{17,9},{25,17},{2,26},{10... | collective-permute-start | bytes 110600 | tf_op jit(solution)/shard_map/ppermute | solution.py:137
  22.5 2.6 %collective-permute-start.14 = (bf16[1,1152]{1,0:T(2,128)(2,1)}, bf16[1,1152]{1,0:T(2,128)(2,1)S(1)}, u32[]{:S(2)}, u32[]{:S(2)}) collective-permute-start(bf16[1,1152]{1,0:T(2,128)(2,1)} %get-tuple-element.50), channel_id=1, source_target_pairs={{0,7},{1,0},{2,1},{3,2},{4,3},{5,4},{6,5},{7,6},{8,15},{9,8},{10,9... | collective-permute-start | bytes 6920 | tf_op jit(solution)/shard_map/ppermute | solution.py:139
  25.1 1.5 %collective-permute-done.14.refs_4_ = bf16[1,1152]{1,0:T(2,128)(2,1)S(1)} collective-permute-done((bf16[1,1152]{1,0:T(2,128)(2,1)}, bf16[1,1152]{1,0:T(2,128)(2,1)S(1)}, u32[]{:S(2)}, u32[]{:S(2)}) %collective-permute-start.14) | collective-permute-done | bytes 2336 | tf_op jit(solution)/shard_map/ppermute | solution.py:139
  26.6 5.0 %collective-permute-done.15.refs_5_ = bf16[1,1152]{1,0:T(2,128)(2,1)S(1)} collective-permute-done((bf16[1,1152]{1,0:T(2,128)(2,1)}, bf16[1,1152]{1,0:T(2,128)(2,1)S(1)}, u32[]{:S(2)}, u32[]{:S(2)}) %collective-permute-start.15) | collective-permute-done | bytes 2336 | tf_op jit(solution)/shard_map/ppermute | solution.py:140
  31.7 0.5 collective-permute-start.7
  32.2 0.1 copy-done.25
  32.3 0.0 copy-done.8
  32.3 0.6 copy-done.11
  32.9 3.1 %shard_map.69 = (bf16[2,72,8,128]{3,2,1,0:T(8,128)(2,1)}, bf16[2,72,128]{2,1,0:T(8,128)(2,1)}, bf16[2,72,128]{2,1,0:T(8,128)(2,1)}, bf16[1,1152]{1,0:T(2,128)(2,1)}, bf16[1,1152]{1,0:T(2,128)(2,1)}) custom-call(bf16[2,72,8,128]{3,2,1,0:T(8,128)(2,1)} %get-tuple-element.64.refs_0_, bf16[2,72,8,128]{3,2,1,0:T(8,128)(2,1)} %refs_1_.11, ...), custom_call_target="tpu_custom_call" | custom-call | tf_op jit(solution)/shard_map/pallas_call | solution.py:119
  36.0 2.6 %collective-permute-start.16 = (bf16[2,72,128]{2,1,0:T(8,128)(2,1)}, bf16[2,72,128]{2,1,0:T(8,128)(2,1)S(1)}, u32[]{:S(2)}, u32[]{:S(2)}) collective-permute-start(bf16[2,72,128]{2,1,0:T(8,128)(2,1)} %get-tuple-element.53), channel_id=1, source_target_pairs={{0,24},{8,0},{16,8},{24,16},{1,25},{9,1},{17,9},{25,17},{2,26},{10... | collective-permute-start | bytes 110600 | tf_op jit(solution)/shard_map/ppermute | solution.py:137
  38.7 0.5 copy-done.18
  39.3 0.0 copy-done.7
  39.3 3.1 %shard_map.66 = (bf16[2,72,8,128]{3,2,1,0:T(8,128)(2,1)}, bf16[2,72,128]{2,1,0:T(8,128)(2,1)}, bf16[2,72,128]{2,1,0:T(8,128)(2,1)}, bf16[1,1152]{1,0:T(2,128)(2,1)}, bf16[1,1152]{1,0:T(2,128)(2,1)}) custom-call(bf16[2,72,8,128]{3,2,1,0:T(8,128)(2,1)} %get-tuple-element.38.refs_0_, bf16[2,72,8,128]{3,2,1,0:T(8,128)(2,1)} %refs_1_.11, ...), custom_call_target="tpu_custom_call" | custom-call | tf_op jit(solution)/shard_map/pallas_call | solution.py:119
  42.4 2.9 %collective-permute-start.8 = (bf16[2,72,128]{2,1,0:T(8,128)(2,1)}, bf16[2,72,128]{2,1,0:T(8,128)(2,1)S(1)}, u32[]{:S(2)}, u32[]{:S(2)}) collective-permute-start(bf16[2,72,128]{2,1,0:T(8,128)(2,1)} %get-tuple-element.44), channel_id=1, source_target_pairs={{0,24},{8,0},{16,8},{24,16},{1,25},{9,1},{17,9},{25,17},{2,26},{10... | collective-permute-start | bytes 110600 | tf_op jit(solution)/shard_map/ppermute | solution.py:137
  45.3 2.2 %collective-permute-start.18 = (bf16[1,1152]{1,0:T(2,128)(2,1)}, bf16[1,1152]{1,0:T(2,128)(2,1)S(1)}, u32[]{:S(2)}, u32[]{:S(2)}) collective-permute-start(bf16[1,1152]{1,0:T(2,128)(2,1)} %get-tuple-element.55), channel_id=1, source_target_pairs={{0,7},{1,0},{2,1},{3,2},{4,3},{5,4},{6,5},{7,6},{8,15},{9,8},{10,9... | collective-permute-start | bytes 6920 | tf_op jit(solution)/shard_map/ppermute | solution.py:139
  47.5 1.5 %collective-permute-done.18.refs_4_ = bf16[1,1152]{1,0:T(2,128)(2,1)S(1)} collective-permute-done((bf16[1,1152]{1,0:T(2,128)(2,1)}, bf16[1,1152]{1,0:T(2,128)(2,1)S(1)}, u32[]{:S(2)}, u32[]{:S(2)}) %collective-permute-start.18) | collective-permute-done | bytes 2336 | tf_op jit(solution)/shard_map/ppermute | solution.py:139
  49.0 3.5 %collective-permute-start.10 = (bf16[1,1152]{1,0:T(2,128)(2,1)}, bf16[1,1152]{1,0:T(2,128)(2,1)S(1)}, u32[]{:S(2)}, u32[]{:S(2)}) collective-permute-start(bf16[1,1152]{1,0:T(2,128)(2,1)} %get-tuple-element.46), channel_id=1, source_target_pairs={{0,7},{1,0},{2,1},{3,2},{4,3},{5,4},{6,5},{7,6},{8,15},{9,8},{10,9... | collective-permute-start | bytes 6920 | tf_op jit(solution)/shard_map/ppermute | solution.py:139
  52.5 1.0 %sort.17 = (s32[8]{0:T(128)}, s32[8]{0:T(128)S(1)}) sort(s32[8]{0:T(128)S(1)} %bitcast.21, s32[8]{0:T(128)S(1)} %iota.9), dimensions={0}, to_apply=%region_0.0 | sort | flops 24 | bytes 128 | tf_op jit(solution)/shard_map/jit(argsort)/sort | solution.py:158
  53.6 0.6 copy-done.6
  54.2 3.1 %shard_map.70 = (bf16[2,72,8,128]{3,2,1,0:T(8,128)(2,1)}, bf16[2,72,128]{2,1,0:T(8,128)(2,1)}, bf16[2,72,128]{2,1,0:T(8,128)(2,1)}, bf16[1,1152]{1,0:T(2,128)(2,1)}, bf16[1,1152]{1,0:T(2,128)(2,1)}) custom-call(bf16[2,72,8,128]{3,2,1,0:T(8,128)(2,1)} %get-tuple-element.52.refs_0_, bf16[2,72,8,128]{3,2,1,0:T(8,128)(2,1)} %refs_1_.11, ...), custom_call_target="tpu_custom_call" | custom-call | tf_op jit(solution)/shard_map/pallas_call | solution.py:119
  57.3 3.5 %collective-permute-start.22 = (bf16[1,1152]{1,0:T(2,128)(2,1)}, bf16[1,1152]{1,0:T(2,128)(2,1)S(1)}, u32[]{:S(2)}, u32[]{:S(2)}) collective-permute-start(bf16[1,1152]{1,0:T(2,128)(2,1)} %get-tuple-element.60), channel_id=1, source_target_pairs={{0,7},{1,0},{2,1},{3,2},{4,3},{5,4},{6,5},{7,6},{8,15},{9,8},{10,9... | collective-permute-start | bytes 6920 | tf_op jit(solution)/shard_map/ppermute | solution.py:139
  60.8 2.7 %collective-permute-start.20 = (bf16[2,72,128]{2,1,0:T(8,128)(2,1)}, bf16[2,72,128]{2,1,0:T(8,128)(2,1)S(1)}, u32[]{:S(2)}, u32[]{:S(2)}) collective-permute-start(bf16[2,72,128]{2,1,0:T(8,128)(2,1)} %get-tuple-element.58), channel_id=1, source_target_pairs={{0,24},{8,0},{16,8},{24,16},{1,25},{9,1},{17,9},{25,17},{2,26},{10... | collective-permute-start | bytes 110600 | tf_op jit(solution)/shard_map/ppermute | solution.py:137
  63.6 0.6 copy-done.2
  64.1 2.7 %shard_map.67 = bf16[2,72,8,128]{3,2,1,0:T(8,128)(2,1)} custom-call(bf16[2,72,8,128]{3,2,1,0:T(8,128)(2,1)} %get-tuple-element.43.refs_0_, bf16[2,72,8,128]{3,2,1,0:T(8,128)(2,1)} %refs_1_.11, bf16[2,72,128]{2,1,0:T(8,128)(2,1)} %copy-done.2, bf16[2,72,128]{2,1,0:T(8,128)(2,1)} %copy-done.3, bf16[1,1152]{1,0:T(2,128)(2,1)} %copy-done.14, ...), custom_call_target="tpu_custom_call" | custom-call | tf_op jit(solution)/shard_map/pallas_call | solution.py:119
  66.9 1.7 %collective-permute-done.21.refs_3_ = bf16[2,72,128]{2,1,0:T(8,128)(2,1)S(1)} collective-permute-done((bf16[2,72,128]{2,1,0:T(8,128)(2,1)}, bf16[2,72,128]{2,1,0:T(8,128)(2,1)S(1)}, u32[]{:S(2)}, u32[]{:S(2)}) %collective-permute-start.21) | collective-permute-done | bytes 36896 | tf_op jit(solution)/shard_map/ppermute | solution.py:138
  68.6 0.6 copy-done.5
  69.2 2.7 %shard_map.71 = bf16[2,72,8,128]{3,2,1,0:T(8,128)(2,1)} custom-call(bf16[2,72,8,128]{3,2,1,0:T(8,128)(2,1)} %get-tuple-element.57.refs_0_, bf16[2,72,8,128]{3,2,1,0:T(8,128)(2,1)} %refs_1_.11, bf16[2,72,128]{2,1,0:T(8,128)(2,1)} %copy-done.4, bf16[2,72,128]{2,1,0:T(8,128)(2,1)} %copy-done.5, bf16[1,1152]{1,0:T(2,128)(2,1)} %copy-done.16, ...), custom_call_target="tpu_custom_call" | custom-call | tf_op jit(solution)/shard_map/pallas_call | solution.py:119
  71.9 1.1 %pad_maximum_fusion = bf16[4,72,8,128]{3,2,1,0:T(8,128)(2,1)S(1)} fusion(bf16[2,72,8,128]{3,2,1,0:T(8,128)(2,1)} %shard_map.71, bf16[2,72,8,128]{3,2,1,0:T(8,128)(2,1)} %shard_map.67), kind=kLoop, calls=%fused_computation.4 | loop fusion | flops 294912 | bytes 1179648 | tf_op jit(solution)/shard_map/concatenate | solution.py:157
  73.0 0.1 copy.12
  73.1 1.4 %gather_fusion = bf16[8,4,72,128]{3,2,1,0:T(8,128)(2,1)} fusion(bf16[4,72,8,128]{3,1,2,0:T(8,128)(2,1)S(1)} %copy.12, s32[1024]{0:T(1024)S(1)} %pad_clamp_fusion), kind=kCustom, calls=%fused_computation | custom fusion | bytes 1179680 | tf_op jit(solution)/shard_map/jit(_take)/gather | solution.py:160
  74.6 3.5 %all-to-all-start = ((bf16[4,72,8,128]{3,1,0,2:T(8,128)(2,1)}), bf16[4,72,8,128]{3,1,0,2:T(8,128)(2,1)S(1)}, u32[]{:S(2)}, u32[]{:S(2)}) async-start(bf16[4,72,8,128]{3,1,0,2:T(8,128)(2,1)} %bitcast.1), calls=%async_computation | async-start | bytes 1179648 | tf_op jit(solution)/shard_map/all_to_all | solution.py:161
  78.8 0.1 select_reduce_fusion
  78.9 15.9 %all-to-all-done = bf16[4,72,8,128]{3,1,0,2:T(8,128)(2,1)S(1)} async-done(((bf16[4,72,8,128]{3,1,0,2:T(8,128)(2,1)}), bf16[4,72,8,128]{3,1,0,2:T(8,128)(2,1)S(1)}, u32[]{:S(2)}, u32[]{:S(2)}) %all-to-all-start) | async-done | bytes 589856 | tf_op jit(solution)/shard_map/all_to_all | solution.py:161
  94.8 0.3 fusion.3
  95.1 0.3 fusion.1
  95.4 0.9 copy.14
  (76 shorter events, 0.3 us)
Async XLA Ops:
  0.0 94.8 %copy-start = (bf16[1,72,72]{2,1,0:T(8,128)(2,1)S(1)}, bf16[1,72,72]{2,1,0:T(8,128)(2,1)}, u32[]{:S(2)}) copy-start(bf16[1,72,72]{2,1,0:T(8,128)(2,1)} %param.9) | copy-start | bytes 31108
  3.9 48.7 %copy-start.26 = (s32[1,8]{1,0:T(1,128)S(1)}, s32[1,8]{1,0:T(1,128)}, u32[]{:S(2)}) copy-start(s32[1,8]{1,0:T(1,128)} %param.8) | copy-start | bytes 100
  3.9 11.7 %collective-permute-start = (bf16[2,72,128]{2,1,0:T(8,128)(2,1)}, bf16[2,72,128]{2,1,0:T(8,128)(2,1)S(1)}, u32[]{:S(2)}, u32[]{:S(2)}) collective-permute-start(bf16[2,72,128]{2,1,0:T(8,128)(2,1)} %get-tuple-element.34), channel_id=1, source_target_pairs={{0,24},{8,0},{16,8},{24,16},{1,25},{9,1},{17,9},{25,17},{2,26},{10... | collective-permute-start | bytes 110600 | tf_op jit(solution)/shard_map/ppermute | solution.py:137
  7.8 7.8 %collective-permute-start.1 = (bf16[2,72,128]{2,1,0:T(8,128)(2,1)}, bf16[2,72,128]{2,1,0:T(8,128)(2,1)S(1)}, u32[]{:S(2)}, u32[]{:S(2)}) collective-permute-start(bf16[2,72,128]{2,1,0:T(8,128)(2,1)} %get-tuple-element.35), channel_id=1, source_target_pairs={{0,8},{8,16},{16,24},{24,0},{1,9},{9,17},{17,25},{25,1},{2,10},{10... | collective-permute-start | bytes 110600 | tf_op jit(solution)/shard_map/ppermute | solution.py:138
  7.8 7.4 %collective-permute-start.2 = (bf16[1,1152]{1,0:T(2,128)(2,1)}, bf16[1,1152]{1,0:T(2,128)(2,1)S(1)}, u32[]{:S(2)}, u32[]{:S(2)}) collective-permute-start(bf16[1,1152]{1,0:T(2,128)(2,1)} %get-tuple-element.36), channel_id=1, source_target_pairs={{0,7},{1,0},{2,1},{3,2},{4,3},{5,4},{6,5},{7,6},{8,15},{9,8},{10,9... | collective-permute-start | bytes 6920 | tf_op jit(solution)/shard_map/ppermute | solution.py:139
  10.5 5.0 %collective-permute-start.3 = (bf16[1,1152]{1,0:T(2,128)(2,1)}, bf16[1,1152]{1,0:T(2,128)(2,1)S(1)}, u32[]{:S(2)}, u32[]{:S(2)}) collective-permute-start(bf16[1,1152]{1,0:T(2,128)(2,1)} %get-tuple-element.37), channel_id=1, source_target_pairs={{0,1},{1,2},{2,3},{3,4},{4,5},{5,6},{6,7},{7,0},{8,9},{9,10},{10,1... | collective-permute-start | bytes 6920 | tf_op jit(solution)/shard_map/ppermute | solution.py:140
  12.5 19.2 %collective-permute-start.12 = (bf16[2,72,128]{2,1,0:T(8,128)(2,1)}, bf16[2,72,128]{2,1,0:T(8,128)(2,1)S(1)}, u32[]{:S(2)}, u32[]{:S(2)}) collective-permute-start(bf16[2,72,128]{2,1,0:T(8,128)(2,1)} %get-tuple-element.48), channel_id=1, source_target_pairs={{0,24},{8,0},{16,8},{24,16},{1,25},{9,1},{17,9},{25,17},{2,26},{10... | collective-permute-start | bytes 110600 | tf_op jit(solution)/shard_map/ppermute | solution.py:137
  15.2 17.1 %collective-permute-start.13 = (bf16[2,72,128]{2,1,0:T(8,128)(2,1)}, bf16[2,72,128]{2,1,0:T(8,128)(2,1)S(1)}, u32[]{:S(2)}, u32[]{:S(2)}) collective-permute-start(bf16[2,72,128]{2,1,0:T(8,128)(2,1)} %get-tuple-element.49), channel_id=1, source_target_pairs={{0,8},{8,16},{16,24},{24,0},{1,9},{9,17},{17,25},{25,1},{2,10},{10... | collective-permute-start | bytes 110600 | tf_op jit(solution)/shard_map/ppermute | solution.py:138
  15.6 0.6 copy-start.12
  16.2 0.6 copy-start.13
  19.9 18.8 %collective-permute-start.4 = (bf16[2,72,128]{2,1,0:T(8,128)(2,1)}, bf16[2,72,128]{2,1,0:T(8,128)(2,1)S(1)}, u32[]{:S(2)}, u32[]{:S(2)}) collective-permute-start(bf16[2,72,128]{2,1,0:T(8,128)(2,1)} %get-tuple-element.39), channel_id=1, source_target_pairs={{0,24},{8,0},{16,8},{24,16},{1,25},{9,1},{17,9},{25,17},{2,26},{10... | collective-permute-start | bytes 110600 | tf_op jit(solution)/shard_map/ppermute | solution.py:137
  22.5 16.2 %collective-permute-start.5 = (bf16[2,72,128]{2,1,0:T(8,128)(2,1)}, bf16[2,72,128]{2,1,0:T(8,128)(2,1)S(1)}, u32[]{:S(2)}, u32[]{:S(2)}) collective-permute-start(bf16[2,72,128]{2,1,0:T(8,128)(2,1)} %get-tuple-element.40), channel_id=1, source_target_pairs={{0,8},{8,16},{16,24},{24,0},{1,9},{9,17},{17,25},{25,1},{2,10},{10... | collective-permute-start | bytes 110600 | tf_op jit(solution)/shard_map/ppermute | solution.py:138
  22.5 4.1 %collective-permute-start.14 = (bf16[1,1152]{1,0:T(2,128)(2,1)}, bf16[1,1152]{1,0:T(2,128)(2,1)S(1)}, u32[]{:S(2)}, u32[]{:S(2)}) collective-permute-start(bf16[1,1152]{1,0:T(2,128)(2,1)} %get-tuple-element.50), channel_id=1, source_target_pairs={{0,7},{1,0},{2,1},{3,2},{4,3},{5,4},{6,5},{7,6},{8,15},{9,8},{10,9... | collective-permute-start | bytes 6920 | tf_op jit(solution)/shard_map/ppermute | solution.py:139
  26.6 5.6 %copy-start.24 = (bf16[1,1152]{1,0:T(2,128)(2,1)}, bf16[1,1152]{1,0:T(2,128)(2,1)S(1)}, u32[]{:S(2)}) copy-start(bf16[1,1152]{1,0:T(2,128)(2,1)S(1)} %collective-permute-done.14.refs_4_) | copy-start | bytes 6916
  26.6 5.0 %collective-permute-start.15 = (bf16[1,1152]{1,0:T(2,128)(2,1)}, bf16[1,1152]{1,0:T(2,128)(2,1)S(1)}, u32[]{:S(2)}, u32[]{:S(2)}) collective-permute-start(bf16[1,1152]{1,0:T(2,128)(2,1)} %get-tuple-element.51), channel_id=1, source_target_pairs={{0,1},{1,2},{2,3},{3,4},{4,5},{5,6},{6,7},{7,0},{8,9},{9,10},{10,1... | collective-permute-start | bytes 6920 | tf_op jit(solution)/shard_map/ppermute | solution.py:140
  31.7 6.9 %collective-permute-start.6 = (bf16[1,1152]{1,0:T(2,128)(2,1)}, bf16[1,1152]{1,0:T(2,128)(2,1)S(1)}, u32[]{:S(2)}, u32[]{:S(2)}) collective-permute-start(bf16[1,1152]{1,0:T(2,128)(2,1)} %get-tuple-element.41), channel_id=1, source_target_pairs={{0,7},{1,0},{2,1},{3,2},{4,3},{5,4},{6,5},{7,6},{8,15},{9,8},{10,9... | collective-permute-start | bytes 6920 | tf_op jit(solution)/shard_map/ppermute | solution.py:139
  31.7 0.6 copy-start.8
  31.7 6.9 %collective-permute-start.7 = (bf16[1,1152]{1,0:T(2,128)(2,1)}, bf16[1,1152]{1,0:T(2,128)(2,1)S(1)}, u32[]{:S(2)}, u32[]{:S(2)}) collective-permute-start(bf16[1,1152]{1,0:T(2,128)(2,1)} %get-tuple-element.42), channel_id=1, source_target_pairs={{0,1},{1,2},{2,3},{3,4},{4,5},{5,6},{6,7},{7,0},{8,9},{9,10},{10,1... | collective-permute-start | bytes 6920 | tf_op jit(solution)/shard_map/ppermute | solution.py:140
  32.3 0.6 copy-start.11
  36.0 17.6 %collective-permute-start.16 = (bf16[2,72,128]{2,1,0:T(8,128)(2,1)}, bf16[2,72,128]{2,1,0:T(8,128)(2,1)S(1)}, u32[]{:S(2)}, u32[]{:S(2)}) collective-permute-start(bf16[2,72,128]{2,1,0:T(8,128)(2,1)} %get-tuple-element.53), channel_id=1, source_target_pairs={{0,24},{8,0},{16,8},{24,16},{1,25},{9,1},{17,9},{25,17},{2,26},{10... | collective-permute-start | bytes 110600 | tf_op jit(solution)/shard_map/ppermute | solution.py:137
  38.6 14.9 %collective-permute-start.17 = (bf16[2,72,128]{2,1,0:T(8,128)(2,1)}, bf16[2,72,128]{2,1,0:T(8,128)(2,1)S(1)}, u32[]{:S(2)}, u32[]{:S(2)}) collective-permute-start(bf16[2,72,128]{2,1,0:T(8,128)(2,1)} %get-tuple-element.54), channel_id=1, source_target_pairs={{0,8},{8,16},{16,24},{24,0},{1,9},{9,17},{17,25},{25,1},{2,10},{10... | collective-permute-start | bytes 110600 | tf_op jit(solution)/shard_map/ppermute | solution.py:138
  38.7 0.6 copy-start.19
  38.7 0.6 copy-start.7
  38.7 0.6 copy-start.10
  42.4 21.1 %collective-permute-start.8 = (bf16[2,72,128]{2,1,0:T(8,128)(2,1)}, bf16[2,72,128]{2,1,0:T(8,128)(2,1)S(1)}, u32[]{:S(2)}, u32[]{:S(2)}) collective-permute-start(bf16[2,72,128]{2,1,0:T(8,128)(2,1)} %get-tuple-element.44), channel_id=1, source_target_pairs={{0,24},{8,0},{16,8},{24,16},{1,25},{9,1},{17,9},{25,17},{2,26},{10... | collective-permute-start | bytes 110600 | tf_op jit(solution)/shard_map/ppermute | solution.py:137
  45.3 3.7 %collective-permute-start.18 = (bf16[1,1152]{1,0:T(2,128)(2,1)}, bf16[1,1152]{1,0:T(2,128)(2,1)S(1)}, u32[]{:S(2)}, u32[]{:S(2)}) collective-permute-start(bf16[1,1152]{1,0:T(2,128)(2,1)} %get-tuple-element.55), channel_id=1, source_target_pairs={{0,7},{1,0},{2,1},{3,2},{4,3},{5,4},{6,5},{7,6},{8,15},{9,8},{10,9... | collective-permute-start | bytes 6920 | tf_op jit(solution)/shard_map/ppermute | solution.py:139
  47.5 5.1 %collective-permute-start.19 = (bf16[1,1152]{1,0:T(2,128)(2,1)}, bf16[1,1152]{1,0:T(2,128)(2,1)S(1)}, u32[]{:S(2)}, u32[]{:S(2)}) collective-permute-start(bf16[1,1152]{1,0:T(2,128)(2,1)} %get-tuple-element.56), channel_id=1, source_target_pairs={{0,1},{1,2},{2,3},{3,4},{4,5},{5,6},{6,7},{7,0},{8,9},{9,10},{10,1... | collective-permute-start | bytes 6920 | tf_op jit(solution)/shard_map/ppermute | solution.py:140
  49.0 4.6 %copy-start.20 = (bf16[1,1152]{1,0:T(2,128)(2,1)}, bf16[1,1152]{1,0:T(2,128)(2,1)S(1)}, u32[]{:S(2)}) copy-start(bf16[1,1152]{1,0:T(2,128)(2,1)S(1)} %collective-permute-done.18.refs_4_) | copy-start | bytes 6916
  49.0 11.8 %collective-permute-start.10 = (bf16[1,1152]{1,0:T(2,128)(2,1)}, bf16[1,1152]{1,0:T(2,128)(2,1)S(1)}, u32[]{:S(2)}, u32[]{:S(2)}) collective-permute-start(bf16[1,1152]{1,0:T(2,128)(2,1)} %get-tuple-element.46), channel_id=1, source_target_pairs={{0,7},{1,0},{2,1},{3,2},{4,3},{5,4},{6,5},{7,6},{8,15},{9,8},{10,9... | collective-permute-start | bytes 6920 | tf_op jit(solution)/shard_map/ppermute | solution.py:139
  52.5 1.1 %copy-start.21 = (bf16[1,1152]{1,0:T(2,128)(2,1)}, bf16[1,1152]{1,0:T(2,128)(2,1)S(1)}, u32[]{:S(2)}) copy-start(bf16[1,1152]{1,0:T(2,128)(2,1)S(1)} %collective-permute-done.19.refs_5_) | copy-start | bytes 6916
  52.5 8.3 %collective-permute-start.11 = (bf16[1,1152]{1,0:T(2,128)(2,1)}, bf16[1,1152]{1,0:T(2,128)(2,1)S(1)}, u32[]{:S(2)}, u32[]{:S(2)}) collective-permute-start(bf16[1,1152]{1,0:T(2,128)(2,1)} %get-tuple-element.47), channel_id=1, source_target_pairs={{0,1},{1,2},{2,3},{3,4},{4,5},{5,6},{6,7},{7,0},{8,9},{9,10},{10,1... | collective-permute-start | bytes 6920 | tf_op jit(solution)/shard_map/ppermute | solution.py:140
  53.6 0.6 copy-start.6
  53.6 10.0 %collective-permute-start.9 = (bf16[2,72,128]{2,1,0:T(8,128)(2,1)}, bf16[2,72,128]{2,1,0:T(8,128)(2,1)S(1)}, u32[]{:S(2)}, u32[]{:S(2)}) collective-permute-start(bf16[2,72,128]{2,1,0:T(8,128)(2,1)} %get-tuple-element.45), channel_id=1, source_target_pairs={{0,8},{8,16},{16,24},{24,0},{1,9},{9,17},{17,25},{25,1},{2,10},{10... | collective-permute-start | bytes 110600 | tf_op jit(solution)/shard_map/ppermute | solution.py:138
  53.6 0.6 copy-start.9
  57.3 9.6 %collective-permute-start.22 = (bf16[1,1152]{1,0:T(2,128)(2,1)}, bf16[1,1152]{1,0:T(2,128)(2,1)S(1)}, u32[]{:S(2)}, u32[]{:S(2)}) collective-permute-start(bf16[1,1152]{1,0:T(2,128)(2,1)} %get-tuple-element.60), channel_id=1, source_target_pairs={{0,7},{1,0},{2,1},{3,2},{4,3},{5,4},{6,5},{7,6},{8,15},{9,8},{10,9... | collective-permute-start | bytes 6920 | tf_op jit(solution)/shard_map/ppermute | solution.py:139
  60.8 2.8 %copy-start.14 = (bf16[1,1152]{1,0:T(2,128)(2,1)}, bf16[1,1152]{1,0:T(2,128)(2,1)S(1)}, u32[]{:S(2)}) copy-start(bf16[1,1152]{1,0:T(2,128)(2,1)S(1)} %collective-permute-done.10.refs_4_) | copy-start | bytes 6916
  60.8 6.1 %collective-permute-start.23 = (bf16[1,1152]{1,0:T(2,128)(2,1)}, bf16[1,1152]{1,0:T(2,128)(2,1)S(1)}, u32[]{:S(2)}, u32[]{:S(2)}) collective-permute-start(bf16[1,1152]{1,0:T(2,128)(2,1)} %get-tuple-element.61), channel_id=1, source_target_pairs={{0,1},{1,2},{2,3},{3,4},{4,5},{5,6},{6,7},{7,0},{8,9},{9,10},{10,1... | collective-permute-start | bytes 6920 | tf_op jit(solution)/shard_map/ppermute | solution.py:140
  60.8 2.7 %copy-start.15 = (bf16[1,1152]{1,0:T(2,128)(2,1)}, bf16[1,1152]{1,0:T(2,128)(2,1)S(1)}, u32[]{:S(2)}) copy-start(bf16[1,1152]{1,0:T(2,128)(2,1)S(1)} %collective-permute-done.11.refs_5_) | copy-start | bytes 6916
  60.8 6.1 %collective-permute-start.20 = (bf16[2,72,128]{2,1,0:T(8,128)(2,1)}, bf16[2,72,128]{2,1,0:T(8,128)(2,1)S(1)}, u32[]{:S(2)}, u32[]{:S(2)}) collective-permute-start(bf16[2,72,128]{2,1,0:T(8,128)(2,1)} %get-tuple-element.58), channel_id=1, source_target_pairs={{0,24},{8,0},{16,8},{24,16},{1,25},{9,1},{17,9},{25,17},{2,26},{10... | collective-permute-start | bytes 110600 | tf_op jit(solution)/shard_map/ppermute | solution.py:137
  63.5 0.6 copy-start.2
  63.5 5.1 %collective-permute-start.21 = (bf16[2,72,128]{2,1,0:T(8,128)(2,1)}, bf16[2,72,128]{2,1,0:T(8,128)(2,1)S(1)}, u32[]{:S(2)}, u32[]{:S(2)}) collective-permute-start(bf16[2,72,128]{2,1,0:T(8,128)(2,1)} %get-tuple-element.59), channel_id=1, source_target_pairs={{0,8},{8,16},{16,24},{24,0},{1,9},{9,17},{17,25},{25,1},{2,10},{10... | collective-permute-start | bytes 110600 | tf_op jit(solution)/shard_map/ppermute | solution.py:138
  63.5 0.6 copy-start.3
  66.9 1.7 %copy-start.16 = (bf16[1,1152]{1,0:T(2,128)(2,1)}, bf16[1,1152]{1,0:T(2,128)(2,1)S(1)}, u32[]{:S(2)}) copy-start(bf16[1,1152]{1,0:T(2,128)(2,1)S(1)} %collective-permute-done.22.refs_4_) | copy-start | bytes 6916
  66.9 1.7 %copy-start.17 = (bf16[1,1152]{1,0:T(2,128)(2,1)}, bf16[1,1152]{1,0:T(2,128)(2,1)S(1)}, u32[]{:S(2)}) copy-start(bf16[1,1152]{1,0:T(2,128)(2,1)S(1)} %collective-permute-done.23.refs_5_) | copy-start | bytes 6916
  66.9 1.7 %copy-start.4 = (bf16[2,72,128]{2,1,0:T(8,128)(2,1)}, bf16[2,72,128]{2,1,0:T(8,128)(2,1)S(1)}, u32[]{:S(2)}) copy-start(bf16[2,72,128]{2,1,0:T(8,128)(2,1)S(1)} %collective-permute-done.20.refs_2_) | copy-start | bytes 110596
  68.6 0.6 copy-start.5
  73.1 5.7 %copy-start.1 = (bf16[16,72,72]{2,1,0:T(8,128)(2,1)S(1)}, bf16[16,72,72]{2,1,0:T(8,128)(2,1)}, u32[]{:S(2)}) copy-start(bf16[16,72,72]{2,1,0:T(8,128)(2,1)} %param.11) | copy-start | bytes 497668
  74.6 20.2 %all-to-all-start = ((bf16[4,72,8,128]{3,1,0,2:T(8,128)(2,1)}), bf16[4,72,8,128]{3,1,0,2:T(8,128)(2,1)S(1)}, u32[]{:S(2)}, u32[]{:S(2)}) async-start(bf16[4,72,8,128]{3,1,0,2:T(8,128)(2,1)} %bitcast.1), calls=%async_computation | async-start | bytes 1179648 | tf_op jit(solution)/shard_map/all_to_all | solution.py:161
  (4 other events, 2.3 us)

commit v11 on v8

--- a/solution.py
+++ b/solution.py
@@ -151,7 +151,11 @@
         halos = result[1:]
     order = jnp.argsort(destination[0])
     band_count = band_table.shape[0]
-    ordered = jnp.take(advected, order, axis=2, mode="clip")
+    rows = advected.shape[2]
+    pick = (order[:, None] == jnp.arange(rows, dtype=order.dtype)[None, :]).astype(advected.dtype)
+    ordered = jnp.einsum(
+        "jg,flgy->fljy", pick, advected, preferred_element_type=jnp.float32
+    ).astype(advected.dtype)
     received = lax.all_to_all(ordered, "tile", split_axis=2, concat_axis=2, tiled=True)
     inverse = diffusion[0]
     diffused = jnp.einsum("kl,tlxy->tkxy", inverse, received, preferred_element_type=jnp.float32)

time: 70.4 us -> 69.7 us (0.990)
  local copies, waits for them, and re-layouts: 6.02 us -> 4.33 us
  matrix products: 0.59 us -> 2.02 us
    ppermute x3, waiting for transfers between devices: 3.01 us -> 0.71 us  [exchange(): lax.ppermute(bottom, 'sec', [(i, (i + 1) % sec) for i in range(sec)])]
    ppermute x3, waiting for transfers between devices: 8.99 us -> 10.5 us  [exchange(): lax.ppermute(last, 'tile', [(i, (i + 1) % tile) for i in range(tile)])]
    gather x1 -> x0, local copies, waits for them, and re-layouts: 1.44 us -> none  [per_device(): ordered = jnp.take(advected, order, axis=2, mode='clip')]
    dot_general x0 -> x1, matrix products: none -> 1.43 us  [per_device(): jnp.einsum('jg,flgy->fljy', pick, advected, preferred_element_type=jnp.fl...]
    pallas_call x1 -> x0, local copies, waits for them, and re-layouts: 1.14 us -> none  [stencil_call(): pl.pallas_call(functools.partial(stencil_kernel, step, emit), out_shape=t...]
    ppermute x3, waiting for transfers between devices: 1.69 us -> 2.78 us  [exchange(): lax.ppermute(first, 'tile', [(i, (i - 1) % tile) for i in range(tile)])]
    dot_general x0 -> x1, local copies, waits for them, and re-layouts: none -> 0.89 us  [per_device(): jnp.einsum('jg,flgy->fljy', pick, advected, preferred_element_type=jnp.fl...]
    ppermute x3, waiting for transfers between devices: 0.8 us -> 0.01 us  [exchange(): north = lax.ppermute(top, 'sec', [(i, (i - 1) % sec) for i in range(sec)])]
where the time goes in v11:
time: 69.7 us; the launch traced here: 69.3 us
  waiting for transfers between devices  29.9 us (43%)
  starting transfers between devices  16.5 us (24%)
  Pallas kernels  14.8 us (21%)
  local copies, waits for them, and re-layouts  4.33 us (6%)
  matrix products  2.02 us (3%)
  other arithmetic  1.11 us (2%)
  between operations  0.74 us (1%)
    all_to_all x1, waiting for transfers between devices, per_device(): lax.all_to_all(ordered, 'tile', split_axis=2, concat_axis=2, tiled=True)  15.9 us
    pallas_call x4, Pallas kernels, stencil_call(): pl.pallas_call(functools.partial(stencil_kernel, step, emit), out_shape=t...  14.8 us
    ppermute x3, waiting for transfers between devices, exchange(): lax.ppermute(last, 'tile', [(i, (i + 1) % tile) for i in range(tile)])  10.5 us
    ppermute x3, starting transfers between devices, exchange(): north = lax.ppermute(top, 'sec', [(i, (i - 1) % sec) for i in range(sec)])  9.14 us
    all_to_all x1, starting transfers between devices, per_device(): lax.all_to_all(ordered, 'tile', split_axis=2, concat_axis=2, tiled=True)  3.54 us
    ppermute x3, waiting for transfers between devices, exchange(): lax.ppermute(first, 'tile', [(i, (i - 1) % tile) for i in range(tile)])  2.78 us
    ppermute x3, starting transfers between devices, exchange(): lax.ppermute(first, 'tile', [(i, (i - 1) % tile) for i in range(tile)])  2.77 us
    unnamed x30, local copies, waits for them, and re-layouts  2.54 us
  transfers between devices with their start and end apart: 13, of which 9 were waited for; matrix products, arithmetic and copies ran while one was open for 2% of the time, Pallas kernels for 0%

profile of v11, /device:TPU:0, one launch (start us, length us, event | category | flops | bytes accessed | tf_op | source)
XLA Modules:
  0.0 69.3 jit_solution(17819307834726473528)
XLA Ops:
  0.0 0.0 copy-start
  0.0 2.3 %shard_map.64 = (bf16[4,72,128]{2,1,0:T(8,128)(2,1)}, bf16[4,72,128]{2,1,0:T(8,128)(2,1)}, bf16[1,2304]{1,0:T(2,128)(2,1)}, bf16[1,2304]{1,0:T(2,128)(2,1)}) custom-call(bf16[4,72,8,128]{3,2,1,0:T(8,128)(2,1)} %refs_0_.3), custom_call_target="tpu_custom_call" | custom-call | tf_op jit(solution)/shard_map/pallas_call | solution.py:119
  2.3 3.9 %collective-permute-start = (bf16[4,72,128]{2,1,0:T(8,128)(2,1)}, bf16[4,72,128]{2,1,0:T(8,128)(2,1)S(1)}, u32[]{:S(2)}, u32[]{:S(2)}) collective-permute-start(bf16[4,72,128]{2,1,0:T(8,128)(2,1)} %get-tuple-element.20), channel_id=1, source_target_pairs={{0,24},{8,0},{16,8},{24,16},{1,25},{9,1},{17,9},{25,17},{2,26},{10... | collective-permute-start | bytes 221192 | tf_op jit(solution)/shard_map/ppermute | solution.py:137
  6.2 0.0 collective-permute-start.1
  6.2 2.8 %collective-permute-start.2 = (bf16[1,2304]{1,0:T(2,128)(2,1)}, bf16[1,2304]{1,0:T(2,128)(2,1)S(1)}, u32[]{:S(2)}, u32[]{:S(2)}) collective-permute-start(bf16[1,2304]{1,0:T(2,128)(2,1)} %get-tuple-element.22), channel_id=1, source_target_pairs={{0,7},{1,0},{2,1},{3,2},{4,3},{5,4},{6,5},{7,6},{8,15},{9,8},{10,9... | collective-permute-start | bytes 13832 | tf_op jit(solution)/shard_map/ppermute | solution.py:139
  9.0 0.0 collective-permute-start.3
  9.0 1.6 %collective-permute-done.2.refs_4_ = bf16[1,2304]{1,0:T(2,128)(2,1)S(1)} collective-permute-done((bf16[1,2304]{1,0:T(2,128)(2,1)}, bf16[1,2304]{1,0:T(2,128)(2,1)S(1)}, u32[]{:S(2)}, u32[]{:S(2)}) %collective-permute-start.2) | collective-permute-done | bytes 4640 | tf_op jit(solution)/shard_map/ppermute | solution.py:139
  10.6 3.5 %collective-permute-done.3.refs_5_ = bf16[1,2304]{1,0:T(2,128)(2,1)S(1)} collective-permute-done((bf16[1,2304]{1,0:T(2,128)(2,1)}, bf16[1,2304]{1,0:T(2,128)(2,1)S(1)}, u32[]{:S(2)}, u32[]{:S(2)}) %collective-permute-start.3) | collective-permute-done | bytes 4640 | tf_op jit(solution)/shard_map/ppermute | solution.py:140
  14.1 0.0 collective-permute-done.refs_2_
  14.1 0.0 collective-permute-done.1.refs_3_
  14.1 0.6 copy-done.13
  14.7 0.0 copy-done.4
  14.7 0.6 copy-done.7
  15.4 4.3 %shard_map.65 = (bf16[4,72,8,128]{3,2,1,0:T(8,128)(2,1)}, bf16[4,72,128]{2,1,0:T(8,128)(2,1)}, bf16[4,72,128]{2,1,0:T(8,128)(2,1)}, bf16[1,2304]{1,0:T(2,128)(2,1)}, bf16[1,2304]{1,0:T(2,128)(2,1)}) custom-call(bf16[4,72,8,128]{3,2,1,0:T(8,128)(2,1)} %refs_0_.3, bf16[2,72,8,128]{3,2,1,0:T(8,128)(2,1)} %refs_1_.5, bf16[4,72,128]{2,1,0:T(8,128)(2,1)} %copy-done.4, ...), custom_call_target="tpu_custom_call" | custom-call | tf_op jit(solution)/shard_map/pallas_call | solution.py:119
  19.7 2.6 %collective-permute-start.4 = (bf16[4,72,128]{2,1,0:T(8,128)(2,1)}, bf16[4,72,128]{2,1,0:T(8,128)(2,1)S(1)}, u32[]{:S(2)}, u32[]{:S(2)}) collective-permute-start(bf16[4,72,128]{2,1,0:T(8,128)(2,1)} %get-tuple-element.25), channel_id=1, source_target_pairs={{0,24},{8,0},{16,8},{24,16},{1,25},{9,1},{17,9},{25,17},{2,26},{10... | collective-permute-start | bytes 221192 | tf_op jit(solution)/shard_map/ppermute | solution.py:137
  22.3 0.0 collective-permute-start.5
  22.3 0.0 collective-permute-start.6
  22.3 0.5 collective-permute-start.7
  22.8 1.1 %collective-permute-done.6.refs_4_ = bf16[1,2304]{1,0:T(2,128)(2,1)S(1)} collective-permute-done((bf16[1,2304]{1,0:T(2,128)(2,1)}, bf16[1,2304]{1,0:T(2,128)(2,1)S(1)}, u32[]{:S(2)}, u32[]{:S(2)}) %collective-permute-start.6) | collective-permute-done | bytes 4640 | tf_op jit(solution)/shard_map/ppermute | solution.py:139
  23.9 3.5 %collective-permute-done.7.refs_5_ = bf16[1,2304]{1,0:T(2,128)(2,1)S(1)} collective-permute-done((bf16[1,2304]{1,0:T(2,128)(2,1)}, bf16[1,2304]{1,0:T(2,128)(2,1)S(1)}, u32[]{:S(2)}, u32[]{:S(2)}) %collective-permute-start.7) | collective-permute-done | bytes 4640 | tf_op jit(solution)/shard_map/ppermute | solution.py:140
  27.4 0.0 collective-permute-done.4.refs_2_
  27.4 0.4 collective-permute-done.5.refs_3_
  27.8 0.2 copy-done.12
  28.0 0.0 copy-done.3
  28.0 0.3 copy-done.6
  28.4 4.3 %shard_map.66 = (bf16[4,72,8,128]{3,2,1,0:T(8,128)(2,1)}, bf16[4,72,128]{2,1,0:T(8,128)(2,1)}, bf16[4,72,128]{2,1,0:T(8,128)(2,1)}, bf16[1,2304]{1,0:T(2,128)(2,1)}, bf16[1,2304]{1,0:T(2,128)(2,1)}) custom-call(bf16[4,72,8,128]{3,2,1,0:T(8,128)(2,1)} %get-tuple-element.24.refs_0_, bf16[2,72,8,128]{3,2,1,0:T(8,128)(2,1)} %refs_1_.5, ...), custom_call_target="tpu_custom_call" | custom-call | tf_op jit(solution)/shard_map/pallas_call | solution.py:119
  32.7 2.6 %collective-permute-start.8 = (bf16[4,72,128]{2,1,0:T(8,128)(2,1)}, bf16[4,72,128]{2,1,0:T(8,128)(2,1)S(1)}, u32[]{:S(2)}, u32[]{:S(2)}) collective-permute-start(bf16[4,72,128]{2,1,0:T(8,128)(2,1)} %get-tuple-element.30), channel_id=1, source_target_pairs={{0,24},{8,0},{16,8},{24,16},{1,25},{9,1},{17,9},{25,17},{2,26},{10... | collective-permute-start | bytes 221192 | tf_op jit(solution)/shard_map/ppermute | solution.py:137
  35.3 0.0 collective-permute-start.9
  35.3 0.0 collective-permute-start.10
  35.3 0.5 collective-permute-start.11
  35.8 1.0 %sort.17 = (s32[8]{0:T(128)}, s32[8]{0:T(128)S(1)}) sort(s32[8]{0:T(128)S(1)} %bitcast.29, s32[8]{0:T(128)S(1)} %iota.13), dimensions={0}, to_apply=%region_0.0 | sort | flops 24 | bytes 128 | tf_op jit(solution)/shard_map/jit(argsort)/sort | solution.py:152
  36.8 0.1 collective-permute-done.10.refs_4_
  36.9 3.5 %collective-permute-done.11.refs_5_ = bf16[1,2304]{1,0:T(2,128)(2,1)S(1)} collective-permute-done((bf16[1,2304]{1,0:T(2,128)(2,1)}, bf16[1,2304]{1,0:T(2,128)(2,1)S(1)}, u32[]{:S(2)}, u32[]{:S(2)}) %collective-permute-start.11) | collective-permute-done | bytes 4640 | tf_op jit(solution)/shard_map/ppermute | solution.py:140
  40.4 0.0 collective-permute-done.8.refs_2_
  40.4 0.4 collective-permute-done.9.refs_3_
  40.8 0.2 copy-done.9
  41.0 0.0 copy-done.2
  41.1 0.4 copy-done.5
  41.4 3.8 %shard_map.67 = bf16[4,72,8,128]{3,2,1,0:T(8,128)(2,1)} custom-call(bf16[4,72,8,128]{3,2,1,0:T(8,128)(2,1)} %get-tuple-element.29.refs_0_, bf16[2,72,8,128]{3,2,1,0:T(8,128)(2,1)} %refs_1_.5, bf16[4,72,128]{2,1,0:T(8,128)(2,1)} %copy-done.2, bf16[4,72,128]{2,1,0:T(8,128)(2,1)} %copy-done.5, bf16[1,2304]{1,0:T(2,128)(2,1)} %copy-done.8, bf16[1,2304]{1,0:T(2,128)(2,1)} %copy-done.9), custom_call_target="tpu_custom_call" | custom-call | tf_op jit(solution)/shard_map/pallas_call | solution.py:119
  45.3 1.4 %fusion.10 = bf16[4,72,128,8]{2,3,1,0:T(8,128)(2,1)S(1)} fusion(bf16[4,72,8,128]{3,2,1,0:T(8,128)(2,1)} %shard_map.67, s32[8]{0:T(128)S(1)} %get-tuple-element.34), kind=kOutput, calls=%fused_computation.14 | convolution fusion | flops 4718656 | bytes 1179680 | tf_op jit(solution)/shard_map/jg,flgy->fljy/dot_general | solution.py:156
  46.7 0.0 copy-start.1
  46.7 0.9 %copy.19 = bf16[4,72,128,8]{2,1,0,3:T(8,128)(2,1)} copy(bf16[4,72,128,8]{2,3,1,0:T(8,128)(2,1)S(1)} %fusion.10) | data formatting | bytes 1179648 | tf_op jit(solution)/shard_map/jg,flgy->fljy/dot_general | solution.py:156
  47.6 3.5 %all-to-all-start = ((bf16[4,72,8,128]{3,1,0,2:T(8,128)(2,1)}), bf16[4,72,8,128]{3,1,0,2:T(8,128)(2,1)S(1)}, u32[]{:S(2)}, u32[]{:S(2)}) async-start(bf16[4,72,8,128]{3,1,0,2:T(8,128)(2,1)} %bitcast.27), calls=%async_computation | async-start | bytes 1179648 | tf_op jit(solution)/shard_map/all_to_all | solution.py:159
  51.8 0.1 select_reduce_fusion
  52.0 15.9 %all-to-all-done = bf16[4,72,8,128]{3,1,0,2:T(8,128)(2,1)S(1)} async-done(((bf16[4,72,8,128]{3,1,0,2:T(8,128)(2,1)}), bf16[4,72,8,128]{3,1,0,2:T(8,128)(2,1)S(1)}, u32[]{:S(2)}, u32[]{:S(2)}) %all-to-all-start) | async-done | bytes 589856 | tf_op jit(solution)/shard_map/all_to_all | solution.py:159
  67.8 0.3 fusion.4
  68.1 0.3 fusion.1
  68.4 0.9 %copy.9 = bf16[4,72,8,128]{3,2,1,0:T(8,128)(2,1)} copy(bf16[4,72,8,128]{3,1,2,0:T(8,128)(2,1)S(1)} %fusion.1) | data formatting | bytes 1179648 | tf_op jit(solution)/shard_map/convert_element_type | solution.py:166
  (21 shorter events, 0.0 us)
Async XLA Ops:
  0.0 67.8 %copy-start = (bf16[1,72,72]{2,1,0:T(8,128)(2,1)S(1)}, bf16[1,72,72]{2,1,0:T(8,128)(2,1)}, u32[]{:S(2)}) copy-start(bf16[1,72,72]{2,1,0:T(8,128)(2,1)} %param.9) | copy-start | bytes 31108
  2.3 33.5 %copy-start.14 = (s32[1,8]{1,0:T(1,128)S(1)}, s32[1,8]{1,0:T(1,128)}, u32[]{:S(2)}) copy-start(s32[1,8]{1,0:T(1,128)} %param.8) | copy-start | bytes 100
  2.3 11.8 %collective-permute-start = (bf16[4,72,128]{2,1,0:T(8,128)(2,1)}, bf16[4,72,128]{2,1,0:T(8,128)(2,1)S(1)}, u32[]{:S(2)}, u32[]{:S(2)}) collective-permute-start(bf16[4,72,128]{2,1,0:T(8,128)(2,1)} %get-tuple-element.20), channel_id=1, source_target_pairs={{0,24},{8,0},{16,8},{24,16},{1,25},{9,1},{17,9},{25,17},{2,26},{10... | collective-permute-start | bytes 221192 | tf_op jit(solution)/shard_map/ppermute | solution.py:137
  6.2 7.9 %collective-permute-start.1 = (bf16[4,72,128]{2,1,0:T(8,128)(2,1)}, bf16[4,72,128]{2,1,0:T(8,128)(2,1)S(1)}, u32[]{:S(2)}, u32[]{:S(2)}) collective-permute-start(bf16[4,72,128]{2,1,0:T(8,128)(2,1)} %get-tuple-element.21), channel_id=1, source_target_pairs={{0,8},{8,16},{16,24},{24,0},{1,9},{9,17},{17,25},{25,1},{2,10},{10... | collective-permute-start | bytes 221192 | tf_op jit(solution)/shard_map/ppermute | solution.py:138
  6.2 4.3 %collective-permute-start.2 = (bf16[1,2304]{1,0:T(2,128)(2,1)}, bf16[1,2304]{1,0:T(2,128)(2,1)S(1)}, u32[]{:S(2)}, u32[]{:S(2)}) collective-permute-start(bf16[1,2304]{1,0:T(2,128)(2,1)} %get-tuple-element.22), channel_id=1, source_target_pairs={{0,7},{1,0},{2,1},{3,2},{4,3},{5,4},{6,5},{7,6},{8,15},{9,8},{10,9... | collective-permute-start | bytes 13832 | tf_op jit(solution)/shard_map/ppermute | solution.py:139
  9.0 5.1 %collective-permute-start.3 = (bf16[1,2304]{1,0:T(2,128)(2,1)}, bf16[1,2304]{1,0:T(2,128)(2,1)S(1)}, u32[]{:S(2)}, u32[]{:S(2)}) collective-permute-start(bf16[1,2304]{1,0:T(2,128)(2,1)} %get-tuple-element.23), channel_id=1, source_target_pairs={{0,1},{1,2},{2,3},{3,4},{4,5},{5,6},{6,7},{7,0},{8,9},{9,10},{10,1... | collective-permute-start | bytes 13832 | tf_op jit(solution)/shard_map/ppermute | solution.py:140
  10.6 3.5 %copy-start.11 = (bf16[1,2304]{1,0:T(2,128)(2,1)}, bf16[1,2304]{1,0:T(2,128)(2,1)S(1)}, u32[]{:S(2)}) copy-start(bf16[1,2304]{1,0:T(2,128)(2,1)S(1)} %collective-permute-done.2.refs_4_) | copy-start | bytes 13828
  14.1 0.6 copy-start.13
  14.1 0.6 copy-start.4
  14.7 0.6 copy-start.7
  19.7 7.8 %collective-permute-start.4 = (bf16[4,72,128]{2,1,0:T(8,128)(2,1)}, bf16[4,72,128]{2,1,0:T(8,128)(2,1)S(1)}, u32[]{:S(2)}, u32[]{:S(2)}) collective-permute-start(bf16[4,72,128]{2,1,0:T(8,128)(2,1)} %get-tuple-element.25), channel_id=1, source_target_pairs={{0,24},{8,0},{16,8},{24,16},{1,25},{9,1},{17,9},{25,17},{2,26},{10... | collective-permute-start | bytes 221192 | tf_op jit(solution)/shard_map/ppermute | solution.py:137
  22.3 5.5 %collective-permute-start.5 = (bf16[4,72,128]{2,1,0:T(8,128)(2,1)}, bf16[4,72,128]{2,1,0:T(8,128)(2,1)S(1)}, u32[]{:S(2)}, u32[]{:S(2)}) collective-permute-start(bf16[4,72,128]{2,1,0:T(8,128)(2,1)} %get-tuple-element.26), channel_id=1, source_target_pairs={{0,8},{8,16},{16,24},{24,0},{1,9},{9,17},{17,25},{25,1},{2,10},{10... | collective-permute-start | bytes 221192 | tf_op jit(solution)/shard_map/ppermute | solution.py:138
  22.3 1.6 %collective-permute-start.6 = (bf16[1,2304]{1,0:T(2,128)(2,1)}, bf16[1,2304]{1,0:T(2,128)(2,1)S(1)}, u32[]{:S(2)}, u32[]{:S(2)}) collective-permute-start(bf16[1,2304]{1,0:T(2,128)(2,1)} %get-tuple-element.27), channel_id=1, source_target_pairs={{0,7},{1,0},{2,1},{3,2},{4,3},{5,4},{6,5},{7,6},{8,15},{9,8},{10,9... | collective-permute-start | bytes 13832 | tf_op jit(solution)/shard_map/ppermute | solution.py:139
  22.3 5.1 %collective-permute-start.7 = (bf16[1,2304]{1,0:T(2,128)(2,1)}, bf16[1,2304]{1,0:T(2,128)(2,1)S(1)}, u32[]{:S(2)}, u32[]{:S(2)}) collective-permute-start(bf16[1,2304]{1,0:T(2,128)(2,1)} %get-tuple-element.28), channel_id=1, source_target_pairs={{0,1},{1,2},{2,3},{3,4},{4,5},{5,6},{6,7},{7,0},{8,9},{9,10},{10,1... | collective-permute-start | bytes 13832 | tf_op jit(solution)/shard_map/ppermute | solution.py:140
  23.9 3.9 %copy-start.10 = (bf16[1,2304]{1,0:T(2,128)(2,1)}, bf16[1,2304]{1,0:T(2,128)(2,1)S(1)}, u32[]{:S(2)}) copy-start(bf16[1,2304]{1,0:T(2,128)(2,1)S(1)} %collective-permute-done.6.refs_4_) | copy-start | bytes 13828
  27.4 0.6 copy-start.12
  27.4 0.6 copy-start.3
  27.8 0.6 copy-start.6
  32.7 7.7 %collective-permute-start.8 = (bf16[4,72,128]{2,1,0:T(8,128)(2,1)}, bf16[4,72,128]{2,1,0:T(8,128)(2,1)S(1)}, u32[]{:S(2)}, u32[]{:S(2)}) collective-permute-start(bf16[4,72,128]{2,1,0:T(8,128)(2,1)} %get-tuple-element.30), channel_id=1, source_target_pairs={{0,24},{8,0},{16,8},{24,16},{1,25},{9,1},{17,9},{25,17},{2,26},{10... | collective-permute-start | bytes 221192 | tf_op jit(solution)/shard_map/ppermute | solution.py:137
  35.3 5.5 %collective-permute-start.9 = (bf16[4,72,128]{2,1,0:T(8,128)(2,1)}, bf16[4,72,128]{2,1,0:T(8,128)(2,1)S(1)}, u32[]{:S(2)}, u32[]{:S(2)}) collective-permute-start(bf16[4,72,128]{2,1,0:T(8,128)(2,1)} %get-tuple-element.31), channel_id=1, source_target_pairs={{0,8},{8,16},{16,24},{24,0},{1,9},{9,17},{17,25},{25,1},{2,10},{10... | collective-permute-start | bytes 221192 | tf_op jit(solution)/shard_map/ppermute | solution.py:138
  35.3 1.6 %collective-permute-start.10 = (bf16[1,2304]{1,0:T(2,128)(2,1)}, bf16[1,2304]{1,0:T(2,128)(2,1)S(1)}, u32[]{:S(2)}, u32[]{:S(2)}) collective-permute-start(bf16[1,2304]{1,0:T(2,128)(2,1)} %get-tuple-element.32), channel_id=1, source_target_pairs={{0,7},{1,0},{2,1},{3,2},{4,3},{5,4},{6,5},{7,6},{8,15},{9,8},{10,9... | collective-permute-start | bytes 13832 | tf_op jit(solution)/shard_map/ppermute | solution.py:139
  35.3 5.1 %collective-permute-start.11 = (bf16[1,2304]{1,0:T(2,128)(2,1)}, bf16[1,2304]{1,0:T(2,128)(2,1)S(1)}, u32[]{:S(2)}, u32[]{:S(2)}) collective-permute-start(bf16[1,2304]{1,0:T(2,128)(2,1)} %get-tuple-element.33), channel_id=1, source_target_pairs={{0,1},{1,2},{2,3},{3,4},{4,5},{5,6},{6,7},{7,0},{8,9},{9,10},{10,1... | collective-permute-start | bytes 13832 | tf_op jit(solution)/shard_map/ppermute | solution.py:140
  36.9 3.9 %copy-start.8 = (bf16[1,2304]{1,0:T(2,128)(2,1)}, bf16[1,2304]{1,0:T(2,128)(2,1)S(1)}, u32[]{:S(2)}) copy-start(bf16[1,2304]{1,0:T(2,128)(2,1)S(1)} %collective-permute-done.10.refs_4_) | copy-start | bytes 13828
  40.4 0.6 copy-start.9
  40.4 0.6 copy-start.2
  40.8 0.6 copy-start.5
  46.7 5.1 %copy-start.1 = (bf16[16,72,72]{2,1,0:T(8,128)(2,1)S(1)}, bf16[16,72,72]{2,1,0:T(8,128)(2,1)}, u32[]{:S(2)}) copy-start(bf16[16,72,72]{2,1,0:T(8,128)(2,1)} %param.11) | copy-start | bytes 497668
  47.6 20.2 %all-to-all-start = ((bf16[4,72,8,128]{3,1,0,2:T(8,128)(2,1)}), bf16[4,72,8,128]{3,1,0,2:T(8,128)(2,1)S(1)}, u32[]{:S(2)}, u32[]{:S(2)}) async-start(bf16[4,72,8,128]{3,1,0,2:T(8,128)(2,1)} %bitcast.27), calls=%async_computation | async-start | bytes 1179648 | tf_op jit(solution)/shard_map/all_to_all | solution.py:159

commit v12 on v11

--- a/solution.py
+++ b/solution.py
@@ -10,7 +10,7 @@
 STEPS = 3
 
 
-LEVEL_BLOCK = 8
+LEVEL_BLOCK = 4
 
 
 def stencil_kernel(step, emit, *refs):

time: 69.7 us -> 69.8 us (level)
  no operation moved by 1% of the time
where the time goes in v12:
time: 69.8 us; the launch traced here: 69.5 us
  waiting for transfers between devices  29.9 us (43%)
  starting transfers between devices  16.5 us (24%)
  Pallas kernels  14.9 us (21%)
  local copies, waits for them, and re-layouts  4.33 us (6%)
  matrix products  2.03 us (3%)
  other arithmetic  1.11 us (2%)
  between operations  0.74 us (1%)
    all_to_all x1, waiting for transfers between devices, per_device(): lax.all_to_all(ordered, 'tile', split_axis=2, concat_axis=2, tiled=True)  15.9 us
    pallas_call x4, Pallas kernels, stencil_call(): pl.pallas_call(functools.partial(stencil_kernel, step, emit), out_shape=t...  14.9 us
    ppermute x3, waiting for transfers between devices, exchange(): lax.ppermute(last, 'tile', [(i, (i + 1) % tile) for i in range(tile)])  10.5 us
    ppermute x3, starting transfers between devices, exchange(): north = lax.ppermute(top, 'sec', [(i, (i - 1) % sec) for i in range(sec)])  9.14 us
    all_to_all x1, starting transfers between devices, per_device(): lax.all_to_all(ordered, 'tile', split_axis=2, concat_axis=2, tiled=True)  3.54 us
    ppermute x3, waiting for transfers between devices, exchange(): lax.ppermute(first, 'tile', [(i, (i - 1) % tile) for i in range(tile)])  2.78 us
    ppermute x3, starting transfers between devices, exchange(): lax.ppermute(first, 'tile', [(i, (i - 1) % tile) for i in range(tile)])  2.77 us
    unnamed x30, local copies, waits for them, and re-layouts  2.54 us
  transfers between devices with their start and end apart: 13, of which 9 were waited for; matrix products, arithmetic and copies ran while one was open for 2% of the time, Pallas kernels for 0%

profile of v12, /device:TPU:0, one launch (start us, length us, event | category | flops | bytes accessed | tf_op | source)
XLA Modules:
  0.0 69.5 jit_solution(17202180610493422407)
XLA Ops:
  0.0 2.3 %shard_map.64 = (bf16[4,72,128]{2,1,0:T(8,128)(2,1)}, bf16[4,72,128]{2,1,0:T(8,128)(2,1)}, bf16[1,2304]{1,0:T(2,128)(2,1)}, bf16[1,2304]{1,0:T(2,128)(2,1)}) custom-call(bf16[4,72,8,128]{3,2,1,0:T(8,128)(2,1)} %refs_0_.3), custom_call_target="tpu_custom_call" | custom-call | tf_op jit(solution)/shard_map/pallas_call | solution.py:119
  2.3 3.9 %collective-permute-start = (bf16[4,72,128]{2,1,0:T(8,128)(2,1)}, bf16[4,72,128]{2,1,0:T(8,128)(2,1)S(1)}, u32[]{:S(2)}, u32[]{:S(2)}) collective-permute-start(bf16[4,72,128]{2,1,0:T(8,128)(2,1)} %get-tuple-element.20), channel_id=1, source_target_pairs={{0,24},{8,0},{16,8},{24,16},{1,25},{9,1},{17,9},{25,17},{2,26},{10... | collective-permute-start | bytes 221192 | tf_op jit(solution)/shard_map/ppermute | solution.py:137
  6.2 0.0 collective-permute-start.1
  6.2 2.8 %collective-permute-start.2 = (bf16[1,2304]{1,0:T(2,128)(2,1)}, bf16[1,2304]{1,0:T(2,128)(2,1)S(1)}, u32[]{:S(2)}, u32[]{:S(2)}) collective-permute-start(bf16[1,2304]{1,0:T(2,128)(2,1)} %get-tuple-element.22), channel_id=1, source_target_pairs={{0,7},{1,0},{2,1},{3,2},{4,3},{5,4},{6,5},{7,6},{8,15},{9,8},{10,9... | collective-permute-start | bytes 13832 | tf_op jit(solution)/shard_map/ppermute | solution.py:139
  9.0 0.0 collective-permute-start.3
  9.0 1.6 %collective-permute-done.2.refs_4_ = bf16[1,2304]{1,0:T(2,128)(2,1)S(1)} collective-permute-done((bf16[1,2304]{1,0:T(2,128)(2,1)}, bf16[1,2304]{1,0:T(2,128)(2,1)S(1)}, u32[]{:S(2)}, u32[]{:S(2)}) %collective-permute-start.2) | collective-permute-done | bytes 4640 | tf_op jit(solution)/shard_map/ppermute | solution.py:139
  10.6 3.5 %collective-permute-done.3.refs_5_ = bf16[1,2304]{1,0:T(2,128)(2,1)S(1)} collective-permute-done((bf16[1,2304]{1,0:T(2,128)(2,1)}, bf16[1,2304]{1,0:T(2,128)(2,1)S(1)}, u32[]{:S(2)}, u32[]{:S(2)}) %collective-permute-start.3) | collective-permute-done | bytes 4640 | tf_op jit(solution)/shard_map/ppermute | solution.py:140
  14.1 0.0 collective-permute-done.refs_2_
  14.1 0.0 collective-permute-done.1.refs_3_
  14.1 0.6 copy-done.13
  14.7 0.0 copy-done.4
  14.7 0.6 copy-done.7
  15.4 4.4 %shard_map.65 = (bf16[4,72,8,128]{3,2,1,0:T(8,128)(2,1)}, bf16[4,72,128]{2,1,0:T(8,128)(2,1)}, bf16[4,72,128]{2,1,0:T(8,128)(2,1)}, bf16[1,2304]{1,0:T(2,128)(2,1)}, bf16[1,2304]{1,0:T(2,128)(2,1)}) custom-call(bf16[4,72,8,128]{3,2,1,0:T(8,128)(2,1)} %refs_0_.3, bf16[2,72,8,128]{3,2,1,0:T(8,128)(2,1)} %refs_1_.5, bf16[4,72,128]{2,1,0:T(8,128)(2,1)} %copy-done.4, ...), custom_call_target="tpu_custom_call" | custom-call | tf_op jit(solution)/shard_map/pallas_call | solution.py:119
  19.7 2.6 %collective-permute-start.4 = (bf16[4,72,128]{2,1,0:T(8,128)(2,1)}, bf16[4,72,128]{2,1,0:T(8,128)(2,1)S(1)}, u32[]{:S(2)}, u32[]{:S(2)}) collective-permute-start(bf16[4,72,128]{2,1,0:T(8,128)(2,1)} %get-tuple-element.25), channel_id=1, source_target_pairs={{0,24},{8,0},{16,8},{24,16},{1,25},{9,1},{17,9},{25,17},{2,26},{10... | collective-permute-start | bytes 221192 | tf_op jit(solution)/shard_map/ppermute | solution.py:137
  22.4 0.0 collective-permute-start.5
  22.4 0.0 collective-permute-start.6
  22.4 0.5 collective-permute-start.7
  22.9 1.1 %collective-permute-done.6.refs_4_ = bf16[1,2304]{1,0:T(2,128)(2,1)S(1)} collective-permute-done((bf16[1,2304]{1,0:T(2,128)(2,1)}, bf16[1,2304]{1,0:T(2,128)(2,1)S(1)}, u32[]{:S(2)}, u32[]{:S(2)}) %collective-permute-start.6) | collective-permute-done | bytes 4640 | tf_op jit(solution)/shard_map/ppermute | solution.py:139
  24.0 3.5 %collective-permute-done.7.refs_5_ = bf16[1,2304]{1,0:T(2,128)(2,1)S(1)} collective-permute-done((bf16[1,2304]{1,0:T(2,128)(2,1)}, bf16[1,2304]{1,0:T(2,128)(2,1)S(1)}, u32[]{:S(2)}, u32[]{:S(2)}) %collective-permute-start.7) | collective-permute-done | bytes 4640 | tf_op jit(solution)/shard_map/ppermute | solution.py:140
  27.5 0.0 collective-permute-done.4.refs_2_
  27.5 0.4 collective-permute-done.5.refs_3_
  27.8 0.2 copy-done.12
  28.1 0.0 copy-done.3
  28.1 0.3 copy-done.6
  28.4 4.4 %shard_map.66 = (bf16[4,72,8,128]{3,2,1,0:T(8,128)(2,1)}, bf16[4,72,128]{2,1,0:T(8,128)(2,1)}, bf16[4,72,128]{2,1,0:T(8,128)(2,1)}, bf16[1,2304]{1,0:T(2,128)(2,1)}, bf16[1,2304]{1,0:T(2,128)(2,1)}) custom-call(bf16[4,72,8,128]{3,2,1,0:T(8,128)(2,1)} %get-tuple-element.24.refs_0_, bf16[2,72,8,128]{3,2,1,0:T(8,128)(2,1)} %refs_1_.5, ...), custom_call_target="tpu_custom_call" | custom-call | tf_op jit(solution)/shard_map/pallas_call | solution.py:119
  32.8 2.6 %collective-permute-start.8 = (bf16[4,72,128]{2,1,0:T(8,128)(2,1)}, bf16[4,72,128]{2,1,0:T(8,128)(2,1)S(1)}, u32[]{:S(2)}, u32[]{:S(2)}) collective-permute-start(bf16[4,72,128]{2,1,0:T(8,128)(2,1)} %get-tuple-element.30), channel_id=1, source_target_pairs={{0,24},{8,0},{16,8},{24,16},{1,25},{9,1},{17,9},{25,17},{2,26},{10... | collective-permute-start | bytes 221192 | tf_op jit(solution)/shard_map/ppermute | solution.py:137
  35.4 0.0 collective-permute-start.9
  35.4 0.0 collective-permute-start.10
  35.4 0.5 collective-permute-start.11
  36.0 0.0 copy-done.14
  36.0 1.0 %sort.17 = (s32[8]{0:T(128)}, s32[8]{0:T(128)S(1)}) sort(s32[8]{0:T(128)S(1)} %bitcast.29, s32[8]{0:T(128)S(1)} %iota.13), dimensions={0}, to_apply=%region_0.0 | sort | flops 24 | bytes 128 | tf_op jit(solution)/shard_map/jit(argsort)/sort | solution.py:152
  36.9 0.1 collective-permute-done.10.refs_4_
  37.0 3.5 %collective-permute-done.11.refs_5_ = bf16[1,2304]{1,0:T(2,128)(2,1)S(1)} collective-permute-done((bf16[1,2304]{1,0:T(2,128)(2,1)}, bf16[1,2304]{1,0:T(2,128)(2,1)S(1)}, u32[]{:S(2)}, u32[]{:S(2)}) %collective-permute-start.11) | collective-permute-done | bytes 4640 | tf_op jit(solution)/shard_map/ppermute | solution.py:140
  40.5 0.0 collective-permute-done.8.refs_2_
  40.5 0.4 collective-permute-done.9.refs_3_
  40.9 0.2 copy-done.9
  41.1 0.0 copy-done.2
  41.2 0.4 copy-done.5
  41.5 3.9 %shard_map.67 = bf16[4,72,8,128]{3,2,1,0:T(8,128)(2,1)} custom-call(bf16[4,72,8,128]{3,2,1,0:T(8,128)(2,1)} %get-tuple-element.29.refs_0_, bf16[2,72,8,128]{3,2,1,0:T(8,128)(2,1)} %refs_1_.5, bf16[4,72,128]{2,1,0:T(8,128)(2,1)} %copy-done.2, bf16[4,72,128]{2,1,0:T(8,128)(2,1)} %copy-done.5, bf16[1,2304]{1,0:T(2,128)(2,1)} %copy-done.8, bf16[1,2304]{1,0:T(2,128)(2,1)} %copy-done.9), custom_call_target="tpu_custom_call" | custom-call | tf_op jit(solution)/shard_map/pallas_call | solution.py:119
  45.4 1.4 %fusion.10 = bf16[4,72,128,8]{2,3,1,0:T(8,128)(2,1)S(1)} fusion(bf16[4,72,8,128]{3,2,1,0:T(8,128)(2,1)} %shard_map.67, s32[8]{0:T(128)S(1)} %get-tuple-element.34), kind=kOutput, calls=%fused_computation.14 | convolution fusion | flops 4718656 | bytes 1179680 | tf_op jit(solution)/shard_map/jg,flgy->fljy/dot_general | solution.py:156
  46.9 0.0 copy-start.1
  46.9 0.9 %copy.19 = bf16[4,72,128,8]{2,1,0,3:T(8,128)(2,1)} copy(bf16[4,72,128,8]{2,3,1,0:T(8,128)(2,1)S(1)} %fusion.10) | data formatting | bytes 1179648 | tf_op jit(solution)/shard_map/jg,flgy->fljy/dot_general | solution.py:156
  47.8 3.5 %all-to-all-start = ((bf16[4,72,8,128]{3,1,0,2:T(8,128)(2,1)}), bf16[4,72,8,128]{3,1,0,2:T(8,128)(2,1)S(1)}, u32[]{:S(2)}, u32[]{:S(2)}) async-start(bf16[4,72,8,128]{3,1,0,2:T(8,128)(2,1)} %bitcast.27), calls=%async_computation | async-start | bytes 1179648 | tf_op jit(solution)/shard_map/all_to_all | solution.py:159
  52.0 0.1 select_reduce_fusion
  52.1 15.9 %all-to-all-done = bf16[4,72,8,128]{3,1,0,2:T(8,128)(2,1)S(1)} async-done(((bf16[4,72,8,128]{3,1,0,2:T(8,128)(2,1)}), bf16[4,72,8,128]{3,1,0,2:T(8,128)(2,1)S(1)}, u32[]{:S(2)}, u32[]{:S(2)}) %all-to-all-start) | async-done | bytes 589856 | tf_op jit(solution)/shard_map/all_to_all | solution.py:159
  68.0 0.3 fusion.4
  68.3 0.3 fusion.1
  68.6 0.9 %copy.9 = bf16[4,72,8,128]{3,2,1,0:T(8,128)(2,1)} copy(bf16[4,72,8,128]{3,1,2,0:T(8,128)(2,1)S(1)} %fusion.1) | data formatting | bytes 1179648 | tf_op jit(solution)/shard_map/convert_element_type | solution.py:166
  (21 shorter events, 0.0 us)
Async XLA Ops:
  0.0 68.0 %copy-start = (bf16[1,72,72]{2,1,0:T(8,128)(2,1)S(1)}, bf16[1,72,72]{2,1,0:T(8,128)(2,1)}, u32[]{:S(2)}) copy-start(bf16[1,72,72]{2,1,0:T(8,128)(2,1)} %param.9) | copy-start | bytes 31108
  2.3 33.6 %copy-start.14 = (s32[1,8]{1,0:T(1,128)S(1)}, s32[1,8]{1,0:T(1,128)}, u32[]{:S(2)}) copy-start(s32[1,8]{1,0:T(1,128)} %param.8) | copy-start | bytes 100
  2.3 11.8 %collective-permute-start = (bf16[4,72,128]{2,1,0:T(8,128)(2,1)}, bf16[4,72,128]{2,1,0:T(8,128)(2,1)S(1)}, u32[]{:S(2)}, u32[]{:S(2)}) collective-permute-start(bf16[4,72,128]{2,1,0:T(8,128)(2,1)} %get-tuple-element.20), channel_id=1, source_target_pairs={{0,24},{8,0},{16,8},{24,16},{1,25},{9,1},{17,9},{25,17},{2,26},{10... | collective-permute-start | bytes 221192 | tf_op jit(solution)/shard_map/ppermute | solution.py:137
  6.2 7.9 %collective-permute-start.1 = (bf16[4,72,128]{2,1,0:T(8,128)(2,1)}, bf16[4,72,128]{2,1,0:T(8,128)(2,1)S(1)}, u32[]{:S(2)}, u32[]{:S(2)}) collective-permute-start(bf16[4,72,128]{2,1,0:T(8,128)(2,1)} %get-tuple-element.21), channel_id=1, source_target_pairs={{0,8},{8,16},{16,24},{24,0},{1,9},{9,17},{17,25},{25,1},{2,10},{10... | collective-permute-start | bytes 221192 | tf_op jit(solution)/shard_map/ppermute | solution.py:138
  6.2 4.3 %collective-permute-start.2 = (bf16[1,2304]{1,0:T(2,128)(2,1)}, bf16[1,2304]{1,0:T(2,128)(2,1)S(1)}, u32[]{:S(2)}, u32[]{:S(2)}) collective-permute-start(bf16[1,2304]{1,0:T(2,128)(2,1)} %get-tuple-element.22), channel_id=1, source_target_pairs={{0,7},{1,0},{2,1},{3,2},{4,3},{5,4},{6,5},{7,6},{8,15},{9,8},{10,9... | collective-permute-start | bytes 13832 | tf_op jit(solution)/shard_map/ppermute | solution.py:139
  9.0 5.1 %collective-permute-start.3 = (bf16[1,2304]{1,0:T(2,128)(2,1)}, bf16[1,2304]{1,0:T(2,128)(2,1)S(1)}, u32[]{:S(2)}, u32[]{:S(2)}) collective-permute-start(bf16[1,2304]{1,0:T(2,128)(2,1)} %get-tuple-element.23), channel_id=1, source_target_pairs={{0,1},{1,2},{2,3},{3,4},{4,5},{5,6},{6,7},{7,0},{8,9},{9,10},{10,1... | collective-permute-start | bytes 13832 | tf_op jit(solution)/shard_map/ppermute | solution.py:140
  10.6 3.5 %copy-start.11 = (bf16[1,2304]{1,0:T(2,128)(2,1)}, bf16[1,2304]{1,0:T(2,128)(2,1)S(1)}, u32[]{:S(2)}) copy-start(bf16[1,2304]{1,0:T(2,128)(2,1)S(1)} %collective-permute-done.2.refs_4_) | copy-start | bytes 13828
  14.1 0.6 copy-start.13
  14.1 0.6 copy-start.4
  14.7 0.6 copy-start.7
  19.7 7.8 %collective-permute-start.4 = (bf16[4,72,128]{2,1,0:T(8,128)(2,1)}, bf16[4,72,128]{2,1,0:T(8,128)(2,1)S(1)}, u32[]{:S(2)}, u32[]{:S(2)}) collective-permute-start(bf16[4,72,128]{2,1,0:T(8,128)(2,1)} %get-tuple-element.25), channel_id=1, source_target_pairs={{0,24},{8,0},{16,8},{24,16},{1,25},{9,1},{17,9},{25,17},{2,26},{10... | collective-permute-start | bytes 221192 | tf_op jit(solution)/shard_map/ppermute | solution.py:137
  22.4 5.5 %collective-permute-start.5 = (bf16[4,72,128]{2,1,0:T(8,128)(2,1)}, bf16[4,72,128]{2,1,0:T(8,128)(2,1)S(1)}, u32[]{:S(2)}, u32[]{:S(2)}) collective-permute-start(bf16[4,72,128]{2,1,0:T(8,128)(2,1)} %get-tuple-element.26), channel_id=1, source_target_pairs={{0,8},{8,16},{16,24},{24,0},{1,9},{9,17},{17,25},{25,1},{2,10},{10... | collective-permute-start | bytes 221192 | tf_op jit(solution)/shard_map/ppermute | solution.py:138
  22.4 1.6 %collective-permute-start.6 = (bf16[1,2304]{1,0:T(2,128)(2,1)}, bf16[1,2304]{1,0:T(2,128)(2,1)S(1)}, u32[]{:S(2)}, u32[]{:S(2)}) collective-permute-start(bf16[1,2304]{1,0:T(2,128)(2,1)} %get-tuple-element.27), channel_id=1, source_target_pairs={{0,7},{1,0},{2,1},{3,2},{4,3},{5,4},{6,5},{7,6},{8,15},{9,8},{10,9... | collective-permute-start | bytes 13832 | tf_op jit(solution)/shard_map/ppermute | solution.py:139
  22.4 5.1 %collective-permute-start.7 = (bf16[1,2304]{1,0:T(2,128)(2,1)}, bf16[1,2304]{1,0:T(2,128)(2,1)S(1)}, u32[]{:S(2)}, u32[]{:S(2)}) collective-permute-start(bf16[1,2304]{1,0:T(2,128)(2,1)} %get-tuple-element.28), channel_id=1, source_target_pairs={{0,1},{1,2},{2,3},{3,4},{4,5},{5,6},{6,7},{7,0},{8,9},{9,10},{10,1... | collective-permute-start | bytes 13832 | tf_op jit(solution)/shard_map/ppermute | solution.py:140
  24.0 3.9 %copy-start.10 = (bf16[1,2304]{1,0:T(2,128)(2,1)}, bf16[1,2304]{1,0:T(2,128)(2,1)S(1)}, u32[]{:S(2)}) copy-start(bf16[1,2304]{1,0:T(2,128)(2,1)S(1)} %collective-permute-done.6.refs_4_) | copy-start | bytes 13828
  27.5 0.6 copy-start.12
  27.5 0.6 copy-start.3
  27.8 0.6 copy-start.6
  32.8 7.7 %collective-permute-start.8 = (bf16[4,72,128]{2,1,0:T(8,128)(2,1)}, bf16[4,72,128]{2,1,0:T(8,128)(2,1)S(1)}, u32[]{:S(2)}, u32[]{:S(2)}) collective-permute-start(bf16[4,72,128]{2,1,0:T(8,128)(2,1)} %get-tuple-element.30), channel_id=1, source_target_pairs={{0,24},{8,0},{16,8},{24,16},{1,25},{9,1},{17,9},{25,17},{2,26},{10... | collective-permute-start | bytes 221192 | tf_op jit(solution)/shard_map/ppermute | solution.py:137
  35.4 5.5 %collective-permute-start.9 = (bf16[4,72,128]{2,1,0:T(8,128)(2,1)}, bf16[4,72,128]{2,1,0:T(8,128)(2,1)S(1)}, u32[]{:S(2)}, u32[]{:S(2)}) collective-permute-start(bf16[4,72,128]{2,1,0:T(8,128)(2,1)} %get-tuple-element.31), channel_id=1, source_target_pairs={{0,8},{8,16},{16,24},{24,0},{1,9},{9,17},{17,25},{25,1},{2,10},{10... | collective-permute-start | bytes 221192 | tf_op jit(solution)/shard_map/ppermute | solution.py:138
  35.4 1.6 %collective-permute-start.10 = (bf16[1,2304]{1,0:T(2,128)(2,1)}, bf16[1,2304]{1,0:T(2,128)(2,1)S(1)}, u32[]{:S(2)}, u32[]{:S(2)}) collective-permute-start(bf16[1,2304]{1,0:T(2,128)(2,1)} %get-tuple-element.32), channel_id=1, source_target_pairs={{0,7},{1,0},{2,1},{3,2},{4,3},{5,4},{6,5},{7,6},{8,15},{9,8},{10,9... | collective-permute-start | bytes 13832 | tf_op jit(solution)/shard_map/ppermute | solution.py:139
  35.4 5.1 %collective-permute-start.11 = (bf16[1,2304]{1,0:T(2,128)(2,1)}, bf16[1,2304]{1,0:T(2,128)(2,1)S(1)}, u32[]{:S(2)}, u32[]{:S(2)}) collective-permute-start(bf16[1,2304]{1,0:T(2,128)(2,1)} %get-tuple-element.33), channel_id=1, source_target_pairs={{0,1},{1,2},{2,3},{3,4},{4,5},{5,6},{6,7},{7,0},{8,9},{9,10},{10,1... | collective-permute-start | bytes 13832 | tf_op jit(solution)/shard_map/ppermute | solution.py:140
  37.0 3.9 %copy-start.8 = (bf16[1,2304]{1,0:T(2,128)(2,1)}, bf16[1,2304]{1,0:T(2,128)(2,1)S(1)}, u32[]{:S(2)}) copy-start(bf16[1,2304]{1,0:T(2,128)(2,1)S(1)} %collective-permute-done.10.refs_4_) | copy-start | bytes 13828
  40.5 0.6 copy-start.9
  40.5 0.6 copy-start.2
  40.9 0.6 copy-start.5
  46.9 5.1 %copy-start.1 = (bf16[16,72,72]{2,1,0:T(8,128)(2,1)S(1)}, bf16[16,72,72]{2,1,0:T(8,128)(2,1)}, u32[]{:S(2)}) copy-start(bf16[16,72,72]{2,1,0:T(8,128)(2,1)} %param.11) | copy-start | bytes 497668
  47.8 20.2 %all-to-all-start = ((bf16[4,72,8,128]{3,1,0,2:T(8,128)(2,1)}), bf16[4,72,8,128]{3,1,0,2:T(8,128)(2,1)S(1)}, u32[]{:S(2)}, u32[]{:S(2)}) async-start(bf16[4,72,8,128]{3,1,0,2:T(8,128)(2,1)} %bitcast.27), calls=%async_computation | async-start | bytes 1179648 | tf_op jit(solution)/shard_map/all_to_all | solution.py:159

commit v13 on v12

--- a/solution.py
+++ b/solution.py
@@ -83,12 +83,16 @@
                 new = out.astype(jnp.bfloat16)
                 out_ref[field, levels_here] = new
                 if emit:
-                    new_scr[levels_here] = new.astype(jnp.float32)
+                    widened = new.astype(jnp.float32)
+                    new_scr[levels_here] = widened
+                    top_ref[field, levels_here] = widened[:, 0, :].astype(top_ref.dtype)
+                    bottom_ref[field, levels_here] = widened[:, rows - 1, :].astype(bottom_ref.dtype)
         elif emit:
             new_scr[...] = q_ref[field].astype(jnp.float32)
-        if emit:
+        if emit and not step:
             top_ref[field] = new_scr[:, 0, :].astype(top_ref.dtype)
             bottom_ref[field] = new_scr[:, rows - 1, :].astype(bottom_ref.dtype)
+        if emit:
             flat = new_scr[...].reshape(planes, cols).astype(jnp.bfloat16)
             pick = lax.broadcasted_iota(jnp.int32, (8, cols), 1)
             which = lax.broadcasted_iota(jnp.int32, (8, cols), 0)

time: 69.8 us -> 69.6 us (level)
  no operation moved by 1% of the time
where the time goes in v13:
time: 69.6 us; the launch traced here: 69.3 us
  waiting for transfers between devices  29.9 us (43%)
  starting transfers between devices  16.5 us (24%)
  Pallas kernels  14.7 us (21%)
  local copies, waits for them, and re-layouts  4.33 us (6%)
  matrix products  2.02 us (3%)
  other arithmetic  1.11 us (2%)
  between operations  0.74 us (1%)
    all_to_all x1, waiting for transfers between devices, per_device(): lax.all_to_all(ordered, 'tile', split_axis=2, concat_axis=2, tiled=True)  15.9 us
    pallas_call x4, Pallas kernels, stencil_call(): pl.pallas_call(functools.partial(stencil_kernel, step, emit), out_shape=t...  14.7 us
    ppermute x3, waiting for transfers between devices, exchange(): lax.ppermute(last, 'tile', [(i, (i + 1) % tile) for i in range(tile)])  10.5 us
    ppermute x3, starting transfers between devices, exchange(): north = lax.ppermute(top, 'sec', [(i, (i - 1) % sec) for i in range(sec)])  9.14 us
    all_to_all x1, starting transfers between devices, per_device(): lax.all_to_all(ordered, 'tile', split_axis=2, concat_axis=2, tiled=True)  3.54 us
    ppermute x3, waiting for transfers between devices, exchange(): lax.ppermute(first, 'tile', [(i, (i - 1) % tile) for i in range(tile)])  2.78 us
    ppermute x3, starting transfers between devices, exchange(): lax.ppermute(first, 'tile', [(i, (i - 1) % tile) for i in range(tile)])  2.77 us
    unnamed x30, local copies, waits for them, and re-layouts  2.54 us
  transfers between devices with their start and end apart: 13, of which 9 were waited for; matrix products, arithmetic and copies ran while one was open for 2% of the time, Pallas kernels for 0%

profile of v13, /device:TPU:0, one launch (start us, length us, event | category | flops | bytes accessed | tf_op | source)
XLA Modules:
  0.0 69.3 jit_solution(1394066052541980052)
XLA Ops:
  0.0 0.0 copy-start
  0.0 2.3 %shard_map.64 = (bf16[4,72,128]{2,1,0:T(8,128)(2,1)}, bf16[4,72,128]{2,1,0:T(8,128)(2,1)}, bf16[1,2304]{1,0:T(2,128)(2,1)}, bf16[1,2304]{1,0:T(2,128)(2,1)}) custom-call(bf16[4,72,8,128]{3,2,1,0:T(8,128)(2,1)} %refs_0_.3), custom_call_target="tpu_custom_call" | custom-call | tf_op jit(solution)/shard_map/pallas_call | solution.py:123
  2.3 3.9 %collective-permute-start = (bf16[4,72,128]{2,1,0:T(8,128)(2,1)}, bf16[4,72,128]{2,1,0:T(8,128)(2,1)S(1)}, u32[]{:S(2)}, u32[]{:S(2)}) collective-permute-start(bf16[4,72,128]{2,1,0:T(8,128)(2,1)} %get-tuple-element.20), channel_id=1, source_target_pairs={{0,24},{8,0},{16,8},{24,16},{1,25},{9,1},{17,9},{25,17},{2,26},{10... | collective-permute-start | bytes 221192 | tf_op jit(solution)/shard_map/ppermute | solution.py:141
  6.2 0.0 collective-permute-start.1
  6.2 2.8 %collective-permute-start.2 = (bf16[1,2304]{1,0:T(2,128)(2,1)}, bf16[1,2304]{1,0:T(2,128)(2,1)S(1)}, u32[]{:S(2)}, u32[]{:S(2)}) collective-permute-start(bf16[1,2304]{1,0:T(2,128)(2,1)} %get-tuple-element.22), channel_id=1, source_target_pairs={{0,7},{1,0},{2,1},{3,2},{4,3},{5,4},{6,5},{7,6},{8,15},{9,8},{10,9... | collective-permute-start | bytes 13832 | tf_op jit(solution)/shard_map/ppermute | solution.py:143
  9.0 0.0 collective-permute-start.3
  9.0 1.6 %collective-permute-done.2.refs_4_ = bf16[1,2304]{1,0:T(2,128)(2,1)S(1)} collective-permute-done((bf16[1,2304]{1,0:T(2,128)(2,1)}, bf16[1,2304]{1,0:T(2,128)(2,1)S(1)}, u32[]{:S(2)}, u32[]{:S(2)}) %collective-permute-start.2) | collective-permute-done | bytes 4640 | tf_op jit(solution)/shard_map/ppermute | solution.py:143
  10.6 3.5 %collective-permute-done.3.refs_5_ = bf16[1,2304]{1,0:T(2,128)(2,1)S(1)} collective-permute-done((bf16[1,2304]{1,0:T(2,128)(2,1)}, bf16[1,2304]{1,0:T(2,128)(2,1)S(1)}, u32[]{:S(2)}, u32[]{:S(2)}) %collective-permute-start.3) | collective-permute-done | bytes 4640 | tf_op jit(solution)/shard_map/ppermute | solution.py:144
  14.1 0.0 collective-permute-done.refs_2_
  14.1 0.0 collective-permute-done.1.refs_3_
  14.1 0.6 copy-done.13
  14.7 0.0 copy-done.4
  14.7 0.6 copy-done.7
  15.4 4.2 %shard_map.65 = (bf16[4,72,8,128]{3,2,1,0:T(8,128)(2,1)}, bf16[4,72,128]{2,1,0:T(8,128)(2,1)}, bf16[4,72,128]{2,1,0:T(8,128)(2,1)}, bf16[1,2304]{1,0:T(2,128)(2,1)}, bf16[1,2304]{1,0:T(2,128)(2,1)}) custom-call(bf16[4,72,8,128]{3,2,1,0:T(8,128)(2,1)} %refs_0_.3, bf16[2,72,8,128]{3,2,1,0:T(8,128)(2,1)} %refs_1_.5, bf16[4,72,128]{2,1,0:T(8,128)(2,1)} %copy-done.4, ...), custom_call_target="tpu_custom_call" | custom-call | tf_op jit(solution)/shard_map/pallas_call | solution.py:123
  19.6 2.6 %collective-permute-start.4 = (bf16[4,72,128]{2,1,0:T(8,128)(2,1)}, bf16[4,72,128]{2,1,0:T(8,128)(2,1)S(1)}, u32[]{:S(2)}, u32[]{:S(2)}) collective-permute-start(bf16[4,72,128]{2,1,0:T(8,128)(2,1)} %get-tuple-element.25), channel_id=1, source_target_pairs={{0,24},{8,0},{16,8},{24,16},{1,25},{9,1},{17,9},{25,17},{2,26},{10... | collective-permute-start | bytes 221192 | tf_op jit(solution)/shard_map/ppermute | solution.py:141
  22.2 0.0 collective-permute-start.5
  22.2 0.0 collective-permute-start.6
  22.3 0.5 collective-permute-start.7
  22.8 1.1 %collective-permute-done.6.refs_4_ = bf16[1,2304]{1,0:T(2,128)(2,1)S(1)} collective-permute-done((bf16[1,2304]{1,0:T(2,128)(2,1)}, bf16[1,2304]{1,0:T(2,128)(2,1)S(1)}, u32[]{:S(2)}, u32[]{:S(2)}) %collective-permute-start.6) | collective-permute-done | bytes 4640 | tf_op jit(solution)/shard_map/ppermute | solution.py:143
  23.8 3.5 %collective-permute-done.7.refs_5_ = bf16[1,2304]{1,0:T(2,128)(2,1)S(1)} collective-permute-done((bf16[1,2304]{1,0:T(2,128)(2,1)}, bf16[1,2304]{1,0:T(2,128)(2,1)S(1)}, u32[]{:S(2)}, u32[]{:S(2)}) %collective-permute-start.7) | collective-permute-done | bytes 4640 | tf_op jit(solution)/shard_map/ppermute | solution.py:144
  27.4 0.0 collective-permute-done.4.refs_2_
  27.4 0.4 collective-permute-done.5.refs_3_
  27.7 0.2 copy-done.12
  27.9 0.0 copy-done.3
  28.0 0.3 copy-done.6
  28.3 4.3 %shard_map.66 = (bf16[4,72,8,128]{3,2,1,0:T(8,128)(2,1)}, bf16[4,72,128]{2,1,0:T(8,128)(2,1)}, bf16[4,72,128]{2,1,0:T(8,128)(2,1)}, bf16[1,2304]{1,0:T(2,128)(2,1)}, bf16[1,2304]{1,0:T(2,128)(2,1)}) custom-call(bf16[4,72,8,128]{3,2,1,0:T(8,128)(2,1)} %get-tuple-element.24.refs_0_, bf16[2,72,8,128]{3,2,1,0:T(8,128)(2,1)} %refs_1_.5, ...), custom_call_target="tpu_custom_call" | custom-call | tf_op jit(solution)/shard_map/pallas_call | solution.py:123
  32.6 2.6 %collective-permute-start.8 = (bf16[4,72,128]{2,1,0:T(8,128)(2,1)}, bf16[4,72,128]{2,1,0:T(8,128)(2,1)S(1)}, u32[]{:S(2)}, u32[]{:S(2)}) collective-permute-start(bf16[4,72,128]{2,1,0:T(8,128)(2,1)} %get-tuple-element.30), channel_id=1, source_target_pairs={{0,24},{8,0},{16,8},{24,16},{1,25},{9,1},{17,9},{25,17},{2,26},{10... | collective-permute-start | bytes 221192 | tf_op jit(solution)/shard_map/ppermute | solution.py:141
  35.2 0.0 collective-permute-start.9
  35.2 0.0 collective-permute-start.10
  35.2 0.5 collective-permute-start.11
  35.7 1.0 %sort.17 = (s32[8]{0:T(128)}, s32[8]{0:T(128)S(1)}) sort(s32[8]{0:T(128)S(1)} %bitcast.29, s32[8]{0:T(128)S(1)} %iota.13), dimensions={0}, to_apply=%region_0.0 | sort | flops 24 | bytes 128 | tf_op jit(solution)/shard_map/jit(argsort)/sort | solution.py:156
  36.7 0.1 collective-permute-done.10.refs_4_
  36.8 3.5 %collective-permute-done.11.refs_5_ = bf16[1,2304]{1,0:T(2,128)(2,1)S(1)} collective-permute-done((bf16[1,2304]{1,0:T(2,128)(2,1)}, bf16[1,2304]{1,0:T(2,128)(2,1)S(1)}, u32[]{:S(2)}, u32[]{:S(2)}) %collective-permute-start.11) | collective-permute-done | bytes 4640 | tf_op jit(solution)/shard_map/ppermute | solution.py:144
  40.3 0.0 collective-permute-done.8.refs_2_
  40.3 0.4 collective-permute-done.9.refs_3_
  40.7 0.2 copy-done.9
  40.9 0.0 copy-done.2
  40.9 0.4 copy-done.5
  41.3 3.9 %shard_map.67 = bf16[4,72,8,128]{3,2,1,0:T(8,128)(2,1)} custom-call(bf16[4,72,8,128]{3,2,1,0:T(8,128)(2,1)} %get-tuple-element.29.refs_0_, bf16[2,72,8,128]{3,2,1,0:T(8,128)(2,1)} %refs_1_.5, bf16[4,72,128]{2,1,0:T(8,128)(2,1)} %copy-done.2, bf16[4,72,128]{2,1,0:T(8,128)(2,1)} %copy-done.5, bf16[1,2304]{1,0:T(2,128)(2,1)} %copy-done.8, bf16[1,2304]{1,0:T(2,128)(2,1)} %copy-done.9), custom_call_target="tpu_custom_call" | custom-call | tf_op jit(solution)/shard_map/pallas_call | solution.py:123
  45.2 1.4 %fusion.10 = bf16[4,72,128,8]{2,3,1,0:T(8,128)(2,1)S(1)} fusion(bf16[4,72,8,128]{3,2,1,0:T(8,128)(2,1)} %shard_map.67, s32[8]{0:T(128)S(1)} %get-tuple-element.34), kind=kOutput, calls=%fused_computation.14 | convolution fusion | flops 4718656 | bytes 1179680 | tf_op jit(solution)/shard_map/jg,flgy->fljy/dot_general | solution.py:160
  46.6 0.0 copy-start.1
  46.6 0.9 %copy.19 = bf16[4,72,128,8]{2,1,0,3:T(8,128)(2,1)} copy(bf16[4,72,128,8]{2,3,1,0:T(8,128)(2,1)S(1)} %fusion.10) | data formatting | bytes 1179648 | tf_op jit(solution)/shard_map/jg,flgy->fljy/dot_general | solution.py:160
  47.5 3.5 %all-to-all-start = ((bf16[4,72,8,128]{3,1,0,2:T(8,128)(2,1)}), bf16[4,72,8,128]{3,1,0,2:T(8,128)(2,1)S(1)}, u32[]{:S(2)}, u32[]{:S(2)}) async-start(bf16[4,72,8,128]{3,1,0,2:T(8,128)(2,1)} %bitcast.27), calls=%async_computation | async-start | bytes 1179648 | tf_op jit(solution)/shard_map/all_to_all | solution.py:163
  51.7 0.1 select_reduce_fusion
  51.9 15.9 %all-to-all-done = bf16[4,72,8,128]{3,1,0,2:T(8,128)(2,1)S(1)} async-done(((bf16[4,72,8,128]{3,1,0,2:T(8,128)(2,1)}), bf16[4,72,8,128]{3,1,0,2:T(8,128)(2,1)S(1)}, u32[]{:S(2)}, u32[]{:S(2)}) %all-to-all-start) | async-done | bytes 589856 | tf_op jit(solution)/shard_map/all_to_all | solution.py:163
  67.8 0.3 fusion.4
  68.1 0.3 fusion.1
  68.4 0.9 %copy.9 = bf16[4,72,8,128]{3,2,1,0:T(8,128)(2,1)} copy(bf16[4,72,8,128]{3,1,2,0:T(8,128)(2,1)S(1)} %fusion.1) | data formatting | bytes 1179648 | tf_op jit(solution)/shard_map/convert_element_type | solution.py:170
  (21 shorter events, 0.0 us)
Async XLA Ops:
  0.0 67.8 %copy-start = (bf16[1,72,72]{2,1,0:T(8,128)(2,1)S(1)}, bf16[1,72,72]{2,1,0:T(8,128)(2,1)}, u32[]{:S(2)}) copy-start(bf16[1,72,72]{2,1,0:T(8,128)(2,1)} %param.9) | copy-start | bytes 31108
  2.3 33.4 %copy-start.14 = (s32[1,8]{1,0:T(1,128)S(1)}, s32[1,8]{1,0:T(1,128)}, u32[]{:S(2)}) copy-start(s32[1,8]{1,0:T(1,128)} %param.8) | copy-start | bytes 100
  2.3 11.8 %collective-permute-start = (bf16[4,72,128]{2,1,0:T(8,128)(2,1)}, bf16[4,72,128]{2,1,0:T(8,128)(2,1)S(1)}, u32[]{:S(2)}, u32[]{:S(2)}) collective-permute-start(bf16[4,72,128]{2,1,0:T(8,128)(2,1)} %get-tuple-element.20), channel_id=1, source_target_pairs={{0,24},{8,0},{16,8},{24,16},{1,25},{9,1},{17,9},{25,17},{2,26},{10... | collective-permute-start | bytes 221192 | tf_op jit(solution)/shard_map/ppermute | solution.py:141
  6.2 7.9 %collective-permute-start.1 = (bf16[4,72,128]{2,1,0:T(8,128)(2,1)}, bf16[4,72,128]{2,1,0:T(8,128)(2,1)S(1)}, u32[]{:S(2)}, u32[]{:S(2)}) collective-permute-start(bf16[4,72,128]{2,1,0:T(8,128)(2,1)} %get-tuple-element.21), channel_id=1, source_target_pairs={{0,8},{8,16},{16,24},{24,0},{1,9},{9,17},{17,25},{25,1},{2,10},{10... | collective-permute-start | bytes 221192 | tf_op jit(solution)/shard_map/ppermute | solution.py:142
  6.2 4.3 %collective-permute-start.2 = (bf16[1,2304]{1,0:T(2,128)(2,1)}, bf16[1,2304]{1,0:T(2,128)(2,1)S(1)}, u32[]{:S(2)}, u32[]{:S(2)}) collective-permute-start(bf16[1,2304]{1,0:T(2,128)(2,1)} %get-tuple-element.22), channel_id=1, source_target_pairs={{0,7},{1,0},{2,1},{3,2},{4,3},{5,4},{6,5},{7,6},{8,15},{9,8},{10,9... | collective-permute-start | bytes 13832 | tf_op jit(solution)/shard_map/ppermute | solution.py:143
  9.0 5.1 %collective-permute-start.3 = (bf16[1,2304]{1,0:T(2,128)(2,1)}, bf16[1,2304]{1,0:T(2,128)(2,1)S(1)}, u32[]{:S(2)}, u32[]{:S(2)}) collective-permute-start(bf16[1,2304]{1,0:T(2,128)(2,1)} %get-tuple-element.23), channel_id=1, source_target_pairs={{0,1},{1,2},{2,3},{3,4},{4,5},{5,6},{6,7},{7,0},{8,9},{9,10},{10,1... | collective-permute-start | bytes 13832 | tf_op jit(solution)/shard_map/ppermute | solution.py:144
  10.6 3.5 %copy-start.11 = (bf16[1,2304]{1,0:T(2,128)(2,1)}, bf16[1,2304]{1,0:T(2,128)(2,1)S(1)}, u32[]{:S(2)}) copy-start(bf16[1,2304]{1,0:T(2,128)(2,1)S(1)} %collective-permute-done.2.refs_4_) | copy-start | bytes 13828
  14.1 0.6 copy-start.13
  14.1 0.6 copy-start.4
  14.7 0.6 copy-start.7
  19.6 7.8 %collective-permute-start.4 = (bf16[4,72,128]{2,1,0:T(8,128)(2,1)}, bf16[4,72,128]{2,1,0:T(8,128)(2,1)S(1)}, u32[]{:S(2)}, u32[]{:S(2)}) collective-permute-start(bf16[4,72,128]{2,1,0:T(8,128)(2,1)} %get-tuple-element.25), channel_id=1, source_target_pairs={{0,24},{8,0},{16,8},{24,16},{1,25},{9,1},{17,9},{25,17},{2,26},{10... | collective-permute-start | bytes 221192 | tf_op jit(solution)/shard_map/ppermute | solution.py:141
  22.2 5.5 %collective-permute-start.5 = (bf16[4,72,128]{2,1,0:T(8,128)(2,1)}, bf16[4,72,128]{2,1,0:T(8,128)(2,1)S(1)}, u32[]{:S(2)}, u32[]{:S(2)}) collective-permute-start(bf16[4,72,128]{2,1,0:T(8,128)(2,1)} %get-tuple-element.26), channel_id=1, source_target_pairs={{0,8},{8,16},{16,24},{24,0},{1,9},{9,17},{17,25},{25,1},{2,10},{10... | collective-permute-start | bytes 221192 | tf_op jit(solution)/shard_map/ppermute | solution.py:142
  22.2 1.6 %collective-permute-start.6 = (bf16[1,2304]{1,0:T(2,128)(2,1)}, bf16[1,2304]{1,0:T(2,128)(2,1)S(1)}, u32[]{:S(2)}, u32[]{:S(2)}) collective-permute-start(bf16[1,2304]{1,0:T(2,128)(2,1)} %get-tuple-element.27), channel_id=1, source_target_pairs={{0,7},{1,0},{2,1},{3,2},{4,3},{5,4},{6,5},{7,6},{8,15},{9,8},{10,9... | collective-permute-start | bytes 13832 | tf_op jit(solution)/shard_map/ppermute | solution.py:143
  22.3 5.1 %collective-permute-start.7 = (bf16[1,2304]{1,0:T(2,128)(2,1)}, bf16[1,2304]{1,0:T(2,128)(2,1)S(1)}, u32[]{:S(2)}, u32[]{:S(2)}) collective-permute-start(bf16[1,2304]{1,0:T(2,128)(2,1)} %get-tuple-element.28), channel_id=1, source_target_pairs={{0,1},{1,2},{2,3},{3,4},{4,5},{5,6},{6,7},{7,0},{8,9},{9,10},{10,1... | collective-permute-start | bytes 13832 | tf_op jit(solution)/shard_map/ppermute | solution.py:144
  23.8 3.9 %copy-start.10 = (bf16[1,2304]{1,0:T(2,128)(2,1)}, bf16[1,2304]{1,0:T(2,128)(2,1)S(1)}, u32[]{:S(2)}) copy-start(bf16[1,2304]{1,0:T(2,128)(2,1)S(1)} %collective-permute-done.6.refs_4_) | copy-start | bytes 13828
  27.3 0.6 copy-start.12
  27.4 0.6 copy-start.3
  27.7 0.6 copy-start.6
  32.6 7.7 %collective-permute-start.8 = (bf16[4,72,128]{2,1,0:T(8,128)(2,1)}, bf16[4,72,128]{2,1,0:T(8,128)(2,1)S(1)}, u32[]{:S(2)}, u32[]{:S(2)}) collective-permute-start(bf16[4,72,128]{2,1,0:T(8,128)(2,1)} %get-tuple-element.30), channel_id=1, source_target_pairs={{0,24},{8,0},{16,8},{24,16},{1,25},{9,1},{17,9},{25,17},{2,26},{10... | collective-permute-start | bytes 221192 | tf_op jit(solution)/shard_map/ppermute | solution.py:141
  35.2 5.5 %collective-permute-start.9 = (bf16[4,72,128]{2,1,0:T(8,128)(2,1)}, bf16[4,72,128]{2,1,0:T(8,128)(2,1)S(1)}, u32[]{:S(2)}, u32[]{:S(2)}) collective-permute-start(bf16[4,72,128]{2,1,0:T(8,128)(2,1)} %get-tuple-element.31), channel_id=1, source_target_pairs={{0,8},{8,16},{16,24},{24,0},{1,9},{9,17},{17,25},{25,1},{2,10},{10... | collective-permute-start | bytes 221192 | tf_op jit(solution)/shard_map/ppermute | solution.py:142
  35.2 1.6 %collective-permute-start.10 = (bf16[1,2304]{1,0:T(2,128)(2,1)}, bf16[1,2304]{1,0:T(2,128)(2,1)S(1)}, u32[]{:S(2)}, u32[]{:S(2)}) collective-permute-start(bf16[1,2304]{1,0:T(2,128)(2,1)} %get-tuple-element.32), channel_id=1, source_target_pairs={{0,7},{1,0},{2,1},{3,2},{4,3},{5,4},{6,5},{7,6},{8,15},{9,8},{10,9... | collective-permute-start | bytes 13832 | tf_op jit(solution)/shard_map/ppermute | solution.py:143
  35.2 5.1 %collective-permute-start.11 = (bf16[1,2304]{1,0:T(2,128)(2,1)}, bf16[1,2304]{1,0:T(2,128)(2,1)S(1)}, u32[]{:S(2)}, u32[]{:S(2)}) collective-permute-start(bf16[1,2304]{1,0:T(2,128)(2,1)} %get-tuple-element.33), channel_id=1, source_target_pairs={{0,1},{1,2},{2,3},{3,4},{4,5},{5,6},{6,7},{7,0},{8,9},{9,10},{10,1... | collective-permute-start | bytes 13832 | tf_op jit(solution)/shard_map/ppermute | solution.py:144
  36.8 3.9 %copy-start.8 = (bf16[1,2304]{1,0:T(2,128)(2,1)}, bf16[1,2304]{1,0:T(2,128)(2,1)S(1)}, u32[]{:S(2)}) copy-start(bf16[1,2304]{1,0:T(2,128)(2,1)S(1)} %collective-permute-done.10.refs_4_) | copy-start | bytes 13828
  40.3 0.6 copy-start.9
  40.3 0.6 copy-start.2
  40.7 0.6 copy-start.5
  46.6 5.1 %copy-start.1 = (bf16[16,72,72]{2,1,0:T(8,128)(2,1)S(1)}, bf16[16,72,72]{2,1,0:T(8,128)(2,1)}, u32[]{:S(2)}) copy-start(bf16[16,72,72]{2,1,0:T(8,128)(2,1)} %param.11) | copy-start | bytes 497668
  47.5 20.2 %all-to-all-start = ((bf16[4,72,8,128]{3,1,0,2:T(8,128)(2,1)}), bf16[4,72,8,128]{3,1,0,2:T(8,128)(2,1)S(1)}, u32[]{:S(2)}, u32[]{:S(2)}) async-start(bf16[4,72,8,128]{3,1,0,2:T(8,128)(2,1)} %bitcast.27), calls=%async_computation | async-start | bytes 1179648 | tf_op jit(solution)/shard_map/all_to_all | solution.py:163

commit v14 on v13

--- a/solution.py
+++ b/solution.py
@@ -88,10 +88,12 @@
                     top_ref[field, levels_here] = widened[:, 0, :].astype(top_ref.dtype)
                     bottom_ref[field, levels_here] = widened[:, rows - 1, :].astype(bottom_ref.dtype)
         elif emit:
-            new_scr[...] = q_ref[field].astype(jnp.float32)
-        if emit and not step:
-            top_ref[field] = new_scr[:, 0, :].astype(top_ref.dtype)
-            bottom_ref[field] = new_scr[:, rows - 1, :].astype(bottom_ref.dtype)
+            for index in range(levels // block):
+                levels_here = pl.ds(index * block, block)
+                widened = q_ref[field, levels_here].astype(jnp.float32)
+                new_scr[levels_here] = widened
+                top_ref[field, levels_here] = widened[:, 0, :].astype(top_ref.dtype)
+                bottom_ref[field, levels_here] = widened[:, rows - 1, :].astype(bottom_ref.dtype)
         if emit:
             flat = new_scr[...].reshape(planes, cols).astype(jnp.bfloat16)
             pick = lax.broadcasted_iota(jnp.int32, (8, cols), 1)

time: 69.6 us -> 69.4 us (level)
  no operation moved by 1% of the time
where the time goes in v14:
time: 69.4 us; the launch traced here: 69.1 us
  waiting for transfers between devices  29.9 us (43%)
  starting transfers between devices  16.5 us (24%)
  Pallas kernels  14.5 us (21%)
  local copies, waits for them, and re-layouts  4.33 us (6%)
  matrix products  2.02 us (3%)
  other arithmetic  1.11 us (2%)
  between operations  0.74 us (1%)
    all_to_all x1, waiting for transfers between devices, per_device(): lax.all_to_all(ordered, 'tile', split_axis=2, concat_axis=2, tiled=True)  15.9 us
    pallas_call x4, Pallas kernels, stencil_call(): pl.pallas_call(functools.partial(stencil_kernel, step, emit), out_shape=t...  14.5 us
    ppermute x3, waiting for transfers between devices, exchange(): lax.ppermute(last, 'tile', [(i, (i + 1) % tile) for i in range(tile)])  10.5 us
    ppermute x3, starting transfers between devices, exchange(): north = lax.ppermute(top, 'sec', [(i, (i - 1) % sec) for i in range(sec)])  9.14 us
    all_to_all x1, starting transfers between devices, per_device(): lax.all_to_all(ordered, 'tile', split_axis=2, concat_axis=2, tiled=True)  3.54 us
    ppermute x3, waiting for transfers between devices, exchange(): lax.ppermute(first, 'tile', [(i, (i - 1) % tile) for i in range(tile)])  2.78 us
    ppermute x3, starting transfers between devices, exchange(): lax.ppermute(first, 'tile', [(i, (i - 1) % tile) for i in range(tile)])  2.77 us
    unnamed x30, local copies, waits for them, and re-layouts  2.54 us
  transfers between devices with their start and end apart: 13, of which 9 were waited for; matrix products, arithmetic and copies ran while one was open for 2% of the time, Pallas kernels for 0%

profile of v14, /device:TPU:0, one launch (start us, length us, event | category | flops | bytes accessed | tf_op | source)
XLA Modules:
  0.0 69.1 jit_solution(4266019688169984114)
XLA Ops:
  0.0 2.1 %shard_map.64 = (bf16[4,72,128]{2,1,0:T(8,128)(2,1)}, bf16[4,72,128]{2,1,0:T(8,128)(2,1)}, bf16[1,2304]{1,0:T(2,128)(2,1)}, bf16[1,2304]{1,0:T(2,128)(2,1)}) custom-call(bf16[4,72,8,128]{3,2,1,0:T(8,128)(2,1)} %refs_0_.3), custom_call_target="tpu_custom_call" | custom-call | tf_op jit(solution)/shard_map/pallas_call | solution.py:125
  2.1 3.9 %collective-permute-start = (bf16[4,72,128]{2,1,0:T(8,128)(2,1)}, bf16[4,72,128]{2,1,0:T(8,128)(2,1)S(1)}, u32[]{:S(2)}, u32[]{:S(2)}) collective-permute-start(bf16[4,72,128]{2,1,0:T(8,128)(2,1)} %get-tuple-element.20), channel_id=1, source_target_pairs={{0,24},{8,0},{16,8},{24,16},{1,25},{9,1},{17,9},{25,17},{2,26},{10... | collective-permute-start | bytes 221192 | tf_op jit(solution)/shard_map/ppermute | solution.py:143
  6.0 0.0 collective-permute-start.1
  6.0 2.8 %collective-permute-start.2 = (bf16[1,2304]{1,0:T(2,128)(2,1)}, bf16[1,2304]{1,0:T(2,128)(2,1)S(1)}, u32[]{:S(2)}, u32[]{:S(2)}) collective-permute-start(bf16[1,2304]{1,0:T(2,128)(2,1)} %get-tuple-element.22), channel_id=1, source_target_pairs={{0,7},{1,0},{2,1},{3,2},{4,3},{5,4},{6,5},{7,6},{8,15},{9,8},{10,9... | collective-permute-start | bytes 13832 | tf_op jit(solution)/shard_map/ppermute | solution.py:145
  8.8 0.0 collective-permute-start.3
  8.8 1.6 %collective-permute-done.2.refs_4_ = bf16[1,2304]{1,0:T(2,128)(2,1)S(1)} collective-permute-done((bf16[1,2304]{1,0:T(2,128)(2,1)}, bf16[1,2304]{1,0:T(2,128)(2,1)S(1)}, u32[]{:S(2)}, u32[]{:S(2)}) %collective-permute-start.2) | collective-permute-done | bytes 4640 | tf_op jit(solution)/shard_map/ppermute | solution.py:145
  10.4 3.5 %collective-permute-done.3.refs_5_ = bf16[1,2304]{1,0:T(2,128)(2,1)S(1)} collective-permute-done((bf16[1,2304]{1,0:T(2,128)(2,1)}, bf16[1,2304]{1,0:T(2,128)(2,1)S(1)}, u32[]{:S(2)}, u32[]{:S(2)}) %collective-permute-start.3) | collective-permute-done | bytes 4640 | tf_op jit(solution)/shard_map/ppermute | solution.py:146
  13.9 0.0 collective-permute-done.refs_2_
  13.9 0.0 collective-permute-done.1.refs_3_
  13.9 0.6 copy-done.13
  14.5 0.0 copy-done.4
  14.5 0.6 copy-done.7
  15.2 4.2 %shard_map.65 = (bf16[4,72,8,128]{3,2,1,0:T(8,128)(2,1)}, bf16[4,72,128]{2,1,0:T(8,128)(2,1)}, bf16[4,72,128]{2,1,0:T(8,128)(2,1)}, bf16[1,2304]{1,0:T(2,128)(2,1)}, bf16[1,2304]{1,0:T(2,128)(2,1)}) custom-call(bf16[4,72,8,128]{3,2,1,0:T(8,128)(2,1)} %refs_0_.3, bf16[2,72,8,128]{3,2,1,0:T(8,128)(2,1)} %refs_1_.5, bf16[4,72,128]{2,1,0:T(8,128)(2,1)} %copy-done.4, ...), custom_call_target="tpu_custom_call" | custom-call | tf_op jit(solution)/shard_map/pallas_call | solution.py:125
  19.4 2.6 %collective-permute-start.4 = (bf16[4,72,128]{2,1,0:T(8,128)(2,1)}, bf16[4,72,128]{2,1,0:T(8,128)(2,1)S(1)}, u32[]{:S(2)}, u32[]{:S(2)}) collective-permute-start(bf16[4,72,128]{2,1,0:T(8,128)(2,1)} %get-tuple-element.25), channel_id=1, source_target_pairs={{0,24},{8,0},{16,8},{24,16},{1,25},{9,1},{17,9},{25,17},{2,26},{10... | collective-permute-start | bytes 221192 | tf_op jit(solution)/shard_map/ppermute | solution.py:143
  22.1 0.0 collective-permute-start.5
  22.1 0.0 collective-permute-start.6
  22.1 0.5 collective-permute-start.7
  22.6 1.1 %collective-permute-done.6.refs_4_ = bf16[1,2304]{1,0:T(2,128)(2,1)S(1)} collective-permute-done((bf16[1,2304]{1,0:T(2,128)(2,1)}, bf16[1,2304]{1,0:T(2,128)(2,1)S(1)}, u32[]{:S(2)}, u32[]{:S(2)}) %collective-permute-start.6) | collective-permute-done | bytes 4640 | tf_op jit(solution)/shard_map/ppermute | solution.py:145
  23.6 3.5 %collective-permute-done.7.refs_5_ = bf16[1,2304]{1,0:T(2,128)(2,1)S(1)} collective-permute-done((bf16[1,2304]{1,0:T(2,128)(2,1)}, bf16[1,2304]{1,0:T(2,128)(2,1)S(1)}, u32[]{:S(2)}, u32[]{:S(2)}) %collective-permute-start.7) | collective-permute-done | bytes 4640 | tf_op jit(solution)/shard_map/ppermute | solution.py:146
  27.2 0.0 collective-permute-done.4.refs_2_
  27.2 0.4 collective-permute-done.5.refs_3_
  27.5 0.2 copy-done.12
  27.7 0.0 copy-done.3
  27.8 0.3 copy-done.6
  28.1 4.3 %shard_map.66 = (bf16[4,72,8,128]{3,2,1,0:T(8,128)(2,1)}, bf16[4,72,128]{2,1,0:T(8,128)(2,1)}, bf16[4,72,128]{2,1,0:T(8,128)(2,1)}, bf16[1,2304]{1,0:T(2,128)(2,1)}, bf16[1,2304]{1,0:T(2,128)(2,1)}) custom-call(bf16[4,72,8,128]{3,2,1,0:T(8,128)(2,1)} %get-tuple-element.24.refs_0_, bf16[2,72,8,128]{3,2,1,0:T(8,128)(2,1)} %refs_1_.5, ...), custom_call_target="tpu_custom_call" | custom-call | tf_op jit(solution)/shard_map/pallas_call | solution.py:125
  32.4 2.6 %collective-permute-start.8 = (bf16[4,72,128]{2,1,0:T(8,128)(2,1)}, bf16[4,72,128]{2,1,0:T(8,128)(2,1)S(1)}, u32[]{:S(2)}, u32[]{:S(2)}) collective-permute-start(bf16[4,72,128]{2,1,0:T(8,128)(2,1)} %get-tuple-element.30), channel_id=1, source_target_pairs={{0,24},{8,0},{16,8},{24,16},{1,25},{9,1},{17,9},{25,17},{2,26},{10... | collective-permute-start | bytes 221192 | tf_op jit(solution)/shard_map/ppermute | solution.py:143
  35.0 0.0 collective-permute-start.9
  35.0 0.0 collective-permute-start.10
  35.0 0.5 collective-permute-start.11
  35.5 1.0 %sort.17 = (s32[8]{0:T(128)}, s32[8]{0:T(128)S(1)}) sort(s32[8]{0:T(128)S(1)} %bitcast.29, s32[8]{0:T(128)S(1)} %iota.13), dimensions={0}, to_apply=%region_0.0 | sort | flops 24 | bytes 128 | tf_op jit(solution)/shard_map/jit(argsort)/sort | solution.py:158
  36.5 0.1 collective-permute-done.10.refs_4_
  36.6 3.5 %collective-permute-done.11.refs_5_ = bf16[1,2304]{1,0:T(2,128)(2,1)S(1)} collective-permute-done((bf16[1,2304]{1,0:T(2,128)(2,1)}, bf16[1,2304]{1,0:T(2,128)(2,1)S(1)}, u32[]{:S(2)}, u32[]{:S(2)}) %collective-permute-start.11) | collective-permute-done | bytes 4640 | tf_op jit(solution)/shard_map/ppermute | solution.py:146
  40.1 0.0 collective-permute-done.8.refs_2_
  40.1 0.4 collective-permute-done.9.refs_3_
  40.5 0.2 copy-done.9
  40.7 0.0 copy-done.2
  40.7 0.4 copy-done.5
  41.1 3.9 %shard_map.67 = bf16[4,72,8,128]{3,2,1,0:T(8,128)(2,1)} custom-call(bf16[4,72,8,128]{3,2,1,0:T(8,128)(2,1)} %get-tuple-element.29.refs_0_, bf16[2,72,8,128]{3,2,1,0:T(8,128)(2,1)} %refs_1_.5, bf16[4,72,128]{2,1,0:T(8,128)(2,1)} %copy-done.2, bf16[4,72,128]{2,1,0:T(8,128)(2,1)} %copy-done.5, bf16[1,2304]{1,0:T(2,128)(2,1)} %copy-done.8, bf16[1,2304]{1,0:T(2,128)(2,1)} %copy-done.9), custom_call_target="tpu_custom_call" | custom-call | tf_op jit(solution)/shard_map/pallas_call | solution.py:125
  45.0 1.4 %fusion.10 = bf16[4,72,128,8]{2,3,1,0:T(8,128)(2,1)S(1)} fusion(bf16[4,72,8,128]{3,2,1,0:T(8,128)(2,1)} %shard_map.67, s32[8]{0:T(128)S(1)} %get-tuple-element.34), kind=kOutput, calls=%fused_computation.14 | convolution fusion | flops 4718656 | bytes 1179680 | tf_op jit(solution)/shard_map/jg,flgy->fljy/dot_general | solution.py:162
  46.4 0.0 copy-start.1
  46.4 0.9 %copy.19 = bf16[4,72,128,8]{2,1,0,3:T(8,128)(2,1)} copy(bf16[4,72,128,8]{2,3,1,0:T(8,128)(2,1)S(1)} %fusion.10) | data formatting | bytes 1179648 | tf_op jit(solution)/shard_map/jg,flgy->fljy/dot_general | solution.py:162
  47.3 3.5 %all-to-all-start = ((bf16[4,72,8,128]{3,1,0,2:T(8,128)(2,1)}), bf16[4,72,8,128]{3,1,0,2:T(8,128)(2,1)S(1)}, u32[]{:S(2)}, u32[]{:S(2)}) async-start(bf16[4,72,8,128]{3,1,0,2:T(8,128)(2,1)} %bitcast.27), calls=%async_computation | async-start | bytes 1179648 | tf_op jit(solution)/shard_map/all_to_all | solution.py:165
  51.5 0.0 copy-done.1
  51.6 0.1 select_reduce_fusion
  51.7 15.9 %all-to-all-done = bf16[4,72,8,128]{3,1,0,2:T(8,128)(2,1)S(1)} async-done(((bf16[4,72,8,128]{3,1,0,2:T(8,128)(2,1)}), bf16[4,72,8,128]{3,1,0,2:T(8,128)(2,1)S(1)}, u32[]{:S(2)}, u32[]{:S(2)}) %all-to-all-start) | async-done | bytes 589856 | tf_op jit(solution)/shard_map/all_to_all | solution.py:165
  67.6 0.3 fusion.4
  67.9 0.3 fusion.1
  68.2 0.9 %copy.9 = bf16[4,72,8,128]{3,2,1,0:T(8,128)(2,1)} copy(bf16[4,72,8,128]{3,1,2,0:T(8,128)(2,1)S(1)} %fusion.1) | data formatting | bytes 1179648 | tf_op jit(solution)/shard_map/convert_element_type | solution.py:172
  (21 shorter events, 0.0 us)
Async XLA Ops:
  0.0 67.6 %copy-start = (bf16[1,72,72]{2,1,0:T(8,128)(2,1)S(1)}, bf16[1,72,72]{2,1,0:T(8,128)(2,1)}, u32[]{:S(2)}) copy-start(bf16[1,72,72]{2,1,0:T(8,128)(2,1)} %param.9) | copy-start | bytes 31108
  2.1 33.4 %copy-start.14 = (s32[1,8]{1,0:T(1,128)S(1)}, s32[1,8]{1,0:T(1,128)}, u32[]{:S(2)}) copy-start(s32[1,8]{1,0:T(1,128)} %param.8) | copy-start | bytes 100
  2.1 11.8 %collective-permute-start = (bf16[4,72,128]{2,1,0:T(8,128)(2,1)}, bf16[4,72,128]{2,1,0:T(8,128)(2,1)S(1)}, u32[]{:S(2)}, u32[]{:S(2)}) collective-permute-start(bf16[4,72,128]{2,1,0:T(8,128)(2,1)} %get-tuple-element.20), channel_id=1, source_target_pairs={{0,24},{8,0},{16,8},{24,16},{1,25},{9,1},{17,9},{25,17},{2,26},{10... | collective-permute-start | bytes 221192 | tf_op jit(solution)/shard_map/ppermute | solution.py:143
  6.0 7.9 %collective-permute-start.1 = (bf16[4,72,128]{2,1,0:T(8,128)(2,1)}, bf16[4,72,128]{2,1,0:T(8,128)(2,1)S(1)}, u32[]{:S(2)}, u32[]{:S(2)}) collective-permute-start(bf16[4,72,128]{2,1,0:T(8,128)(2,1)} %get-tuple-element.21), channel_id=1, source_target_pairs={{0,8},{8,16},{16,24},{24,0},{1,9},{9,17},{17,25},{25,1},{2,10},{10... | collective-permute-start | bytes 221192 | tf_op jit(solution)/shard_map/ppermute | solution.py:144
  6.0 4.3 %collective-permute-start.2 = (bf16[1,2304]{1,0:T(2,128)(2,1)}, bf16[1,2304]{1,0:T(2,128)(2,1)S(1)}, u32[]{:S(2)}, u32[]{:S(2)}) collective-permute-start(bf16[1,2304]{1,0:T(2,128)(2,1)} %get-tuple-element.22), channel_id=1, source_target_pairs={{0,7},{1,0},{2,1},{3,2},{4,3},{5,4},{6,5},{7,6},{8,15},{9,8},{10,9... | collective-permute-start | bytes 13832 | tf_op jit(solution)/shard_map/ppermute | solution.py:145
  8.8 5.1 %collective-permute-start.3 = (bf16[1,2304]{1,0:T(2,128)(2,1)}, bf16[1,2304]{1,0:T(2,128)(2,1)S(1)}, u32[]{:S(2)}, u32[]{:S(2)}) collective-permute-start(bf16[1,2304]{1,0:T(2,128)(2,1)} %get-tuple-element.23), channel_id=1, source_target_pairs={{0,1},{1,2},{2,3},{3,4},{4,5},{5,6},{6,7},{7,0},{8,9},{9,10},{10,1... | collective-permute-start | bytes 13832 | tf_op jit(solution)/shard_map/ppermute | solution.py:146
  10.4 3.5 %copy-start.11 = (bf16[1,2304]{1,0:T(2,128)(2,1)}, bf16[1,2304]{1,0:T(2,128)(2,1)S(1)}, u32[]{:S(2)}) copy-start(bf16[1,2304]{1,0:T(2,128)(2,1)S(1)} %collective-permute-done.2.refs_4_) | copy-start | bytes 13828
  13.9 0.6 copy-start.13
  13.9 0.6 copy-start.4
  14.5 0.6 copy-start.7
  19.4 7.8 %collective-permute-start.4 = (bf16[4,72,128]{2,1,0:T(8,128)(2,1)}, bf16[4,72,128]{2,1,0:T(8,128)(2,1)S(1)}, u32[]{:S(2)}, u32[]{:S(2)}) collective-permute-start(bf16[4,72,128]{2,1,0:T(8,128)(2,1)} %get-tuple-element.25), channel_id=1, source_target_pairs={{0,24},{8,0},{16,8},{24,16},{1,25},{9,1},{17,9},{25,17},{2,26},{10... | collective-permute-start | bytes 221192 | tf_op jit(solution)/shard_map/ppermute | solution.py:143
  22.1 5.5 %collective-permute-start.5 = (bf16[4,72,128]{2,1,0:T(8,128)(2,1)}, bf16[4,72,128]{2,1,0:T(8,128)(2,1)S(1)}, u32[]{:S(2)}, u32[]{:S(2)}) collective-permute-start(bf16[4,72,128]{2,1,0:T(8,128)(2,1)} %get-tuple-element.26), channel_id=1, source_target_pairs={{0,8},{8,16},{16,24},{24,0},{1,9},{9,17},{17,25},{25,1},{2,10},{10... | collective-permute-start | bytes 221192 | tf_op jit(solution)/shard_map/ppermute | solution.py:144
  22.1 1.6 %collective-permute-start.6 = (bf16[1,2304]{1,0:T(2,128)(2,1)}, bf16[1,2304]{1,0:T(2,128)(2,1)S(1)}, u32[]{:S(2)}, u32[]{:S(2)}) collective-permute-start(bf16[1,2304]{1,0:T(2,128)(2,1)} %get-tuple-element.27), channel_id=1, source_target_pairs={{0,7},{1,0},{2,1},{3,2},{4,3},{5,4},{6,5},{7,6},{8,15},{9,8},{10,9... | collective-permute-start | bytes 13832 | tf_op jit(solution)/shard_map/ppermute | solution.py:145
  22.1 5.1 %collective-permute-start.7 = (bf16[1,2304]{1,0:T(2,128)(2,1)}, bf16[1,2304]{1,0:T(2,128)(2,1)S(1)}, u32[]{:S(2)}, u32[]{:S(2)}) collective-permute-start(bf16[1,2304]{1,0:T(2,128)(2,1)} %get-tuple-element.28), channel_id=1, source_target_pairs={{0,1},{1,2},{2,3},{3,4},{4,5},{5,6},{6,7},{7,0},{8,9},{9,10},{10,1... | collective-permute-start | bytes 13832 | tf_op jit(solution)/shard_map/ppermute | solution.py:146
  23.6 3.9 %copy-start.10 = (bf16[1,2304]{1,0:T(2,128)(2,1)}, bf16[1,2304]{1,0:T(2,128)(2,1)S(1)}, u32[]{:S(2)}) copy-start(bf16[1,2304]{1,0:T(2,128)(2,1)S(1)} %collective-permute-done.6.refs_4_) | copy-start | bytes 13828
  27.2 0.6 copy-start.12
  27.2 0.6 copy-start.3
  27.5 0.6 copy-start.6
  32.4 7.7 %collective-permute-start.8 = (bf16[4,72,128]{2,1,0:T(8,128)(2,1)}, bf16[4,72,128]{2,1,0:T(8,128)(2,1)S(1)}, u32[]{:S(2)}, u32[]{:S(2)}) collective-permute-start(bf16[4,72,128]{2,1,0:T(8,128)(2,1)} %get-tuple-element.30), channel_id=1, source_target_pairs={{0,24},{8,0},{16,8},{24,16},{1,25},{9,1},{17,9},{25,17},{2,26},{10... | collective-permute-start | bytes 221192 | tf_op jit(solution)/shard_map/ppermute | solution.py:143
  35.0 5.5 %collective-permute-start.9 = (bf16[4,72,128]{2,1,0:T(8,128)(2,1)}, bf16[4,72,128]{2,1,0:T(8,128)(2,1)S(1)}, u32[]{:S(2)}, u32[]{:S(2)}) collective-permute-start(bf16[4,72,128]{2,1,0:T(8,128)(2,1)} %get-tuple-element.31), channel_id=1, source_target_pairs={{0,8},{8,16},{16,24},{24,0},{1,9},{9,17},{17,25},{25,1},{2,10},{10... | collective-permute-start | bytes 221192 | tf_op jit(solution)/shard_map/ppermute | solution.py:144
  35.0 1.6 %collective-permute-start.10 = (bf16[1,2304]{1,0:T(2,128)(2,1)}, bf16[1,2304]{1,0:T(2,128)(2,1)S(1)}, u32[]{:S(2)}, u32[]{:S(2)}) collective-permute-start(bf16[1,2304]{1,0:T(2,128)(2,1)} %get-tuple-element.32), channel_id=1, source_target_pairs={{0,7},{1,0},{2,1},{3,2},{4,3},{5,4},{6,5},{7,6},{8,15},{9,8},{10,9... | collective-permute-start | bytes 13832 | tf_op jit(solution)/shard_map/ppermute | solution.py:145
  35.0 5.1 %collective-permute-start.11 = (bf16[1,2304]{1,0:T(2,128)(2,1)}, bf16[1,2304]{1,0:T(2,128)(2,1)S(1)}, u32[]{:S(2)}, u32[]{:S(2)}) collective-permute-start(bf16[1,2304]{1,0:T(2,128)(2,1)} %get-tuple-element.33), channel_id=1, source_target_pairs={{0,1},{1,2},{2,3},{3,4},{4,5},{5,6},{6,7},{7,0},{8,9},{9,10},{10,1... | collective-permute-start | bytes 13832 | tf_op jit(solution)/shard_map/ppermute | solution.py:146
  36.6 3.9 %copy-start.8 = (bf16[1,2304]{1,0:T(2,128)(2,1)}, bf16[1,2304]{1,0:T(2,128)(2,1)S(1)}, u32[]{:S(2)}) copy-start(bf16[1,2304]{1,0:T(2,128)(2,1)S(1)} %collective-permute-done.10.refs_4_) | copy-start | bytes 13828
  40.1 0.6 copy-start.9
  40.1 0.6 copy-start.2
  40.5 0.6 copy-start.5
  46.4 5.1 %copy-start.1 = (bf16[16,72,72]{2,1,0:T(8,128)(2,1)S(1)}, bf16[16,72,72]{2,1,0:T(8,128)(2,1)}, u32[]{:S(2)}) copy-start(bf16[16,72,72]{2,1,0:T(8,128)(2,1)} %param.11) | copy-start | bytes 497668
  47.3 20.2 %all-to-all-start = ((bf16[4,72,8,128]{3,1,0,2:T(8,128)(2,1)}), bf16[4,72,8,128]{3,1,0,2:T(8,128)(2,1)S(1)}, u32[]{:S(2)}, u32[]{:S(2)}) async-start(bf16[4,72,8,128]{3,1,0,2:T(8,128)(2,1)} %bitcast.27), calls=%async_computation | async-start | bytes 1179648 | tf_op jit(solution)/shard_map/all_to_all | solution.py:165
